TPU v7x, 32 devices: a whole 2x2x4 slice. The times are simulated.
32 devices in a mesh: dp: 8 (over y, x, core), mp: 4 (over z).
Axes of the slice: x: 2, y: 2, z: 4, core: 2. Of those that a mesh axis runs over, the one named last changes fastest.
Arguments:
- tokens: bfloat16 [16384, 2048], P(('dp', 'mp')), may hold values from -6 to 6
- norm1_gain: float32 [2048], replicated, may hold values from 0.5 to 1.5
- w_query: bfloat16 [2048, 2048], P(None, 'mp'), may hold values from -0.125 to 0.125
- w_key: bfloat16 [2048, 2048], P(None, 'mp'), may hold values from -0.125 to 0.125
- w_value: bfloat16 [2048, 2048], P(None, 'mp'), may hold values from -0.125 to 0.125
- w_out: bfloat16 [2048, 2048], P('mp'), may hold values from -1 to 1
- gate_logit: float32 [16], P('mp'), may hold values from -1.5 to 1.5
- norm2_gain: float32 [2048], replicated, may hold values from 0.5 to 1.5
- w_gate: bfloat16 [2048, 8192], P(None, 'mp'), may hold values from -0.125 to 0.125
- w_up: bfloat16 [2048, 8192], P(None, 'mp'), may hold values from -0.125 to 0.125
- w_down: bfloat16 [8192, 2048], P('mp'), may hold values from -0.0625 to 0.0625
- doc_lengths: int32 [32], replicated, may hold values from 1 to 8192, 15872 in all
- out_grad: bfloat16 [16384, 2048], P(('dp', 'mp')), may hold values from -6 to 6
Outputs:
- output: bfloat16 [16384, 2048], P(('dp', 'mp'))
- input_grad: float32 [16384, 2048], P(('dp', 'mp'))
- grad_norm1_gain: float32 [2048], replicated
- grad_w_query: float32 [2048, 2048], P('dp', 'mp')
- grad_w_key: float32 [2048, 2048], P('dp', 'mp')
- grad_w_value: float32 [2048, 2048], P('dp', 'mp')
- grad_w_out: float32 [2048, 2048], P('mp', 'dp')
- grad_gate_logit: float32 [16], replicated
- grad_norm2_gain: float32 [2048], replicated
- grad_w_gate: float32 [2048, 8192], P('dp', 'mp')
- grad_w_up: float32 [2048, 8192], P('dp', 'mp')
- grad_w_down: float32 [8192, 2048], P('mp', 'dp')
Inputs may be any that keep to these rules, and one draw needn't show every extreme that they name: `doc_lengths`: the documents lie one after another from position 0; their lengths sum to 15872, the last 512 positions are padding, and the longest document has exactly 8192 positions.
All inputs are finite; a program needn't handle non-finite values.
Results may differ from a plain program's by a relative error of at most 0.02.
Values may be sent and summed in bfloat16 or wider, within the bound.
No kernel may reach another device: no remote copies, remote signals or barrier semaphores. Data moves between devices by JAX's collectives and lax.ppermute only.
A program may use at most 320 MiB of HBM per device.

v0:
```python
import math

import jax
import jax.numpy as jnp
from jax import lax
from jax.sharding import PartitionSpec as P

SEG = 2048


eps_norm = 1e-05
neg_fill = -1e30
highest = lax.Precision.HIGHEST


def carried_in(value, axis, combine, identity):
    size, place = (lax.axis_size(axis), lax.axis_index(axis))
    everything = jax.tree.map(lambda part: lax.all_gather(part, axis), value)
    start = jax.tree.map(
        lambda part, zero: jnp.broadcast_to(jnp.asarray(zero, part.dtype), part.shape),
        value,
        identity,
    )

    def carried_hop(k, before):
        reached = k < place
        new = combine(before, jax.tree.map(lambda part: part[k], everything))
        return jax.tree.map(lambda a, b: jnp.where(reached, a, b), new, before)

    return lax.fori_loop(0, size, carried_hop, start)


def prefix(value, axis, combine, identity):
    size, place = (lax.axis_size(axis), lax.axis_index(axis))
    everything = jax.tree.map(
        lambda part, kind: lax.all_gather(part.astype(kind), axis),
        value,
        jax.tree.map(lambda a: jnp.bfloat16 if a.dtype == jnp.float32 else a.dtype, value),
    )
    start = jax.tree.map(
        lambda part, zero: jnp.broadcast_to(jnp.asarray(zero, part.dtype), part.shape),
        value,
        identity,
    )

    def prefix_hop(k, before):
        at = size - 1 - k
        reached = at > place
        new = combine(
            before, jax.tree.map(lambda part, own: part[at].astype(own.dtype), everything, value)
        )
        return jax.tree.map(lambda a, b: jnp.where(reached, a, b), new, before)

    return lax.fori_loop(0, size, prefix_hop, start)


def inverse_rms(values):
    return lax.rsqrt(jnp.mean(values * values, axis=-1, keepdims=True) + eps_norm)


def norm_backward(values, inverse, gain, upstream):
    scaled = upstream * gain
    inner = jnp.mean(values * scaled, axis=-1, keepdims=True)
    return inverse * scaled - values * inverse * inverse * inverse * inner


def feature(values):
    return jnp.where(values > 0, values + 1.0, jnp.exp(jnp.minimum(values, 0.0)))


def feature_slope(values):
    return jnp.where(values > 0, 1.0, jnp.exp(jnp.minimum(values, 0.0)))


def link_states(earlier, later):
    return (
        earlier[0] * later[0],
        later[0] * earlier[1] + later[1],
        later[0] * earlier[2] + later[2],
    )


def fold_states(state, item):
    return (link_states(state, item), None)


def document_ids(doc_lengths, first, count):
    bounds = jnp.cumsum(doc_lengths)
    position = first + jnp.arange(count, dtype=jnp.int32)
    before = jnp.sum((bounds[None, :] <= position[:, None]).astype(jnp.int32), axis=1)
    return jnp.where(position < bounds[-1], before, doc_lengths.shape[0] + position)


def block_allowed(doc_index, row_start, seg_start, block_rows):
    query_docs = lax.dynamic_slice_in_dim(doc_index, row_start, block_rows, 0)
    query_pos = row_start + jnp.arange(block_rows, dtype=jnp.int32)
    key_pos = seg_start + jnp.arange(SEG, dtype=jnp.int32)
    return (key_pos[None, :] <= query_pos[:, None]) & (doc_index[None, :] == query_docs[:, None])


def local(
    tokens,
    norm1_gain,
    w_query,
    w_key,
    w_value,
    w_out,
    gate_logit,
    norm2_gain,
    w_gate,
    w_up,
    w_down,
    doc_lengths,
    out_grad,
):
    heads_here = gate_logit.shape[0]
    head_size = w_query.shape[1] // heads_here
    local_rows = tokens.shape[0]
    group_rows = local_rows * lax.axis_size("mp")
    seg_count = group_rows // SEG
    block_rows = min(512, SEG)
    block_count = group_rows // block_rows
    score_scale = 1.0 / math.sqrt(head_size)
    group_first = lax.axis_index("dp") * group_rows
    shifted_ids = document_ids(doc_lengths, group_first - 1, group_rows + 1)
    doc_index = shifted_ids[1:]
    before_doc = jnp.where(group_first > 0, shifted_ids[0], -1)
    seg_docs = doc_index.reshape(seg_count, SEG)
    seg_first = seg_docs[:, 0]
    seg_last = seg_docs[:, -1]
    prev_last = jnp.concatenate([before_doc[None], seg_last[:-1]])
    cont_flag = jnp.where(seg_first == prev_last, 1.0, 0.0).astype(jnp.float32)
    keep_flag = jnp.where(seg_last == prev_last, 1.0, 0.0).astype(jnp.float32)
    read_mask = jnp.where(seg_docs == seg_first[:, None], 1.0, 0.0).astype(jnp.float32)
    write_mask = jnp.where(seg_docs == seg_last[:, None], 1.0, 0.0).astype(jnp.float32)
    seg_shape = (seg_count, SEG, heads_here, head_size)
    head_shape = (group_rows, heads_here, head_size)
    x_rows = tokens.astype(jnp.float32)
    inverse1 = inverse_rms(x_rows)
    normed1 = (x_rows * inverse1 * norm1_gain).astype(jnp.bfloat16)
    normed1_all = lax.all_gather(normed1, "mp", axis=0, tiled=True)
    query_rows = (
        jnp.dot(normed1_all, w_query, preferred_element_type=jnp.float32)
        .astype(jnp.bfloat16)
        .reshape(head_shape)
    )
    key_rows = (
        jnp.dot(normed1_all, w_key, preferred_element_type=jnp.float32)
        .astype(jnp.bfloat16)
        .reshape(head_shape)
    )
    value_rows = (
        jnp.dot(normed1_all, w_value, preferred_element_type=jnp.float32)
        .astype(jnp.bfloat16)
        .reshape(head_shape)
    )

    def block_scores(block_index):
        row_start = block_index * block_rows
        seg_start = row_start // SEG * SEG
        query_block = lax.dynamic_slice_in_dim(query_rows, row_start, block_rows, 0)
        allowed = block_allowed(doc_index, row_start, seg_start, block_rows)
        raw_scores = jnp.einsum(
            "qhd,khd->hqk", query_block, key_rows, preferred_element_type=jnp.float32
        )
        scores = jnp.where(allowed[None], raw_scores * score_scale, neg_fill)
        return (row_start, seg_start, query_block, key_rows, value_rows, scores)

    def attend(block_index):
        _, _, _, _, value_seg, scores = block_scores(block_index)
        row_max = jnp.max(scores, axis=-1, keepdims=True)
        weights_exp = jnp.exp(scores - row_max)
        row_sum = jnp.sum(weights_exp, axis=-1, keepdims=True)
        prob_low = (weights_exp / row_sum).astype(jnp.bfloat16)
        block_out = jnp.einsum(
            "hqk,khd->qhd", prob_low, value_seg, preferred_element_type=jnp.float32
        )
        return (block_out, row_max[..., 0] + jnp.log(row_sum[..., 0]))

    dot_blocks, log_sums = lax.map(attend, jnp.arange(block_count, dtype=jnp.int32))
    dot_out = dot_blocks.reshape(head_shape)
    query_f = query_rows.astype(jnp.float32).reshape(seg_shape)
    key_f = key_rows.astype(jnp.float32).reshape(seg_shape)
    value_f = value_rows.astype(jnp.float32).reshape(seg_shape)
    sig_q = feature(query_f)
    sig_k = feature(key_f)
    updates = jnp.einsum("st,sthd,sthe->shde", write_mask, sig_k, value_f, precision=highest)
    norm_updates = jnp.einsum("st,sthd->shd", write_mask, sig_k, precision=highest)
    start_state = (
        jnp.ones((1,), jnp.float32),
        jnp.zeros(updates.shape[1:], jnp.float32),
        jnp.zeros(norm_updates.shape[1:], jnp.float32),
    )
    summary, _ = lax.scan(fold_states, start_state, (keep_flag[:, None], updates, norm_updates))
    _, memory_in, norm_in = carried_in(summary, "dp", link_states, start_state)

    def carry_forward(state, item):
        flag, read_flag, update, norm_update = item
        memory, norm_sum = state
        return (
            (flag * memory + update, flag * norm_sum + norm_update),
            (read_flag * memory, read_flag * norm_sum),
        )

    _, (read_mem, read_norm) = lax.scan(
        carry_forward, (memory_in, norm_in), (keep_flag, cont_flag, updates, norm_updates)
    )
    numer = jnp.einsum("sthd,shde->sthe", sig_q, read_mem, precision=highest)
    denom_raw = jnp.einsum("sthd,shd->sth", sig_q, read_norm, precision=highest)
    denom = jnp.maximum(denom_raw, 1.0)
    mem_out = (read_mask[:, :, None, None] * numer / denom[..., None]).reshape(head_shape)
    gate_vec = jax.nn.sigmoid(gate_logit)
    gate = gate_vec[None, :, None]
    mixed = (
        (gate * mem_out + (1.0 - gate) * dot_out)
        .astype(jnp.bfloat16)
        .reshape(group_rows, heads_here * head_size)
    )
    piece = mixed
    attn_sum = lax.psum_scatter(
        jnp.dot(piece, w_out, preferred_element_type=jnp.float32),
        "mp",
        scatter_dimension=0,
        tiled=True,
    )
    resid = x_rows + attn_sum
    inverse2 = inverse_rms(resid)
    normed2 = (resid * inverse2 * norm2_gain).astype(jnp.bfloat16)
    normed2_all = lax.all_gather(normed2, "mp", axis=0, tiled=True)
    gate_pre = jnp.dot(normed2_all, w_gate, preferred_element_type=jnp.float32).astype(jnp.bfloat16)
    up_pre = jnp.dot(normed2_all, w_up, preferred_element_type=jnp.float32).astype(jnp.bfloat16)
    gate_f = gate_pre.astype(jnp.float32)
    up_f = up_pre.astype(jnp.float32)
    sig_gate = jax.nn.sigmoid(gate_f)
    act = (gate_f * sig_gate * up_f).astype(jnp.bfloat16)
    piece = act
    mlp_sum = lax.psum_scatter(
        jnp.dot(piece, w_down, preferred_element_type=jnp.float32).astype(jnp.bfloat16),
        "mp",
        scatter_dimension=0,
        tiled=True,
    ).astype(jnp.float32)
    output = (resid + mlp_sum).astype(jnp.bfloat16)
    grad_rows_all = lax.all_gather(out_grad, "mp", axis=0, tiled=True)
    d_act = jnp.dot(grad_rows_all, w_down.T, preferred_element_type=jnp.float32)
    grad_down = jnp.dot(act.T, grad_rows_all, preferred_element_type=jnp.float32)
    d_gate = (d_act * up_f * sig_gate * (1.0 + gate_f * (1.0 - sig_gate))).astype(jnp.bfloat16)
    d_up = (d_act * gate_f * sig_gate).astype(jnp.bfloat16)
    grad_gate = jnp.dot(normed2_all.T, d_gate, preferred_element_type=jnp.float32)
    grad_up = jnp.dot(normed2_all.T, d_up, preferred_element_type=jnp.float32)
    d_norm2 = lax.psum_scatter(
        (
            jnp.dot(d_gate, w_gate.T, preferred_element_type=jnp.float32)
            + jnp.dot(d_up, w_up.T, preferred_element_type=jnp.float32)
        ).astype(jnp.bfloat16),
        "mp",
        scatter_dimension=0,
        tiled=True,
    ).astype(jnp.float32)
    gain2_part = jnp.sum(d_norm2 * resid * inverse2, axis=0)
    d_resid = out_grad.astype(jnp.float32) + norm_backward(resid, inverse2, norm2_gain, d_norm2)
    resid_grad_all = lax.all_gather(d_resid.astype(jnp.bfloat16), "mp", axis=0, tiled=True)
    grad_out = jnp.dot(mixed.T, resid_grad_all, preferred_element_type=jnp.float32)
    d_mixed = jnp.dot(resid_grad_all, w_out.T, preferred_element_type=jnp.float32).reshape(
        head_shape
    )
    gate_part = jnp.sum(d_mixed * (mem_out - dot_out), axis=(0, 2)) * gate_vec * (1.0 - gate_vec)
    d_dot = ((1.0 - gate) * d_mixed).astype(jnp.bfloat16)
    d_mem = (gate * d_mixed).reshape(seg_shape)

    def attend_back(carry, block_index):
        key_acc, value_acc = carry
        row_start, seg_start, query_block, key_seg, value_seg, scores = block_scores(block_index)
        probs_full = jnp.exp(scores - log_sums[block_index][..., None])
        d_block = lax.dynamic_slice_in_dim(d_dot, row_start, block_rows, 0)
        d_probs = jnp.einsum("qhd,khd->hqk", d_block, value_seg, preferred_element_type=jnp.float32)
        inner = jnp.sum(probs_full * d_probs, axis=-1, keepdims=True)
        d_raw = (probs_full * (d_probs - inner) * score_scale).astype(jnp.bfloat16)
        d_query_block = jnp.einsum(
            "hqk,khd->qhd", d_raw, key_seg, preferred_element_type=jnp.float32
        )
        d_key_seg = jnp.einsum(
            "hqk,qhd->khd", d_raw, query_block, preferred_element_type=jnp.float32
        )
        d_value_seg = jnp.einsum(
            "hqk,qhd->khd",
            probs_full.astype(jnp.bfloat16),
            d_block,
            preferred_element_type=jnp.float32,
        )
        key_acc = key_acc + d_key_seg
        value_acc = value_acc + d_value_seg
        return ((key_acc, value_acc), d_query_block)

    zero_grad = jnp.zeros(head_shape, jnp.float32)
    (dk_dot, dv_dot), dq_blocks = lax.scan(
        attend_back, (zero_grad, zero_grad), jnp.arange(block_count, dtype=jnp.int32)
    )
    dq_dot = dq_blocks.reshape(head_shape)
    d_numer = read_mask[:, :, None, None] * d_mem / denom[..., None]
    d_denom = -jnp.sum(d_numer * numer, axis=-1) / denom * jnp.where(denom_raw > 1.0, 1.0, 0.0)
    d_sig_q = (
        jnp.einsum("sthe,shde->sthd", d_numer, read_mem, precision=highest)
        + d_denom[..., None] * read_norm[:, None]
    )
    d_read_mem = jnp.einsum("sthd,sthe->shde", sig_q, d_numer, precision=highest)
    d_read_norm = jnp.einsum("sth,sthd->shd", d_denom, sig_q, precision=highest)
    back_mem = cont_flag[:, None, None, None] * d_read_mem
    back_norm = cont_flag[:, None, None] * d_read_norm
    back_summary, _ = lax.scan(
        fold_states, start_state, (keep_flag[:, None], back_mem, back_norm), reverse=True
    )
    _, grad_in, grad_norm_in = prefix(back_summary, "dp", link_states, start_state)

    def carry_back(state, item):
        flag, mem_read, norm_read = item
        grad_memory, grad_norm = state
        return (
            (flag * grad_memory + mem_read, flag * grad_norm + norm_read),
            (grad_memory, grad_norm),
        )

    _, (d_carried, d_carried_norm) = lax.scan(
        carry_back, (grad_in, grad_norm_in), (keep_flag, back_mem, back_norm), reverse=True
    )
    d_sig_k = write_mask[:, :, None, None] * (
        jnp.einsum("sthe,shde->sthd", value_f, d_carried, precision=highest)
        + d_carried_norm[:, None]
    )
    d_val_mem = write_mask[:, :, None, None] * jnp.einsum(
        "sthd,shde->sthe", sig_k, d_carried, precision=highest
    )
    flat_cols = heads_here * head_size
    d_query = (
        (dq_dot + (d_sig_q * feature_slope(query_f)).reshape(head_shape))
        .astype(jnp.bfloat16)
        .reshape(group_rows, flat_cols)
    )
    d_key = (
        (dk_dot + (d_sig_k * feature_slope(key_f)).reshape(head_shape))
        .astype(jnp.bfloat16)
        .reshape(group_rows, flat_cols)
    )
    d_value = (
        (dv_dot + d_val_mem.reshape(head_shape)).astype(jnp.bfloat16).reshape(group_rows, flat_cols)
    )
    grad_query = jnp.dot(normed1_all.T, d_query, preferred_element_type=jnp.float32)
    grad_key = jnp.dot(normed1_all.T, d_key, preferred_element_type=jnp.float32)
    grad_value = jnp.dot(normed1_all.T, d_value, preferred_element_type=jnp.float32)
    total_term = jnp.dot(d_query, w_query.T, preferred_element_type=jnp.float32)
    total_term = total_term + jnp.dot(d_key, w_key.T, preferred_element_type=jnp.float32)
    d_norm1 = lax.psum_scatter(
        (total_term + jnp.dot(d_value, w_value.T, preferred_element_type=jnp.float32)).astype(
            jnp.bfloat16
        ),
        "mp",
        scatter_dimension=0,
        tiled=True,
    ).astype(jnp.float32)
    gain1_part = jnp.sum(d_norm1 * x_rows * inverse1, axis=0)
    input_grad = d_resid + norm_backward(x_rows, inverse1, norm1_gain, d_norm1)
    gate_full = lax.dynamic_update_slice_in_dim(
        jnp.zeros((heads_here * lax.axis_size("mp"),), jnp.float32),
        gate_part,
        lax.axis_index("mp") * heads_here,
        0,
    )
    gain1_sum, gain2_sum, gate_sum = lax.psum((gain1_part, gain2_part, gate_full), ("dp", "mp"))
    query_sum, key_sum, value_sum, out_sum, gate_w_sum, up_sum, down_sum = (
        lax.psum_scatter(
            grad_query.astype(jnp.bfloat16), "dp", scatter_dimension=0, tiled=True
        ).astype(jnp.float32),
        lax.psum_scatter(
            grad_key.astype(jnp.bfloat16), "dp", scatter_dimension=0, tiled=True
        ).astype(jnp.float32),
        lax.psum_scatter(
            grad_value.astype(jnp.bfloat16), "dp", scatter_dimension=0, tiled=True
        ).astype(jnp.float32),
        lax.psum_scatter(
            grad_out.astype(jnp.bfloat16), "dp", scatter_dimension=1, tiled=True
        ).astype(jnp.float32),
        lax.psum_scatter(
            grad_gate.astype(jnp.bfloat16), "dp", scatter_dimension=0, tiled=True
        ).astype(jnp.float32),
        lax.psum_scatter(
            grad_up.astype(jnp.bfloat16), "dp", scatter_dimension=0, tiled=True
        ).astype(jnp.float32),
        lax.psum_scatter(
            grad_down.astype(jnp.bfloat16), "dp", scatter_dimension=1, tiled=True
        ).astype(jnp.float32),
    )
    return (
        output,
        input_grad,
        gain1_sum,
        query_sum,
        key_sum,
        value_sum,
        out_sum,
        gate_sum,
        gain2_sum,
        gate_w_sum,
        up_sum,
        down_sum,
    )


def solution(mesh):
    return jax.shard_map(
        local,
        mesh=mesh,
        in_specs=(
            P(("dp", "mp"), None),
            P(),
            P(None, "mp"),
            P(None, "mp"),
            P(None, "mp"),
            P("mp", None),
            P("mp"),
            P(),
            P(None, "mp"),
            P(None, "mp"),
            P("mp", None),
            P(),
            P(("dp", "mp"), None),
        ),
        out_specs=(
            P(("dp", "mp"), None),
            P(("dp", "mp"), None),
            P(),
            P("dp", "mp"),
            P("dp", "mp"),
            P("dp", "mp"),
            P("mp", "dp"),
            P(),
            P(),
            P("dp", "mp"),
            P("dp", "mp"),
            P("mp", "dp"),
        ),
        check_vma=False,
    )
```

profile of v0, /device:TPU:0, one launch (start us, length us, event | category | flops | bytes accessed | tf_op | source)
XLA Modules:
  0.0 2484.7 jit_solution(1175721058208208151)
XLA Ops:
  20.1 16.1 all-reduce
  39.6 126.4 %all-gather.15.cloned.1.call-done = bf16[2048,2048]{1,0:T(8,128)(2,1)} async-done(((bf16[512,2048]{1,0:T(8,128)(2,1)}), bf16[2048,2048]{1,0:T(8,128)(2,1)}) %all-gather.15.cloned.1.call-update) | async-done | bytes 8388624 | tf_op jit(solution)/shard_map/all_gather | solution.py:141
  166.0 9.9 convolution_convert_fusion.11
  179.8 10.2 fusion.98
  194.2 11.7 fusion.105
  217.6 168.0 %while.42 = (s32[]{:T(128)}, f32[4,512,4,128]{1,0,3,2:T(4,128)}, f32[4,4,512]{2,1,0:T(4,128)}, s32[4]{0:T(128)S(1)}, s32[2048]{0:T(1024)S(1)}, /*index=5*/bf16[2...) while((s32[]{:T(128)}, f32[4,512,4,128]{1,0,3,2:T(4,128)}, ...), condition=%wide.region_8.9_spmd, body=%wide.region_5.8_spmd.sunk | while | flops 2200961536 | bytes 72976784 | solution.py:180
  238.9 21.0 dynamic_update_slice.42
  280.8 21.0 dynamic_update_slice.42
  322.7 21.0 dynamic_update_slice.42
  364.6 21.0 dynamic_update_slice.42
  396.6 8.9 all-gather.6
  405.5 24.0 while.43
  446.5 8.1 fusion.194
  454.7 277.9 %reduce-scatter.12.cloned.1.call-done = f32[512,2048]{1,0:T(8,128)} async-done(((f32[2048,2048]{1,0:T(8,128)}), f32[512,2048]{1,0:T(8,128)}) %reduce-scatter.12.cloned.1.call-update) | async-done | bytes 4194320 | tf_op jit(solution)/shard_map/reduce_scatter | solution.py:220
  740.6 149.7 %all-gather.17.cloned.1.call-done = bf16[2048,2048]{1,0:T(8,128)(2,1)} async-done(((bf16[512,2048]{1,0:T(8,128)(2,1)}), bf16[2048,2048]{1,0:T(8,128)(2,1)}) %all-gather.17.cloned.1.call-update) | async-done | bytes 8388624 | tf_op jit(solution)/shard_map/all_gather | solution.py:229
  890.3 24.2 convolution_convert_fusion.4
  914.5 21.8 convolution_convert_fusion.5
  936.3 103.3 %all-gather.19.cloned.1.call-done = bf16[2048,2048]{1,0:T(8,128)(2,1)} async-done(((bf16[512,2048]{1,0:T(8,128)(2,1)}), bf16[2048,2048]{1,0:T(8,128)(2,1)}) %all-gather.19.cloned.1.call-update) | async-done | bytes 8388624 | tf_op jit(solution)/shard_map/all_gather | solution.py:244
  1039.5 32.2 %fusion.81 = (bf16[2048,2048]{1,0:T(8,128)(2,1)}, bf16[2048,2048]{1,0:T(8,128)(2,1)}) fusion(bf16[2048,2048]{1,0:T(8,128)(2,1)} %convolution_convert_fusion.5, bf16[2048,2048]{1,0:T(8,128)(2,1)} %convolution_convert_fusion.4, bf16[2048,2048]{1,0:T(8,128)(2,1)} %all-gather.19.cloned.1.call-done, bf16[2048,2048]{1,0:T(8,128)(2,1)} %param.31), kind=kOutput, calls=%fused_computation.85 | convolution fusion | flops 17242783744 | bytes 50331648 | tf_op jit(solution)/shard_map/dot_general | solution.py:245
  1071.7 24.3 fusion.195
  1096.0 25.6 %add_convert_fusion.1 = bf16[2048,2048]{1,0:T(8,128)(2,1)} fusion(f32[2048,2048]{1,0:T(8,128)} %fusion.195, bf16[2048,2048]{1,0:T(8,128)(2,1)} %get-tuple-element.898, bf16[2048,2048]{1,0:T(8,128)(2,1)} %param.30), kind=kOutput, calls=%fused_computation.87 | convolution fusion | flops 17188257792 | bytes 41943040 | tf_op jit(solution)/shard_map/dot_general | solution.py:254
  1121.7 142.9 %reduce-scatter.16.cloned.1.call-done = bf16[512,2048]{1,0:T(8,128)(2,1)} async-done(((bf16[2048,2048]{1,0:T(8,128)(2,1)}), bf16[512,2048]{1,0:T(8,128)(2,1)}) %reduce-scatter.16.cloned.1.call-update) | async-done | bytes 2097168 | tf_op jit(solution)/shard_map/reduce_scatter | solution.py:251
  1274.8 150.3 %all-gather.21.cloned.1.call-done = bf16[2048,2048]{1,0:T(8,128)(2,1)} async-done(((bf16[512,2048]{1,0:T(8,128)(2,1)}), bf16[2048,2048]{1,0:T(8,128)(2,1)}) %all-gather.21.cloned.1.call-update) | async-done | bytes 8388624 | tf_op jit(solution)/shard_map/all_gather | solution.py:262
  1425.1 13.6 fusion.123
  1444.3 13.2 fusion.163
  1457.6 27.0 %convolution_convert_fusion = bf16[2048,2048]{1,0:T(8,128)(2,1)} fusion(bf16[2048,2048]{1,0:T(8,128)(2,1)} %all-gather.19.cloned.1.call-done, bf16[2048,2048]{1,0:T(8,128)(2,1)} %convolution_convert_fusion.4, bf16[2048,2048]{1,0:T(8,128)(2,1)} %convolution_convert_fusion.5), kind=kOutput, calls=%fused_computation.93 | convolution fusion | flops 17217617920 | bytes 33554432 | tf_op jit(solution)/shard_map/dot_general | solution.py:246
  1484.7 24.1 convolution_convert_fusion.1
  1510.2 15.0 all-reduce.1
  1525.2 23.9 convolution_convert_fusion.2
  1573.8 8.8 all-gather.7
  1582.5 10.5 convolution_convert_fusion.6
  1593.0 406.8 %while.44 = (s32[]{:T(128)}, f32[2048,4,128]{0,2,1:T(8,128)}, f32[2048,4,128]{0,2,1:T(8,128)}, f32[4,512,4,128]{3,2,1,0:T(4,128)}, s32[4]{0:T(128)S(1)}, /*index...) while((s32[]{:T(128)}, f32[2048,4,128]{0,2,1:T(8,128)}, ...), condition=%wide.region_16.17_spmd.clone, body=%wide.region_14.16_spmd.clone.sunk | while | flops 5485111808 | bytes 239159920 | solution.py:296
  1598.4 10.3 fusion.289
  1608.7 9.1 bitcast_add_fusion.12
  1619.8 8.1 fusion.288
  1627.9 30.6 %fusion.290 = f32[1,512,4,128]{3,1,2,0:T(8,128)S(1)} fusion(bf16[2048,4,128]{2,0,1:T(8,128)(2,1)} %get-tuple-element.1243, f32[4,512,2048]{2,1,0:T(8,128)} %fusion.288, f32[4,512,2048]{2,1,0:T(8,128)} %fusion.289, f32[4,512]{1,0:T(4,128)S(1)} %dynamic-slice_bitcast_fusion.2, pred[512,2048]{1,0:T(8,128)(4,1)} %copy-done.5), kind=kOutput, calls=%fused_computation.42.clone.1 | convolution fusion | flops 1119883264 | bytes 37756928 | tf_op jit(solution)/shard_map/while/body/eval_jaxpr/hqk,khd->qhd/dot_general | solution.py:279
  1658.6 34.8 %bitcast_add_fusion.11 = f32[2048,4,128]{0,2,1:T(8,128)} fusion(f32[2048,4,128]{0,2,1:T(8,128)} %get-tuple-element.1218, f32[4,512,2048]{2,1,0:T(8,128)} %fusion.288, f32[4,512,2048]{2,1,0:T(8,128)} %fusion.289, f32[4,512]{1,0:T(4,128)S(1)} %dynamic-slice_bitcast_fusion.2, pred[512,2048]{1,0:T(8,128)(4,1)} %copy-done.5, pred[]{:T(512)S(6)} %compare.20, ...), kind=kOutput, calls=%fused_computation.40.clone.1 | convolution fusion | flops 1121980416 | bytes 78135304 | tf_op jit(solution)/shard_map/while/body/eval_jaxpr/hqk,qhd->khd/dot_general | solution.py:282
  1700.0 10.3 fusion.289
  1710.3 9.1 bitcast_add_fusion.12
  1721.4 8.1 fusion.288
  1729.5 30.6 %fusion.290 = f32[1,512,4,128]{3,1,2,0:T(8,128)S(1)} fusion(bf16[2048,4,128]{2,0,1:T(8,128)(2,1)} %get-tuple-element.1243, f32[4,512,2048]{2,1,0:T(8,128)} %fusion.288, f32[4,512,2048]{2,1,0:T(8,128)} %fusion.289, f32[4,512]{1,0:T(4,128)S(1)} %dynamic-slice_bitcast_fusion.2, pred[512,2048]{1,0:T(8,128)(4,1)} %copy-done.5), kind=kOutput, calls=%fused_computation.42.clone.1 | convolution fusion | flops 1119883264 | bytes 37756928 | tf_op jit(solution)/shard_map/while/body/eval_jaxpr/hqk,khd->qhd/dot_general | solution.py:279
  1760.2 34.8 %bitcast_add_fusion.11 = f32[2048,4,128]{0,2,1:T(8,128)} fusion(f32[2048,4,128]{0,2,1:T(8,128)} %get-tuple-element.1218, f32[4,512,2048]{2,1,0:T(8,128)} %fusion.288, f32[4,512,2048]{2,1,0:T(8,128)} %fusion.289, f32[4,512]{1,0:T(4,128)S(1)} %dynamic-slice_bitcast_fusion.2, pred[512,2048]{1,0:T(8,128)(4,1)} %copy-done.5, pred[]{:T(512)S(6)} %compare.20, ...), kind=kOutput, calls=%fused_computation.40.clone.1 | convolution fusion | flops 1121980416 | bytes 78135304 | tf_op jit(solution)/shard_map/while/body/eval_jaxpr/hqk,qhd->khd/dot_general | solution.py:282
  1801.5 10.3 fusion.289
  1811.9 9.1 bitcast_add_fusion.12
  1822.9 8.1 fusion.288
  1831.0 30.6 %fusion.290 = f32[1,512,4,128]{3,1,2,0:T(8,128)S(1)} fusion(bf16[2048,4,128]{2,0,1:T(8,128)(2,1)} %get-tuple-element.1243, f32[4,512,2048]{2,1,0:T(8,128)} %fusion.288, f32[4,512,2048]{2,1,0:T(8,128)} %fusion.289, f32[4,512]{1,0:T(4,128)S(1)} %dynamic-slice_bitcast_fusion.2, pred[512,2048]{1,0:T(8,128)(4,1)} %copy-done.5), kind=kOutput, calls=%fused_computation.42.clone.1 | convolution fusion | flops 1119883264 | bytes 37756928 | tf_op jit(solution)/shard_map/while/body/eval_jaxpr/hqk,khd->qhd/dot_general | solution.py:279
  1861.7 34.8 %bitcast_add_fusion.11 = f32[2048,4,128]{0,2,1:T(8,128)} fusion(f32[2048,4,128]{0,2,1:T(8,128)} %get-tuple-element.1218, f32[4,512,2048]{2,1,0:T(8,128)} %fusion.288, f32[4,512,2048]{2,1,0:T(8,128)} %fusion.289, f32[4,512]{1,0:T(4,128)S(1)} %dynamic-slice_bitcast_fusion.2, pred[512,2048]{1,0:T(8,128)(4,1)} %copy-done.5, pred[]{:T(512)S(6)} %compare.20, ...), kind=kOutput, calls=%fused_computation.40.clone.1 | convolution fusion | flops 1121980416 | bytes 78135304 | tf_op jit(solution)/shard_map/while/body/eval_jaxpr/hqk,qhd->khd/dot_general | solution.py:282
  1903.1 10.3 fusion.289
  1913.4 9.1 bitcast_add_fusion.12
  1924.5 8.1 fusion.288
  1932.6 30.6 %fusion.290 = f32[1,512,4,128]{3,1,2,0:T(8,128)S(1)} fusion(bf16[2048,4,128]{2,0,1:T(8,128)(2,1)} %get-tuple-element.1243, f32[4,512,2048]{2,1,0:T(8,128)} %fusion.288, f32[4,512,2048]{2,1,0:T(8,128)} %fusion.289, f32[4,512]{1,0:T(4,128)S(1)} %dynamic-slice_bitcast_fusion.2, pred[512,2048]{1,0:T(8,128)(4,1)} %copy-done.5), kind=kOutput, calls=%fused_computation.42.clone.1 | convolution fusion | flops 1119883264 | bytes 37756928 | tf_op jit(solution)/shard_map/while/body/eval_jaxpr/hqk,khd->qhd/dot_general | solution.py:279
  1963.2 34.8 %bitcast_add_fusion.11 = f32[2048,4,128]{0,2,1:T(8,128)} fusion(f32[2048,4,128]{0,2,1:T(8,128)} %get-tuple-element.1218, f32[4,512,2048]{2,1,0:T(8,128)} %fusion.288, f32[4,512,2048]{2,1,0:T(8,128)} %fusion.289, f32[4,512]{1,0:T(4,128)S(1)} %dynamic-slice_bitcast_fusion.2, pred[512,2048]{1,0:T(8,128)(4,1)} %copy-done.5, pred[]{:T(512)S(6)} %compare.20, ...), kind=kOutput, calls=%fused_computation.40.clone.1 | convolution fusion | flops 1121980416 | bytes 78135304 | tf_op jit(solution)/shard_map/while/body/eval_jaxpr/hqk,qhd->khd/dot_general | solution.py:282
  2004.3 8.5 fusion.196
  2018.7 24.0 while.45
  2050.5 9.9 convolution_convert_fusion.8
  2060.7 8.0 fusion.114
  2068.7 8.2 fusion.197
  2083.7 16.6 add_convert_fusion
  2100.4 25.9 %convolution_convert_fusion.3 = bf16[2048,2048]{1,0:T(8,128)(2,1)} fusion(bf16[2048,2048]{1,0:T(8,128)(2,1)} %param.31, bf16[2048,2048]{1,0:T(8,128)(2,1)} %convolution_convert_fusion.4, bf16[2048,2048]{1,0:T(8,128)(2,1)} %convolution_convert_fusion.5), kind=kOutput, calls=%fused_computation.96 | convolution fusion | flops 17217617920 | bytes 33554432 | tf_op jit(solution)/shard_map/dot_general | solution.py:238
  2140.3 33.5 %reduce-scatter.24.cloned.1.call-done = bf16[256,512]{1,0:T(8,128)(2,1)} async-done(((bf16[2048,512]{1,0:T(8,128)(2,1)}), bf16[256,512]{1,0:T(8,128)(2,1)}) %reduce-scatter.24.cloned.1.call-update) | async-done | bytes 262160 | tf_op jit(solution)/shard_map/reduce_scatter | solution.py:376
  2175.6 145.1 %reduce-scatter.18.cloned.1.call-done = bf16[512,2048]{1,0:T(8,128)(2,1)} async-done(((bf16[2048,2048]{1,0:T(8,128)(2,1)}), bf16[512,2048]{1,0:T(8,128)(2,1)}) %reduce-scatter.18.cloned.1.call-update) | async-done | bytes 2097168 | tf_op jit(solution)/shard_map/reduce_scatter | solution.py:352
  2324.5 45.5 %all-reduce.2 = (f32[2048]{0:T(1024)}, f32[16]{0:T(128)}, f32[2048]{0:T(1024)}) all-reduce(f32[2048]{0:T(1024)S(1)} %get-tuple-element.821, f32[16]{0:T(128)S(1)} %multiply_dynamic-update-slice_fusion, f32[2048]{0:T(1024)S(1)} %copy-done.45), channel_id=1, replica_groups=mesh['dp'=8,'mp'=4] {'dp','mp'}, use_global_device_ids=true, to_apply=%region_23.24 | all-reduce | flops 4112 | bytes 32896 | tf_op jit(solution)/shard_map/psum | solution.py:368
  2370.0 99.1 %reduce-scatter.14.cloned.1.call-done = bf16[512,2048]{1,0:T(8,128)(2,1)} async-done(((bf16[2048,2048]{1,0:T(8,128)(2,1)}), bf16[512,2048]{1,0:T(8,128)(2,1)}) %reduce-scatter.14.cloned.1.call-update) | async-done | bytes 2097168 | tf_op jit(solution)/shard_map/reduce_scatter | solution.py:237
  2469.1 8.6 fusion.91
  (417 shorter events, 303.1 us)
Async XLA Ops:
  7.2 172.7 %copy-start = (bf16[2048,512]{1,0:T(8,128)(2,1)S(1)}, bf16[2048,512]{1,0:T(8,128)(2,1)}, u32[]{:S(2)}) copy-start(bf16[2048,512]{1,0:T(8,128)(2,1)} %param.23) | copy-start | bytes 6291460
  7.2 8.6 copy-start.68
  7.2 29.7 %copy-start.62 = (f32[4]{0:T(128)S(1)}, f32[4]{0:T(128)}, u32[]{:S(2)}) copy-start(f32[4]{0:T(128)} %param.27) | copy-start | bytes 52
  7.2 158.8 %all-gather.15.cloned.1.call-start = ((), (), s32[]{:S(2)}) async-start(), calls=%async_computation.11 | async-start | bytes 10485760 | tf_op jit(solution)/shard_map/all_gather | solution.py:141
  13.6 392.0 %all-gather.23.cloned.1.call-start = ((), (), s32[]{:S(2)}) async-start(), calls=%async_computation.26 | async-start | bytes 2359296 | tf_op jit(solution)/shard_map/all_gather | solution.py:18
  39.6 170.2 %copy-start.40 = (f32[2048]{0:T(1024)}, f32[2048]{0:T(1024)S(1)}, u32[]{:S(2)}) copy-start(f32[2048]{0:T(1024)S(1)} %get-tuple-element.905) | copy-start | bytes 24580
  217.6 515.1 %reduce-scatter.12.cloned.1.call-start = ((), (), s32[]{:S(2)}) async-start(), calls=%async_computation.12 | async-start | bytes 20971520 | tf_op jit(solution)/shard_map/reduce_scatter | solution.py:220
  391.8 13.7 copy-start.15
  391.8 13.7 copy-start.34
  391.8 13.7 copy-start.67
  429.6 13.5 copy-start.16
  429.6 7.0 copy-start.6
  454.7 283.5 %copy-start.29 = (f32[2048]{0:T(1024)S(1)}, f32[2048]{0:T(1024)}, u32[]{:S(2)}) copy-start(f32[2048]{0:T(1024)} %param.28) | copy-start | bytes 24580
  454.7 435.6 %all-gather.17.cloned.1.call-start = ((), (), s32[]{:S(2)}) async-start(), calls=%async_computation.13 | async-start | bytes 10485760 | tf_op jit(solution)/shard_map/all_gather | solution.py:229
  739.9 299.6 %all-gather.19.cloned.1.call-start = ((), (), s32[]{:S(2)}) async-start(), calls=%async_computation.15 | async-start | bytes 10485760 | tf_op jit(solution)/shard_map/all_gather | solution.py:244
  740.5 524.1 %reduce-scatter.16.cloned.1.call-start = ((), (), s32[]{:S(2)}) async-start(), calls=%async_computation.16 | async-start | bytes 10485760 | tf_op jit(solution)/shard_map/reduce_scatter | solution.py:251
  890.3 24.2 copy-start.59
  1121.6 143.0 %copy-start.30 = (f32[2048]{0:T(1024)S(1)}, f32[2048]{0:T(1024)}, u32[]{:S(2)}) copy-start(f32[2048]{0:T(1024)} %param.28) | copy-start | bytes 24580
  1121.6 143.0 %copy-start.36 = (f32[512]{0:T(512)S(1)}, f32[512]{0:T(512)}, u32[]{:S(2)}) copy-start(f32[512]{0:T(512)} %copy-done.35) | copy-start | bytes 6148
  1121.7 303.5 %all-gather.21.cloned.1.call-start = ((), (), s32[]{:S(2)}) async-start(), calls=%async_computation.17 | async-start | bytes 10485760 | tf_op jit(solution)/shard_map/all_gather | solution.py:262
  1274.7 743.9 %all-gather.25.cloned.1.call-start = ((), (), s32[]{:S(2)}) async-start(), calls=%async_computation.27 | async-start | bytes 1179648 | tf_op jit(solution)/shard_map/all_gather | solution.py:36
  1457.6 668.8 %reduce-scatter.32.cloned.1.call-start = ((), (), s32[]{:S(2)}) async-start(), calls=%async_computation.25 | async-start | bytes 9437184 | tf_op jit(solution)/shard_map/reduce_scatter | solution.py:388
  1484.6 644.4 %reduce-scatter.30.cloned.1.call-start = ((), (), s32[]{:S(2)}) async-start(), calls=%async_computation.24 | async-start | bytes 9437184 | tf_op jit(solution)/shard_map/reduce_scatter | solution.py:385
  1508.8 623.0 %reduce-scatter.28.cloned.1.call-start = ((), (), s32[]{:S(2)}) async-start(), calls=%async_computation.23 | async-start | bytes 9437184 | tf_op jit(solution)/shard_map/reduce_scatter | solution.py:382
  1549.1 585.9 %reduce-scatter.26.cloned.1.call-start = ((), (), s32[]{:S(2)}) async-start(), calls=%async_computation.22 | async-start | bytes 2359296 | tf_op jit(solution)/shard_map/reduce_scatter | solution.py:379
  1553.7 7.3 copy-start.63
  1582.5 10.5 copy-start.24
  1598.3 10.3 copy-start.5
  1598.4 10.3 copy-start.12
  1598.4 10.3 copy-start.64
  1608.7 11.1 copy-start.4
  1700.0 10.4 copy-start.5
  1700.0 10.4 copy-start.12
  1700.0 10.4 copy-start.64
  1710.3 11.1 copy-start.4
  1801.5 10.3 copy-start.5
  1801.5 10.3 copy-start.12
  1801.5 10.3 copy-start.64
  1811.9 11.1 copy-start.4
  1903.1 10.3 copy-start.5
  1903.1 10.3 copy-start.12
  1903.1 10.3 copy-start.64
  1913.4 11.1 copy-start.4
  1999.9 136.8 %reduce-scatter.20.cloned.1.call-start = ((), (), s32[]{:S(2)}) async-start(), calls=%async_computation.19 | async-start | bytes 2359296 | tf_op jit(solution)/shard_map/reduce_scatter | solution.py:370
  1999.9 12.8 slice-start
  2004.3 8.5 slice-start.1
  2018.5 24.1 copy-start.42
  2018.6 119.9 %reduce-scatter.22.cloned.1.call-start = ((), (), s32[]{:S(2)}) async-start(), calls=%async_computation.20 | async-start | bytes 2359296 | tf_op jit(solution)/shard_map/reduce_scatter | solution.py:373
  2060.4 113.4 %reduce-scatter.24.cloned.1.call-start = ((), (), s32[]{:S(2)}) async-start(), calls=%async_computation.21 | async-start | bytes 2359296 | tf_op jit(solution)/shard_map/reduce_scatter | solution.py:376
  2060.6 8.1 copy-start.22
  2060.6 8.1 copy-start.61
  2060.7 16.3 slice-start.2
  2068.7 8.2 copy-start.14
  2068.7 8.2 slice-start.3
  2083.4 237.3 %reduce-scatter.18.cloned.1.call-start = ((), (), s32[]{:S(2)}) async-start(), calls=%async_computation.18 | async-start | bytes 10485760 | tf_op jit(solution)/shard_map/reduce_scatter | solution.py:352
  2100.3 368.8 %reduce-scatter.14.cloned.1.call-start = ((), (), s32[]{:S(2)}) async-start(), calls=%async_computation.14 | async-start | bytes 10485760 | tf_op jit(solution)/shard_map/reduce_scatter | solution.py:237
  2126.3 8.4 copy-start.55
  2126.3 8.5 copy-start.52
  2129.1 191.6 %copy-start.32 = (f32[2048]{0:T(1024)S(1)}, f32[2048]{0:T(1024)}, u32[]{:S(2)}) copy-start(f32[2048]{0:T(1024)} %param.22) | copy-start | bytes 24580
  2129.1 191.6 %copy-start.39 = (f32[512]{0:T(512)S(1)}, f32[512]{0:T(512)}, u32[]{:S(2)}) copy-start(f32[512]{0:T(512)} %copy-done.38) | copy-start | bytes 6148
  2134.7 189.8 %copy-start.45 = (f32[2048]{0:T(1024)S(1)}, f32[2048]{0:T(1024)}, u32[]{:S(2)}) copy-start(f32[2048]{0:T(1024)} %get-tuple-element.819) | copy-start | bytes 24580
  2134.7 334.5 %copy-start.31 = (f32[2048]{0:T(1024)S(1)}, f32[2048]{0:T(1024)}, u32[]{:S(2)}) copy-start(f32[2048]{0:T(1024)} %param.28) | copy-start | bytes 24580
  2134.7 334.5 %copy-start.37 = (f32[512]{0:T(512)S(1)}, f32[512]{0:T(512)}, u32[]{:S(2)}) copy-start(f32[512]{0:T(512)} %copy-done.35) | copy-start | bytes 6148
  2134.7 334.5 %copy-start.47 = (f32[512]{0:T(512)S(1)}, f32[512]{0:T(512)}, u32[]{:S(2)}) copy-start(f32[512]{0:T(512)} %copy-done.46) | copy-start | bytes 6148
  (44 other events, 168.4 us)
Sparse Core Ops, SparseCore 0:
  13.7 152.3 all-gather.14
  217.7 25.9 all-gather.22
  454.8 277.8 reduce-scatter.11
  740.0 150.2 all-gather.16
  891.7 147.7 all-gather.18
  1121.8 142.8 reduce-scatter.15
  1274.9 150.2 all-gather.20
  1457.7 21.5 all-gather.24
  1484.7 69.7 reduce-scatter.31
  1557.9 71.5 reduce-scatter.29
  1632.9 71.5 reduce-scatter.27
  2000.0 39.5 reduce-scatter.25
  2043.5 41.1 reduce-scatter.19
  2088.4 41.1 reduce-scatter.21
  2132.6 41.1 reduce-scatter.23
  2176.0 144.6 reduce-scatter.17
  2322.9 146.2 reduce-scatter.13
where the time goes:
time: 2500 us; the launch traced here: 2480 us
  waiting for transfers between devices  1230 us (49%)
  matrix products  826 us (33%)
  local copies, waits for them, and re-layouts  170 us (7%)
  other arithmetic  127 us (5%)
  blocking collectives  94.3 us (4%)
    reduce_scatter x1, waiting for transfers between devices, local(): lax.psum_scatter(jnp.dot(piece, w_out, preferred_element_type=jnp.float32...  278 us
    all_gather x1, waiting for transfers between devices, local(): lax.all_gather(d_resid.astype(jnp.bfloat16), 'mp', axis=0, tiled=True)  150 us
    all_gather x1, waiting for transfers between devices, local(): normed2_all = lax.all_gather(normed2, 'mp', axis=0, tiled=True)  150 us
    reduce_scatter x1, waiting for transfers between devices, local(): lax.psum_scatter((total_term + jnp.dot(d_value, w_value.T, preferred_elem...  145 us
    reduce_scatter x1, waiting for transfers between devices, local(): lax.psum_scatter((jnp.dot(d_gate, w_gate.T, preferred_element_type=jnp.fl...  143 us
    dot_general x4, matrix products, attend_back(): jnp.einsum('hqk,qhd->khd', d_raw, query_block, preferred_element_type=jnp...  139 us
    all_gather x1, waiting for transfers between devices, local(): normed1_all = lax.all_gather(normed1, 'mp', axis=0, tiled=True)  126 us
    dot_general x4, matrix products, attend_back(): jnp.einsum('hqk,khd->qhd', d_raw, key_seg, preferred_element_type=jnp.flo...  123 us
  transfers between devices with their start and end apart: 17, of which 9 were waited for; matrix products, arithmetic and copies ran while one was open for 35% of the time, Pallas kernels for 0%

commit v1 on v0

v1 whole, which is shorter than its diff:
```python
import functools
import math

import jax
import jax.numpy as jnp
from jax import lax
from jax.experimental import pallas as pl
from jax.experimental.pallas import tpu as pltpu
from jax.sharding import PartitionSpec as P

SEG = 2048


eps_norm = 1e-05
neg_fill = -1e30
highest = lax.Precision.HIGHEST


def carried_in(value, axis, combine, identity):
    size, place = (lax.axis_size(axis), lax.axis_index(axis))
    everything = jax.tree.map(lambda part: lax.all_gather(part, axis), value)
    start = jax.tree.map(
        lambda part, zero: jnp.broadcast_to(jnp.asarray(zero, part.dtype), part.shape),
        value,
        identity,
    )

    def carried_hop(k, before):
        reached = k < place
        new = combine(before, jax.tree.map(lambda part: part[k], everything))
        return jax.tree.map(lambda a, b: jnp.where(reached, a, b), new, before)

    return lax.fori_loop(0, size, carried_hop, start)


def prefix(value, axis, combine, identity):
    size, place = (lax.axis_size(axis), lax.axis_index(axis))
    everything = jax.tree.map(
        lambda part, kind: lax.all_gather(part.astype(kind), axis),
        value,
        jax.tree.map(lambda a: jnp.bfloat16 if a.dtype == jnp.float32 else a.dtype, value),
    )
    start = jax.tree.map(
        lambda part, zero: jnp.broadcast_to(jnp.asarray(zero, part.dtype), part.shape),
        value,
        identity,
    )

    def prefix_hop(k, before):
        at = size - 1 - k
        reached = at > place
        new = combine(
            before, jax.tree.map(lambda part, own: part[at].astype(own.dtype), everything, value)
        )
        return jax.tree.map(lambda a, b: jnp.where(reached, a, b), new, before)

    return lax.fori_loop(0, size, prefix_hop, start)


def inverse_rms(values):
    return lax.rsqrt(jnp.mean(values * values, axis=-1, keepdims=True) + eps_norm)


def norm_backward(values, inverse, gain, upstream):
    scaled = upstream * gain
    inner = jnp.mean(values * scaled, axis=-1, keepdims=True)
    return inverse * scaled - values * inverse * inverse * inverse * inner


def feature(values):
    return jnp.where(values > 0, values + 1.0, jnp.exp(jnp.minimum(values, 0.0)))


def feature_slope(values):
    return jnp.where(values > 0, 1.0, jnp.exp(jnp.minimum(values, 0.0)))


def link_states(earlier, later):
    return (
        earlier[0] * later[0],
        later[0] * earlier[1] + later[1],
        later[0] * earlier[2] + later[2],
    )


def fold_states(state, item):
    return (link_states(state, item), None)


def document_ids(doc_lengths, first, count):
    bounds = jnp.cumsum(doc_lengths)
    position = first + jnp.arange(count, dtype=jnp.int32)
    before = jnp.sum((bounds[None, :] <= position[:, None]).astype(jnp.int32), axis=1)
    return jnp.where(position < bounds[-1], before, doc_lengths.shape[0] + position)


def block_allowed(doc_index, row_start, seg_start, block_rows):
    query_docs = lax.dynamic_slice_in_dim(doc_index, row_start, block_rows, 0)
    query_pos = row_start + jnp.arange(block_rows, dtype=jnp.int32)
    key_pos = seg_start + jnp.arange(SEG, dtype=jnp.int32)
    return (key_pos[None, :] <= query_pos[:, None]) & (doc_index[None, :] == query_docs[:, None])


NEG = -1e30
BQ = 256


def _mask(qi, docq, dock, seg):
    row = (qi * BQ) % seg + lax.broadcasted_iota(jnp.int32, (BQ, seg), 0)
    col = lax.broadcasted_iota(jnp.int32, (BQ, seg), 1)
    return (col <= row) & (docq == dock)


def _fwd_kernel(scale, seg, q_ref, k_ref, v_ref, docq_ref, dock_ref, o_ref, lse_ref):
    qi = pl.program_id(1)
    q = q_ref[0]
    k = k_ref[0]
    v = v_ref[0]
    s = lax.dot_general(q, k, (((1,), (1,)), ((), ())), preferred_element_type=jnp.float32)
    allowed = _mask(qi, docq_ref[...], dock_ref[...], seg)
    s = jnp.where(allowed, s * scale, NEG)
    m = jnp.max(s, axis=1, keepdims=True)
    e = jnp.exp(s - m)
    l = jnp.sum(e, axis=1, keepdims=True)
    p = (e / l).astype(jnp.bfloat16)
    o_ref[0] = jnp.dot(p, v, preferred_element_type=jnp.float32)
    lse_ref[0] = m + jnp.log(l)


def _bwd_kernel(scale, seg, q_ref, k_ref, v_ref, do_ref, lse_ref, docq_ref, dock_ref,
                dq_ref, dk_ref, dv_ref):
    qi = pl.program_id(1)

    @pl.when((qi * BQ) % seg == 0)
    def _():
        dk_ref[...] = jnp.zeros_like(dk_ref)
        dv_ref[...] = jnp.zeros_like(dv_ref)

    q = q_ref[0]
    k = k_ref[0]
    v = v_ref[0]
    do = do_ref[0]
    s = lax.dot_general(q, k, (((1,), (1,)), ((), ())), preferred_element_type=jnp.float32)
    allowed = _mask(qi, docq_ref[...], dock_ref[...], seg)
    s = jnp.where(allowed, s * scale, NEG)
    p = jnp.exp(s - lse_ref[0])
    dp = lax.dot_general(do, v, (((1,), (1,)), ((), ())), preferred_element_type=jnp.float32)
    delta = jnp.sum(p * dp, axis=1, keepdims=True)
    ds = (p * (dp - delta) * scale).astype(jnp.bfloat16)
    dq_ref[0] = jnp.dot(ds, k, preferred_element_type=jnp.float32)
    dk_ref[0] += lax.dot_general(ds, q, (((0,), (0,)), ((), ())), preferred_element_type=jnp.float32)
    dv_ref[0] += lax.dot_general(p.astype(jnp.bfloat16), do, (((0,), (0,)), ((), ())),
                                 preferred_element_type=jnp.float32)


def attention_fwd(q, k, v, doc, scale):
    H, T, d = q.shape
    seg = min(SEG, T)
    nq = T // BQ
    docq = doc.reshape(T, 1)
    dock = doc.reshape(1, T)
    qspec = pl.BlockSpec((1, BQ, d), lambda h, i: (h, i, 0))
    kspec = pl.BlockSpec((1, seg, d), lambda h, i: (h, i * BQ // seg, 0))
    flops = 4 * H * T * seg * d
    return pl.pallas_call(
        functools.partial(_fwd_kernel, scale, seg),
        grid=(H, nq),
        in_specs=[qspec, kspec, kspec,
                  pl.BlockSpec((BQ, 1), lambda h, i: (i, 0)),
                  pl.BlockSpec((1, seg), lambda h, i: (0, i * BQ // seg))],
        out_specs=[pl.BlockSpec((1, BQ, d), lambda h, i: (h, i, 0)),
                   pl.BlockSpec((1, BQ, 1), lambda h, i: (h, i, 0))],
        out_shape=[jax.ShapeDtypeStruct((H, T, d), jnp.float32),
                   jax.ShapeDtypeStruct((H, T, 1), jnp.float32)],
        compiler_params=pltpu.CompilerParams(dimension_semantics=("arbitrary", "arbitrary")),
        cost_estimate=pl.CostEstimate(flops=flops, transcendentals=H * T * seg,
                                      bytes_accessed=H * T * d * 10),
    )(q, k, v, docq, dock)


def attention_bwd(q, k, v, do, lse, doc, scale):
    H, T, d = q.shape
    seg = min(SEG, T)
    nq = T // BQ
    docq = doc.reshape(T, 1)
    dock = doc.reshape(1, T)
    qspec = pl.BlockSpec((1, BQ, d), lambda h, i: (h, i, 0))
    kspec = pl.BlockSpec((1, seg, d), lambda h, i: (h, i * BQ // seg, 0))
    flops = 10 * H * T * seg * d
    return pl.pallas_call(
        functools.partial(_bwd_kernel, scale, seg),
        grid=(H, nq),
        in_specs=[qspec, kspec, kspec, qspec,
                  pl.BlockSpec((1, BQ, 1), lambda h, i: (h, i, 0)),
                  pl.BlockSpec((BQ, 1), lambda h, i: (i, 0)),
                  pl.BlockSpec((1, seg), lambda h, i: (0, i * BQ // seg))],
        out_specs=[qspec, kspec, kspec],
        out_shape=[jax.ShapeDtypeStruct((H, T, d), jnp.float32)] * 3,
        compiler_params=pltpu.CompilerParams(dimension_semantics=("arbitrary", "arbitrary")),
        cost_estimate=pl.CostEstimate(flops=flops, transcendentals=H * T * seg,
                                      bytes_accessed=H * T * d * 24),
    )(q, k, v, do, lse, docq, dock)


def local(
    tokens,
    norm1_gain,
    w_query,
    w_key,
    w_value,
    w_out,
    gate_logit,
    norm2_gain,
    w_gate,
    w_up,
    w_down,
    doc_lengths,
    out_grad,
):
    heads_here = gate_logit.shape[0]
    head_size = w_query.shape[1] // heads_here
    local_rows = tokens.shape[0]
    mp_size = lax.axis_size("mp")
    dp_size = lax.axis_size("dp")
    group_rows = local_rows * mp_size
    seg_count = group_rows // SEG
    score_scale = 1.0 / math.sqrt(head_size)
    group_first = lax.axis_index("dp") * group_rows
    shifted_ids = document_ids(doc_lengths, group_first - 1, group_rows + 1)
    doc_index = shifted_ids[1:]
    before_doc = jnp.where(group_first > 0, shifted_ids[0], -1)
    seg_docs = doc_index.reshape(seg_count, SEG)
    seg_first = seg_docs[:, 0]
    seg_last = seg_docs[:, -1]
    prev_last = jnp.concatenate([before_doc[None], seg_last[:-1]])
    cont_flag = jnp.where(seg_first == prev_last, 1.0, 0.0).astype(jnp.float32)
    keep_flag = jnp.where(seg_last == prev_last, 1.0, 0.0).astype(jnp.float32)
    read_mask = jnp.where(seg_docs == seg_first[:, None], 1.0, 0.0).astype(jnp.float32)
    write_mask = jnp.where(seg_docs == seg_last[:, None], 1.0, 0.0).astype(jnp.float32)
    width = w_out.shape[1]

    def to_heads(rows):
        return rows.reshape(group_rows, heads_here, head_size).transpose(1, 0, 2)

    def from_heads(heads):
        return heads.transpose(1, 0, 2).reshape(group_rows, heads_here * head_size)

    seg_shape = (heads_here, seg_count, SEG, head_size)
    piece = width // dp_size
    w_out_piece = lax.dynamic_slice_in_dim(w_out, lax.axis_index("dp") * piece, piece, axis=1)
    w_out_full = lax.all_gather(
        lax.all_gather(w_out_piece, "mp", axis=0, tiled=True), "dp", axis=1, tiled=True
    )
    x_rows = tokens.astype(jnp.float32)
    inverse1 = inverse_rms(x_rows)
    normed1 = (x_rows * inverse1 * norm1_gain).astype(jnp.bfloat16)
    normed1_all = lax.all_gather(normed1, "mp", axis=0, tiled=True)
    query_h = to_heads(
        jnp.dot(normed1_all, w_query, preferred_element_type=jnp.float32).astype(jnp.bfloat16)
    )
    key_h = to_heads(
        jnp.dot(normed1_all, w_key, preferred_element_type=jnp.float32).astype(jnp.bfloat16)
    )
    value_h = to_heads(
        jnp.dot(normed1_all, w_value, preferred_element_type=jnp.float32).astype(jnp.bfloat16)
    )
    dot_out, log_sums = attention_fwd(query_h, key_h, value_h, doc_index, score_scale)
    query_f = query_h.astype(jnp.float32).reshape(seg_shape)
    key_f = key_h.astype(jnp.float32).reshape(seg_shape)
    value_f = value_h.astype(jnp.float32).reshape(seg_shape)
    sig_q = feature(query_f)
    sig_k = feature(key_f)
    updates = jnp.einsum("st,hstd,hste->shde", write_mask, sig_k, value_f, precision=highest)
    norm_updates = jnp.einsum("st,hstd->shd", write_mask, sig_k, precision=highest)
    start_state = (
        jnp.ones((1,), jnp.float32),
        jnp.zeros(updates.shape[1:], jnp.float32),
        jnp.zeros(norm_updates.shape[1:], jnp.float32),
    )
    summary, _ = lax.scan(fold_states, start_state, (keep_flag[:, None], updates, norm_updates))
    _, memory_in, norm_in = carried_in(summary, "dp", link_states, start_state)

    def carry_forward(state, item):
        flag, read_flag, update, norm_update = item
        memory, norm_sum = state
        return (
            (flag * memory + update, flag * norm_sum + norm_update),
            (read_flag * memory, read_flag * norm_sum),
        )

    _, (read_mem, read_norm) = lax.scan(
        carry_forward, (memory_in, norm_in), (keep_flag, cont_flag, updates, norm_updates)
    )
    numer = jnp.einsum("hstd,shde->hste", sig_q, read_mem, precision=highest)
    denom_raw = jnp.einsum("hstd,shd->hst", sig_q, read_norm, precision=highest)
    denom = jnp.maximum(denom_raw, 1.0)
    mem_out = (read_mask[None, :, :, None] * numer / denom[..., None]).reshape(dot_out.shape)
    gate_vec = jax.nn.sigmoid(gate_logit)
    gate = gate_vec[:, None, None]
    mixed_cols = from_heads(gate * mem_out + (1.0 - gate) * dot_out).astype(jnp.bfloat16)
    mixed = lax.all_to_all(mixed_cols, "mp", 0, 1, tiled=True)
    attn_sum = jnp.dot(mixed, w_out_full, preferred_element_type=jnp.float32)
    resid = x_rows + attn_sum
    inverse2 = inverse_rms(resid)
    normed2 = (resid * inverse2 * norm2_gain).astype(jnp.bfloat16)
    normed2_all = lax.all_gather(normed2, "mp", axis=0, tiled=True)
    gate_pre = jnp.dot(normed2_all, w_gate, preferred_element_type=jnp.float32).astype(jnp.bfloat16)
    up_pre = jnp.dot(normed2_all, w_up, preferred_element_type=jnp.float32).astype(jnp.bfloat16)
    gate_f = gate_pre.astype(jnp.float32)
    up_f = up_pre.astype(jnp.float32)
    sig_gate = jax.nn.sigmoid(gate_f)
    act = (gate_f * sig_gate * up_f).astype(jnp.bfloat16)
    mlp_sum = lax.psum_scatter(
        jnp.dot(act, w_down, preferred_element_type=jnp.float32).astype(jnp.bfloat16),
        "mp",
        scatter_dimension=0,
        tiled=True,
    ).astype(jnp.float32)
    output = (resid + mlp_sum).astype(jnp.bfloat16)
    grad_rows_all = lax.all_gather(out_grad, "mp", axis=0, tiled=True)
    d_act = jnp.dot(grad_rows_all, w_down.T, preferred_element_type=jnp.float32)
    grad_down = jnp.dot(act.T, grad_rows_all, preferred_element_type=jnp.float32)
    d_gate = (d_act * up_f * sig_gate * (1.0 + gate_f * (1.0 - sig_gate))).astype(jnp.bfloat16)
    d_up = (d_act * gate_f * sig_gate).astype(jnp.bfloat16)
    grad_gate = jnp.dot(normed2_all.T, d_gate, preferred_element_type=jnp.float32)
    grad_up = jnp.dot(normed2_all.T, d_up, preferred_element_type=jnp.float32)
    d_norm2 = lax.psum_scatter(
        (
            jnp.dot(d_gate, w_gate.T, preferred_element_type=jnp.float32)
            + jnp.dot(d_up, w_up.T, preferred_element_type=jnp.float32)
        ).astype(jnp.bfloat16),
        "mp",
        scatter_dimension=0,
        tiled=True,
    ).astype(jnp.float32)
    gain2_part = jnp.sum(d_norm2 * resid * inverse2, axis=0)
    d_resid = out_grad.astype(jnp.float32) + norm_backward(resid, inverse2, norm2_gain, d_norm2)
    d_resid_low = d_resid.astype(jnp.bfloat16)
    grad_out = jnp.dot(mixed.T, d_resid_low, preferred_element_type=jnp.float32)
    d_mixed_rows = jnp.dot(d_resid_low, w_out_full.T, preferred_element_type=jnp.float32)
    d_mixed = to_heads(
        lax.all_to_all(d_mixed_rows.astype(jnp.bfloat16), "mp", 1, 0, tiled=True)
    ).astype(jnp.float32)
    gate_part = jnp.sum(d_mixed * (mem_out - dot_out), axis=(1, 2)) * gate_vec * (1.0 - gate_vec)
    d_dot = ((1.0 - gate) * d_mixed).astype(jnp.bfloat16)
    d_mem = (gate * d_mixed).reshape(seg_shape)
    dq_dot, dk_dot, dv_dot = attention_bwd(
        query_h, key_h, value_h, d_dot, log_sums, doc_index, score_scale
    )
    d_numer = read_mask[None, :, :, None] * d_mem / denom[..., None]
    d_denom = -jnp.sum(d_numer * numer, axis=-1) / denom * jnp.where(denom_raw > 1.0, 1.0, 0.0)
    d_sig_q = (
        jnp.einsum("hste,shde->hstd", d_numer, read_mem, precision=highest)
        + d_denom[..., None] * read_norm.transpose(1, 0, 2)[:, :, None]
    )
    d_read_mem = jnp.einsum("hstd,hste->shde", sig_q, d_numer, precision=highest)
    d_read_norm = jnp.einsum("hst,hstd->shd", d_denom, sig_q, precision=highest)
    back_mem = cont_flag[:, None, None, None] * d_read_mem
    back_norm = cont_flag[:, None, None] * d_read_norm
    back_summary, _ = lax.scan(
        fold_states, start_state, (keep_flag[:, None], back_mem, back_norm), reverse=True
    )
    _, grad_in, grad_norm_in = prefix(back_summary, "dp", link_states, start_state)

    def carry_back(state, item):
        flag, mem_read, norm_read = item
        grad_memory, grad_norm = state
        return (
            (flag * grad_memory + mem_read, flag * grad_norm + norm_read),
            (grad_memory, grad_norm),
        )

    _, (d_carried, d_carried_norm) = lax.scan(
        carry_back, (grad_in, grad_norm_in), (keep_flag, back_mem, back_norm), reverse=True
    )
    write4 = write_mask[None, :, :, None]
    d_sig_k = write4 * (
        jnp.einsum("hste,shde->hstd", value_f, d_carried, precision=highest)
        + d_carried_norm.transpose(1, 0, 2)[:, :, None]
    )
    d_val_mem = write4 * jnp.einsum("hstd,shde->hste", sig_k, d_carried, precision=highest)
    d_query = from_heads(
        dq_dot + (d_sig_q * feature_slope(query_f)).reshape(dq_dot.shape)
    ).astype(jnp.bfloat16)
    d_key = from_heads(
        dk_dot + (d_sig_k * feature_slope(key_f)).reshape(dk_dot.shape)
    ).astype(jnp.bfloat16)
    d_value = from_heads(dv_dot + d_val_mem.reshape(dv_dot.shape)).astype(jnp.bfloat16)
    grad_query = jnp.dot(normed1_all.T, d_query, preferred_element_type=jnp.float32)
    grad_key = jnp.dot(normed1_all.T, d_key, preferred_element_type=jnp.float32)
    grad_value = jnp.dot(normed1_all.T, d_value, preferred_element_type=jnp.float32)
    total_term = jnp.dot(d_query, w_query.T, preferred_element_type=jnp.float32)
    total_term = total_term + jnp.dot(d_key, w_key.T, preferred_element_type=jnp.float32)
    d_norm1 = lax.psum_scatter(
        (total_term + jnp.dot(d_value, w_value.T, preferred_element_type=jnp.float32)).astype(
            jnp.bfloat16
        ),
        "mp",
        scatter_dimension=0,
        tiled=True,
    ).astype(jnp.float32)
    gain1_part = jnp.sum(d_norm1 * x_rows * inverse1, axis=0)
    input_grad = d_resid + norm_backward(x_rows, inverse1, norm1_gain, d_norm1)
    gate_full = lax.dynamic_update_slice_in_dim(
        jnp.zeros((heads_here * mp_size,), jnp.float32),
        gate_part,
        lax.axis_index("mp") * heads_here,
        0,
    )
    gain1_sum, gain2_sum, gate_sum = lax.psum((gain1_part, gain2_part, gate_full), ("dp", "mp"))

    def over_dp(grad, dim):
        return lax.psum_scatter(
            grad.astype(jnp.bfloat16), "dp", scatter_dimension=dim, tiled=True
        ).astype(jnp.float32)

    out_sum = lax.psum_scatter(
        over_dp(grad_out, 1).astype(jnp.bfloat16), "mp", scatter_dimension=0, tiled=True
    ).astype(jnp.float32)
    query_sum, key_sum, value_sum, gate_w_sum, up_sum, down_sum = (
        over_dp(grad_query, 0),
        over_dp(grad_key, 0),
        over_dp(grad_value, 0),
        over_dp(grad_gate, 0),
        over_dp(grad_up, 0),
        over_dp(grad_down, 1),
    )
    return (
        output,
        input_grad,
        gain1_sum,
        query_sum,
        key_sum,
        value_sum,
        out_sum,
        gate_sum,
        gain2_sum,
        gate_w_sum,
        up_sum,
        down_sum,
    )


def solution(mesh):
    return jax.shard_map(
        local,
        mesh=mesh,
        in_specs=(
            P(("dp", "mp"), None),
            P(),
            P(None, "mp"),
            P(None, "mp"),
            P(None, "mp"),
            P("mp", None),
            P("mp"),
            P(),
            P(None, "mp"),
            P(None, "mp"),
            P("mp", None),
            P(),
            P(("dp", "mp"), None),
        ),
        out_specs=(
            P(("dp", "mp"), None),
            P(("dp", "mp"), None),
            P(),
            P("dp", "mp"),
            P("dp", "mp"),
            P("dp", "mp"),
            P("mp", "dp"),
            P(),
            P(),
            P("dp", "mp"),
            P("dp", "mp"),
            P("mp", "dp"),
        ),
        check_vma=False,
    )
```

time: 2500 us -> 1880 us (0.75)
  matrix products: 826 us -> 424 us
  waiting for transfers between devices: 1230 us -> 944 us
  Pallas kernels: 0 us -> 128 us
  local copies, waits for them, and re-layouts: 170 us -> 67.9 us
  blocking collectives: 94.3 us -> 191 us
  other arithmetic: 127 us -> 90.8 us
    dot_general x40 -> x13, matrix products: 532 us -> 124 us  [the longest x1 26.6 us: local(): jnp.dot(act, w_down, preferred_element_type=jnp.float32)]
    all_gather x1 -> x2, waiting for transfers between devices: 150 us -> 0.02 us  [the longest x1 0.02 us: local(): lax.all_gather(w_out_piece, 'mp', axis=0, tiled=True)]
    pallas_call x0 -> x2, Pallas kernels: none -> 128 us  [the longest x1 76.7 us: attention_bwd(): pl.pallas_call(functools.partial(_bwd_kernel, scale, seg), grid=(H, nq),...]
    reduce_scatter x9, waiting for transfers between devices: 411 us -> 287 us  [the longest x1 143 us: local(): lax.psum_scatter(jnp.dot(act, w_down, preferred_element_type=jnp.float32)...]
    all_to_all x0 -> x2, blocking collectives: none -> 106 us  [the longest x1 53.5 us: local(): mixed = lax.all_to_all(mixed_cols, 'mp', 0, 1, tiled=True)]
    dynamic_update_slice x12 -> x0, local copies, waits for them, and re-layouts: 100 us -> none  [local(): lax.map(attend, jnp.arange(block_count, dtype=jnp.int32))]
    convert_element_type x0 -> x6, local copies, waits for them, and re-layouts: none -> 32 us  [the longest x2 15 us: local(): from_heads(gate * mem_out + (1.0 - gate) * dot_out).astype(jnp.bfloat16)]
    reduce_scatter x1, waiting for transfers between devices: 143 us -> 116 us  [local(): lax.psum_scatter((jnp.dot(d_gate, w_gate.T, preferred_element_type=jnp.fl...]
  transfers between devices with their start and end apart: 17 -> 18, of which waited for: 9 -> 10; matrix products, arithmetic and copies ran while one was open for 35% -> 23% of each run, Pallas kernels for 0% -> 7%
where the time goes in v1:
time: 1880 us; the launch traced here: 1870 us
  waiting for transfers between devices  944 us (50%)
  matrix products  424 us (23%)
  blocking collectives  191 us (10%)
  Pallas kernels  128 us (7%)
  other arithmetic  90.8 us (5%)
  local copies, waits for them, and re-layouts  67.9 us (4%)
    all_gather x1, waiting for transfers between devices, local(): normed2_all = lax.all_gather(normed2, 'mp', axis=0, tiled=True)  147 us
    all_gather x1, waiting for transfers between devices, local(): normed1_all = lax.all_gather(normed1, 'mp', axis=0, tiled=True)  145 us
    reduce_scatter x1, waiting for transfers between devices, local(): lax.psum_scatter((total_term + jnp.dot(d_value, w_value.T, preferred_elem...  144 us
    reduce_scatter x1, waiting for transfers between devices, local(): lax.psum_scatter(jnp.dot(act, w_down, preferred_element_type=jnp.float32)...  143 us
    reduce_scatter x7, waiting for transfers between devices, over_dp(): lax.psum_scatter(grad.astype(jnp.bfloat16), 'dp', scatter_dimension=dim,...  117 us
    reduce_scatter x1, waiting for transfers between devices, local(): lax.psum_scatter((jnp.dot(d_gate, w_gate.T, preferred_element_type=jnp.fl...  116 us
    all_gather x1, waiting for transfers between devices, local(): grad_rows_all = lax.all_gather(out_grad, 'mp', axis=0, tiled=True)  103 us
    pallas_call x1, Pallas kernels, attention_bwd(): pl.pallas_call(functools.partial(_bwd_kernel, scale, seg), grid=(H, nq),...  76.7 us
  transfers between devices with their start and end apart: 18, of which 10 were waited for; matrix products, arithmetic and copies ran while one was open for 23% of the time, Pallas kernels for 7%

profile of v1, /device:TPU:0, one launch (start us, length us, event | category | flops | bytes accessed | tf_op | source)
XLA Modules:
  0.0 1870.2 jit_solution(7890522532663073946)
XLA Ops:
  21.3 144.7 %all-gather.16.cloned.1.call-done = bf16[2048,2048]{1,0:T(8,128)(2,1)} async-done(((bf16[512,2048]{1,0:T(8,128)(2,1)}), bf16[2048,2048]{1,0:T(8,128)(2,1)}) %all-gather.16.cloned.1.call-update) | async-done | bytes 8388624 | tf_op jit(solution)/shard_map/all_gather | solution.py:257
  166.0 9.9 convolution_convert_fusion.11
  175.9 4.1 copy.82
  180.0 9.9 convolution_convert_fusion.12
  193.9 7.8 fusion.84
  204.2 14.2 all-reduce
  220.5 9.2 convolution_convert_fusion.13
  229.7 3.9 copy.80
  233.7 4.6 fusion.52
  238.8 8.2 all-gather.6
  247.0 51.1 %shard_map.220 = (f32[4,2048,128]{2,1,0:T(8,128)}, f32[4,2048,1]{2,1,0:T(8,128)}) custom-call(bf16[4,2048,128]{2,1,0:T(8,128)(2,1)} %bitcast.193, bf16[4,2048,128]{2,1,0:T(8,128)(2,1)} %bitcast.189, bf16[4,2048,128]{2,1,0:T(8,128)(2,1)} %bitcast.191, s32[2048,1]{1,0:T(8,128)} %copy.86.docq_ref, s32[1,2048]{1,0:T(1,128)} %bitcast.209), custom_call_target="tpu_custom_call" | custom-call | flops 8589934592 | bytes 10485760 | tf_op jit(solution)/shard_map/pallas_call | solution.py:165
  298.2 23.9 %while.22 = (s32[]{:T(128)}, f32[4,128,128]{2,1,0:T(8,128)S(1)}, f32[4,128]{1,0:T(4,128)S(1)}, s32[]{:T(128)}, f32[8,1]{0,1:T(1,128)S(1)}, /*index=5*/f32[8,4,12...) while((s32[]{:T(128)}, f32[4,128,128]{2,1,0:T(8,128)S(1)}, ...), condition=%wide.region_4.5_spmd.clone, body=%wide.region_3.4_spmd.clone.sunk | while | flops 264196 | bytes 792727 | solution.py:33
  322.1 6.2 fusion.59
  328.4 5.0 fusion.61
  335.4 10.9 copy.87
  346.2 4.1 convert_element_type.237
  350.3 53.5 %all_to_all.29 = bf16[4,512,512]{2,1,0:T(8,128)(2,1)} all-to-all(bf16[4,512,512]{2,1,0:T(8,128)(2,1)} %convert_element_type.237), channel_id=1, replica_groups=mesh['dp'=8,'mp'=4] {'mp'}, dimensions={0} | all-to-all | bytes 4194304 | tf_op jit(solution)/shard_map/all_to_all | solution.py:301
  403.9 4.1 copy.88
  408.0 9.8 multiply_reduce_fusion.1
  422.2 147.3 %all-gather.22.cloned.1.call-done = bf16[2048,2048]{1,0:T(8,128)(2,1)} async-done(((bf16[512,2048]{1,0:T(8,128)(2,1)}), bf16[2048,2048]{1,0:T(8,128)(2,1)}) %all-gather.22.cloned.1.call-update) | async-done | bytes 8388624 | tf_op jit(solution)/shard_map/all_gather | solution.py:306
  569.5 24.2 %convolution_convert_fusion.5 = bf16[2048,2048]{1,0:T(8,128)(2,1)} fusion(bf16[2048,2048]{1,0:T(8,128)(2,1)} %all-gather.22.cloned.1.call-done, bf16[2048,2048]{1,0:T(8,128)(2,1)} %param.26), kind=kOutput, calls=%fused_computation.38 | convolution fusion | flops 17184063488 | bytes 25165824 | tf_op jit(solution)/shard_map/dot_general | solution.py:308
  593.8 21.8 %convolution_convert_fusion.6 = bf16[2048,2048]{1,0:T(8,128)(2,1)} fusion(bf16[2048,2048]{1,0:T(8,128)(2,1)S(1)} %copy-done.34, bf16[2048,2048]{1,0:T(8,128)(2,1)} %param.25), kind=kOutput, calls=%fused_computation.39 | convolution fusion | flops 17184063488 | bytes 25165824 | tf_op jit(solution)/shard_map/dot_general | solution.py:307
  615.6 103.2 %all-gather.24.cloned.1.call-done = bf16[2048,2048]{1,0:T(8,128)(2,1)} async-done(((bf16[512,2048]{1,0:T(8,128)(2,1)}), bf16[2048,2048]{1,0:T(8,128)(2,1)}) %all-gather.24.cloned.1.call-update) | async-done | bytes 8388624 | tf_op jit(solution)/shard_map/all_gather | solution.py:320
  718.8 32.2 %fusion.13 = (bf16[2048,2048]{1,0:T(8,128)(2,1)}, bf16[2048,2048]{1,0:T(8,128)(2,1)}) fusion(bf16[2048,2048]{1,0:T(8,128)(2,1)} %convolution_convert_fusion.6, bf16[2048,2048]{1,0:T(8,128)(2,1)} %convolution_convert_fusion.5, bf16[2048,2048]{1,0:T(8,128)(2,1)} %all-gather.24.cloned.1.call-done, bf16[2048,2048]{1,0:T(8,128)(2,1)} %param.27), kind=kOutput, calls=%fused_computation.25 | convolution fusion | flops 17242783744 | bytes 50331648 | tf_op jit(solution)/shard_map/dot_general | solution.py:321
  751.0 24.4 %fusion.133 = f32[2048,2048]{1,0:T(8,128)} fusion(bf16[2048,2048]{1,0:T(8,128)(2,1)} %get-tuple-element.509, bf16[2048,2048]{1,0:T(8,128)(2,1)} %param.25), kind=kOutput, calls=%fused_computation.186 | convolution fusion | flops 17179869184 | bytes 33554432 | tf_op jit(solution)/shard_map/dot_general | solution.py:329
  775.4 25.7 %add_convert_fusion.1 = bf16[2048,2048]{1,0:T(8,128)(2,1)} fusion(f32[2048,2048]{1,0:T(8,128)} %fusion.133, bf16[2048,2048]{1,0:T(8,128)(2,1)} %get-tuple-element.508, bf16[2048,2048]{1,0:T(8,128)(2,1)} %param.26), kind=kOutput, calls=%fused_computation.27 | convolution fusion | flops 17188257792 | bytes 41943040 | tf_op jit(solution)/shard_map/dot_general | solution.py:330
  801.1 26.6 %convolution_convert_fusion.4 = bf16[2048,2048]{1,0:T(8,128)(2,1)} fusion(bf16[2048,2048]{1,0:T(8,128)(2,1)} %param.27, bf16[2048,2048]{1,0:T(8,128)(2,1)} %convolution_convert_fusion.5, bf16[2048,2048]{1,0:T(8,128)(2,1)} %convolution_convert_fusion.6), kind=kOutput, calls=%fused_computation.37 | convolution fusion | flops 17217617920 | bytes 33554432 | tf_op jit(solution)/shard_map/dot_general | solution.py:314
  827.8 116.2 %reduce-scatter.14.cloned.1.call-done = bf16[512,2048]{1,0:T(8,128)(2,1)} async-done(((bf16[2048,2048]{1,0:T(8,128)(2,1)}), bf16[512,2048]{1,0:T(8,128)(2,1)}) %reduce-scatter.14.cloned.1.call-update) | async-done | bytes 2097168 | tf_op jit(solution)/shard_map/reduce_scatter | solution.py:327
  944.0 4.8 fusion.28
  948.8 142.8 %reduce-scatter.12.cloned.1.call-done = bf16[512,2048]{1,0:T(8,128)(2,1)} async-done(((bf16[2048,2048]{1,0:T(8,128)(2,1)}), bf16[512,2048]{1,0:T(8,128)(2,1)}) %reduce-scatter.12.cloned.1.call-update) | async-done | bytes 2097168 | tf_op jit(solution)/shard_map/reduce_scatter | solution.py:313
  1091.6 6.3 fusion.25
  1097.9 9.7 convolution_convert_fusion.10
  1107.8 52.3 %all_to_all.30 = bf16[512,4,512]{2,0,1:T(8,128)(2,1)S(1)} all-to-all(bf16[512,4,512]{2,0,1:T(8,128)(2,1)S(1)} %bitcast.188), channel_id=1, replica_groups=mesh['dp'=8,'mp'=4] {'mp'}, dimensions={1} | all-to-all | bytes 4194304 | tf_op jit(solution)/shard_map/all_to_all | solution.py:342
  1162.8 5.2 reshape.277
  1168.0 13.3 fusion.93
  1181.8 10.6 convolution_convert_fusion.3
  1192.4 26.6 %convolution_convert_fusion = bf16[2048,2048]{1,0:T(8,128)(2,1)} fusion(bf16[2048,2048]{1,0:T(8,128)(2,1)} %all-gather.24.cloned.1.call-done, bf16[2048,2048]{1,0:T(8,128)(2,1)} %convolution_convert_fusion.5, bf16[2048,2048]{1,0:T(8,128)(2,1)} %convolution_convert_fusion.6), kind=kOutput, calls=%fused_computation.33 | convolution fusion | flops 17217617920 | bytes 33554432 | tf_op jit(solution)/shard_map/dot_general | solution.py:322
  1219.3 25.1 %convolution_convert_fusion.1 = bf16[2048,2048]{1,0:T(8,128)(2,1)} fusion(bf16[2048,2048]{1,0:T(8,128)(2,1)} %all-gather.22.cloned.1.call-done, bf16[2048,2048]{1,0:T(8,128)(2,1)} %get-tuple-element.508), kind=kOutput, calls=%fused_computation.34 | convolution fusion | flops 17184063488 | bytes 25165824 | tf_op jit(solution)/shard_map/dot_general | solution.py:326
  1244.4 24.1 %convolution_convert_fusion.2 = bf16[2048,2048]{1,0:T(8,128)(2,1)} fusion(bf16[2048,2048]{1,0:T(8,128)(2,1)} %all-gather.22.cloned.1.call-done, bf16[2048,2048]{1,0:T(8,128)(2,1)} %get-tuple-element.509), kind=kOutput, calls=%fused_computation.35 | convolution fusion | flops 17184063488 | bytes 25165824 | tf_op jit(solution)/shard_map/dot_general | solution.py:325
  1269.8 13.4 all-reduce.1
  1283.3 9.1 fusion.48
  1292.4 76.7 %shard_map.221 = (f32[4,2048,128]{2,1,0:T(8,128)}, f32[4,2048,128]{2,1,0:T(8,128)}, f32[4,2048,128]{2,1,0:T(8,128)}) custom-call(bf16[4,2048,128]{2,1,0:T(8,128)(2,1)} %bitcast.194, bf16[4,2048,128]{2,1,0:T(8,128)(2,1)} %bitcast.190, bf16[4,2048,128]{2,1,0:T(8,128)(2,1)} %bitcast.192, bf16[4,2048,128]{2,1,0:T(8,128)(2,1)} %get-tuple-element.510.do_ref, ...), custom_call_target="tpu_custom_call" | custom-call | flops 21474836480 | bytes 25165824 | tf_op jit(solution)/shard_map/pallas_call | solution.py:190
  1369.1 10.1 fusion.67
  1379.2 3.9 copy.94
  1383.2 4.7 fusion.55
  1388.6 8.6 all-gather.7
  1397.2 9.7 convolution_convert_fusion.9
  1407.4 18.9 %while.23 = (s32[]{:T(128)}, f32[4,128,128]{2,1,0:T(8,128)S(1)}, f32[4,128]{1,0:T(4,128)S(1)}, s32[]{:T(128)}, bf16[8,1]{0,1:T(2,128)(2,1)S(1)}, /*index=5*/bf16...) while((s32[]{:T(128)}, f32[4,128,128]{2,1,0:T(8,128)S(1)}, ...), condition=%wide.region_11.12_spmd.clone, body=%wide.region_10.11_spmd.clone.sunk | while | flops 330249 | bytes 660695 | solution.py:57
  1426.3 8.1 fusion.66
  1434.4 3.9 copy.97
  1438.3 11.6 convolution_convert_fusion.8
  1450.1 7.8 fusion.63
  1457.9 3.9 copy.100
  1461.9 10.2 convolution_convert_fusion.7
  1472.3 10.1 fusion.134
  1482.5 8.5 fusion.135
  1491.1 16.6 add_convert_fusion
  1516.2 31.5 %reduce-scatter.18.cloned.1.call-done = bf16[256,512]{1,0:T(8,128)(2,1)} async-done(((bf16[2048,512]{1,0:T(8,128)(2,1)}), bf16[256,512]{1,0:T(8,128)(2,1)}) %reduce-scatter.18.cloned.1.call-update) | async-done | bytes 262160 | tf_op jit(solution)/shard_map/reduce_scatter | solution.py:413
  1549.5 42.5 %reduce-scatter.20.cloned.1.call-done = bf16[256,512]{1,0:T(8,128)(2,1)} async-done(((bf16[2048,512]{1,0:T(8,128)(2,1)}), bf16[256,512]{1,0:T(8,128)(2,1)}) %reduce-scatter.20.cloned.1.call-update) | async-done | bytes 262160 | tf_op jit(solution)/shard_map/reduce_scatter | solution.py:413
  1593.8 42.5 %reduce-scatter.22.cloned.1.call-done = bf16[256,512]{1,0:T(8,128)(2,1)} async-done(((bf16[2048,512]{1,0:T(8,128)(2,1)}), bf16[256,512]{1,0:T(8,128)(2,1)}) %reduce-scatter.22.cloned.1.call-update) | async-done | bytes 262160 | tf_op jit(solution)/shard_map/reduce_scatter | solution.py:413
  1638.1 27.7 %reduce-scatter.26.cloned.1.call-done = bf16[512,256]{1,0:T(8,128)(2,1)} async-done(((bf16[2048,256]{1,0:T(8,128)(2,1)}), bf16[512,256]{1,0:T(8,128)(2,1)}) %reduce-scatter.26.cloned.1.call-update) | async-done | bytes 262160 | tf_op jit(solution)/shard_map/reduce_scatter | solution.py:417
  1667.6 143.6 %reduce-scatter.16.cloned.1.call-done = bf16[512,2048]{1,0:T(8,128)(2,1)} async-done(((bf16[2048,2048]{1,0:T(8,128)(2,1)}), bf16[512,2048]{1,0:T(8,128)(2,1)}) %reduce-scatter.16.cloned.1.call-update) | async-done | bytes 2097168 | tf_op jit(solution)/shard_map/reduce_scatter | solution.py:394
  1815.0 41.2 %all-reduce.2 = (f32[2048]{0:T(1024)}, f32[16]{0:T(128)}, f32[2048]{0:T(1024)}) all-reduce(f32[2048]{0:T(1024)S(1)} %get-tuple-element.473, f32[16]{0:T(128)S(1)} %multiply_dynamic-update-slice_fusion, f32[2048]{0:T(1024)S(1)} %copy-done.24), channel_id=1, replica_groups=mesh['dp'=8,'mp'=4] {'dp','mp'}, use_global_device_ids=true, to_apply=%region_15.16 | all-reduce | flops 4112 | bytes 32896 | tf_op jit(solution)/shard_map/psum | solution.py:410
  1856.2 6.9 fusion.23
  (218 shorter events, 90.8 us)
Async XLA Ops:
  7.2 213.3 %copy-start = (bf16[2048,512]{1,0:T(8,128)(2,1)S(1)}, bf16[2048,512]{1,0:T(8,128)(2,1)}, u32[]{:S(2)}) copy-start(bf16[2048,512]{1,0:T(8,128)(2,1)} %param.19) | copy-start | bytes 6291460
  7.2 8.1 copy-start.33
  7.2 158.8 %all-gather.16.cloned.1.call-start = ((), (), s32[]{:S(2)}) async-start(), calls=%async_computation.13 | async-start | bytes 10485760 | tf_op jit(solution)/shard_map/all_gather | solution.py:257
  9.5 0.6 copy-start.20
  13.5 188.2 %all-gather.18.cloned.1.call-start = ((), (), s32[]{:S(2)}) async-start(), calls=%async_computation.14 | async-start | bytes 1310720 | tf_op jit(solution)/shard_map/all_gather | solution.py:252
  15.3 282.9 %all-gather.26.cloned.1.call-start = ((), (), s32[]{:S(2)}) async-start(), calls=%async_computation.29 | async-start | bytes 2359296 | tf_op jit(solution)/shard_map/all_gather | solution.py:21
  17.5 201.6 %copy-start.19 = (s32[2048]{0:T(1024)}, s32[2048]{0:T(1024)S(1)}, u32[]{:S(2)}) copy-start(s32[2048]{0:T(1024)S(1)} %slice.22) | copy-start | bytes 24580
  21.3 212.4 %copy-start.25 = (f32[2048]{0:T(1024)}, f32[2048]{0:T(1024)S(1)}, u32[]{:S(2)}) copy-start(f32[2048]{0:T(1024)S(1)} %get-tuple-element.514) | copy-start | bytes 24580
  21.3 312.2 %copy-start.17 = (f32[2048]{0:T(1024)}, f32[2048]{0:T(1024)S(1)}, u32[]{:S(2)}) copy-start(f32[2048]{0:T(1024)S(1)} %get-tuple-element.513) | copy-start | bytes 24580
  193.9 8.5 copy-start.37
  193.9 26.6 %copy-start.36 = (f32[4]{0:T(128)S(1)}, f32[4]{0:T(128)}, u32[]{:S(2)}) copy-start(f32[4]{0:T(128)} %param.23) | copy-start | bytes 52
  201.7 206.3 %all-gather.20.cloned.1.call-start = ((), (), s32[]{:S(2)}) async-start(), calls=%async_computation.15 | async-start | bytes 9437184 | tf_op jit(solution)/shard_map/all_gather | solution.py:251
  202.3 367.3 %all-gather.22.cloned.1.call-start = ((), (), s32[]{:S(2)}) async-start(), calls=%async_computation.16 | async-start | bytes 10485760 | tf_op jit(solution)/shard_map/all_gather | solution.py:306
  220.5 113.0 %copy-start.27 = (f32[4]{0:T(128)}, f32[4]{0:T(128)S(1)}, u32[]{:S(2)}) copy-start(f32[4]{0:T(128)S(1)} %get-tuple-element.507) | copy-start | bytes 52
  220.5 113.0 %copy-start.29 = (f32[4]{0:T(128)}, f32[4]{0:T(128)S(1)}, u32[]{:S(2)}) copy-start(f32[4]{0:T(128)S(1)} %get-tuple-element.506) | copy-start | bytes 52
  322.0 11.3 copy-start.5
  322.1 6.3 copy-start.7
  322.1 11.3 copy-start.31
  328.3 5.1 copy-start.12
  328.3 5.1 copy-start.3
  333.4 2.0 copy-start.4
  333.4 2.0 copy-start.10
  408.0 11.8 copy-start.14
  417.8 2.0 copy-start.1
  417.8 2.0 copy-start.22
  421.6 297.2 %all-gather.24.cloned.1.call-start = ((), (), s32[]{:S(2)}) async-start(), calls=%async_computation.18 | async-start | bytes 10485760 | tf_op jit(solution)/shard_map/all_gather | solution.py:320
  422.1 521.9 %reduce-scatter.14.cloned.1.call-start = ((), (), s32[]{:S(2)}) async-start(), calls=%async_computation.19 | async-start | bytes 10485760 | tf_op jit(solution)/shard_map/reduce_scatter | solution.py:327
  569.5 24.2 %copy-start.34 = (bf16[2048,2048]{1,0:T(8,128)(2,1)S(1)}, bf16[2048,2048]{1,0:T(8,128)(2,1)}, u32[]{:S(2)}) copy-start(bf16[2048,2048]{1,0:T(8,128)(2,1)} %all-gather.22.cloned.1.call-done) | copy-start | bytes 25165828
  801.1 290.6 %reduce-scatter.12.cloned.1.call-start = ((), (), s32[]{:S(2)}) async-start(), calls=%async_computation.17 | async-start | bytes 10485760 | tf_op jit(solution)/shard_map/reduce_scatter | solution.py:313
  827.7 116.3 %copy-start.15 = (f32[2048]{0:T(1024)S(1)}, f32[2048]{0:T(1024)}, u32[]{:S(2)}) copy-start(f32[2048]{0:T(1024)} %param.24) | copy-start | bytes 24580
  827.7 116.3 %copy-start.23 = (f32[512]{0:T(512)S(1)}, f32[512]{0:T(512)}, u32[]{:S(2)}) copy-start(f32[512]{0:T(512)} %copy-done.22) | copy-start | bytes 6148
  827.7 579.6 %all-gather.28.cloned.1.call-start = ((), (), s32[]{:S(2)}) async-start(), calls=%async_computation.30 | async-start | bytes 1179648 | tf_op jit(solution)/shard_map/all_gather | solution.py:39
  1097.9 9.7 copy-start.2
  1162.8 5.3 copy-start.11
  1162.8 5.3 copy-start.18
  1162.8 5.3 copy-start.28
  1181.3 309.7 %reduce-scatter.24.cloned.1.call-start = ((), (), s32[]{:S(2)}) async-start(), calls=%async_computation.24 | async-start | bytes 9437184 | tf_op jit(solution)/shard_map/reduce_scatter | solution.py:413
  1192.4 315.3 %reduce-scatter.32.cloned.1.call-start = ((), (), s32[]{:S(2)}) async-start(), calls=%async_computation.28 | async-start | bytes 9437184 | tf_op jit(solution)/shard_map/reduce_scatter | solution.py:413
  1219.1 291.4 %reduce-scatter.30.cloned.1.call-start = ((), (), s32[]{:S(2)}) async-start(), calls=%async_computation.27 | async-start | bytes 9437184 | tf_op jit(solution)/shard_map/reduce_scatter | solution.py:413
  1244.4 268.9 %reduce-scatter.28.cloned.1.call-start = ((), (), s32[]{:S(2)}) async-start(), calls=%async_computation.26 | async-start | bytes 9437184 | tf_op jit(solution)/shard_map/reduce_scatter | solution.py:413
  1268.5 14.7 copy-start.30
  1268.6 279.2 %reduce-scatter.18.cloned.1.call-start = ((), (), s32[]{:S(2)}) async-start(), calls=%async_computation.21 | async-start | bytes 2359296 | tf_op jit(solution)/shard_map/reduce_scatter | solution.py:413
  1283.2 9.1 copy-start.13
  1292.4 76.7 %copy-start.6 = (f32[4,128,128]{2,1,0:T(8,128)S(1)}, f32[4,128,128]{2,1,0:T(8,128)}, u32[]{:S(2)}) copy-start(f32[4,128,128]{2,1,0:T(8,128)} %copy-done.5) | copy-start | bytes 786436
  1292.4 76.7 %copy-start.32 = (f32[4,128]{1,0:T(4,128)S(1)}, f32[4,128]{1,0:T(4,128)}, u32[]{:S(2)}) copy-start(f32[4,128]{1,0:T(4,128)} %copy-done.31) | copy-start | bytes 6148
  1383.2 14.0 copy-start.8
  1406.9 19.4 %copy-start.26 = (f32[2048]{0:T(1024)S(1)}, f32[2048]{0:T(1024)}, u32[]{:S(2)}) copy-start(f32[2048]{0:T(1024)} %copy-done.25) | copy-start | bytes 24580
  1406.9 185.1 %reduce-scatter.20.cloned.1.call-start = ((), (), s32[]{:S(2)}) async-start(), calls=%async_computation.22 | async-start | bytes 2359296 | tf_op jit(solution)/shard_map/reduce_scatter | solution.py:413
  1449.9 186.4 %reduce-scatter.22.cloned.1.call-start = ((), (), s32[]{:S(2)}) async-start(), calls=%async_computation.23 | async-start | bytes 2359296 | tf_op jit(solution)/shard_map/reduce_scatter | solution.py:413
  1472.1 193.8 %reduce-scatter.26.cloned.1.call-start = ((), (), s32[]{:S(2)}) async-start(), calls=%async_computation.25 | async-start | bytes 1310720 | tf_op jit(solution)/shard_map/reduce_scatter | solution.py:417
  1472.3 10.1 copy-start.9
  1472.3 10.1 copy-start.35
  1491.0 320.2 %reduce-scatter.16.cloned.1.call-start = ((), (), s32[]{:S(2)}) async-start(), calls=%async_computation.20 | async-start | bytes 10485760 | tf_op jit(solution)/shard_map/reduce_scatter | solution.py:394
  1510.4 300.7 %copy-start.16 = (f32[2048]{0:T(1024)S(1)}, f32[2048]{0:T(1024)}, u32[]{:S(2)}) copy-start(f32[2048]{0:T(1024)} %param.18) | copy-start | bytes 24580
  1510.4 300.7 %copy-start.21 = (f32[512]{0:T(512)S(1)}, f32[512]{0:T(512)}, u32[]{:S(2)}) copy-start(f32[512]{0:T(512)} %copy-done.20) | copy-start | bytes 6148
  1516.1 298.9 %copy-start.24 = (f32[2048]{0:T(1024)S(1)}, f32[2048]{0:T(1024)}, u32[]{:S(2)}) copy-start(f32[2048]{0:T(1024)} %get-tuple-element.471) | copy-start | bytes 24580
Sparse Core Ops, SparseCore 0:
  13.6 152.3 all-gather.15
  168.1 26.1 all-gather.17
  201.8 26.0 all-gather.25
  229.6 55.9 all-gather.19
  421.7 147.7 all-gather.21
  570.9 147.7 all-gather.23
  801.2 142.7 reduce-scatter.13
  946.4 145.2 reduce-scatter.11
  1181.4 22.5 all-gather.27
  1207.3 71.3 reduce-scatter.23
  1282.2 71.3 reduce-scatter.31
  1356.9 71.5 reduce-scatter.29
  1431.9 71.4 reduce-scatter.27
  1506.6 41.0 reduce-scatter.17
  1550.9 41.1 reduce-scatter.19
  1595.2 41.1 reduce-scatter.21
  1638.5 27.3 reduce-scatter.25
  1668.0 143.1 reduce-scatter.15

commit v2 on v1

--- a/solution.py
+++ b/solution.py
@@ -55,6 +55,54 @@
         return jax.tree.map(lambda a, b: jnp.where(reached, a, b), new, before)
 
     return lax.fori_loop(0, size, prefix_hop, start)
+
+
+def ring_pairs(n, step):
+    return [(j, (j + step) % n) for j in range(n)]
+
+
+def ring_gather(rows, axis, compute):
+    n, place = lax.axis_size(axis), lax.axis_index(axis)
+    count = rows.shape[0]
+    half = count // 2
+    own = compute(rows)
+    outs = [
+        lax.dynamic_update_slice_in_dim(
+            jnp.zeros((n * count,) + part.shape[1:], part.dtype), part, place * count, 0
+        )
+        for part in own
+    ]
+    ahead, behind = rows[:half], rows[half:]
+    for step in range(1, n):
+        ahead = lax.ppermute(ahead, axis, ring_pairs(n, 1))
+        behind = lax.ppermute(behind, axis, ring_pairs(n, -1))
+        for got, start in (
+            (compute(ahead), ((place - step) % n) * count),
+            (compute(behind), ((place + step) % n) * count + half),
+        ):
+            outs = [
+                lax.dynamic_update_slice_in_dim(out, part, start, 0)
+                for out, part in zip(outs, got)
+            ]
+    return outs
+
+
+def ring_scatter(partial, axis, kind=jnp.bfloat16):
+    n, place = lax.axis_size(axis), lax.axis_index(axis)
+    count = partial.shape[0] // n
+    half = count // 2
+
+    def chunk(owner, start):
+        return lax.dynamic_slice_in_dim(partial, owner * count + start, half, 0).astype(jnp.float32)
+
+    ahead = chunk((place - 1) % n, 0)
+    behind = chunk((place + 1) % n, half)
+    for step in range(1, n):
+        ahead = lax.ppermute(ahead.astype(kind), axis, ring_pairs(n, 1)).astype(jnp.float32)
+        ahead = ahead + chunk((place - 1 - step) % n, 0)
+        behind = lax.ppermute(behind.astype(kind), axis, ring_pairs(n, -1)).astype(jnp.float32)
+        behind = behind + chunk((place + 1 + step) % n, half)
+    return jnp.concatenate([ahead, behind], axis=0)
 
 
 def inverse_rms(values):
@@ -254,16 +302,14 @@
     x_rows = tokens.astype(jnp.float32)
     inverse1 = inverse_rms(x_rows)
     normed1 = (x_rows * inverse1 * norm1_gain).astype(jnp.bfloat16)
-    normed1_all = lax.all_gather(normed1, "mp", axis=0, tiled=True)
-    query_h = to_heads(
-        jnp.dot(normed1_all, w_query, preferred_element_type=jnp.float32).astype(jnp.bfloat16)
-    )
-    key_h = to_heads(
-        jnp.dot(normed1_all, w_key, preferred_element_type=jnp.float32).astype(jnp.bfloat16)
-    )
-    value_h = to_heads(
-        jnp.dot(normed1_all, w_value, preferred_element_type=jnp.float32).astype(jnp.bfloat16)
-    )
+    def project_qkv(rows):
+        return (rows,) + tuple(
+            jnp.dot(rows, weight, preferred_element_type=jnp.float32).astype(jnp.bfloat16)
+            for weight in (w_query, w_key, w_value)
+        )
+
+    normed1_all, query_rows, key_rows, value_rows = ring_gather(normed1, "mp", project_qkv)
+    query_h, key_h, value_h = (to_heads(a) for a in (query_rows, key_rows, value_rows))
     dot_out, log_sums = attention_fwd(query_h, key_h, value_h, doc_index, score_scale)
     query_f = query_h.astype(jnp.float32).reshape(seg_shape)
     key_f = key_h.astype(jnp.float32).reshape(seg_shape)
@@ -303,36 +349,31 @@
     resid = x_rows + attn_sum
     inverse2 = inverse_rms(resid)
     normed2 = (resid * inverse2 * norm2_gain).astype(jnp.bfloat16)
-    normed2_all = lax.all_gather(normed2, "mp", axis=0, tiled=True)
-    gate_pre = jnp.dot(normed2_all, w_gate, preferred_element_type=jnp.float32).astype(jnp.bfloat16)
-    up_pre = jnp.dot(normed2_all, w_up, preferred_element_type=jnp.float32).astype(jnp.bfloat16)
+    def project_ffn(rows):
+        return (rows,) + tuple(
+            jnp.dot(rows, weight, preferred_element_type=jnp.float32).astype(jnp.bfloat16)
+            for weight in (w_gate, w_up)
+        )
+
+    normed2_all, gate_pre, up_pre = ring_gather(normed2, "mp", project_ffn)
     gate_f = gate_pre.astype(jnp.float32)
     up_f = up_pre.astype(jnp.float32)
     sig_gate = jax.nn.sigmoid(gate_f)
     act = (gate_f * sig_gate * up_f).astype(jnp.bfloat16)
-    mlp_sum = lax.psum_scatter(
-        jnp.dot(act, w_down, preferred_element_type=jnp.float32).astype(jnp.bfloat16),
-        "mp",
-        scatter_dimension=0,
-        tiled=True,
-    ).astype(jnp.float32)
+    mlp_sum = ring_scatter(jnp.dot(act, w_down, preferred_element_type=jnp.float32), "mp")
     output = (resid + mlp_sum).astype(jnp.bfloat16)
-    grad_rows_all = lax.all_gather(out_grad, "mp", axis=0, tiled=True)
+    (grad_rows_all,) = ring_gather(out_grad, "mp", lambda rows: (rows,))
     d_act = jnp.dot(grad_rows_all, w_down.T, preferred_element_type=jnp.float32)
     grad_down = jnp.dot(act.T, grad_rows_all, preferred_element_type=jnp.float32)
     d_gate = (d_act * up_f * sig_gate * (1.0 + gate_f * (1.0 - sig_gate))).astype(jnp.bfloat16)
     d_up = (d_act * gate_f * sig_gate).astype(jnp.bfloat16)
     grad_gate = jnp.dot(normed2_all.T, d_gate, preferred_element_type=jnp.float32)
     grad_up = jnp.dot(normed2_all.T, d_up, preferred_element_type=jnp.float32)
-    d_norm2 = lax.psum_scatter(
-        (
-            jnp.dot(d_gate, w_gate.T, preferred_element_type=jnp.float32)
-            + jnp.dot(d_up, w_up.T, preferred_element_type=jnp.float32)
-        ).astype(jnp.bfloat16),
+    d_norm2 = ring_scatter(
+        jnp.dot(d_gate, w_gate.T, preferred_element_type=jnp.float32)
+        + jnp.dot(d_up, w_up.T, preferred_element_type=jnp.float32),
         "mp",
-        scatter_dimension=0,
-        tiled=True,
-    ).astype(jnp.float32)
+    )
     gain2_part = jnp.sum(d_norm2 * resid * inverse2, axis=0)
     d_resid = out_grad.astype(jnp.float32) + norm_backward(resid, inverse2, norm2_gain, d_norm2)
     d_resid_low = d_resid.astype(jnp.bfloat16)
@@ -391,14 +432,9 @@
     grad_value = jnp.dot(normed1_all.T, d_value, preferred_element_type=jnp.float32)
     total_term = jnp.dot(d_query, w_query.T, preferred_element_type=jnp.float32)
     total_term = total_term + jnp.dot(d_key, w_key.T, preferred_element_type=jnp.float32)
-    d_norm1 = lax.psum_scatter(
-        (total_term + jnp.dot(d_value, w_value.T, preferred_element_type=jnp.float32)).astype(
-            jnp.bfloat16
-        ),
-        "mp",
-        scatter_dimension=0,
-        tiled=True,
-    ).astype(jnp.float32)
+    d_norm1 = ring_scatter(
+        total_term + jnp.dot(d_value, w_value.T, preferred_element_type=jnp.float32), "mp"
+    )
     gain1_part = jnp.sum(d_norm1 * x_rows * inverse1, axis=0)
     input_grad = d_resid + norm_backward(x_rows, inverse1, norm1_gain, d_norm1)
     gate_full = lax.dynamic_update_slice_in_dim(

time: 1880 us -> 1720 us (0.915)
  waiting for transfers between devices: 944 us -> 568 us
  starting transfers between devices: 2.1 us -> 110 us
  local copies, waits for them, and re-layouts: 67.9 us -> 174 us
  blocking collectives: 191 us -> 135 us
  matrix products: 424 us -> 462 us
    ppermute x0 -> x36, waiting for transfers between devices: none -> 567 us  [the longest x9 188 us: ring_scatter(): lax.ppermute(behind.astype(kind), axis, ring_pairs(n, -1))]
    reduce_scatter x3 -> x0, waiting for transfers between devices: 403 us -> none  [the longest x1 144 us: local(): lax.psum_scatter((total_term + jnp.dot(d_value, w_value.T, preferred_elem...]
    all_gather x3 -> x0, waiting for transfers between devices: 395 us -> none  [the longest x1 147 us: local(): normed2_all = lax.all_gather(normed2, 'mp', axis=0, tiled=True)]
    reduce_scatter x7, waiting for transfers between devices: 117 us -> 0.01 us  [over_dp(): lax.psum_scatter(grad.astype(jnp.bfloat16), 'dp', scatter_dimension=dim,...]
    ppermute x0 -> x36, starting transfers between devices: none -> 103 us  [the longest x9 34.8 us: ring_gather(): ahead = lax.ppermute(ahead, axis, ring_pairs(n, 1))]
    dynamic_update_slice x0 -> x36, local copies, waits for them, and re-layouts: none -> 54.1 us  [the longest x35 52.6 us: ring_gather(): lax.dynamic_update_slice_in_dim(out, part, start, 0)]
    all_to_all x1 -> x0, blocking collectives: 53.5 us -> none  [local(): mixed = lax.all_to_all(mixed_cols, 'mp', 0, 1, tiled=True)]
    dot_general x5 -> x35, matrix products: 75 us -> 116 us  [the longest x14 59.7 us: project_ffn(): jnp.dot(rows, weight, preferred_element_type=jnp.float32)]
  transfers between devices with their start and end apart: 18 -> 49, of which waited for: 10 -> 29; matrix products, arithmetic and copies ran while one was open for 23% -> 35% of each run, Pallas kernels for 7% -> 7%
where the time goes in v2:
time: 1720 us; the launch traced here: 1710 us
  waiting for transfers between devices  568 us (33%)
  matrix products  462 us (27%)
  local copies, waits for them, and re-layouts  174 us (10%)
  blocking collectives  135 us (8%)
  Pallas kernels  127 us (7%)
  starting transfers between devices  110 us (6%)
  other arithmetic  108 us (6%)
  between operations  17.7 us (1%)
    ppermute x9, waiting for transfers between devices, ring_scatter(): lax.ppermute(behind.astype(kind), axis, ring_pairs(n, -1))  188 us
    ppermute x9, waiting for transfers between devices, ring_gather(): ahead = lax.ppermute(ahead, axis, ring_pairs(n, 1))  149 us
    ppermute x9, waiting for transfers between devices, ring_scatter(): lax.ppermute(ahead.astype(kind), axis, ring_pairs(n, 1)).astype(jnp.float32)  146 us
    ppermute x9, waiting for transfers between devices, ring_gather(): behind = lax.ppermute(behind, axis, ring_pairs(n, -1))  83.7 us
    pallas_call x1, Pallas kernels, attention_bwd(): pl.pallas_call(functools.partial(_bwd_kernel, scale, seg), grid=(H, nq),...  76.3 us
    dot_general x14, matrix products, project_ffn(): jnp.dot(rows, weight, preferred_element_type=jnp.float32)  59.7 us
    dot_general x21, matrix products, project_qkv(): jnp.dot(rows, weight, preferred_element_type=jnp.float32)  56.4 us
    dynamic_update_slice x35, local copies, waits for them, and re-layouts, ring_gather(): lax.dynamic_update_slice_in_dim(out, part, start, 0)  52.6 us
  transfers between devices with their start and end apart: 49, of which 29 were waited for; matrix products, arithmetic and copies ran while one was open for 35% of the time, Pallas kernels for 7%

profile of v2, /device:TPU:0, one launch (start us, length us, event | category | flops | bytes accessed | tf_op | source)
XLA Modules:
  0.0 1706.8 jit_solution(4108735474889240136)
XLA Ops:
  38.9 22.7 %collective-permute-done.1 = bf16[256,2048]{1,0:T(8,128)(2,1)S(1)} collective-permute-done((bf16[256,2048]{1,0:T(8,128)(2,1)}, bf16[256,2048]{1,0:T(8,128)(2,1)S(1)}, u32[]{:S(2)}, u32[]{:S(2)}) %collective-permute-start.1) | collective-permute-done | bytes 1048608 | tf_op jit(solution)/shard_map/ppermute | solution.py:78
  66.5 20.1 %collective-permute-done = bf16[256,2048]{1,0:T(8,128)(2,1)} collective-permute-done((bf16[256,2048]{1,0:T(8,128)(2,1)}, bf16[256,2048]{1,0:T(8,128)(2,1)}, u32[]{:S(2)}, u32[]{:S(2)}) %collective-permute-start) | collective-permute-done | bytes 1048608 | tf_op jit(solution)/shard_map/ppermute | solution.py:77
  116.0 18.0 %collective-permute-start.5 = (bf16[256,2048]{1,0:T(8,128)(2,1)}, bf16[256,2048]{1,0:T(8,128)(2,1)}, u32[]{:S(2)}, u32[]{:S(2)}) collective-permute-start(bf16[256,2048]{1,0:T(8,128)(2,1)} %collective-permute-done.3), channel_id=1, source_target_pairs={{0,3},{1,0},{2,1},{3,2},{4,7},{5,4},{6,5},{7,6},{8,11},{9,8},{10,9... | collective-permute-start | bytes 3145736 | tf_op jit(solution)/shard_map/ppermute | solution.py:78
  150.2 10.0 collective-permute-done.5
  168.1 7.9 collective-permute-done.4
  199.9 7.8 fusion.94
  215.6 13.4 all-reduce
  262.8 8.3 all-gather.6
  271.1 50.7 %shard_map.220 = (f32[4,2048,128]{2,1,0:T(8,128)}, f32[4,2048,1]{2,1,0:T(8,128)}) custom-call(bf16[4,2048,128]{2,1,0:T(8,128)(2,1)} %bitcast.253, bf16[4,2048,128]{2,1,0:T(8,128)(2,1)} %bitcast.249, bf16[4,2048,128]{2,1,0:T(8,128)(2,1)} %bitcast.251, s32[2048,1]{1,0:T(8,128)} %copy.158.docq_ref, s32[1,2048]{1,0:T(1,128)} %bitcast.266), custom_call_target="tpu_custom_call" | custom-call | flops 8589934592 | bytes 10485760 | tf_op jit(solution)/shard_map/pallas_call | solution.py:213
  321.9 23.9 %while.22 = (s32[]{:T(128)}, f32[4,128,128]{2,1,0:T(8,128)S(1)}, f32[4,128]{1,0:T(4,128)S(1)}, s32[]{:T(128)}, f32[8,1]{0,1:T(1,128)S(1)}, /*index=5*/f32[8,4,12...) while((s32[]{:T(128)}, f32[4,128,128]{2,1,0:T(8,128)S(1)}, ...), condition=%wide.region_4.5_spmd.clone, body=%wide.region_3.4_spmd.clone.sunk | while | flops 264196 | bytes 792727 | solution.py:33
  359.1 10.9 copy.159
  383.0 58.0 %collective-permute-done.20 = bf16[256,2048]{1,0:T(8,128)(2,1)S(1)} collective-permute-done((bf16[256,2048]{1,0:T(8,128)(2,1)}, bf16[256,2048]{1,0:T(8,128)(2,1)S(1)}, u32[]{:S(2)}, u32[]{:S(2)}) %collective-permute-start.20) | collective-permute-done | bytes 1048608 | tf_op jit(solution)/shard_map/ppermute | solution.py:77
  441.0 30.5 %collective-permute-start.22 = (bf16[256,2048]{1,0:T(8,128)(2,1)S(1)}, bf16[256,2048]{1,0:T(8,128)(2,1)S(1)}, u32[]{:S(2)}, u32[]{:S(2)}) collective-permute-start(bf16[256,2048]{1,0:T(8,128)(2,1)S(1)} %collective-permute-done.20), channel_id=1, source_target_pairs={{0,1},{1,2},{2,3},{3,0},{4,5},{5,6},{6,7},{7,4},{8,9},{9,10},{10,1... | collective-permute-start | bytes 3145736 | tf_op jit(solution)/shard_map/ppermute | solution.py:77
  484.0 11.0 collective-permute-done.22
  496.2 22.2 %collective-permute-done.23 = bf16[256,2048]{1,0:T(8,128)(2,1)S(1)} collective-permute-done((bf16[256,2048]{1,0:T(8,128)(2,1)S(1)}, bf16[256,2048]{1,0:T(8,128)(2,1)S(1)}, u32[]{:S(2)}, u32[]{:S(2)}) %collective-permute-start.23) | collective-permute-done | bytes 1048608 | tf_op jit(solution)/shard_map/ppermute | solution.py:78
  523.9 9.8 multiply_reduce_fusion.3
  542.9 9.1 fusion.48
  556.5 9.3 fusion.49
  569.4 17.9 %collective-permute-done.6 = bf16[256,2048]{1,0:T(8,128)(2,1)S(1)} collective-permute-done((bf16[256,2048]{1,0:T(8,128)(2,1)S(1)}, bf16[256,2048]{1,0:T(8,128)(2,1)S(1)}, u32[]{:S(2)}, u32[]{:S(2)}) %collective-permute-start.6) | collective-permute-done | bytes 1048608 | tf_op jit(solution)/shard_map/ppermute | solution.py:77
  601.2 24.0 %collective-permute-done.9 = bf16[256,2048]{1,0:T(8,128)(2,1)S(1)} collective-permute-done((bf16[256,2048]{1,0:T(8,128)(2,1)S(1)}, bf16[256,2048]{1,0:T(8,128)(2,1)S(1)}, u32[]{:S(2)}, u32[]{:S(2)}) %collective-permute-start.9) | collective-permute-done | bytes 1048608 | tf_op jit(solution)/shard_map/ppermute | solution.py:78
  625.1 7.1 collective-permute-done.8
  646.0 26.8 %collective-permute-done.10 = bf16[256,2048]{1,0:T(8,128)(2,1)S(1)} collective-permute-done((bf16[256,2048]{1,0:T(8,128)(2,1)S(1)}, bf16[256,2048]{1,0:T(8,128)(2,1)S(1)}, u32[]{:S(2)}, u32[]{:S(2)}) %collective-permute-start.10) | collective-permute-done | bytes 1048608 | tf_op jit(solution)/shard_map/ppermute | solution.py:77
  686.8 31.8 %fusion.13 = (bf16[2048,2048]{1,0:T(8,128)(2,1)}, bf16[2048,2048]{1,0:T(8,128)(2,1)}) fusion(bf16[2048,2048]{1,0:T(8,128)(2,1)} %fusion.69, bf16[2048,2048]{1,0:T(8,128)(2,1)} %fusion.63, bf16[2048,2048]{1,0:T(8,128)(2,1)} %constant_dynamic-update-slice_fusion.14, bf16[2048,2048]{1,0:T(8,128)(2,1)} %param.27), kind=kOutput, calls=%fused_computation.25 | convolution fusion | flops 17242783744 | bytes 50331648 | tf_op jit(solution)/shard_map/dot_general | solution.py:366
  718.6 24.3 %fusion.148 = f32[2048,2048]{1,0:T(8,128)} fusion(bf16[2048,2048]{1,0:T(8,128)(2,1)} %get-tuple-element.513, bf16[2048,2048]{1,0:T(8,128)(2,1)} %param.25), kind=kOutput, calls=%fused_computation.294 | convolution fusion | flops 17179869184 | bytes 33554432 | tf_op jit(solution)/shard_map/dot_general | solution.py:373
  743.0 26.4 %convolution_add_fusion = f32[2048,2048]{1,0:T(8,128)} fusion(f32[2048,2048]{1,0:T(8,128)} %fusion.148, bf16[2048,2048]{1,0:T(8,128)(2,1)} %get-tuple-element.512, bf16[2048,2048]{1,0:T(8,128)(2,1)} %param.26), kind=kOutput, calls=%fused_computation.27 | convolution fusion | flops 17184063488 | bytes 50331648 | tf_op jit(solution)/shard_map/dot_general | solution.py:374
  775.8 24.4 %fusion.140 = f32[2048,2048]{1,0:T(8,128)S(1)} fusion(bf16[2048,2048]{1,0:T(8,128)(2,1)} %param.27, bf16[2048,2048]{1,0:T(8,128)(2,1)} %fusion.63, bf16[2048,2048]{1,0:T(8,128)(2,1)} %fusion.69), kind=kOutput, calls=%fused_computation.288 | convolution fusion | flops 17213423616 | bytes 41943040 | tf_op jit(solution)/shard_map/dot_general | solution.py:363
  804.4 18.0 %collective-permute-done.27 = bf16[256,2048]{1,0:T(8,128)(2,1)S(1)} collective-permute-done((bf16[256,2048]{1,0:T(8,128)(2,1)S(1)}, bf16[256,2048]{1,0:T(8,128)(2,1)S(1)}, u32[]{:S(2)}, u32[]{:S(2)}) %collective-permute-start.27) | collective-permute-done | bytes 1048608 | tf_op jit(solution)/shard_map/ppermute | solution.py:103
  829.2 15.6 collective-permute-done.12
  844.9 22.5 %collective-permute-done.15 = bf16[256,2048]{1,0:T(8,128)(2,1)S(1)} collective-permute-done((bf16[256,2048]{1,0:T(8,128)(2,1)S(1)}, bf16[256,2048]{1,0:T(8,128)(2,1)S(1)}, u32[]{:S(2)}, u32[]{:S(2)}) %collective-permute-start.15) | collective-permute-done | bytes 1048608 | tf_op jit(solution)/shard_map/ppermute | solution.py:103
  873.4 16.4 collective-permute-done.25
  889.8 22.4 %collective-permute-done.28 = bf16[256,2048]{1,0:T(8,128)(2,1)S(1)} collective-permute-done((bf16[256,2048]{1,0:T(8,128)(2,1)S(1)}, bf16[256,2048]{1,0:T(8,128)(2,1)S(1)}, u32[]{:S(2)}, u32[]{:S(2)}) %collective-permute-start.28) | collective-permute-done | bytes 1048608 | tf_op jit(solution)/shard_map/ppermute | solution.py:103
  920.3 14.5 collective-permute-done.13
  934.8 22.4 %collective-permute-done.16 = bf16[256,2048]{1,0:T(8,128)(2,1)} collective-permute-done((bf16[256,2048]{1,0:T(8,128)(2,1)}, bf16[256,2048]{1,0:T(8,128)(2,1)}, u32[]{:S(2)}, u32[]{:S(2)}) %collective-permute-start.16) | collective-permute-done | bytes 1048608 | tf_op jit(solution)/shard_map/ppermute | solution.py:103
  964.3 15.6 collective-permute-done.26
  979.9 22.2 %collective-permute-done.29 = bf16[256,2048]{1,0:T(8,128)(2,1)} collective-permute-done((bf16[256,2048]{1,0:T(8,128)(2,1)}, bf16[256,2048]{1,0:T(8,128)(2,1)}, u32[]{:S(2)}, u32[]{:S(2)}) %collective-permute-start.29) | collective-permute-done | bytes 1048608 | tf_op jit(solution)/shard_map/ppermute | solution.py:103
  1007.2 17.6 %collective-permute-done.14 = bf16[256,2048]{1,0:T(8,128)(2,1)S(1)} collective-permute-done((bf16[256,2048]{1,0:T(8,128)(2,1)S(1)}, bf16[256,2048]{1,0:T(8,128)(2,1)S(1)}, u32[]{:S(2)}, u32[]{:S(2)}) %collective-permute-start.14) | collective-permute-done | bytes 1048608 | tf_op jit(solution)/shard_map/ppermute | solution.py:101
  1024.8 20.3 %collective-permute-done.17 = bf16[256,2048]{1,0:T(8,128)(2,1)S(1)} collective-permute-done((bf16[256,2048]{1,0:T(8,128)(2,1)S(1)}, bf16[256,2048]{1,0:T(8,128)(2,1)S(1)}, u32[]{:S(2)}, u32[]{:S(2)}) %collective-permute-start.17) | collective-permute-done | bytes 1048608 | tf_op jit(solution)/shard_map/ppermute | solution.py:103
  1058.1 51.1 %all_to_all.29 = bf16[512,4,512]{2,0,1:T(8,128)(2,1)S(1)} all-to-all(bf16[512,4,512]{2,0,1:T(8,128)(2,1)S(1)} %bitcast.247), channel_id=1, replica_groups=mesh['dp'=8,'mp'=4] {'mp'}, dimensions={1} | all-to-all | bytes 4194304 | tf_op jit(solution)/shard_map/all_to_all | solution.py:383
  1117.1 13.3 fusion.103
  1130.6 10.7 convolution_convert_fusion.3
  1142.7 11.9 all-reduce.1
  1177.3 76.3 %shard_map.221 = (f32[4,2048,128]{2,1,0:T(8,128)}, f32[4,2048,128]{2,1,0:T(8,128)}, f32[4,2048,128]{2,1,0:T(8,128)}) custom-call(bf16[4,2048,128]{2,1,0:T(8,128)(2,1)} %bitcast.254, bf16[4,2048,128]{2,1,0:T(8,128)(2,1)} %bitcast.250, bf16[4,2048,128]{2,1,0:T(8,128)(2,1)} %bitcast.252, bf16[4,2048,128]{2,1,0:T(8,128)(2,1)} %get-tuple-element.538.do_ref, ...), custom_call_target="tpu_custom_call" | custom-call | flops 21474836480 | bytes 25165824 | tf_op jit(solution)/shard_map/pallas_call | solution.py:238
  1253.6 9.5 fusion.62
  1272.5 8.8 all-gather.7
  1281.3 9.5 convolution_convert_fusion.6
  1290.9 18.8 %while.23 = (s32[]{:T(128)}, f32[4,128,128]{2,1,0:T(8,128)S(1)}, f32[4,128]{1,0:T(4,128)S(1)}, s32[]{:T(128)}, bf16[8,1]{0,1:T(2,128)(2,1)S(1)}, /*index=5*/bf16...) while((s32[]{:T(128)}, f32[4,128,128]{2,1,0:T(8,128)S(1)}, ...), condition=%wide.region_9.10_spmd.clone, body=%wide.region_8.9_spmd.clone.sunk | while | flops 330249 | bytes 660695 | solution.py:57
  1309.7 8.3 fusion.61
  1322.0 10.1 convolution_convert_fusion.5
  1332.5 7.8 fusion.58
  1344.3 10.2 convolution_convert_fusion.4
  1354.8 26.6 %convolution_convert_fusion = bf16[2048,2048]{1,0:T(8,128)(2,1)} fusion(bf16[2048,2048]{1,0:T(8,128)(2,1)} %constant_dynamic-update-slice_fusion.14, bf16[2048,2048]{1,0:T(8,128)(2,1)} %fusion.63, bf16[2048,2048]{1,0:T(8,128)(2,1)} %fusion.69), kind=kOutput, calls=%fused_computation.33 | convolution fusion | flops 17217617920 | bytes 33554432 | tf_op jit(solution)/shard_map/dot_general | solution.py:367
  1389.2 24.1 %convolution_convert_fusion.1 = bf16[2048,2048]{1,0:T(8,128)(2,1)} fusion(bf16[2048,2048]{1,0:T(8,128)(2,1)} %constant_dynamic-update-slice_fusion, bf16[2048,2048]{1,0:T(8,128)(2,1)} %get-tuple-element.512), kind=kOutput, calls=%fused_computation.34 | convolution fusion | flops 17184063488 | bytes 25165824 | tf_op jit(solution)/shard_map/dot_general | solution.py:371
  1413.4 23.9 %convolution_convert_fusion.2 = bf16[2048,2048]{1,0:T(8,128)(2,1)} fusion(bf16[2048,2048]{1,0:T(8,128)(2,1)} %constant_dynamic-update-slice_fusion, bf16[2048,2048]{1,0:T(8,128)(2,1)} %get-tuple-element.513), kind=kOutput, calls=%fused_computation.35 | convolution fusion | flops 17184063488 | bytes 25165824 | tf_op jit(solution)/shard_map/dot_general | solution.py:370
  1437.6 10.3 fusion.149
  1448.0 8.5 fusion.150
  1456.5 23.4 %add_add_fusion = f32[2048,2048]{1,0:T(8,128)} fusion(f32[2048,2048]{1,0:T(8,128)} %fusion.149, f32[2048,2048]{1,0:T(8,128)} %fusion.150, bf16[2048,512]{0,1:T(8,128)(2,1)} %bitcast.246, bf16[2048,512]{1,0:T(8,128)(2,1)} %param.21), kind=kOutput, calls=%fused_computation.26 | convolution fusion | flops 4303355904 | bytes 54525952 | tf_op jit(solution)/shard_map/dot_general | solution.py:436
  1486.6 24.0 %collective-permute-done.30 = bf16[256,2048]{1,0:T(8,128)(2,1)S(1)} collective-permute-done((bf16[256,2048]{1,0:T(8,128)(2,1)S(1)}, bf16[256,2048]{1,0:T(8,128)(2,1)S(1)}, u32[]{:S(2)}, u32[]{:S(2)}) %collective-permute-start.30) | collective-permute-done | bytes 1048608 | tf_op jit(solution)/shard_map/ppermute | solution.py:101
  1510.7 20.8 %collective-permute-done.33 = bf16[256,2048]{1,0:T(8,128)(2,1)S(1)} collective-permute-done((bf16[256,2048]{1,0:T(8,128)(2,1)S(1)}, bf16[256,2048]{1,0:T(8,128)(2,1)S(1)}, u32[]{:S(2)}, u32[]{:S(2)}) %collective-permute-start.33) | collective-permute-done | bytes 1048608 | tf_op jit(solution)/shard_map/ppermute | solution.py:103
  1538.5 24.0 %collective-permute-done.31 = bf16[256,2048]{1,0:T(8,128)(2,1)S(1)} collective-permute-done((bf16[256,2048]{1,0:T(8,128)(2,1)S(1)}, bf16[256,2048]{1,0:T(8,128)(2,1)S(1)}, u32[]{:S(2)}, u32[]{:S(2)}) %collective-permute-start.31) | collective-permute-done | bytes 1048608 | tf_op jit(solution)/shard_map/ppermute | solution.py:101
  1562.5 20.3 %collective-permute-done.34 = bf16[256,2048]{1,0:T(8,128)(2,1)S(1)} collective-permute-done((bf16[256,2048]{1,0:T(8,128)(2,1)S(1)}, bf16[256,2048]{1,0:T(8,128)(2,1)S(1)}, u32[]{:S(2)}, u32[]{:S(2)}) %collective-permute-start.34) | collective-permute-done | bytes 1048608 | tf_op jit(solution)/shard_map/ppermute | solution.py:103
  1597.1 18.5 %collective-permute-done.32 = bf16[256,2048]{1,0:T(8,128)(2,1)} collective-permute-done((bf16[256,2048]{1,0:T(8,128)(2,1)}, bf16[256,2048]{1,0:T(8,128)(2,1)}, u32[]{:S(2)}, u32[]{:S(2)}) %collective-permute-start.32) | collective-permute-done | bytes 1048608 | tf_op jit(solution)/shard_map/ppermute | solution.py:101
  1615.6 19.6 %collective-permute-done.35 = bf16[256,2048]{1,0:T(8,128)(2,1)} collective-permute-done((bf16[256,2048]{1,0:T(8,128)(2,1)S(1)}, bf16[256,2048]{1,0:T(8,128)(2,1)}, u32[]{:S(2)}, u32[]{:S(2)}) %collective-permute-start.35) | collective-permute-done | bytes 1048608 | tf_op jit(solution)/shard_map/ppermute | solution.py:103
  1640.7 41.3 %all-reduce.2 = (f32[2048]{0:T(1024)}, f32[16]{0:T(128)}, f32[2048]{0:T(1024)}) all-reduce(f32[2048]{0:T(1024)S(1)} %get-tuple-element.473, f32[16]{0:T(128)S(1)} %multiply_dynamic-update-slice_fusion, f32[2048]{0:T(1024)S(1)} %copy-done.49), channel_id=1, replica_groups=mesh['dp'=8,'mp'=4] {'dp','mp'}, use_global_device_ids=true, to_apply=%region_12.13 | all-reduce | flops 4112 | bytes 32896 | tf_op jit(solution)/shard_map/psum | solution.py:446
  1682.0 7.5 fusion.20
  (457 shorter events, 453.0 us)
Async XLA Ops:
  7.2 225.3 %copy-start = (bf16[2048,512]{1,0:T(8,128)(2,1)S(1)}, bf16[2048,512]{1,0:T(8,128)(2,1)}, u32[]{:S(2)}) copy-start(bf16[2048,512]{1,0:T(8,128)(2,1)} %param.19) | copy-start | bytes 6291460
  7.2 200.7 %all-gather.13.cloned.1.call-start = ((), (), s32[]{:S(2)}) async-start(), calls=%async_computation.10 | async-start | bytes 1310720 | tf_op jit(solution)/shard_map/all_gather | solution.py:300
  9.1 312.8 %all-gather.17.cloned.1.call-start = ((), (), s32[]{:S(2)}) async-start(), calls=%async_computation.20 | async-start | bytes 2359296 | tf_op jit(solution)/shard_map/all_gather | solution.py:21
  18.0 43.7 %collective-permute-start.1 = (bf16[256,2048]{1,0:T(8,128)(2,1)}, bf16[256,2048]{1,0:T(8,128)(2,1)S(1)}, u32[]{:S(2)}, u32[]{:S(2)}) collective-permute-start(bf16[256,2048]{1,0:T(8,128)(2,1)} %get-tuple-element.545), channel_id=1, source_target_pairs={{0,3},{1,0},{2,1},{3,2},{4,7},{5,4},{6,5},{7,6},{8,11},{9,8},{10,9... | collective-permute-start | bytes 3145736 | tf_op jit(solution)/shard_map/ppermute | solution.py:78
  23.1 63.5 %collective-permute-start = (bf16[256,2048]{1,0:T(8,128)(2,1)}, bf16[256,2048]{1,0:T(8,128)(2,1)}, u32[]{:S(2)}, u32[]{:S(2)}) collective-permute-start(bf16[256,2048]{1,0:T(8,128)(2,1)} %get-tuple-element.546), channel_id=1, source_target_pairs={{0,1},{1,2},{2,3},{3,0},{4,5},{5,6},{6,7},{7,4},{8,9},{9,10},{10,1... | collective-permute-start | bytes 3145736 | tf_op jit(solution)/shard_map/ppermute | solution.py:77
  24.7 204.8 %copy-start.48 = (s32[2048]{0:T(1024)}, s32[2048]{0:T(1024)S(1)}, u32[]{:S(2)}) copy-start(s32[2048]{0:T(1024)S(1)} %slice.46) | copy-start | bytes 24580
  32.5 225.1 %copy-start.54 = (f32[2048]{0:T(1024)}, f32[2048]{0:T(1024)S(1)}, u32[]{:S(2)}) copy-start(f32[2048]{0:T(1024)S(1)} %get-tuple-element.548) | copy-start | bytes 24580
  32.5 324.6 %copy-start.44 = (f32[2048]{0:T(1024)}, f32[2048]{0:T(1024)S(1)}, u32[]{:S(2)}) copy-start(f32[2048]{0:T(1024)S(1)} %get-tuple-element.547) | copy-start | bytes 24580
  38.9 50.4 %copy-start.19 = (bf16[2048,512]{0,1:T(8,128)(2,1)}, bf16[2048,512]{0,1:T(8,128)(2,1)S(1)}, u32[]{:S(2)}) copy-start(bf16[2048,512]{0,1:T(8,128)(2,1)S(1)} %fusion.91) | copy-start | bytes 6291460
  61.7 174.6 %copy-start.26 = (bf16[256,2048]{1,0:T(8,128)(2,1)}, bf16[256,2048]{1,0:T(8,128)(2,1)S(1)}, u32[]{:S(2)}) copy-start(bf16[256,2048]{1,0:T(8,128)(2,1)S(1)} %collective-permute-done.1) | copy-start | bytes 3145732
  61.7 44.8 %collective-permute-start.3 = (bf16[256,2048]{1,0:T(8,128)(2,1)S(1)}, bf16[256,2048]{1,0:T(8,128)(2,1)}, u32[]{:S(2)}, u32[]{:S(2)}) collective-permute-start(bf16[256,2048]{1,0:T(8,128)(2,1)S(1)} %collective-permute-done.1), channel_id=1, source_target_pairs={{0,3},{1,0},{2,1},{3,2},{4,7},{5,4},{6,5},{7,6},{8,11},{9,8},{10,9... | collective-permute-start | bytes 3145736 | tf_op jit(solution)/shard_map/ppermute | solution.py:78
  86.6 47.5 %collective-permute-start.2 = (bf16[256,2048]{1,0:T(8,128)(2,1)}, bf16[256,2048]{1,0:T(8,128)(2,1)}, u32[]{:S(2)}, u32[]{:S(2)}) collective-permute-start(bf16[256,2048]{1,0:T(8,128)(2,1)} %collective-permute-done), channel_id=1, source_target_pairs={{0,1},{1,2},{2,3},{3,0},{4,5},{5,6},{6,7},{7,4},{8,9},{9,10},{10,1... | collective-permute-start | bytes 3145736 | tf_op jit(solution)/shard_map/ppermute | solution.py:77
  116.0 44.2 %collective-permute-start.5 = (bf16[256,2048]{1,0:T(8,128)(2,1)}, bf16[256,2048]{1,0:T(8,128)(2,1)}, u32[]{:S(2)}, u32[]{:S(2)}) collective-permute-start(bf16[256,2048]{1,0:T(8,128)(2,1)} %collective-permute-done.3), channel_id=1, source_target_pairs={{0,3},{1,0},{2,1},{3,2},{4,7},{5,4},{6,5},{7,6},{8,11},{9,8},{10,9... | collective-permute-start | bytes 3145736 | tf_op jit(solution)/shard_map/ppermute | solution.py:78
  144.3 31.8 %collective-permute-start.4 = (bf16[256,2048]{1,0:T(8,128)(2,1)}, bf16[256,2048]{1,0:T(8,128)(2,1)}, u32[]{:S(2)}, u32[]{:S(2)}) collective-permute-start(bf16[256,2048]{1,0:T(8,128)(2,1)} %collective-permute-done.2), channel_id=1, source_target_pairs={{0,1},{1,2},{2,3},{3,0},{4,5},{5,6},{6,7},{7,4},{8,9},{9,10},{10,1... | collective-permute-start | bytes 3145736 | tf_op jit(solution)/shard_map/ppermute | solution.py:77
  207.8 316.1 %all-gather.15.cloned.1.call-start = ((), (), s32[]{:S(2)}) async-start(), calls=%async_computation.11 | async-start | bytes 9437184 | tf_op jit(solution)/shard_map/all_gather | solution.py:299
  211.7 169.5 %collective-permute-start.19 = (bf16[256,2048]{1,0:T(8,128)(2,1)}, bf16[256,2048]{1,0:T(8,128)(2,1)}, u32[]{:S(2)}, u32[]{:S(2)}) collective-permute-start(bf16[256,2048]{1,0:T(8,128)(2,1)} %get-tuple-element.541), channel_id=1, source_target_pairs={{0,3},{1,0},{2,1},{3,2},{4,7},{5,4},{6,5},{7,6},{8,11},{9,8},{10,9... | collective-permute-start | bytes 3145736 | tf_op jit(solution)/shard_map/ppermute | solution.py:78
  214.2 164.9 %collective-permute-start.18 = (bf16[256,2048]{1,0:T(8,128)(2,1)}, bf16[256,2048]{1,0:T(8,128)(2,1)}, u32[]{:S(2)}, u32[]{:S(2)}) collective-permute-start(bf16[256,2048]{1,0:T(8,128)(2,1)} %get-tuple-element.542), channel_id=1, source_target_pairs={{0,1},{1,2},{2,3},{3,0},{4,5},{5,6},{6,7},{7,4},{8,9},{9,10},{10,1... | collective-permute-start | bytes 3145736 | tf_op jit(solution)/shard_map/ppermute | solution.py:77
  230.9 126.2 %copy-start.56 = (f32[4]{0:T(128)}, f32[4]{0:T(128)S(1)}, u32[]{:S(2)}) copy-start(f32[4]{0:T(128)S(1)} %get-tuple-element.511) | copy-start | bytes 52
  230.9 126.2 %copy-start.59 = (f32[4]{0:T(128)}, f32[4]{0:T(128)S(1)}, u32[]{:S(2)}) copy-start(f32[4]{0:T(128)S(1)} %get-tuple-element.510) | copy-start | bytes 52
  374.1 145.3 %all-to-all-start = ((bf16[4,512,512]{2,1,0:T(8,128)(2,1)}), bf16[4,512,512]{2,1,0:T(8,128)(2,1)}, u32[]{:S(2)}, u32[]{:S(2)}) async-start(bf16[4,512,512]{2,1,0:T(8,128)(2,1)} %convert_element_type.435), calls=%async_computation | async-start | bytes 4194304 | tf_op jit(solution)/shard_map/all_to_all | solution.py:347
  379.0 911.8 %all-gather.19.cloned.1.call-start = ((), (), s32[]{:S(2)}) async-start(), calls=%async_computation.21 | async-start | bytes 1179648 | tf_op jit(solution)/shard_map/all_gather | solution.py:39
  379.0 96.8 %copy-start.5 = (bf16[512,2048]{1,0:T(8,128)(2,1)S(1)}, bf16[512,2048]{1,0:T(8,128)(2,1)}, u32[]{:S(2)}) copy-start(bf16[512,2048]{1,0:T(8,128)(2,1)} %param.29) | copy-start | bytes 6291460
  379.0 61.9 %collective-permute-start.20 = (bf16[256,2048]{1,0:T(8,128)(2,1)}, bf16[256,2048]{1,0:T(8,128)(2,1)S(1)}, u32[]{:S(2)}, u32[]{:S(2)}) collective-permute-start(bf16[256,2048]{1,0:T(8,128)(2,1)} %collective-permute-done.18), channel_id=1, source_target_pairs={{0,1},{1,2},{2,3},{3,0},{4,5},{5,6},{6,7},{7,4},{8,9},{9,10},{10,1... | collective-permute-start | bytes 3145736 | tf_op jit(solution)/shard_map/ppermute | solution.py:77
  381.1 96.2 %collective-permute-start.21 = (bf16[256,2048]{1,0:T(8,128)(2,1)}, bf16[256,2048]{1,0:T(8,128)(2,1)S(1)}, u32[]{:S(2)}, u32[]{:S(2)}) collective-permute-start(bf16[256,2048]{1,0:T(8,128)(2,1)} %collective-permute-done.19), channel_id=1, source_target_pairs={{0,3},{1,0},{2,1},{3,2},{4,7},{5,4},{6,5},{7,6},{8,11},{9,8},{10,9... | collective-permute-start | bytes 3145736 | tf_op jit(solution)/shard_map/ppermute | solution.py:78
  441.0 54.1 %collective-permute-start.22 = (bf16[256,2048]{1,0:T(8,128)(2,1)S(1)}, bf16[256,2048]{1,0:T(8,128)(2,1)S(1)}, u32[]{:S(2)}, u32[]{:S(2)}) collective-permute-start(bf16[256,2048]{1,0:T(8,128)(2,1)S(1)} %collective-permute-done.20), channel_id=1, source_target_pairs={{0,1},{1,2},{2,3},{3,0},{4,5},{5,6},{6,7},{7,4},{8,9},{9,10},{10,1... | collective-permute-start | bytes 3145736 | tf_op jit(solution)/shard_map/ppermute | solution.py:77
  477.3 41.0 %collective-permute-start.23 = (bf16[256,2048]{1,0:T(8,128)(2,1)S(1)}, bf16[256,2048]{1,0:T(8,128)(2,1)S(1)}, u32[]{:S(2)}, u32[]{:S(2)}) collective-permute-start(bf16[256,2048]{1,0:T(8,128)(2,1)S(1)} %collective-permute-done.21), channel_id=1, source_target_pairs={{0,3},{1,0},{2,1},{3,2},{4,7},{5,4},{6,5},{7,6},{8,11},{9,8},{10,9... | collective-permute-start | bytes 3145736 | tf_op jit(solution)/shard_map/ppermute | solution.py:78
  536.4 29.4 %collective-permute-start.7 = (bf16[256,2048]{1,0:T(8,128)(2,1)S(1)}, bf16[256,2048]{1,0:T(8,128)(2,1)S(1)}, u32[]{:S(2)}, u32[]{:S(2)}) collective-permute-start(bf16[256,2048]{1,0:T(8,128)(2,1)S(1)} %get-tuple-element.543), channel_id=1, source_target_pairs={{0,3},{1,0},{2,1},{3,2},{4,7},{5,4},{6,5},{7,6},{8,11},{9,8},{10,9... | collective-permute-start | bytes 3145736 | tf_op jit(solution)/shard_map/ppermute | solution.py:78
  538.3 49.0 %collective-permute-start.6 = (bf16[256,2048]{1,0:T(8,128)(2,1)S(1)}, bf16[256,2048]{1,0:T(8,128)(2,1)S(1)}, u32[]{:S(2)}, u32[]{:S(2)}) collective-permute-start(bf16[256,2048]{1,0:T(8,128)(2,1)S(1)} %get-tuple-element.544), channel_id=1, source_target_pairs={{0,1},{1,2},{2,3},{3,0},{4,5},{5,6},{6,7},{7,4},{8,9},{9,10},{10,1... | collective-permute-start | bytes 3145736 | tf_op jit(solution)/shard_map/ppermute | solution.py:77
  565.8 59.3 %collective-permute-start.9 = (bf16[256,2048]{1,0:T(8,128)(2,1)S(1)}, bf16[256,2048]{1,0:T(8,128)(2,1)S(1)}, u32[]{:S(2)}, u32[]{:S(2)}) collective-permute-start(bf16[256,2048]{1,0:T(8,128)(2,1)S(1)} %collective-permute-done.7), channel_id=1, source_target_pairs={{0,3},{1,0},{2,1},{3,2},{4,7},{5,4},{6,5},{7,6},{8,11},{9,8},{10,9... | collective-permute-start | bytes 3145736 | tf_op jit(solution)/shard_map/ppermute | solution.py:78
  587.3 45.0 %collective-permute-start.8 = (bf16[256,2048]{1,0:T(8,128)(2,1)S(1)}, bf16[256,2048]{1,0:T(8,128)(2,1)S(1)}, u32[]{:S(2)}, u32[]{:S(2)}) collective-permute-start(bf16[256,2048]{1,0:T(8,128)(2,1)S(1)} %collective-permute-done.6), channel_id=1, source_target_pairs={{0,1},{1,2},{2,3},{3,0},{4,5},{5,6},{6,7},{7,4},{8,9},{9,10},{10,1... | collective-permute-start | bytes 3145736 | tf_op jit(solution)/shard_map/ppermute | solution.py:77
  625.1 54.4 %collective-permute-start.11 = (bf16[256,2048]{1,0:T(8,128)(2,1)S(1)}, bf16[256,2048]{1,0:T(8,128)(2,1)S(1)}, u32[]{:S(2)}, u32[]{:S(2)}) collective-permute-start(bf16[256,2048]{1,0:T(8,128)(2,1)S(1)} %collective-permute-done.9), channel_id=1, source_target_pairs={{0,3},{1,0},{2,1},{3,2},{4,7},{5,4},{6,5},{7,6},{8,11},{9,8},{10,9... | collective-permute-start | bytes 3145736 | tf_op jit(solution)/shard_map/ppermute | solution.py:78
  632.3 40.5 %collective-permute-start.10 = (bf16[256,2048]{1,0:T(8,128)(2,1)S(1)}, bf16[256,2048]{1,0:T(8,128)(2,1)S(1)}, u32[]{:S(2)}, u32[]{:S(2)}) collective-permute-start(bf16[256,2048]{1,0:T(8,128)(2,1)S(1)} %collective-permute-done.8), channel_id=1, source_target_pairs={{0,1},{1,2},{2,3},{3,0},{4,5},{5,6},{6,7},{7,4},{8,9},{9,10},{10,1... | collective-permute-start | bytes 3145736 | tf_op jit(solution)/shard_map/ppermute | solution.py:77
  771.9 32.5 %collective-permute-start.24 = (bf16[256,2048]{1,0:T(8,128)(2,1)S(1)}, bf16[256,2048]{1,0:T(8,128)(2,1)S(1)}, u32[]{:S(2)}, u32[]{:S(2)}) collective-permute-start(bf16[256,2048]{1,0:T(8,128)(2,1)S(1)} %get-tuple-element.528), channel_id=1, source_target_pairs={{0,1},{1,2},{2,3},{3,0},{4,5},{5,6},{6,7},{7,4},{8,9},{9,10},{10,1... | collective-permute-start | bytes 3145736 | tf_op jit(solution)/shard_map/ppermute | solution.py:101
  773.4 49.0 %collective-permute-start.27 = (bf16[256,2048]{1,0:T(8,128)(2,1)S(1)}, bf16[256,2048]{1,0:T(8,128)(2,1)S(1)}, u32[]{:S(2)}, u32[]{:S(2)}) collective-permute-start(bf16[256,2048]{1,0:T(8,128)(2,1)S(1)} %get-tuple-element.529), channel_id=1, source_target_pairs={{0,3},{1,0},{2,1},{3,2},{4,7},{5,4},{6,5},{7,6},{8,11},{9,8},{10,9... | collective-permute-start | bytes 3145736 | tf_op jit(solution)/shard_map/ppermute | solution.py:103
  800.2 116.3 %copy-start.15 = (f32[2048,2048]{1,0:T(8,128)}, f32[2048,2048]{1,0:T(8,128)S(1)}, u32[]{:S(2)}) copy-start(f32[2048,2048]{1,0:T(8,128)S(1)} %fusion.140) | copy-start | bytes 50331652
  800.6 44.3 %collective-permute-start.12 = (bf16[256,2048]{1,0:T(8,128)(2,1)S(1)}, bf16[256,2048]{1,0:T(8,128)(2,1)S(1)}, u32[]{:S(2)}, u32[]{:S(2)}) collective-permute-start(bf16[256,2048]{1,0:T(8,128)(2,1)S(1)} %get-tuple-element.536), channel_id=1, source_target_pairs={{0,1},{1,2},{2,3},{3,0},{4,5},{5,6},{6,7},{7,4},{8,9},{9,10},{10,1... | collective-permute-start | bytes 3145736 | tf_op jit(solution)/shard_map/ppermute | solution.py:101
  800.6 66.7 %collective-permute-start.15 = (bf16[256,2048]{1,0:T(8,128)(2,1)S(1)}, bf16[256,2048]{1,0:T(8,128)(2,1)S(1)}, u32[]{:S(2)}, u32[]{:S(2)}) collective-permute-start(bf16[256,2048]{1,0:T(8,128)(2,1)S(1)} %get-tuple-element.537), channel_id=1, source_target_pairs={{0,3},{1,0},{2,1},{3,2},{4,7},{5,4},{6,5},{7,6},{8,11},{9,8},{10,9... | collective-permute-start | bytes 3145736 | tf_op jit(solution)/shard_map/ppermute | solution.py:103
  825.3 64.5 %collective-permute-start.25 = (bf16[256,2048]{1,0:T(8,128)(2,1)S(1)}, bf16[256,2048]{1,0:T(8,128)(2,1)S(1)}, u32[]{:S(2)}, u32[]{:S(2)}) collective-permute-start(bf16[256,2048]{1,0:T(8,128)(2,1)S(1)} %get-tuple-element.526), channel_id=1, source_target_pairs={{0,1},{1,2},{2,3},{3,0},{4,5},{5,6},{6,7},{7,4},{8,9},{9,10},{10,1... | collective-permute-start | bytes 3145736 | tf_op jit(solution)/shard_map/ppermute | solution.py:101
  826.0 86.3 %collective-permute-start.28 = (bf16[256,2048]{1,0:T(8,128)(2,1)S(1)}, bf16[256,2048]{1,0:T(8,128)(2,1)S(1)}, u32[]{:S(2)}, u32[]{:S(2)}) collective-permute-start(bf16[256,2048]{1,0:T(8,128)(2,1)S(1)} %get-tuple-element.527), channel_id=1, source_target_pairs={{0,3},{1,0},{2,1},{3,2},{4,7},{5,4},{6,5},{7,6},{8,11},{9,8},{10,9... | collective-permute-start | bytes 3145736 | tf_op jit(solution)/shard_map/ppermute | solution.py:103
  869.4 65.4 %collective-permute-start.13 = (bf16[256,2048]{1,0:T(8,128)(2,1)}, bf16[256,2048]{1,0:T(8,128)(2,1)S(1)}, u32[]{:S(2)}, u32[]{:S(2)}) collective-permute-start(bf16[256,2048]{1,0:T(8,128)(2,1)} %get-tuple-element.534), channel_id=1, source_target_pairs={{0,1},{1,2},{2,3},{3,0},{4,5},{5,6},{6,7},{7,4},{8,9},{9,10},{10,1... | collective-permute-start | bytes 3145736 | tf_op jit(solution)/shard_map/ppermute | solution.py:101
  870.0 87.3 %collective-permute-start.16 = (bf16[256,2048]{1,0:T(8,128)(2,1)}, bf16[256,2048]{1,0:T(8,128)(2,1)}, u32[]{:S(2)}, u32[]{:S(2)}) collective-permute-start(bf16[256,2048]{1,0:T(8,128)(2,1)} %get-tuple-element.535), channel_id=1, source_target_pairs={{0,3},{1,0},{2,1},{3,2},{4,7},{5,4},{6,5},{7,6},{8,11},{9,8},{10,9... | collective-permute-start | bytes 3145736 | tf_op jit(solution)/shard_map/ppermute | solution.py:103
  916.5 63.4 %collective-permute-start.26 = (bf16[256,2048]{1,0:T(8,128)(2,1)}, bf16[256,2048]{1,0:T(8,128)(2,1)}, u32[]{:S(2)}, u32[]{:S(2)}) collective-permute-start(bf16[256,2048]{1,0:T(8,128)(2,1)} %get-tuple-element.524), channel_id=1, source_target_pairs={{0,1},{1,2},{2,3},{3,0},{4,5},{5,6},{6,7},{7,4},{8,9},{9,10},{10,1... | collective-permute-start | bytes 3145736 | tf_op jit(solution)/shard_map/ppermute | solution.py:101
  917.1 85.1 %collective-permute-start.29 = (bf16[256,2048]{1,0:T(8,128)(2,1)}, bf16[256,2048]{1,0:T(8,128)(2,1)}, u32[]{:S(2)}, u32[]{:S(2)}) collective-permute-start(bf16[256,2048]{1,0:T(8,128)(2,1)} %get-tuple-element.525), channel_id=1, source_target_pairs={{0,3},{1,0},{2,1},{3,2},{4,7},{5,4},{6,5},{7,6},{8,11},{9,8},{10,9... | collective-permute-start | bytes 3145736 | tf_op jit(solution)/shard_map/ppermute | solution.py:103
  960.4 64.4 %collective-permute-start.14 = (bf16[256,2048]{1,0:T(8,128)(2,1)S(1)}, bf16[256,2048]{1,0:T(8,128)(2,1)S(1)}, u32[]{:S(2)}, u32[]{:S(2)}) collective-permute-start(bf16[256,2048]{1,0:T(8,128)(2,1)S(1)} %get-tuple-element.532), channel_id=1, source_target_pairs={{0,1},{1,2},{2,3},{3,0},{4,5},{5,6},{6,7},{7,4},{8,9},{9,10},{10,1... | collective-permute-start | bytes 3145736 | tf_op jit(solution)/shard_map/ppermute | solution.py:101
  961.0 44.6 %copy-start.53 = (f32[512]{0:T(512)S(1)}, f32[512]{0:T(512)}, u32[]{:S(2)}) copy-start(f32[512]{0:T(512)} %copy-done.52) | copy-start | bytes 6148
  961.0 84.1 %collective-permute-start.17 = (bf16[256,2048]{1,0:T(8,128)(2,1)S(1)}, bf16[256,2048]{1,0:T(8,128)(2,1)S(1)}, u32[]{:S(2)}, u32[]{:S(2)}) collective-permute-start(bf16[256,2048]{1,0:T(8,128)(2,1)S(1)} %get-tuple-element.533), channel_id=1, source_target_pairs={{0,3},{1,0},{2,1},{3,2},{4,7},{5,4},{6,5},{7,6},{8,11},{9,8},{10,9... | collective-permute-start | bytes 3145736 | tf_op jit(solution)/shard_map/ppermute | solution.py:103
  1130.4 460.9 %reduce-scatter.15.cloned.1.call-start = ((), (), s32[]{:S(2)}) async-start(), calls=%async_computation.15 | async-start | bytes 9437184 | tf_op jit(solution)/shard_map/reduce_scatter | solution.py:449
  1141.3 450.4 %reduce-scatter.9.cloned.1.call-start = ((), (), s32[]{:S(2)}) async-start(), calls=%async_computation.12 | async-start | bytes 2359296 | tf_op jit(solution)/shard_map/reduce_scatter | solution.py:449
  1177.3 76.3 %copy-start.21 = (f32[4,128,128]{2,1,0:T(8,128)S(1)}, f32[4,128,128]{2,1,0:T(8,128)}, u32[]{:S(2)}) copy-start(f32[4,128,128]{2,1,0:T(8,128)} %copy-done.20) | copy-start | bytes 786436
  1177.3 76.3 %copy-start.63 = (f32[4,128]{1,0:T(4,128)S(1)}, f32[4,128]{1,0:T(4,128)}, u32[]{:S(2)}) copy-start(f32[4,128]{1,0:T(4,128)} %copy-done.62) | copy-start | bytes 6148
  1290.8 302.7 %reduce-scatter.11.cloned.1.call-start = ((), (), s32[]{:S(2)}) async-start(), calls=%async_computation.13 | async-start | bytes 2359296 | tf_op jit(solution)/shard_map/reduce_scatter | solution.py:449
  1332.1 263.2 %reduce-scatter.13.cloned.1.call-start = ((), (), s32[]{:S(2)}) async-start(), calls=%async_computation.14 | async-start | bytes 2359296 | tf_op jit(solution)/shard_map/reduce_scatter | solution.py:449
  1354.5 335.0 %reduce-scatter.23.cloned.1.call-start = ((), (), s32[]{:S(2)}) async-start(), calls=%async_computation.19 | async-start | bytes 9437184 | tf_op jit(solution)/shard_map/reduce_scatter | solution.py:449
  1381.4 310.8 %reduce-scatter.21.cloned.1.call-start = ((), (), s32[]{:S(2)}) async-start(), calls=%async_computation.18 | async-start | bytes 9437184 | tf_op jit(solution)/shard_map/reduce_scatter | solution.py:449
  1413.4 281.6 %reduce-scatter.19.cloned.1.call-start = ((), (), s32[]{:S(2)}) async-start(), calls=%async_computation.17 | async-start | bytes 9437184 | tf_op jit(solution)/shard_map/reduce_scatter | solution.py:449
  1437.3 260.5 %reduce-scatter.17.cloned.1.call-start = ((), (), s32[]{:S(2)}) async-start(), calls=%async_computation.16 | async-start | bytes 1310720 | tf_op jit(solution)/shard_map/reduce_scatter | solution.py:453
  1482.8 27.9 %collective-permute-start.30 = (bf16[256,2048]{1,0:T(8,128)(2,1)S(1)}, bf16[256,2048]{1,0:T(8,128)(2,1)S(1)}, u32[]{:S(2)}, u32[]{:S(2)}) collective-permute-start(bf16[256,2048]{1,0:T(8,128)(2,1)S(1)} %get-tuple-element.520), channel_id=1, source_target_pairs={{0,1},{1,2},{2,3},{3,0},{4,5},{5,6},{6,7},{7,4},{8,9},{9,10},{10,1... | collective-permute-start | bytes 3145736 | tf_op jit(solution)/shard_map/ppermute | solution.py:101
  1483.8 47.7 %collective-permute-start.33 = (bf16[256,2048]{1,0:T(8,128)(2,1)S(1)}, bf16[256,2048]{1,0:T(8,128)(2,1)S(1)}, u32[]{:S(2)}, u32[]{:S(2)}) collective-permute-start(bf16[256,2048]{1,0:T(8,128)(2,1)S(1)} %get-tuple-element.521), channel_id=1, source_target_pairs={{0,3},{1,0},{2,1},{3,2},{4,7},{5,4},{6,5},{7,6},{8,11},{9,8},{10,9... | collective-permute-start | bytes 3145736 | tf_op jit(solution)/shard_map/ppermute | solution.py:103
  1534.6 27.9 %collective-permute-start.31 = (bf16[256,2048]{1,0:T(8,128)(2,1)S(1)}, bf16[256,2048]{1,0:T(8,128)(2,1)S(1)}, u32[]{:S(2)}, u32[]{:S(2)}) collective-permute-start(bf16[256,2048]{1,0:T(8,128)(2,1)S(1)} %get-tuple-element.518), channel_id=1, source_target_pairs={{0,1},{1,2},{2,3},{3,0},{4,5},{5,6},{6,7},{7,4},{8,9},{9,10},{10,1... | collective-permute-start | bytes 3145736 | tf_op jit(solution)/shard_map/ppermute | solution.py:101
  1535.6 55.7 %copy-start.58 = (f32[4]{0:T(128)S(1)}, f32[4]{0:T(128)}, u32[]{:S(2)}) copy-start(f32[4]{0:T(128)} %copy-done.56) | copy-start | bytes 52
  1535.6 55.8 %copy-start.61 = (f32[4]{0:T(128)S(1)}, f32[4]{0:T(128)}, u32[]{:S(2)}) copy-start(f32[4]{0:T(128)} %get-tuple-element.469) | copy-start | bytes 52
  1535.6 47.2 %collective-permute-start.34 = (bf16[256,2048]{1,0:T(8,128)(2,1)S(1)}, bf16[256,2048]{1,0:T(8,128)(2,1)S(1)}, u32[]{:S(2)}, u32[]{:S(2)}) collective-permute-start(bf16[256,2048]{1,0:T(8,128)(2,1)S(1)} %get-tuple-element.519), channel_id=1, source_target_pairs={{0,3},{1,0},{2,1},{3,2},{4,7},{5,4},{6,5},{7,6},{8,11},{9,8},{10,9... | collective-permute-start | bytes 3145736 | tf_op jit(solution)/shard_map/ppermute | solution.py:103
  1587.4 28.1 %collective-permute-start.32 = (bf16[256,2048]{1,0:T(8,128)(2,1)}, bf16[256,2048]{1,0:T(8,128)(2,1)}, u32[]{:S(2)}, u32[]{:S(2)}) collective-permute-start(bf16[256,2048]{1,0:T(8,128)(2,1)} %get-tuple-element.516), channel_id=1, source_target_pairs={{0,1},{1,2},{2,3},{3,0},{4,5},{5,6},{6,7},{7,4},{8,9},{9,10},{10,1... | collective-permute-start | bytes 3145736 | tf_op jit(solution)/shard_map/ppermute | solution.py:101
  1588.2 47.0 %collective-permute-start.35 = (bf16[256,2048]{1,0:T(8,128)(2,1)S(1)}, bf16[256,2048]{1,0:T(8,128)(2,1)}, u32[]{:S(2)}, u32[]{:S(2)}) collective-permute-start(bf16[256,2048]{1,0:T(8,128)(2,1)S(1)} %get-tuple-element.517), channel_id=1, source_target_pairs={{0,3},{1,0},{2,1},{3,2},{4,7},{5,4},{6,5},{7,6},{8,11},{9,8},{10,9... | collective-permute-start | bytes 3145736 | tf_op jit(solution)/shard_map/ppermute | solution.py:103
  (60 other events, 735.2 us)
Sparse Core Ops, SparseCore 0:
  9.6 41.3 all-gather.12
  207.9 26.0 all-gather.16
  235.9 55.8 all-gather.14
  1130.5 21.5 all-gather.18
  1155.5 71.2 reduce-scatter.14
  1290.9 39.8 reduce-scatter.8
  1334.1 41.0 reduce-scatter.10
  1379.1 41.0 reduce-scatter.12
  1423.7 71.2 reduce-scatter.22
  1498.3 71.4 reduce-scatter.20
  1573.3 71.4 reduce-scatter.18
  1646.9 28.2 reduce-scatter.16

commit v3 on v2

--- a/solution.py
+++ b/solution.py
@@ -16,45 +16,49 @@
 highest = lax.Precision.HIGHEST
 
 
-def carried_in(value, axis, combine, identity):
+def gather_states(state, axis, kind):
+    flag, memory, norm = state
+    heads, size = norm.shape
+    packed = jnp.concatenate(
+        [memory.reshape(heads * size, size), norm, jnp.broadcast_to(flag.reshape(1, 1), (1, size))],
+        axis=0,
+    )
+    everything = lax.all_gather(packed.astype(kind), axis).astype(jnp.float32)
+    return (
+        everything[:, heads * size + heads, 0],
+        everything[:, : heads * size].reshape((-1, heads, size, size)),
+        everything[:, heads * size : heads * size + heads],
+    )
+
+
+def combine_selected(weights, states):
+    _, memory, norm = states
+    return (
+        jnp.sum(weights[:, None, None, None] * memory, axis=0),
+        jnp.sum(weights[:, None, None] * norm, axis=0),
+    )
+
+
+def carried_in(value, axis):
     size, place = (lax.axis_size(axis), lax.axis_index(axis))
-    everything = jax.tree.map(lambda part: lax.all_gather(part, axis), value)
-    start = jax.tree.map(
-        lambda part, zero: jnp.broadcast_to(jnp.asarray(zero, part.dtype), part.shape),
-        value,
-        identity,
-    )
-
-    def carried_hop(k, before):
-        reached = k < place
-        new = combine(before, jax.tree.map(lambda part: part[k], everything))
-        return jax.tree.map(lambda a, b: jnp.where(reached, a, b), new, before)
-
-    return lax.fori_loop(0, size, carried_hop, start)
-
-
-def prefix(value, axis, combine, identity):
+    states = gather_states(value, axis, jnp.float32)
+    flags = states[0]
+    k = jnp.arange(size)[:, None]
+    j = jnp.arange(size)[None, :]
+    factors = jnp.where((j > k) & (j < place), flags[None, :], 1.0)
+    weights = jnp.where(jnp.arange(size) < place, jnp.prod(factors, axis=1), 0.0)
+    return combine_selected(weights, states)
+
+
+def prefix(value, axis):
     size, place = (lax.axis_size(axis), lax.axis_index(axis))
-    everything = jax.tree.map(
-        lambda part, kind: lax.all_gather(part.astype(kind), axis),
-        value,
-        jax.tree.map(lambda a: jnp.bfloat16 if a.dtype == jnp.float32 else a.dtype, value),
-    )
-    start = jax.tree.map(
-        lambda part, zero: jnp.broadcast_to(jnp.asarray(zero, part.dtype), part.shape),
-        value,
-        identity,
-    )
-
-    def prefix_hop(k, before):
-        at = size - 1 - k
-        reached = at > place
-        new = combine(
-            before, jax.tree.map(lambda part, own: part[at].astype(own.dtype), everything, value)
-        )
-        return jax.tree.map(lambda a, b: jnp.where(reached, a, b), new, before)
-
-    return lax.fori_loop(0, size, prefix_hop, start)
+    states = gather_states(value, axis, jnp.bfloat16)
+    flags = states[0]
+    k = jnp.arange(size)[:, None]
+    j = jnp.arange(size)[None, :]
+    factors = jnp.where((j > place) & (j < k), flags[None, :], 1.0)
+    weights = jnp.where(jnp.arange(size) > place, jnp.prod(factors, axis=1), 0.0)
+    return combine_selected(weights, states)
 
 
 def ring_pairs(n, step):
@@ -310,6 +314,7 @@
 
     normed1_all, query_rows, key_rows, value_rows = ring_gather(normed1, "mp", project_qkv)
     query_h, key_h, value_h = (to_heads(a) for a in (query_rows, key_rows, value_rows))
+    grad_rows, query_h = lax.optimization_barrier((out_grad, query_h))
     dot_out, log_sums = attention_fwd(query_h, key_h, value_h, doc_index, score_scale)
     query_f = query_h.astype(jnp.float32).reshape(seg_shape)
     key_f = key_h.astype(jnp.float32).reshape(seg_shape)
@@ -324,7 +329,7 @@
         jnp.zeros(norm_updates.shape[1:], jnp.float32),
     )
     summary, _ = lax.scan(fold_states, start_state, (keep_flag[:, None], updates, norm_updates))
-    _, memory_in, norm_in = carried_in(summary, "dp", link_states, start_state)
+    memory_in, norm_in = carried_in(summary, "dp")
 
     def carry_forward(state, item):
         flag, read_flag, update, norm_update = item
@@ -360,9 +365,8 @@
     up_f = up_pre.astype(jnp.float32)
     sig_gate = jax.nn.sigmoid(gate_f)
     act = (gate_f * sig_gate * up_f).astype(jnp.bfloat16)
-    mlp_sum = ring_scatter(jnp.dot(act, w_down, preferred_element_type=jnp.float32), "mp")
-    output = (resid + mlp_sum).astype(jnp.bfloat16)
-    (grad_rows_all,) = ring_gather(out_grad, "mp", lambda rows: (rows,))
+    mlp_part = jnp.dot(act, w_down, preferred_element_type=jnp.float32)
+    grad_rows_all = lax.all_gather(grad_rows, "mp", axis=0, tiled=True)
     d_act = jnp.dot(grad_rows_all, w_down.T, preferred_element_type=jnp.float32)
     grad_down = jnp.dot(act.T, grad_rows_all, preferred_element_type=jnp.float32)
     d_gate = (d_act * up_f * sig_gate * (1.0 + gate_f * (1.0 - sig_gate))).astype(jnp.bfloat16)
@@ -382,6 +386,8 @@
     d_mixed = to_heads(
         lax.all_to_all(d_mixed_rows.astype(jnp.bfloat16), "mp", 1, 0, tiled=True)
     ).astype(jnp.float32)
+    mlp_part, d_mixed = lax.optimization_barrier((mlp_part, d_mixed))
+    output = (resid + ring_scatter(mlp_part, "mp")).astype(jnp.bfloat16)
     gate_part = jnp.sum(d_mixed * (mem_out - dot_out), axis=(1, 2)) * gate_vec * (1.0 - gate_vec)
     d_dot = ((1.0 - gate) * d_mixed).astype(jnp.bfloat16)
     d_mem = (gate * d_mixed).reshape(seg_shape)
@@ -401,7 +407,7 @@
     back_summary, _ = lax.scan(
         fold_states, start_state, (keep_flag[:, None], back_mem, back_norm), reverse=True
     )
-    _, grad_in, grad_norm_in = prefix(back_summary, "dp", link_states, start_state)
+    grad_in, grad_norm_in = prefix(back_summary, "dp")
 
     def carry_back(state, item):
         flag, mem_read, norm_read = item
@@ -443,7 +449,9 @@
         lax.axis_index("mp") * heads_here,
         0,
     )
-    gain1_sum, gain2_sum, gate_sum = lax.psum((gain1_part, gain2_part, gate_full), ("dp", "mp"))
+    gain1_sum, gain2_sum, gate_sum = lax.psum(
+        lax.psum((gain1_part, gain2_part, gate_full), "mp"), "dp"
+    )
 
     def over_dp(grad, dim):
         return lax.psum_scatter(

time: 1720 us -> 1640 us (0.953)
  blocking collectives: 135 us -> 42.6 us
  waiting for transfers between devices: 568 us -> 615 us
    all_to_all x1, waiting for transfers between devices: 0.01 us -> 89.8 us  [local(): mixed = lax.all_to_all(mixed_cols, 'mp', 0, 1, tiled=True)]
    ppermute x9 -> x6, waiting for transfers between devices: 149 us -> 86.3 us  [ring_gather(): ahead = lax.ppermute(ahead, axis, ring_pairs(n, 1))]
    all_to_all x1 -> x0, blocking collectives: 51.1 us -> none  [local(): lax.all_to_all(d_mixed_rows.astype(jnp.bfloat16), 'mp', 1, 0, tiled=True)]
    select_n x32 -> x2, other arithmetic: 27.6 us -> 0.01 us  [the longest x1 0.01 us: prefix(): jnp.where(jnp.arange(size) > place, jnp.prod(factors, axis=1), 0.0)]
    unnamed x2 -> x0, blocking collectives: 25.3 us -> none
    all_to_all x0 -> x1, waiting for transfers between devices: none -> 21.7 us  [local(): lax.all_to_all(d_mixed_rows.astype(jnp.bfloat16), 'mp', 1, 0, tiled=True)]
    dynamic_update_slice x35 -> x29, local copies, waits for them, and re-layouts: 52.6 us -> 39.9 us  [ring_gather(): lax.dynamic_update_slice_in_dim(out, part, start, 0)]
    ppermute x9 -> x6, waiting for transfers between devices: 83.7 us -> 95.4 us  [ring_gather(): behind = lax.ppermute(behind, axis, ring_pairs(n, -1))]
  transfers between devices with their start and end apart: 49 -> 45, of which waited for: 29 -> 28; matrix products, arithmetic and copies ran while one was open for 35% -> 34% of each run, Pallas kernels for 7% -> 8%
where the time goes in v3:
time: 1640 us; the launch traced here: 1630 us
  waiting for transfers between devices  615 us (38%)
  matrix products  459 us (28%)
  local copies, waits for them, and re-layouts  162 us (10%)
  Pallas kernels  127 us (8%)
  starting transfers between devices  110 us (7%)
  other arithmetic  93.3 us (6%)
  blocking collectives  42.6 us (3%)
  between operations  17.4 us (1%)
    ppermute x9, waiting for transfers between devices, ring_scatter(): lax.ppermute(behind.astype(kind), axis, ring_pairs(n, -1))  177 us
    ppermute x9, waiting for transfers between devices, ring_scatter(): lax.ppermute(ahead.astype(kind), axis, ring_pairs(n, 1)).astype(jnp.float32)  144 us
    ppermute x6, waiting for transfers between devices, ring_gather(): behind = lax.ppermute(behind, axis, ring_pairs(n, -1))  95.4 us
    all_to_all x1, waiting for transfers between devices, local(): mixed = lax.all_to_all(mixed_cols, 'mp', 0, 1, tiled=True)  89.8 us
    ppermute x6, waiting for transfers between devices, ring_gather(): ahead = lax.ppermute(ahead, axis, ring_pairs(n, 1))  86.3 us
    pallas_call x1, Pallas kernels, attention_bwd(): pl.pallas_call(functools.partial(_bwd_kernel, scale, seg), grid=(H, nq),...  76.3 us
    dot_general x14, matrix products, project_ffn(): jnp.dot(rows, weight, preferred_element_type=jnp.float32)  59.5 us
    dot_general x21, matrix products, project_qkv(): jnp.dot(rows, weight, preferred_element_type=jnp.float32)  56.4 us
  transfers between devices with their start and end apart: 45, of which 28 were waited for; matrix products, arithmetic and copies ran while one was open for 34% of the time, Pallas kernels for 8%

profile of v3, /device:TPU:0, one launch (start us, length us, event | category | flops | bytes accessed | tf_op | source)
XLA Modules:
  0.0 1626.6 jit_solution(8421802847188241242)
XLA Ops:
  18.0 5.1 collective-permute-start.1
  40.6 21.1 %collective-permute-done.1 = bf16[256,2048]{1,0:T(8,128)(2,1)S(1)} collective-permute-done((bf16[256,2048]{1,0:T(8,128)(2,1)}, bf16[256,2048]{1,0:T(8,128)(2,1)S(1)}, u32[]{:S(2)}, u32[]{:S(2)}) %collective-permute-start.1) | collective-permute-done | bytes 1048608 | tf_op jit(solution)/shard_map/ppermute | solution.py:82
  66.5 20.1 %collective-permute-done = bf16[256,2048]{1,0:T(8,128)(2,1)} collective-permute-done((bf16[256,2048]{1,0:T(8,128)(2,1)}, bf16[256,2048]{1,0:T(8,128)(2,1)}, u32[]{:S(2)}, u32[]{:S(2)}) %collective-permute-start) | collective-permute-done | bytes 1048608 | tf_op jit(solution)/shard_map/ppermute | solution.py:81
  116.0 18.0 %collective-permute-start.5 = (bf16[256,2048]{1,0:T(8,128)(2,1)}, bf16[256,2048]{1,0:T(8,128)(2,1)}, u32[]{:S(2)}, u32[]{:S(2)}) collective-permute-start(bf16[256,2048]{1,0:T(8,128)(2,1)} %collective-permute-done.3), channel_id=1, source_target_pairs={{0,3},{1,0},{2,1},{3,2},{4,7},{5,4},{6,5},{7,6},{8,11},{9,8},{10,9... | collective-permute-start | bytes 3145736 | tf_op jit(solution)/shard_map/ppermute | solution.py:82
  150.3 10.0 collective-permute-done.5
  164.7 11.4 collective-permute-done.4
  236.6 11.8 copy.225
  248.4 50.9 %shard_map.220 = (f32[4,2048,128]{2,1,0:T(8,128)}, f32[4,2048,1]{2,1,0:T(8,128)}) custom-call(bf16[4,2048,128]{2,1,0:T(8,128)(2,1)} %bitcast.197, bf16[4,2048,128]{2,1,0:T(8,128)(2,1)} %bitcast.193, bf16[4,2048,128]{2,1,0:T(8,128)(2,1)} %bitcast.195, s32[2048,1]{1,0:T(8,128)} %copy.243.docq_ref, s32[1,2048]{1,0:T(1,128)} %bitcast.219), custom_call_target="tpu_custom_call" | custom-call | flops 8589934592 | bytes 10485760 | tf_op jit(solution)/shard_map/pallas_call | solution.py:217
  303.0 6.2 fusion.46
  316.4 10.9 copy.244
  336.5 89.8 %all-to-all-done = bf16[4,512,512]{2,1,0:T(8,128)(2,1)} async-done(((bf16[4,512,512]{2,1,0:T(8,128)(2,1)}), bf16[4,512,512]{2,1,0:T(8,128)(2,1)}, u32[]{:S(2)}, u32[]{:S(2)}) %all-to-all-start) | async-done | bytes 2097184 | tf_op jit(solution)/shard_map/all_to_all | solution.py:352
  430.4 9.8 multiply_reduce_fusion.4
  449.9 9.2 fusion.40
  463.5 9.3 fusion.41
  472.8 41.1 %collective-permute-done.7 = bf16[256,2048]{1,0:T(8,128)(2,1)S(1)} collective-permute-done((bf16[256,2048]{1,0:T(8,128)(2,1)S(1)}, bf16[256,2048]{1,0:T(8,128)(2,1)S(1)}, u32[]{:S(2)}, u32[]{:S(2)}) %collective-permute-start.7) | collective-permute-done | bytes 1048608 | tf_op jit(solution)/shard_map/ppermute | solution.py:82
  513.9 21.6 %collective-permute-done.6 = bf16[256,2048]{1,0:T(8,128)(2,1)S(1)} collective-permute-done((bf16[256,2048]{1,0:T(8,128)(2,1)S(1)}, bf16[256,2048]{1,0:T(8,128)(2,1)S(1)}, u32[]{:S(2)}, u32[]{:S(2)}) %collective-permute-start.6) | collective-permute-done | bytes 1048608 | tf_op jit(solution)/shard_map/ppermute | solution.py:81
  550.8 18.4 %collective-permute-done.9 = bf16[256,2048]{1,0:T(8,128)(2,1)S(1)} collective-permute-done((bf16[256,2048]{1,0:T(8,128)(2,1)S(1)}, bf16[256,2048]{1,0:T(8,128)(2,1)S(1)}, u32[]{:S(2)}, u32[]{:S(2)}) %collective-permute-start.9) | collective-permute-done | bytes 1048608 | tf_op jit(solution)/shard_map/ppermute | solution.py:82
  573.4 21.8 %collective-permute-done.8 = bf16[256,2048]{1,0:T(8,128)(2,1)S(1)} collective-permute-done((bf16[256,2048]{1,0:T(8,128)(2,1)S(1)}, bf16[256,2048]{1,0:T(8,128)(2,1)S(1)}, u32[]{:S(2)}, u32[]{:S(2)}) %collective-permute-start.8) | collective-permute-done | bytes 1048608 | tf_op jit(solution)/shard_map/ppermute | solution.py:81
  595.2 31.5 %collective-permute-start.10 = (bf16[256,2048]{1,0:T(8,128)(2,1)S(1)}, bf16[256,2048]{1,0:T(8,128)(2,1)S(1)}, u32[]{:S(2)}, u32[]{:S(2)}) collective-permute-start(bf16[256,2048]{1,0:T(8,128)(2,1)S(1)} %collective-permute-done.8), channel_id=1, source_target_pairs={{0,1},{1,2},{2,3},{3,0},{4,5},{5,6},{6,7},{7,4},{8,9},{9,10},{10,1... | collective-permute-start | bytes 3145736 | tf_op jit(solution)/shard_map/ppermute | solution.py:81
  640.2 11.5 collective-permute-done.10
  665.5 31.8 %fusion.9 = (bf16[2048,2048]{1,0:T(8,128)(2,1)}, bf16[2048,2048]{1,0:T(8,128)(2,1)}) fusion(bf16[2048,2048]{1,0:T(8,128)(2,1)} %fusion.61, bf16[2048,2048]{1,0:T(8,128)(2,1)} %fusion.55, bf16[2048,2048]{1,0:T(8,128)(2,1)} %all-gather.12.cloned.1.call-done, bf16[2048,2048]{1,0:T(8,128)(2,1)} %param.23), kind=kOutput, calls=%fused_computation.15 | convolution fusion | flops 17242783744 | bytes 50331648 | tf_op jit(solution)/shard_map/dot_general | solution.py:370
  697.3 24.4 %fusion.134 = f32[2048,2048]{1,0:T(8,128)} fusion(bf16[2048,2048]{1,0:T(8,128)(2,1)} %get-tuple-element.142, bf16[2048,2048]{1,0:T(8,128)(2,1)} %param.21), kind=kOutput, calls=%fused_computation.286 | convolution fusion | flops 17179869184 | bytes 33554432 | tf_op jit(solution)/shard_map/dot_general | solution.py:377
  721.7 26.7 %convolution_add_fusion = f32[2048,2048]{1,0:T(8,128)} fusion(f32[2048,2048]{1,0:T(8,128)} %fusion.134, bf16[2048,2048]{1,0:T(8,128)(2,1)} %get-tuple-element.141, bf16[2048,2048]{1,0:T(8,128)(2,1)} %param.22), kind=kOutput, calls=%fused_computation.17 | convolution fusion | flops 17184063488 | bytes 50331648 | tf_op jit(solution)/shard_map/dot_general | solution.py:378
  754.7 24.0 %collective-permute-done.12 = bf16[256,2048]{1,0:T(8,128)(2,1)S(1)} collective-permute-done((bf16[256,2048]{1,0:T(8,128)(2,1)S(1)}, bf16[256,2048]{1,0:T(8,128)(2,1)S(1)}, u32[]{:S(2)}, u32[]{:S(2)}) %collective-permute-start.12) | collective-permute-done | bytes 1048608 | tf_op jit(solution)/shard_map/ppermute | solution.py:105
  778.8 19.5 %collective-permute-done.15 = bf16[256,2048]{1,0:T(8,128)(2,1)S(1)} collective-permute-done((bf16[256,2048]{1,0:T(8,128)(2,1)S(1)}, bf16[256,2048]{1,0:T(8,128)(2,1)S(1)}, u32[]{:S(2)}, u32[]{:S(2)}) %collective-permute-start.15) | collective-permute-done | bytes 1048608 | tf_op jit(solution)/shard_map/ppermute | solution.py:107
  805.1 24.1 %collective-permute-done.13 = bf16[256,2048]{1,0:T(8,128)(2,1)S(1)} collective-permute-done((bf16[256,2048]{1,0:T(8,128)(2,1)S(1)}, bf16[256,2048]{1,0:T(8,128)(2,1)S(1)}, u32[]{:S(2)}, u32[]{:S(2)}) %collective-permute-start.13) | collective-permute-done | bytes 1048608 | tf_op jit(solution)/shard_map/ppermute | solution.py:105
  829.2 20.0 %collective-permute-done.16 = bf16[256,2048]{1,0:T(8,128)(2,1)S(1)} collective-permute-done((bf16[256,2048]{1,0:T(8,128)(2,1)S(1)}, bf16[256,2048]{1,0:T(8,128)(2,1)S(1)}, u32[]{:S(2)}, u32[]{:S(2)}) %collective-permute-start.16) | collective-permute-done | bytes 1048608 | tf_op jit(solution)/shard_map/ppermute | solution.py:107
  856.9 24.2 %collective-permute-done.14 = bf16[256,2048]{1,0:T(8,128)(2,1)} collective-permute-done((bf16[256,2048]{1,0:T(8,128)(2,1)}, bf16[256,2048]{1,0:T(8,128)(2,1)}, u32[]{:S(2)}, u32[]{:S(2)}) %collective-permute-start.14) | collective-permute-done | bytes 1048608 | tf_op jit(solution)/shard_map/ppermute | solution.py:105
  881.1 19.3 %collective-permute-done.17 = bf16[256,2048]{1,0:T(8,128)(2,1)} collective-permute-done((bf16[256,2048]{1,0:T(8,128)(2,1)S(1)}, bf16[256,2048]{1,0:T(8,128)(2,1)}, u32[]{:S(2)}, u32[]{:S(2)}) %collective-permute-start.17) | collective-permute-done | bytes 1048608 | tf_op jit(solution)/shard_map/ppermute | solution.py:107
  908.5 9.8 convolution_convert_fusion.7
  924.3 25.9 %fusion.128 = f32[2048,2048]{1,0:T(8,128)} fusion(bf16[2048,2048]{1,0:T(8,128)(2,1)} %param.23, bf16[2048,2048]{1,0:T(8,128)(2,1)} %fusion.55, bf16[2048,2048]{1,0:T(8,128)(2,1)} %fusion.61), kind=kOutput, calls=%fused_computation.282 | convolution fusion | flops 17213423616 | bytes 41943040 | tf_op jit(solution)/shard_map/dot_general | solution.py:368
  950.3 21.7 %all-to-all-done.1 = bf16[512,4,512]{2,0,1:T(8,128)(2,1)} async-done(((bf16[512,4,512]{2,0,1:T(8,128)(2,1)}), bf16[512,4,512]{2,0,1:T(8,128)(2,1)}, u32[]{:S(2)}, u32[]{:S(2)}) %all-to-all-start.1) | async-done | bytes 2097184 | tf_op jit(solution)/shard_map/all_to_all | solution.py:387
  976.2 5.3 reshape.367
  987.7 5.2 multiply_reduce_fusion.1
  992.9 9.1 fusion.97
  1006.1 10.6 convolution_convert_fusion.3
  1029.6 76.3 %shard_map.221 = (f32[4,2048,128]{2,1,0:T(8,128)}, f32[4,2048,128]{2,1,0:T(8,128)}, f32[4,2048,128]{2,1,0:T(8,128)}) custom-call(bf16[4,2048,128]{2,1,0:T(8,128)(2,1)} %bitcast.199, bf16[4,2048,128]{2,1,0:T(8,128)(2,1)} %bitcast.194, bf16[4,2048,128]{2,1,0:T(8,128)(2,1)} %bitcast.196, bf16[4,2048,128]{2,1,0:T(8,128)(2,1)} %get-tuple-element.167.do_ref, ...), custom_call_target="tpu_custom_call" | custom-call | flops 21474836480 | bytes 25165824 | tf_op jit(solution)/shard_map/pallas_call | solution.py:242
  1106.0 10.1 fusion.54
  1120.0 9.9 convolution_convert_fusion.6
  1132.6 6.2 fusion.53
  1142.8 10.2 convolution_convert_fusion.5
  1153.0 8.2 fusion.50
  1165.2 10.0 convolution_convert_fusion.4
  1175.3 26.8 %convolution_convert_fusion = bf16[2048,2048]{1,0:T(8,128)(2,1)} fusion(bf16[2048,2048]{1,0:T(8,128)(2,1)} %all-gather.12.cloned.1.call-done, bf16[2048,2048]{1,0:T(8,128)(2,1)} %fusion.55, bf16[2048,2048]{1,0:T(8,128)(2,1)} %fusion.61), kind=kOutput, calls=%fused_computation.23 | convolution fusion | flops 17217617920 | bytes 33554432 | tf_op jit(solution)/shard_map/dot_general | solution.py:371
  1210.1 24.0 %convolution_convert_fusion.1 = bf16[2048,2048]{1,0:T(8,128)(2,1)} fusion(bf16[2048,2048]{1,0:T(8,128)(2,1)} %constant_dynamic-update-slice_fusion, bf16[2048,2048]{1,0:T(8,128)(2,1)} %get-tuple-element.141), kind=kOutput, calls=%fused_computation.24 | convolution fusion | flops 17184063488 | bytes 25165824 | tf_op jit(solution)/shard_map/dot_general | solution.py:375
  1234.1 23.7 %convolution_convert_fusion.2 = bf16[2048,2048]{1,0:T(8,128)(2,1)} fusion(bf16[2048,2048]{1,0:T(8,128)(2,1)} %constant_dynamic-update-slice_fusion, bf16[2048,2048]{1,0:T(8,128)(2,1)} %get-tuple-element.142), kind=kOutput, calls=%fused_computation.25 | convolution fusion | flops 17184063488 | bytes 25165824 | tf_op jit(solution)/shard_map/dot_general | solution.py:374
  1265.8 9.9 fusion.135
  1275.7 9.0 fusion.136
  1284.7 23.4 %add_add_fusion = f32[2048,2048]{1,0:T(8,128)} fusion(f32[2048,2048]{1,0:T(8,128)} %fusion.135, f32[2048,2048]{1,0:T(8,128)} %fusion.136, bf16[2048,512]{0,1:T(8,128)(2,1)} %bitcast.188, bf16[2048,512]{1,0:T(8,128)(2,1)} %param.17), kind=kOutput, calls=%fused_computation.16 | convolution fusion | flops 4303355904 | bytes 54525952 | tf_op jit(solution)/shard_map/dot_general | solution.py:442
  1321.7 16.9 %collective-permute-done.24 = bf16[256,2048]{1,0:T(8,128)(2,1)S(1)} collective-permute-done((bf16[256,2048]{1,0:T(8,128)(2,1)S(1)}, bf16[256,2048]{1,0:T(8,128)(2,1)S(1)}, u32[]{:S(2)}, u32[]{:S(2)}) %collective-permute-start.24) | collective-permute-done | bytes 1048608 | tf_op jit(solution)/shard_map/ppermute | solution.py:105
  1338.6 22.5 %collective-permute-done.27 = bf16[256,2048]{1,0:T(8,128)(2,1)S(1)} collective-permute-done((bf16[256,2048]{1,0:T(8,128)(2,1)S(1)}, bf16[256,2048]{1,0:T(8,128)(2,1)S(1)}, u32[]{:S(2)}, u32[]{:S(2)}) %collective-permute-start.27) | collective-permute-done | bytes 1048608 | tf_op jit(solution)/shard_map/ppermute | solution.py:107
  1369.4 14.1 collective-permute-done.19
  1383.6 22.5 %collective-permute-done.22 = bf16[256,2048]{1,0:T(8,128)(2,1)S(1)} collective-permute-done((bf16[256,2048]{1,0:T(8,128)(2,1)S(1)}, bf16[256,2048]{1,0:T(8,128)(2,1)S(1)}, u32[]{:S(2)}, u32[]{:S(2)}) %collective-permute-start.22) | collective-permute-done | bytes 1048608 | tf_op jit(solution)/shard_map/ppermute | solution.py:107
  1414.3 14.2 collective-permute-done.25
  1429.5 21.5 %collective-permute-done.28 = bf16[256,2048]{1,0:T(8,128)(2,1)} collective-permute-done((bf16[256,2048]{1,0:T(8,128)(2,1)}, bf16[256,2048]{1,0:T(8,128)(2,1)}, u32[]{:S(2)}, u32[]{:S(2)}) %collective-permute-start.28) | collective-permute-done | bytes 1048608 | tf_op jit(solution)/shard_map/ppermute | solution.py:107
  1459.6 14.0 collective-permute-done.20
  1473.7 22.3 %collective-permute-done.23 = bf16[256,2048]{1,0:T(8,128)(2,1)} collective-permute-done((bf16[256,2048]{1,0:T(8,128)(2,1)}, bf16[256,2048]{1,0:T(8,128)(2,1)}, u32[]{:S(2)}, u32[]{:S(2)}) %collective-permute-start.23) | collective-permute-done | bytes 1048608 | tf_op jit(solution)/shard_map/ppermute | solution.py:107
  1496.0 5.7 dynamic-slice_add_fusion.3
  1501.7 5.4 fusion.33
  1512.5 12.1 collective-permute-done.26
  1524.6 29.4 %collective-permute-done.29 = bf16[256,2048]{1,0:T(8,128)(2,1)} collective-permute-done((bf16[256,2048]{1,0:T(8,128)(2,1)S(1)}, bf16[256,2048]{1,0:T(8,128)(2,1)}, u32[]{:S(2)}, u32[]{:S(2)}) %collective-permute-start.29) | collective-permute-done | bytes 1048608 | tf_op jit(solution)/shard_map/ppermute | solution.py:107
  1559.4 17.8 %all-reduce.1 = (f32[2048]{0:T(1024)S(1)}, f32[16]{0:T(128)S(1)}, f32[2048]{0:T(1024)S(1)}) all-reduce(f32[2048]{0:T(1024)S(1)} %get-tuple-element.127, f32[16]{0:T(128)S(1)} %multiply_dynamic-update-slice_fusion, f32[2048]{0:T(1024)S(1)} %copy-done.53), channel_id=1, replica_groups=mesh['dp'=8,'mp'=4] {'mp'}, use_global_device_ids=true, to_apply=%region_14.15 | all-reduce | flops 4112 | bytes 32896 | tf_op jit(solution)/shard_map/psum | solution.py:453
  1577.1 24.9 %all-reduce = (f32[2048]{0:T(1024)}, f32[16]{0:T(128)}, f32[2048]{0:T(1024)}) all-reduce(f32[2048]{0:T(1024)S(1)} %get-tuple-element.132, f32[16]{0:T(128)S(1)} %get-tuple-element.133, f32[2048]{0:T(1024)S(1)} %get-tuple-element.134), channel_id=1, replica_groups=mesh['dp'=8,'mp'=4] {'dp'}, use_global_device_ids=true, to_apply=%region_15.16 | all-reduce | flops 4112 | bytes 32896 | tf_op jit(solution)/shard_map/psum | solution.py:452
  1602.0 7.5 fusion.16
  (400 shorter events, 379.9 us)
Async XLA Ops:
  7.2 210.1 %copy-start = (bf16[2048,512]{1,0:T(8,128)(2,1)S(1)}, bf16[2048,512]{1,0:T(8,128)(2,1)}, u32[]{:S(2)}) copy-start(bf16[2048,512]{1,0:T(8,128)(2,1)} %param.15) | copy-start | bytes 6291460
  7.2 205.8 %all-gather.8.cloned.1.call-start = ((), (), s32[]{:S(2)}) async-start(), calls=%async_computation.10 | async-start | bytes 1310720 | tf_op jit(solution)/shard_map/all_gather | solution.py:304
  9.1 290.2 %all-gather.16.cloned.1.call-start = ((), (), s32[]{:S(2)}) async-start(), calls=%async_computation.22 | async-start | bytes 2396160 | tf_op jit(solution)/shard_map/all_gather | solution.py:26
  18.0 43.7 %collective-permute-start.1 = (bf16[256,2048]{1,0:T(8,128)(2,1)}, bf16[256,2048]{1,0:T(8,128)(2,1)S(1)}, u32[]{:S(2)}, u32[]{:S(2)}) collective-permute-start(bf16[256,2048]{1,0:T(8,128)(2,1)} %get-tuple-element.170), channel_id=1, source_target_pairs={{0,3},{1,0},{2,1},{3,2},{4,7},{5,4},{6,5},{7,6},{8,11},{9,8},{10,9... | collective-permute-start | bytes 3145736 | tf_op jit(solution)/shard_map/ppermute | solution.py:82
  23.1 63.5 %collective-permute-start = (bf16[256,2048]{1,0:T(8,128)(2,1)}, bf16[256,2048]{1,0:T(8,128)(2,1)}, u32[]{:S(2)}, u32[]{:S(2)}) collective-permute-start(bf16[256,2048]{1,0:T(8,128)(2,1)} %get-tuple-element.171), channel_id=1, source_target_pairs={{0,1},{1,2},{2,3},{3,0},{4,5},{5,6},{6,7},{7,4},{8,9},{9,10},{10,1... | collective-permute-start | bytes 3145736 | tf_op jit(solution)/shard_map/ppermute | solution.py:81
  24.7 189.6 %copy-start.52 = (s32[2048]{0:T(1024)}, s32[2048]{0:T(1024)S(1)}, u32[]{:S(2)}) copy-start(s32[2048]{0:T(1024)S(1)} %slice.62) | copy-start | bytes 24580
  32.6 175.0 %copy-start.58 = (f32[2048]{0:T(1024)}, f32[2048]{0:T(1024)S(1)}, u32[]{:S(2)}) copy-start(f32[2048]{0:T(1024)S(1)} %get-tuple-element.173) | copy-start | bytes 24580
  32.6 281.9 %copy-start.48 = (f32[2048]{0:T(1024)}, f32[2048]{0:T(1024)S(1)}, u32[]{:S(2)}) copy-start(f32[2048]{0:T(1024)S(1)} %get-tuple-element.172) | copy-start | bytes 24580
  61.7 159.4 %copy-start.27 = (bf16[256,2048]{1,0:T(8,128)(2,1)}, bf16[256,2048]{1,0:T(8,128)(2,1)S(1)}, u32[]{:S(2)}) copy-start(bf16[256,2048]{1,0:T(8,128)(2,1)S(1)} %collective-permute-done.1) | copy-start | bytes 3145732
  61.7 44.8 %collective-permute-start.3 = (bf16[256,2048]{1,0:T(8,128)(2,1)S(1)}, bf16[256,2048]{1,0:T(8,128)(2,1)}, u32[]{:S(2)}, u32[]{:S(2)}) collective-permute-start(bf16[256,2048]{1,0:T(8,128)(2,1)S(1)} %collective-permute-done.1), channel_id=1, source_target_pairs={{0,3},{1,0},{2,1},{3,2},{4,7},{5,4},{6,5},{7,6},{8,11},{9,8},{10,9... | collective-permute-start | bytes 3145736 | tf_op jit(solution)/shard_map/ppermute | solution.py:82
  86.6 47.5 %collective-permute-start.2 = (bf16[256,2048]{1,0:T(8,128)(2,1)}, bf16[256,2048]{1,0:T(8,128)(2,1)}, u32[]{:S(2)}, u32[]{:S(2)}) collective-permute-start(bf16[256,2048]{1,0:T(8,128)(2,1)} %collective-permute-done), channel_id=1, source_target_pairs={{0,1},{1,2},{2,3},{3,0},{4,5},{5,6},{6,7},{7,4},{8,9},{9,10},{10,1... | collective-permute-start | bytes 3145736 | tf_op jit(solution)/shard_map/ppermute | solution.py:81
  116.0 44.2 %collective-permute-start.5 = (bf16[256,2048]{1,0:T(8,128)(2,1)}, bf16[256,2048]{1,0:T(8,128)(2,1)}, u32[]{:S(2)}, u32[]{:S(2)}) collective-permute-start(bf16[256,2048]{1,0:T(8,128)(2,1)} %collective-permute-done.3), channel_id=1, source_target_pairs={{0,3},{1,0},{2,1},{3,2},{4,7},{5,4},{6,5},{7,6},{8,11},{9,8},{10,9... | collective-permute-start | bytes 3145736 | tf_op jit(solution)/shard_map/ppermute | solution.py:82
  139.2 36.9 %collective-permute-start.4 = (bf16[256,2048]{1,0:T(8,128)(2,1)}, bf16[256,2048]{1,0:T(8,128)(2,1)}, u32[]{:S(2)}, u32[]{:S(2)}) collective-permute-start(bf16[256,2048]{1,0:T(8,128)(2,1)} %collective-permute-done.2), channel_id=1, source_target_pairs={{0,1},{1,2},{2,3},{3,0},{4,5},{5,6},{6,7},{7,4},{8,9},{9,10},{10,1... | collective-permute-start | bytes 3145736 | tf_op jit(solution)/shard_map/ppermute | solution.py:81
  212.9 217.5 %all-gather.10.cloned.1.call-start = ((), (), s32[]{:S(2)}) async-start(), calls=%async_computation.11 | async-start | bytes 9437184 | tf_op jit(solution)/shard_map/all_gather | solution.py:303
  215.7 98.8 %copy-start.60 = (f32[4]{0:T(128)}, f32[4]{0:T(128)S(1)}, u32[]{:S(2)}) copy-start(f32[4]{0:T(128)S(1)} %get-tuple-element.140) | copy-start | bytes 52
  215.7 98.8 %copy-start.63 = (f32[4]{0:T(128)}, f32[4]{0:T(128)S(1)}, u32[]{:S(2)}) copy-start(f32[4]{0:T(128)S(1)} %get-tuple-element.139) | copy-start | bytes 52
  331.4 94.9 %all-to-all-start = ((bf16[4,512,512]{2,1,0:T(8,128)(2,1)}), bf16[4,512,512]{2,1,0:T(8,128)(2,1)}, u32[]{:S(2)}, u32[]{:S(2)}) async-start(bf16[4,512,512]{2,1,0:T(8,128)(2,1)} %convert_element_type.394), calls=%async_computation | async-start | bytes 4194304 | tf_op jit(solution)/shard_map/all_to_all | solution.py:352
  335.9 329.7 %all-gather.12.cloned.1.call-start = ((), (), s32[]{:S(2)}) async-start(), calls=%async_computation.12 | async-start | bytes 10485760 | tf_op jit(solution)/shard_map/all_gather | solution.py:369
  443.0 70.9 %collective-permute-start.7 = (bf16[256,2048]{1,0:T(8,128)(2,1)S(1)}, bf16[256,2048]{1,0:T(8,128)(2,1)S(1)}, u32[]{:S(2)}, u32[]{:S(2)}) collective-permute-start(bf16[256,2048]{1,0:T(8,128)(2,1)S(1)} %get-tuple-element.168), channel_id=1, source_target_pairs={{0,3},{1,0},{2,1},{3,2},{4,7},{5,4},{6,5},{7,6},{8,11},{9,8},{10,9... | collective-permute-start | bytes 3145736 | tf_op jit(solution)/shard_map/ppermute | solution.py:82
  443.6 91.9 %collective-permute-start.6 = (bf16[256,2048]{1,0:T(8,128)(2,1)S(1)}, bf16[256,2048]{1,0:T(8,128)(2,1)S(1)}, u32[]{:S(2)}, u32[]{:S(2)}) collective-permute-start(bf16[256,2048]{1,0:T(8,128)(2,1)S(1)} %get-tuple-element.169), channel_id=1, source_target_pairs={{0,1},{1,2},{2,3},{3,0},{4,5},{5,6},{6,7},{7,4},{8,9},{9,10},{10,1... | collective-permute-start | bytes 3145736 | tf_op jit(solution)/shard_map/ppermute | solution.py:81
  459.1 77.9 %slice-start.2 = ((s8[8388608]{0:T(1024)(128)(4,1)}), s8[4194304]{0:T(1024)(128)(4,1)S(1)}, s32[]{:S(2)}) async-start(s8[8388608]{0:T(1024)(128)(4,1)} %bitcast.229), calls=%async_computation.25 | async-start | bytes 8388608
  463.5 73.5 %slice-start.3 = ((s8[8388608]{0:T(1024)(128)(4,1)}), s8[4194304]{0:T(1024)(128)(4,1)S(1)}, s32[]{:S(2)}) async-start(s8[8388608]{0:T(1024)(128)(4,1)} %bitcast.229), calls=%async_computation.26 | async-start | bytes 8388608
  513.9 55.2 %collective-permute-start.9 = (bf16[256,2048]{1,0:T(8,128)(2,1)S(1)}, bf16[256,2048]{1,0:T(8,128)(2,1)S(1)}, u32[]{:S(2)}, u32[]{:S(2)}) collective-permute-start(bf16[256,2048]{1,0:T(8,128)(2,1)S(1)} %collective-permute-done.7), channel_id=1, source_target_pairs={{0,3},{1,0},{2,1},{3,2},{4,7},{5,4},{6,5},{7,6},{8,11},{9,8},{10,9... | collective-permute-start | bytes 3145736 | tf_op jit(solution)/shard_map/ppermute | solution.py:82
  535.5 59.7 %collective-permute-start.8 = (bf16[256,2048]{1,0:T(8,128)(2,1)S(1)}, bf16[256,2048]{1,0:T(8,128)(2,1)S(1)}, u32[]{:S(2)}, u32[]{:S(2)}) collective-permute-start(bf16[256,2048]{1,0:T(8,128)(2,1)S(1)} %collective-permute-done.6), channel_id=1, source_target_pairs={{0,1},{1,2},{2,3},{3,0},{4,5},{5,6},{6,7},{7,4},{8,9},{9,10},{10,1... | collective-permute-start | bytes 3145736 | tf_op jit(solution)/shard_map/ppermute | solution.py:81
  569.1 67.7 %copy-start.32 = (bf16[256,2048]{1,0:T(8,128)(2,1)}, bf16[256,2048]{1,0:T(8,128)(2,1)S(1)}, u32[]{:S(2)}) copy-start(bf16[256,2048]{1,0:T(8,128)(2,1)S(1)} %collective-permute-done.9) | copy-start | bytes 3145732
  569.1 89.3 %collective-permute-start.11 = (bf16[256,2048]{1,0:T(8,128)(2,1)S(1)}, bf16[256,2048]{1,0:T(8,128)(2,1)S(1)}, u32[]{:S(2)}, u32[]{:S(2)}) collective-permute-start(bf16[256,2048]{1,0:T(8,128)(2,1)S(1)} %collective-permute-done.9), channel_id=1, source_target_pairs={{0,3},{1,0},{2,1},{3,2},{4,7},{5,4},{6,5},{7,6},{8,11},{9,8},{10,9... | collective-permute-start | bytes 3145736 | tf_op jit(solution)/shard_map/ppermute | solution.py:82
  595.2 56.5 %collective-permute-start.10 = (bf16[256,2048]{1,0:T(8,128)(2,1)S(1)}, bf16[256,2048]{1,0:T(8,128)(2,1)S(1)}, u32[]{:S(2)}, u32[]{:S(2)}) collective-permute-start(bf16[256,2048]{1,0:T(8,128)(2,1)S(1)} %collective-permute-done.8), channel_id=1, source_target_pairs={{0,1},{1,2},{2,3},{3,0},{4,5},{5,6},{6,7},{7,4},{8,9},{9,10},{10,1... | collective-permute-start | bytes 3145736 | tf_op jit(solution)/shard_map/ppermute | solution.py:81
  750.9 27.9 %collective-permute-start.12 = (bf16[256,2048]{1,0:T(8,128)(2,1)S(1)}, bf16[256,2048]{1,0:T(8,128)(2,1)S(1)}, u32[]{:S(2)}, u32[]{:S(2)}) collective-permute-start(bf16[256,2048]{1,0:T(8,128)(2,1)S(1)} %get-tuple-element.165), channel_id=1, source_target_pairs={{0,1},{1,2},{2,3},{3,0},{4,5},{5,6},{6,7},{7,4},{8,9},{9,10},{10,1... | collective-permute-start | bytes 3145736 | tf_op jit(solution)/shard_map/ppermute | solution.py:105
  751.0 47.3 %collective-permute-start.15 = (bf16[256,2048]{1,0:T(8,128)(2,1)S(1)}, bf16[256,2048]{1,0:T(8,128)(2,1)S(1)}, u32[]{:S(2)}, u32[]{:S(2)}) collective-permute-start(bf16[256,2048]{1,0:T(8,128)(2,1)S(1)} %get-tuple-element.166), channel_id=1, source_target_pairs={{0,3},{1,0},{2,1},{3,2},{4,7},{5,4},{6,5},{7,6},{8,11},{9,8},{10,9... | collective-permute-start | bytes 3145736 | tf_op jit(solution)/shard_map/ppermute | solution.py:107
  801.2 27.9 %collective-permute-start.13 = (bf16[256,2048]{1,0:T(8,128)(2,1)S(1)}, bf16[256,2048]{1,0:T(8,128)(2,1)S(1)}, u32[]{:S(2)}, u32[]{:S(2)}) collective-permute-start(bf16[256,2048]{1,0:T(8,128)(2,1)S(1)} %get-tuple-element.163), channel_id=1, source_target_pairs={{0,1},{1,2},{2,3},{3,0},{4,5},{5,6},{6,7},{7,4},{8,9},{9,10},{10,1... | collective-permute-start | bytes 3145736 | tf_op jit(solution)/shard_map/ppermute | solution.py:105
  801.8 47.3 %collective-permute-start.16 = (bf16[256,2048]{1,0:T(8,128)(2,1)S(1)}, bf16[256,2048]{1,0:T(8,128)(2,1)S(1)}, u32[]{:S(2)}, u32[]{:S(2)}) collective-permute-start(bf16[256,2048]{1,0:T(8,128)(2,1)S(1)} %get-tuple-element.164), channel_id=1, source_target_pairs={{0,3},{1,0},{2,1},{3,2},{4,7},{5,4},{6,5},{7,6},{8,11},{9,8},{10,9... | collective-permute-start | bytes 3145736 | tf_op jit(solution)/shard_map/ppermute | solution.py:107
  853.0 28.1 %collective-permute-start.14 = (bf16[256,2048]{1,0:T(8,128)(2,1)}, bf16[256,2048]{1,0:T(8,128)(2,1)}, u32[]{:S(2)}, u32[]{:S(2)}) collective-permute-start(bf16[256,2048]{1,0:T(8,128)(2,1)} %get-tuple-element.161), channel_id=1, source_target_pairs={{0,1},{1,2},{2,3},{3,0},{4,5},{5,6},{6,7},{7,4},{8,9},{9,10},{10,1... | collective-permute-start | bytes 3145736 | tf_op jit(solution)/shard_map/ppermute | solution.py:105
  853.3 47.1 %collective-permute-start.17 = (bf16[256,2048]{1,0:T(8,128)(2,1)S(1)}, bf16[256,2048]{1,0:T(8,128)(2,1)}, u32[]{:S(2)}, u32[]{:S(2)}) collective-permute-start(bf16[256,2048]{1,0:T(8,128)(2,1)S(1)} %get-tuple-element.162), channel_id=1, source_target_pairs={{0,3},{1,0},{2,1},{3,2},{4,7},{5,4},{6,5},{7,6},{8,11},{9,8},{10,9... | collective-permute-start | bytes 3145736 | tf_op jit(solution)/shard_map/ppermute | solution.py:107
  856.9 47.0 %copy-start.2 = (f32[512,2048]{1,0:T(8,128)S(1)}, f32[512,2048]{1,0:T(8,128)}, u32[]{:S(2)}) copy-start(f32[512,2048]{1,0:T(8,128)} %copy-done.1) | copy-start | bytes 12582916
  856.9 47.0 %copy-start.51 = (f32[2048]{0:T(1024)S(1)}, f32[2048]{0:T(1024)}, u32[]{:S(2)}) copy-start(f32[2048]{0:T(1024)} %param.20) | copy-start | bytes 24580
  856.9 47.0 %copy-start.57 = (f32[512]{0:T(512)S(1)}, f32[512]{0:T(512)}, u32[]{:S(2)}) copy-start(f32[512]{0:T(512)} %copy-done.56) | copy-start | bytes 6148
  919.8 52.1 %all-to-all-start.1 = ((bf16[512,4,512]{2,0,1:T(8,128)(2,1)}), bf16[512,4,512]{2,0,1:T(8,128)(2,1)}, u32[]{:S(2)}, u32[]{:S(2)}) async-start(bf16[512,4,512]{2,0,1:T(8,128)(2,1)} %bitcast.192), calls=%async_computation.1 | async-start | bytes 4194304 | tf_op jit(solution)/shard_map/all_to_all | solution.py:387
  924.3 205.7 %all-gather.14.cloned.1.call-start = ((), (), s32[]{:S(2)}) async-start(), calls=%async_computation.13 | async-start | bytes 1198080 | tf_op jit(solution)/shard_map/all_gather | solution.py:26
  1006.1 495.6 %reduce-scatter.15.cloned.1.call-start = ((), (), s32[]{:S(2)}) async-start(), calls=%async_computation.17 | async-start | bytes 9437184 | tf_op jit(solution)/shard_map/reduce_scatter | solution.py:457
  1016.8 490.4 %reduce-scatter.9.cloned.1.call-start = ((), (), s32[]{:S(2)}) async-start(), calls=%async_computation.14 | async-start | bytes 2359296 | tf_op jit(solution)/shard_map/reduce_scatter | solution.py:457
  1029.6 76.3 %copy-start.43 = (f32[512,128]{1,0:T(8,128)S(1)}, f32[512,128]{1,0:T(8,128)}, u32[]{:S(2)}) copy-start(f32[512,128]{1,0:T(8,128)} %copy-done.42) | copy-start | bytes 786436
  1029.6 76.3 %copy-start.67 = (f32[4,128]{1,0:T(4,128)S(1)}, f32[4,128]{1,0:T(4,128)}, u32[]{:S(2)}) copy-start(f32[4,128]{1,0:T(4,128)} %copy-done.66) | copy-start | bytes 6148
  1130.0 379.0 %reduce-scatter.11.cloned.1.call-start = ((), (), s32[]{:S(2)}) async-start(), calls=%async_computation.15 | async-start | bytes 2359296 | tf_op jit(solution)/shard_map/reduce_scatter | solution.py:457
  1153.0 357.8 %reduce-scatter.13.cloned.1.call-start = ((), (), s32[]{:S(2)}) async-start(), calls=%async_computation.16 | async-start | bytes 2359296 | tf_op jit(solution)/shard_map/reduce_scatter | solution.py:457
  1175.2 434.3 %reduce-scatter.23.cloned.1.call-start = ((), (), s32[]{:S(2)}) async-start(), calls=%async_computation.21 | async-start | bytes 9437184 | tf_op jit(solution)/shard_map/reduce_scatter | solution.py:457
  1202.1 410.2 %reduce-scatter.21.cloned.1.call-start = ((), (), s32[]{:S(2)}) async-start(), calls=%async_computation.20 | async-start | bytes 9437184 | tf_op jit(solution)/shard_map/reduce_scatter | solution.py:457
  1234.0 381.0 %reduce-scatter.19.cloned.1.call-start = ((), (), s32[]{:S(2)}) async-start(), calls=%async_computation.19 | async-start | bytes 9437184 | tf_op jit(solution)/shard_map/reduce_scatter | solution.py:457
  1257.9 360.0 %reduce-scatter.17.cloned.1.call-start = ((), (), s32[]{:S(2)}) async-start(), calls=%async_computation.18 | async-start | bytes 1310720 | tf_op jit(solution)/shard_map/reduce_scatter | solution.py:461
  1261.9 52.6 %collective-permute-start.18 = (bf16[256,2048]{1,0:T(8,128)(2,1)}, bf16[256,2048]{1,0:T(8,128)(2,1)S(1)}, u32[]{:S(2)}, u32[]{:S(2)}) collective-permute-start(bf16[256,2048]{1,0:T(8,128)(2,1)} %get-tuple-element.157), channel_id=1, source_target_pairs={{0,1},{1,2},{2,3},{3,0},{4,5},{5,6},{6,7},{7,4},{8,9},{9,10},{10,1... | collective-permute-start | bytes 3145736 | tf_op jit(solution)/shard_map/ppermute | solution.py:105
  1262.0 52.6 %collective-permute-start.21 = (bf16[256,2048]{1,0:T(8,128)(2,1)}, bf16[256,2048]{1,0:T(8,128)(2,1)}, u32[]{:S(2)}, u32[]{:S(2)}) collective-permute-start(bf16[256,2048]{1,0:T(8,128)(2,1)} %get-tuple-element.158), channel_id=1, source_target_pairs={{0,3},{1,0},{2,1},{3,2},{4,7},{5,4},{6,5},{7,6},{8,11},{9,8},{10,9... | collective-permute-start | bytes 3145736 | tf_op jit(solution)/shard_map/ppermute | solution.py:107
  1310.7 27.9 %collective-permute-start.24 = (bf16[256,2048]{1,0:T(8,128)(2,1)S(1)}, bf16[256,2048]{1,0:T(8,128)(2,1)S(1)}, u32[]{:S(2)}, u32[]{:S(2)}) collective-permute-start(bf16[256,2048]{1,0:T(8,128)(2,1)S(1)} %get-tuple-element.149), channel_id=1, source_target_pairs={{0,1},{1,2},{2,3},{3,0},{4,5},{5,6},{6,7},{7,4},{8,9},{9,10},{10,1... | collective-permute-start | bytes 3145736 | tf_op jit(solution)/shard_map/ppermute | solution.py:105
  1310.8 50.4 %collective-permute-start.27 = (bf16[256,2048]{1,0:T(8,128)(2,1)S(1)}, bf16[256,2048]{1,0:T(8,128)(2,1)S(1)}, u32[]{:S(2)}, u32[]{:S(2)}) collective-permute-start(bf16[256,2048]{1,0:T(8,128)(2,1)S(1)} %get-tuple-element.150), channel_id=1, source_target_pairs={{0,3},{1,0},{2,1},{3,2},{4,7},{5,4},{6,5},{7,6},{8,11},{9,8},{10,9... | collective-permute-start | bytes 3145736 | tf_op jit(solution)/shard_map/ppermute | solution.py:107
  1317.8 65.8 %collective-permute-start.19 = (bf16[256,2048]{1,0:T(8,128)(2,1)S(1)}, bf16[256,2048]{1,0:T(8,128)(2,1)S(1)}, u32[]{:S(2)}, u32[]{:S(2)}) collective-permute-start(bf16[256,2048]{1,0:T(8,128)(2,1)S(1)} %get-tuple-element.155), channel_id=1, source_target_pairs={{0,1},{1,2},{2,3},{3,0},{4,5},{5,6},{6,7},{7,4},{8,9},{9,10},{10,1... | collective-permute-start | bytes 3145736 | tf_op jit(solution)/shard_map/ppermute | solution.py:105
  1317.8 88.2 %collective-permute-start.22 = (bf16[256,2048]{1,0:T(8,128)(2,1)S(1)}, bf16[256,2048]{1,0:T(8,128)(2,1)S(1)}, u32[]{:S(2)}, u32[]{:S(2)}) collective-permute-start(bf16[256,2048]{1,0:T(8,128)(2,1)S(1)} %get-tuple-element.156), channel_id=1, source_target_pairs={{0,3},{1,0},{2,1},{3,2},{4,7},{5,4},{6,5},{7,6},{8,11},{9,8},{10,9... | collective-permute-start | bytes 3145736 | tf_op jit(solution)/shard_map/ppermute | solution.py:107
  1365.4 63.2 %collective-permute-start.25 = (bf16[256,2048]{1,0:T(8,128)(2,1)}, bf16[256,2048]{1,0:T(8,128)(2,1)S(1)}, u32[]{:S(2)}, u32[]{:S(2)}) collective-permute-start(bf16[256,2048]{1,0:T(8,128)(2,1)} %get-tuple-element.147), channel_id=1, source_target_pairs={{0,1},{1,2},{2,3},{3,0},{4,5},{5,6},{6,7},{7,4},{8,9},{9,10},{10,1... | collective-permute-start | bytes 3145736 | tf_op jit(solution)/shard_map/ppermute | solution.py:105
  1365.9 48.3 %copy-start.62 = (f32[4]{0:T(128)S(1)}, f32[4]{0:T(128)}, u32[]{:S(2)}) copy-start(f32[4]{0:T(128)} %copy-done.60) | copy-start | bytes 52
  1365.9 48.3 %copy-start.65 = (f32[4]{0:T(128)S(1)}, f32[4]{0:T(128)}, u32[]{:S(2)}) copy-start(f32[4]{0:T(128)} %get-tuple-element.115) | copy-start | bytes 52
  1365.9 85.1 %collective-permute-start.28 = (bf16[256,2048]{1,0:T(8,128)(2,1)}, bf16[256,2048]{1,0:T(8,128)(2,1)}, u32[]{:S(2)}, u32[]{:S(2)}) collective-permute-start(bf16[256,2048]{1,0:T(8,128)(2,1)} %get-tuple-element.148), channel_id=1, source_target_pairs={{0,3},{1,0},{2,1},{3,2},{4,7},{5,4},{6,5},{7,6},{8,11},{9,8},{10,9... | collective-permute-start | bytes 3145736 | tf_op jit(solution)/shard_map/ppermute | solution.py:107
  1410.4 63.3 %collective-permute-start.20 = (bf16[256,2048]{1,0:T(8,128)(2,1)}, bf16[256,2048]{1,0:T(8,128)(2,1)}, u32[]{:S(2)}, u32[]{:S(2)}) collective-permute-start(bf16[256,2048]{1,0:T(8,128)(2,1)} %get-tuple-element.153), channel_id=1, source_target_pairs={{0,1},{1,2},{2,3},{3,0},{4,5},{5,6},{6,7},{7,4},{8,9},{9,10},{10,1... | collective-permute-start | bytes 3145736 | tf_op jit(solution)/shard_map/ppermute | solution.py:105
  1411.0 85.0 %collective-permute-start.23 = (bf16[256,2048]{1,0:T(8,128)(2,1)}, bf16[256,2048]{1,0:T(8,128)(2,1)}, u32[]{:S(2)}, u32[]{:S(2)}) collective-permute-start(bf16[256,2048]{1,0:T(8,128)(2,1)} %get-tuple-element.154), channel_id=1, source_target_pairs={{0,3},{1,0},{2,1},{3,2},{4,7},{5,4},{6,5},{7,6},{8,11},{9,8},{10,9... | collective-permute-start | bytes 3145736 | tf_op jit(solution)/shard_map/ppermute | solution.py:107
  1455.8 68.8 %collective-permute-start.26 = (bf16[256,2048]{1,0:T(8,128)(2,1)}, bf16[256,2048]{1,0:T(8,128)(2,1)}, u32[]{:S(2)}, u32[]{:S(2)}) collective-permute-start(bf16[256,2048]{1,0:T(8,128)(2,1)} %get-tuple-element.145), channel_id=1, source_target_pairs={{0,1},{1,2},{2,3},{3,0},{4,5},{5,6},{6,7},{7,4},{8,9},{9,10},{10,1... | collective-permute-start | bytes 3145736 | tf_op jit(solution)/shard_map/ppermute | solution.py:105
  1456.2 97.8 %collective-permute-start.29 = (bf16[256,2048]{1,0:T(8,128)(2,1)S(1)}, bf16[256,2048]{1,0:T(8,128)(2,1)}, u32[]{:S(2)}, u32[]{:S(2)}) collective-permute-start(bf16[256,2048]{1,0:T(8,128)(2,1)S(1)} %get-tuple-element.146), channel_id=1, source_target_pairs={{0,3},{1,0},{2,1},{3,2},{4,7},{5,4},{6,5},{7,6},{8,11},{9,8},{10,9... | collective-permute-start | bytes 3145736 | tf_op jit(solution)/shard_map/ppermute | solution.py:107
  1512.5 44.9 %copy-start.47 = (f32[2048]{0:T(1024)S(1)}, f32[2048]{0:T(1024)}, u32[]{:S(2)}) copy-start(f32[2048]{0:T(1024)} %param.14) | copy-start | bytes 24580
  1512.5 44.9 %copy-start.55 = (f32[512]{0:T(512)S(1)}, f32[512]{0:T(512)}, u32[]{:S(2)}) copy-start(f32[512]{0:T(512)} %copy-done.54) | copy-start | bytes 6148
  (58 other events, 444.3 us)
Sparse Core Ops, SparseCore 0:
  9.6 41.3 all-gather.7
  213.0 26.1 all-gather.15
  241.1 55.8 all-gather.9
  337.9 266.9 all-gather.11
  1006.2 26.1 all-gather.13
  1035.7 71.2 reduce-scatter.14
  1130.1 43.5 reduce-scatter.8
  1177.0 41.0 reduce-scatter.10
  1221.4 41.0 reduce-scatter.12
  1265.8 71.2 reduce-scatter.22
  1340.6 71.4 reduce-scatter.20
  1415.5 71.4 reduce-scatter.18
  1501.8 44.1 reduce-scatter.16

commit v4 on v3

--- a/solution.py
+++ b/solution.py
@@ -8,11 +8,11 @@
 from jax.experimental.pallas import tpu as pltpu
 from jax.sharding import PartitionSpec as P
 
+
 SEG = 2048
 
 
 eps_norm = 1e-05
-neg_fill = -1e30
 highest = lax.Precision.HIGHEST
 
 
@@ -102,10 +102,10 @@
     ahead = chunk((place - 1) % n, 0)
     behind = chunk((place + 1) % n, half)
     for step in range(1, n):
-        ahead = lax.ppermute(ahead.astype(kind), axis, ring_pairs(n, 1)).astype(jnp.float32)
-        ahead = ahead + chunk((place - 1 - step) % n, 0)
-        behind = lax.ppermute(behind.astype(kind), axis, ring_pairs(n, -1)).astype(jnp.float32)
-        behind = behind + chunk((place + 1 + step) % n, half)
+        ahead = lax.ppermute(ahead.astype(kind), axis, ring_pairs(n, 1))
+        behind = lax.ppermute(behind.astype(kind), axis, ring_pairs(n, -1))
+        ahead = ahead.astype(jnp.float32) + chunk((place - 1 - step) % n, 0)
+        behind = behind.astype(jnp.float32) + chunk((place + 1 + step) % n, half)
     return jnp.concatenate([ahead, behind], axis=0)
 
 
@@ -144,13 +144,6 @@
     position = first + jnp.arange(count, dtype=jnp.int32)
     before = jnp.sum((bounds[None, :] <= position[:, None]).astype(jnp.int32), axis=1)
     return jnp.where(position < bounds[-1], before, doc_lengths.shape[0] + position)
-
-
-def block_allowed(doc_index, row_start, seg_start, block_rows):
-    query_docs = lax.dynamic_slice_in_dim(doc_index, row_start, block_rows, 0)
-    query_pos = row_start + jnp.arange(block_rows, dtype=jnp.int32)
-    key_pos = seg_start + jnp.arange(SEG, dtype=jnp.int32)
-    return (key_pos[None, :] <= query_pos[:, None]) & (doc_index[None, :] == query_docs[:, None])
 
 
 NEG = -1e30
@@ -306,6 +299,7 @@
     x_rows = tokens.astype(jnp.float32)
     inverse1 = inverse_rms(x_rows)
     normed1 = (x_rows * inverse1 * norm1_gain).astype(jnp.bfloat16)
+
     def project_qkv(rows):
         return (rows,) + tuple(
             jnp.dot(rows, weight, preferred_element_type=jnp.float32).astype(jnp.bfloat16)
@@ -354,6 +348,7 @@
     resid = x_rows + attn_sum
     inverse2 = inverse_rms(resid)
     normed2 = (resid * inverse2 * norm2_gain).astype(jnp.bfloat16)
+
     def project_ffn(rows):
         return (rows,) + tuple(
             jnp.dot(rows, weight, preferred_element_type=jnp.float32).astype(jnp.bfloat16)
@@ -366,7 +361,7 @@
     sig_gate = jax.nn.sigmoid(gate_f)
     act = (gate_f * sig_gate * up_f).astype(jnp.bfloat16)
     mlp_part = jnp.dot(act, w_down, preferred_element_type=jnp.float32)
-    grad_rows_all = lax.all_gather(grad_rows, "mp", axis=0, tiled=True)
+    (grad_rows_all,) = ring_gather(grad_rows, "mp", lambda rows: (rows,))
     d_act = jnp.dot(grad_rows_all, w_down.T, preferred_element_type=jnp.float32)
     grad_down = jnp.dot(act.T, grad_rows_all, preferred_element_type=jnp.float32)
     d_gate = (d_act * up_f * sig_gate * (1.0 + gate_f * (1.0 - sig_gate))).astype(jnp.bfloat16)

time: 1640 us -> 1620 us (0.988)
  waiting for transfers between devices: 615 us -> 581 us
    all_to_all x1, waiting for transfers between devices: 89.8 us -> 0.01 us  [local(): mixed = lax.all_to_all(mixed_cols, 'mp', 0, 1, tiled=True)]
    ppermute x6 -> x9, waiting for transfers between devices: 86.3 us -> 135 us  [ring_gather(): ahead = lax.ppermute(ahead, axis, ring_pairs(n, 1))]
    dynamic_update_slice x29 -> x35, local copies, waits for them, and re-layouts: 39.9 us -> 47.5 us  [ring_gather(): lax.dynamic_update_slice_in_dim(out, part, start, 0)]
    ppermute x6 -> x9, waiting for transfers between devices: 95.4 us -> 103 us  [ring_gather(): behind = lax.ppermute(behind, axis, ring_pairs(n, -1))]
    ppermute x6 -> x9, starting transfers between devices: 35.1 us -> 36.1 us  [ring_gather(): ahead = lax.ppermute(ahead, axis, ring_pairs(n, 1))]
  transfers between devices with their start and end apart: 45 -> 50, of which waited for: 28 -> 30; matrix products, arithmetic and copies ran while one was open for 34% -> 34% of each run, Pallas kernels for 8% -> 8%
where the time goes in v4:
time: 1620 us; the launch traced here: 1610 us
  waiting for transfers between devices  581 us (36%)
  matrix products  458 us (28%)
  local copies, waits for them, and re-layouts  171 us (11%)
  Pallas kernels  127 us (8%)
  starting transfers between devices  120 us (7%)
  other arithmetic  93.1 us (6%)
  blocking collectives  41.6 us (3%)
  between operations  17.7 us (1%)
    ppermute x9, waiting for transfers between devices, ring_scatter(): behind = lax.ppermute(behind.astype(kind), axis, ring_pairs(n, -1))  176 us
    ppermute x9, waiting for transfers between devices, ring_scatter(): ahead = lax.ppermute(ahead.astype(kind), axis, ring_pairs(n, 1))  146 us
    ppermute x9, waiting for transfers between devices, ring_gather(): ahead = lax.ppermute(ahead, axis, ring_pairs(n, 1))  135 us
    ppermute x9, waiting for transfers between devices, ring_gather(): behind = lax.ppermute(behind, axis, ring_pairs(n, -1))  103 us
    pallas_call x1, Pallas kernels, attention_bwd(): pl.pallas_call(functools.partial(_bwd_kernel, scale, seg), grid=(H, nq),...  76.3 us
    dot_general x14, matrix products, project_ffn(): jnp.dot(rows, weight, preferred_element_type=jnp.float32)  59.6 us
    dot_general x21, matrix products, project_qkv(): jnp.dot(rows, weight, preferred_element_type=jnp.float32)  56.3 us
    pallas_call x1, Pallas kernels, attention_fwd(): pl.pallas_call(functools.partial(_fwd_kernel, scale, seg), grid=(H, nq),...  50.8 us
  transfers between devices with their start and end apart: 50, of which 30 were waited for; matrix products, arithmetic and copies ran while one was open for 34% of the time, Pallas kernels for 8%

profile of v4, /device:TPU:0, one launch (start us, length us, event | category | flops | bytes accessed | tf_op | source)
XLA Modules:
  0.0 1609.7 jit_solution(9950909479668072926)
XLA Ops:
  18.0 5.1 collective-permute-start.1
  40.6 21.1 %collective-permute-done.1 = bf16[256,2048]{1,0:T(8,128)(2,1)S(1)} collective-permute-done((bf16[256,2048]{1,0:T(8,128)(2,1)}, bf16[256,2048]{1,0:T(8,128)(2,1)S(1)}, u32[]{:S(2)}, u32[]{:S(2)}) %collective-permute-start.1) | collective-permute-done | bytes 1048608 | tf_op jit(solution)/shard_map/ppermute | solution.py:82
  66.5 20.1 %collective-permute-done = bf16[256,2048]{1,0:T(8,128)(2,1)} collective-permute-done((bf16[256,2048]{1,0:T(8,128)(2,1)}, bf16[256,2048]{1,0:T(8,128)(2,1)}, u32[]{:S(2)}, u32[]{:S(2)}) %collective-permute-start) | collective-permute-done | bytes 1048608 | tf_op jit(solution)/shard_map/ppermute | solution.py:81
  116.1 18.0 %collective-permute-start.5 = (bf16[256,2048]{1,0:T(8,128)(2,1)}, bf16[256,2048]{1,0:T(8,128)(2,1)}, u32[]{:S(2)}, u32[]{:S(2)}) collective-permute-start(bf16[256,2048]{1,0:T(8,128)(2,1)} %collective-permute-done.3), channel_id=1, source_target_pairs={{0,3},{1,0},{2,1},{3,2},{4,7},{5,4},{6,5},{7,6},{8,11},{9,8},{10,9... | collective-permute-start | bytes 3145736 | tf_op jit(solution)/shard_map/ppermute | solution.py:82
  150.3 10.0 collective-permute-done.5
  164.7 11.4 collective-permute-done.4
  212.9 11.5 all-gather.9.cloned.1.call-start
  256.6 50.8 %shard_map.220 = (f32[4,2048,128]{2,1,0:T(8,128)}, f32[4,2048,1]{2,1,0:T(8,128)}) custom-call(bf16[4,2048,128]{2,1,0:T(8,128)(2,1)} %bitcast.197, bf16[4,2048,128]{2,1,0:T(8,128)(2,1)} %bitcast.193, bf16[4,2048,128]{2,1,0:T(8,128)(2,1)} %bitcast.195, s32[2048,1]{1,0:T(8,128)} %copy.243.docq_ref, s32[1,2048]{1,0:T(1,128)} %bitcast.219), custom_call_target="tpu_custom_call" | custom-call | flops 8589934592 | bytes 10485760 | tf_op jit(solution)/shard_map/pallas_call | solution.py:210
  311.2 6.2 fusion.46
  324.5 10.9 copy.244
  347.9 57.9 %collective-permute-done.14 = bf16[256,2048]{1,0:T(8,128)(2,1)S(1)} collective-permute-done((bf16[256,2048]{1,0:T(8,128)(2,1)}, bf16[256,2048]{1,0:T(8,128)(2,1)S(1)}, u32[]{:S(2)}, u32[]{:S(2)}) %collective-permute-start.14) | collective-permute-done | bytes 1048608 | tf_op jit(solution)/shard_map/ppermute | solution.py:81
  405.8 28.8 %collective-permute-start.16 = (bf16[256,2048]{1,0:T(8,128)(2,1)S(1)}, bf16[256,2048]{1,0:T(8,128)(2,1)S(1)}, u32[]{:S(2)}, u32[]{:S(2)}) collective-permute-start(bf16[256,2048]{1,0:T(8,128)(2,1)S(1)} %collective-permute-done.14), channel_id=1, source_target_pairs={{0,1},{1,2},{2,3},{3,0},{4,5},{5,6},{6,7},{7,4},{8,9},{9,10},{10,1... | collective-permute-start | bytes 3145736 | tf_op jit(solution)/shard_map/ppermute | solution.py:81
  445.9 12.2 collective-permute-done.16
  459.2 21.3 %collective-permute-done.17 = bf16[256,2048]{1,0:T(8,128)(2,1)S(1)} collective-permute-done((bf16[256,2048]{1,0:T(8,128)(2,1)S(1)}, bf16[256,2048]{1,0:T(8,128)(2,1)S(1)}, u32[]{:S(2)}, u32[]{:S(2)}) %collective-permute-start.17) | collective-permute-done | bytes 1048608 | tf_op jit(solution)/shard_map/ppermute | solution.py:82
  486.0 9.8 multiply_reduce_fusion.4
  505.2 9.1 fusion.40
  518.7 9.3 fusion.41
  528.0 15.8 collective-permute-done.7
  561.9 29.6 %collective-permute-done.9 = bf16[256,2048]{1,0:T(8,128)(2,1)S(1)} collective-permute-done((bf16[256,2048]{1,0:T(8,128)(2,1)S(1)}, bf16[256,2048]{1,0:T(8,128)(2,1)S(1)}, u32[]{:S(2)}, u32[]{:S(2)}) %collective-permute-start.9) | collective-permute-done | bytes 1048608 | tf_op jit(solution)/shard_map/ppermute | solution.py:82
  608.9 26.6 %collective-permute-done.10 = bf16[256,2048]{1,0:T(8,128)(2,1)S(1)} collective-permute-done((bf16[256,2048]{1,0:T(8,128)(2,1)S(1)}, bf16[256,2048]{1,0:T(8,128)(2,1)S(1)}, u32[]{:S(2)}, u32[]{:S(2)}) %collective-permute-start.10) | collective-permute-done | bytes 1048608 | tf_op jit(solution)/shard_map/ppermute | solution.py:81
  649.6 31.8 %fusion.9 = (bf16[2048,2048]{1,0:T(8,128)(2,1)}, bf16[2048,2048]{1,0:T(8,128)(2,1)}) fusion(bf16[2048,2048]{1,0:T(8,128)(2,1)} %fusion.61, bf16[2048,2048]{1,0:T(8,128)(2,1)} %fusion.55, bf16[2048,2048]{1,0:T(8,128)(2,1)} %constant_dynamic-update-slice_fusion.14, bf16[2048,2048]{1,0:T(8,128)(2,1)} %param.23), kind=kOutput, calls=%fused_computation.15 | convolution fusion | flops 17242783744 | bytes 50331648 | tf_op jit(solution)/shard_map/dot_general | solution.py:365
  681.4 24.4 %fusion.135 = f32[2048,2048]{1,0:T(8,128)} fusion(bf16[2048,2048]{1,0:T(8,128)(2,1)} %get-tuple-element.142, bf16[2048,2048]{1,0:T(8,128)(2,1)} %param.21), kind=kOutput, calls=%fused_computation.294 | convolution fusion | flops 17179869184 | bytes 33554432 | tf_op jit(solution)/shard_map/dot_general | solution.py:372
  705.8 26.4 %convolution_add_fusion = f32[2048,2048]{1,0:T(8,128)} fusion(f32[2048,2048]{1,0:T(8,128)} %fusion.135, bf16[2048,2048]{1,0:T(8,128)(2,1)} %get-tuple-element.141, bf16[2048,2048]{1,0:T(8,128)(2,1)} %param.22), kind=kOutput, calls=%fused_computation.17 | convolution fusion | flops 17184063488 | bytes 50331648 | tf_op jit(solution)/shard_map/dot_general | solution.py:373
  738.6 24.0 %collective-permute-done.18 = bf16[256,2048]{1,0:T(8,128)(2,1)S(1)} collective-permute-done((bf16[256,2048]{1,0:T(8,128)(2,1)S(1)}, bf16[256,2048]{1,0:T(8,128)(2,1)S(1)}, u32[]{:S(2)}, u32[]{:S(2)}) %collective-permute-start.18) | collective-permute-done | bytes 1048608 | tf_op jit(solution)/shard_map/ppermute | solution.py:105
  762.6 19.5 %collective-permute-done.21 = bf16[256,2048]{1,0:T(8,128)(2,1)S(1)} collective-permute-done((bf16[256,2048]{1,0:T(8,128)(2,1)S(1)}, bf16[256,2048]{1,0:T(8,128)(2,1)S(1)}, u32[]{:S(2)}, u32[]{:S(2)}) %collective-permute-start.21) | collective-permute-done | bytes 1048608 | tf_op jit(solution)/shard_map/ppermute | solution.py:106
  788.9 24.0 %collective-permute-done.19 = bf16[256,2048]{1,0:T(8,128)(2,1)S(1)} collective-permute-done((bf16[256,2048]{1,0:T(8,128)(2,1)S(1)}, bf16[256,2048]{1,0:T(8,128)(2,1)S(1)}, u32[]{:S(2)}, u32[]{:S(2)}) %collective-permute-start.19) | collective-permute-done | bytes 1048608 | tf_op jit(solution)/shard_map/ppermute | solution.py:105
  812.9 20.6 %collective-permute-done.22 = bf16[256,2048]{1,0:T(8,128)(2,1)S(1)} collective-permute-done((bf16[256,2048]{1,0:T(8,128)(2,1)S(1)}, bf16[256,2048]{1,0:T(8,128)(2,1)S(1)}, u32[]{:S(2)}, u32[]{:S(2)}) %collective-permute-start.22) | collective-permute-done | bytes 1048608 | tf_op jit(solution)/shard_map/ppermute | solution.py:106
  841.3 24.2 %collective-permute-done.20 = bf16[256,2048]{1,0:T(8,128)(2,1)} collective-permute-done((bf16[256,2048]{1,0:T(8,128)(2,1)}, bf16[256,2048]{1,0:T(8,128)(2,1)}, u32[]{:S(2)}, u32[]{:S(2)}) %collective-permute-start.20) | collective-permute-done | bytes 1048608 | tf_op jit(solution)/shard_map/ppermute | solution.py:105
  865.5 19.1 %collective-permute-done.23 = bf16[256,2048]{1,0:T(8,128)(2,1)} collective-permute-done((bf16[256,2048]{1,0:T(8,128)(2,1)S(1)}, bf16[256,2048]{1,0:T(8,128)(2,1)}, u32[]{:S(2)}, u32[]{:S(2)}) %collective-permute-start.23) | collective-permute-done | bytes 1048608 | tf_op jit(solution)/shard_map/ppermute | solution.py:106
  892.7 9.8 convolution_convert_fusion.7
  908.5 26.0 %fusion.128 = f32[2048,2048]{1,0:T(8,128)} fusion(bf16[2048,2048]{1,0:T(8,128)(2,1)} %param.23, bf16[2048,2048]{1,0:T(8,128)(2,1)} %fusion.55, bf16[2048,2048]{1,0:T(8,128)(2,1)} %fusion.61), kind=kOutput, calls=%fused_computation.289 | convolution fusion | flops 17213423616 | bytes 41943040 | tf_op jit(solution)/shard_map/dot_general | solution.py:363
  934.5 21.5 %all-to-all-done.1 = bf16[512,4,512]{2,0,1:T(8,128)(2,1)} async-done(((bf16[512,4,512]{2,0,1:T(8,128)(2,1)}), bf16[512,4,512]{2,0,1:T(8,128)(2,1)}, u32[]{:S(2)}, u32[]{:S(2)}) %all-to-all-start.1) | async-done | bytes 2097184 | tf_op jit(solution)/shard_map/all_to_all | solution.py:382
  960.1 5.2 reshape.367
  971.6 5.3 multiply_reduce_fusion.1
  976.9 9.1 fusion.97
  990.1 10.7 convolution_convert_fusion.3
  1013.7 76.3 %shard_map.221 = (f32[4,2048,128]{2,1,0:T(8,128)}, f32[4,2048,128]{2,1,0:T(8,128)}, f32[4,2048,128]{2,1,0:T(8,128)}) custom-call(bf16[4,2048,128]{2,1,0:T(8,128)(2,1)} %bitcast.199, bf16[4,2048,128]{2,1,0:T(8,128)(2,1)} %bitcast.194, bf16[4,2048,128]{2,1,0:T(8,128)(2,1)} %bitcast.196, bf16[4,2048,128]{2,1,0:T(8,128)(2,1)} %get-tuple-element.167.do_ref, ...), custom_call_target="tpu_custom_call" | custom-call | flops 21474836480 | bytes 25165824 | tf_op jit(solution)/shard_map/pallas_call | solution.py:235
  1090.0 10.1 fusion.54
  1104.0 9.9 convolution_convert_fusion.6
  1116.6 6.2 fusion.53
  1126.8 9.9 convolution_convert_fusion.5
  1136.8 8.2 fusion.50
  1148.9 9.9 convolution_convert_fusion.4
  1158.9 26.9 %convolution_convert_fusion = bf16[2048,2048]{1,0:T(8,128)(2,1)} fusion(bf16[2048,2048]{1,0:T(8,128)(2,1)} %constant_dynamic-update-slice_fusion.14, bf16[2048,2048]{1,0:T(8,128)(2,1)} %fusion.55, bf16[2048,2048]{1,0:T(8,128)(2,1)} %fusion.61), kind=kOutput, calls=%fused_computation.23 | convolution fusion | flops 17217617920 | bytes 33554432 | tf_op jit(solution)/shard_map/dot_general | solution.py:366
  1193.8 23.8 %convolution_convert_fusion.1 = bf16[2048,2048]{1,0:T(8,128)(2,1)} fusion(bf16[2048,2048]{1,0:T(8,128)(2,1)} %constant_dynamic-update-slice_fusion, bf16[2048,2048]{1,0:T(8,128)(2,1)} %get-tuple-element.141), kind=kOutput, calls=%fused_computation.24 | convolution fusion | flops 17184063488 | bytes 25165824 | tf_op jit(solution)/shard_map/dot_general | solution.py:370
  1217.6 23.8 %convolution_convert_fusion.2 = bf16[2048,2048]{1,0:T(8,128)(2,1)} fusion(bf16[2048,2048]{1,0:T(8,128)(2,1)} %constant_dynamic-update-slice_fusion, bf16[2048,2048]{1,0:T(8,128)(2,1)} %get-tuple-element.142), kind=kOutput, calls=%fused_computation.25 | convolution fusion | flops 17184063488 | bytes 25165824 | tf_op jit(solution)/shard_map/dot_general | solution.py:369
  1249.5 10.6 fusion.136
  1260.1 8.1 fusion.137
  1268.1 23.5 %add_add_fusion = f32[2048,2048]{1,0:T(8,128)} fusion(f32[2048,2048]{1,0:T(8,128)} %fusion.136, f32[2048,2048]{1,0:T(8,128)} %fusion.137, bf16[2048,512]{0,1:T(8,128)(2,1)} %bitcast.188, bf16[2048,512]{1,0:T(8,128)(2,1)} %param.17), kind=kOutput, calls=%fused_computation.16 | convolution fusion | flops 4303355904 | bytes 54525952 | tf_op jit(solution)/shard_map/dot_general | solution.py:437
  1305.2 16.9 %collective-permute-done.30 = bf16[256,2048]{1,0:T(8,128)(2,1)S(1)} collective-permute-done((bf16[256,2048]{1,0:T(8,128)(2,1)S(1)}, bf16[256,2048]{1,0:T(8,128)(2,1)S(1)}, u32[]{:S(2)}, u32[]{:S(2)}) %collective-permute-start.30) | collective-permute-done | bytes 1048608 | tf_op jit(solution)/shard_map/ppermute | solution.py:105
  1322.1 22.4 %collective-permute-done.33 = bf16[256,2048]{1,0:T(8,128)(2,1)S(1)} collective-permute-done((bf16[256,2048]{1,0:T(8,128)(2,1)S(1)}, bf16[256,2048]{1,0:T(8,128)(2,1)S(1)}, u32[]{:S(2)}, u32[]{:S(2)}) %collective-permute-start.33) | collective-permute-done | bytes 1048608 | tf_op jit(solution)/shard_map/ppermute | solution.py:106
  1352.8 14.3 collective-permute-done.25
  1367.1 22.3 %collective-permute-done.28 = bf16[256,2048]{1,0:T(8,128)(2,1)S(1)} collective-permute-done((bf16[256,2048]{1,0:T(8,128)(2,1)S(1)}, bf16[256,2048]{1,0:T(8,128)(2,1)S(1)}, u32[]{:S(2)}, u32[]{:S(2)}) %collective-permute-start.28) | collective-permute-done | bytes 1048608 | tf_op jit(solution)/shard_map/ppermute | solution.py:106
  1397.7 14.4 collective-permute-done.31
  1413.1 21.3 %collective-permute-done.34 = bf16[256,2048]{1,0:T(8,128)(2,1)} collective-permute-done((bf16[256,2048]{1,0:T(8,128)(2,1)}, bf16[256,2048]{1,0:T(8,128)(2,1)}, u32[]{:S(2)}, u32[]{:S(2)}) %collective-permute-start.34) | collective-permute-done | bytes 1048608 | tf_op jit(solution)/shard_map/ppermute | solution.py:106
  1442.7 14.5 collective-permute-done.26
  1457.2 22.1 %collective-permute-done.29 = bf16[256,2048]{1,0:T(8,128)(2,1)} collective-permute-done((bf16[256,2048]{1,0:T(8,128)(2,1)}, bf16[256,2048]{1,0:T(8,128)(2,1)}, u32[]{:S(2)}, u32[]{:S(2)}) %collective-permute-start.29) | collective-permute-done | bytes 1048608 | tf_op jit(solution)/shard_map/ppermute | solution.py:106
  1479.3 5.7 dynamic-slice_add_fusion.3
  1485.0 5.4 fusion.33
  1495.9 13.5 collective-permute-done.32
  1509.4 28.5 %collective-permute-done.35 = bf16[256,2048]{1,0:T(8,128)(2,1)} collective-permute-done((bf16[256,2048]{1,0:T(8,128)(2,1)S(1)}, bf16[256,2048]{1,0:T(8,128)(2,1)}, u32[]{:S(2)}, u32[]{:S(2)}) %collective-permute-start.35) | collective-permute-done | bytes 1048608 | tf_op jit(solution)/shard_map/ppermute | solution.py:106
  1543.3 17.8 %all-reduce.1 = (f32[2048]{0:T(1024)S(1)}, f32[16]{0:T(128)S(1)}, f32[2048]{0:T(1024)S(1)}) all-reduce(f32[2048]{0:T(1024)S(1)} %get-tuple-element.127, f32[16]{0:T(128)S(1)} %multiply_dynamic-update-slice_fusion, f32[2048]{0:T(1024)S(1)} %copy-done.54), channel_id=1, replica_groups=mesh['dp'=8,'mp'=4] {'mp'}, use_global_device_ids=true, to_apply=%region_14.15 | all-reduce | flops 4112 | bytes 32896 | tf_op jit(solution)/shard_map/psum | solution.py:448
  1561.1 23.8 %all-reduce = (f32[2048]{0:T(1024)}, f32[16]{0:T(128)}, f32[2048]{0:T(1024)}) all-reduce(f32[2048]{0:T(1024)S(1)} %get-tuple-element.132, f32[16]{0:T(128)S(1)} %get-tuple-element.133, f32[2048]{0:T(1024)S(1)} %get-tuple-element.134), channel_id=1, replica_groups=mesh['dp'=8,'mp'=4] {'dp'}, use_global_device_ids=true, to_apply=%region_15.16 | all-reduce | flops 4112 | bytes 32896 | tf_op jit(solution)/shard_map/psum | solution.py:447
  1584.9 7.5 fusion.16
  (420 shorter events, 407.6 us)
Async XLA Ops:
  7.2 220.9 %copy-start = (bf16[2048,512]{1,0:T(8,128)(2,1)S(1)}, bf16[2048,512]{1,0:T(8,128)(2,1)}, u32[]{:S(2)}) copy-start(bf16[2048,512]{1,0:T(8,128)(2,1)} %param.15) | copy-start | bytes 6291460
  7.2 217.2 %all-gather.7.cloned.1.call-start = ((), (), s32[]{:S(2)}) async-start(), calls=%async_computation.10 | async-start | bytes 1310720 | tf_op jit(solution)/shard_map/all_gather | solution.py:297
  9.1 298.3 %all-gather.13.cloned.1.call-start = ((), (), s32[]{:S(2)}) async-start(), calls=%async_computation.21 | async-start | bytes 2396160 | tf_op jit(solution)/shard_map/all_gather | solution.py:26
  18.0 43.6 %collective-permute-start.1 = (bf16[256,2048]{1,0:T(8,128)(2,1)}, bf16[256,2048]{1,0:T(8,128)(2,1)S(1)}, u32[]{:S(2)}, u32[]{:S(2)}) collective-permute-start(bf16[256,2048]{1,0:T(8,128)(2,1)} %get-tuple-element.172), channel_id=1, source_target_pairs={{0,3},{1,0},{2,1},{3,2},{4,7},{5,4},{6,5},{7,6},{8,11},{9,8},{10,9... | collective-permute-start | bytes 3145736 | tf_op jit(solution)/shard_map/ppermute | solution.py:82
  23.1 63.5 %collective-permute-start = (bf16[256,2048]{1,0:T(8,128)(2,1)}, bf16[256,2048]{1,0:T(8,128)(2,1)}, u32[]{:S(2)}, u32[]{:S(2)}) collective-permute-start(bf16[256,2048]{1,0:T(8,128)(2,1)} %get-tuple-element.173), channel_id=1, source_target_pairs={{0,1},{1,2},{2,3},{3,0},{4,5},{5,6},{6,7},{7,4},{8,9},{9,10},{10,1... | collective-permute-start | bytes 3145736 | tf_op jit(solution)/shard_map/ppermute | solution.py:81
  24.8 200.3 %copy-start.53 = (s32[2048]{0:T(1024)}, s32[2048]{0:T(1024)S(1)}, u32[]{:S(2)}) copy-start(s32[2048]{0:T(1024)S(1)} %slice.70) | copy-start | bytes 24580
  32.6 174.9 %copy-start.59 = (f32[2048]{0:T(1024)}, f32[2048]{0:T(1024)S(1)}, u32[]{:S(2)}) copy-start(f32[2048]{0:T(1024)S(1)} %get-tuple-element.175) | copy-start | bytes 24580
  32.6 290.0 %copy-start.49 = (f32[2048]{0:T(1024)}, f32[2048]{0:T(1024)S(1)}, u32[]{:S(2)}) copy-start(f32[2048]{0:T(1024)S(1)} %get-tuple-element.174) | copy-start | bytes 24580
  61.7 170.1 %copy-start.28 = (bf16[256,2048]{1,0:T(8,128)(2,1)}, bf16[256,2048]{1,0:T(8,128)(2,1)S(1)}, u32[]{:S(2)}) copy-start(bf16[256,2048]{1,0:T(8,128)(2,1)S(1)} %collective-permute-done.1) | copy-start | bytes 3145732
  61.7 44.9 %collective-permute-start.3 = (bf16[256,2048]{1,0:T(8,128)(2,1)S(1)}, bf16[256,2048]{1,0:T(8,128)(2,1)}, u32[]{:S(2)}, u32[]{:S(2)}) collective-permute-start(bf16[256,2048]{1,0:T(8,128)(2,1)S(1)} %collective-permute-done.1), channel_id=1, source_target_pairs={{0,3},{1,0},{2,1},{3,2},{4,7},{5,4},{6,5},{7,6},{8,11},{9,8},{10,9... | collective-permute-start | bytes 3145736 | tf_op jit(solution)/shard_map/ppermute | solution.py:82
  86.6 47.4 %collective-permute-start.2 = (bf16[256,2048]{1,0:T(8,128)(2,1)}, bf16[256,2048]{1,0:T(8,128)(2,1)}, u32[]{:S(2)}, u32[]{:S(2)}) collective-permute-start(bf16[256,2048]{1,0:T(8,128)(2,1)} %collective-permute-done), channel_id=1, source_target_pairs={{0,1},{1,2},{2,3},{3,0},{4,5},{5,6},{6,7},{7,4},{8,9},{9,10},{10,1... | collective-permute-start | bytes 3145736 | tf_op jit(solution)/shard_map/ppermute | solution.py:81
  116.1 44.2 %collective-permute-start.5 = (bf16[256,2048]{1,0:T(8,128)(2,1)}, bf16[256,2048]{1,0:T(8,128)(2,1)}, u32[]{:S(2)}, u32[]{:S(2)}) collective-permute-start(bf16[256,2048]{1,0:T(8,128)(2,1)} %collective-permute-done.3), channel_id=1, source_target_pairs={{0,3},{1,0},{2,1},{3,2},{4,7},{5,4},{6,5},{7,6},{8,11},{9,8},{10,9... | collective-permute-start | bytes 3145736 | tf_op jit(solution)/shard_map/ppermute | solution.py:82
  139.2 36.9 %collective-permute-start.4 = (bf16[256,2048]{1,0:T(8,128)(2,1)}, bf16[256,2048]{1,0:T(8,128)(2,1)}, u32[]{:S(2)}, u32[]{:S(2)}) collective-permute-start(bf16[256,2048]{1,0:T(8,128)(2,1)} %collective-permute-done.2), channel_id=1, source_target_pairs={{0,1},{1,2},{2,3},{3,0},{4,5},{5,6},{6,7},{7,4},{8,9},{9,10},{10,1... | collective-permute-start | bytes 3145736 | tf_op jit(solution)/shard_map/ppermute | solution.py:81
  212.9 273.1 %all-gather.9.cloned.1.call-start = ((), (), s32[]{:S(2)}) async-start(), calls=%async_computation.11 | async-start | bytes 9437184 | tf_op jit(solution)/shard_map/all_gather | solution.py:296
  226.5 96.1 %copy-start.61 = (f32[4]{0:T(128)}, f32[4]{0:T(128)S(1)}, u32[]{:S(2)}) copy-start(f32[4]{0:T(128)S(1)} %get-tuple-element.140) | copy-start | bytes 52
  226.5 96.1 %copy-start.64 = (f32[4]{0:T(128)}, f32[4]{0:T(128)S(1)}, u32[]{:S(2)}) copy-start(f32[4]{0:T(128)S(1)} %get-tuple-element.139) | copy-start | bytes 52
  254.6 91.4 %collective-permute-start.13 = (bf16[256,2048]{1,0:T(8,128)(2,1)}, bf16[256,2048]{1,0:T(8,128)(2,1)S(1)}, u32[]{:S(2)}, u32[]{:S(2)}) collective-permute-start(bf16[256,2048]{1,0:T(8,128)(2,1)} %get-tuple-element.168), channel_id=1, source_target_pairs={{0,3},{1,0},{2,1},{3,2},{4,7},{5,4},{6,5},{7,6},{8,11},{9,8},{10,9... | collective-permute-start | bytes 3145736 | tf_op jit(solution)/shard_map/ppermute | solution.py:82
  255.3 88.7 %collective-permute-start.12 = (bf16[256,2048]{1,0:T(8,128)(2,1)}, bf16[256,2048]{1,0:T(8,128)(2,1)}, u32[]{:S(2)}, u32[]{:S(2)}) collective-permute-start(bf16[256,2048]{1,0:T(8,128)(2,1)} %get-tuple-element.169), channel_id=1, source_target_pairs={{0,1},{1,2},{2,3},{3,0},{4,5},{5,6},{6,7},{7,4},{8,9},{9,10},{10,1... | collective-permute-start | bytes 3145736 | tf_op jit(solution)/shard_map/ppermute | solution.py:81
  339.5 142.0 %all-to-all-start = ((bf16[4,512,512]{2,1,0:T(8,128)(2,1)}), bf16[4,512,512]{2,1,0:T(8,128)(2,1)}, u32[]{:S(2)}, u32[]{:S(2)}) async-start(bf16[4,512,512]{2,1,0:T(8,128)(2,1)} %convert_element_type.394), calls=%async_computation | async-start | bytes 4194304 | tf_op jit(solution)/shard_map/all_to_all | solution.py:346
  344.0 95.0 %copy-start.5 = (bf16[512,2048]{1,0:T(8,128)(2,1)S(1)}, bf16[512,2048]{1,0:T(8,128)(2,1)}, u32[]{:S(2)}) copy-start(bf16[512,2048]{1,0:T(8,128)(2,1)} %param.25) | copy-start | bytes 6291460
  344.0 61.8 %collective-permute-start.14 = (bf16[256,2048]{1,0:T(8,128)(2,1)}, bf16[256,2048]{1,0:T(8,128)(2,1)S(1)}, u32[]{:S(2)}, u32[]{:S(2)}) collective-permute-start(bf16[256,2048]{1,0:T(8,128)(2,1)} %collective-permute-done.12), channel_id=1, source_target_pairs={{0,1},{1,2},{2,3},{3,0},{4,5},{5,6},{6,7},{7,4},{8,9},{9,10},{10,1... | collective-permute-start | bytes 3145736 | tf_op jit(solution)/shard_map/ppermute | solution.py:81
  346.0 94.5 %collective-permute-start.15 = (bf16[256,2048]{1,0:T(8,128)(2,1)S(1)}, bf16[256,2048]{1,0:T(8,128)(2,1)S(1)}, u32[]{:S(2)}, u32[]{:S(2)}) collective-permute-start(bf16[256,2048]{1,0:T(8,128)(2,1)S(1)} %collective-permute-done.13), channel_id=1, source_target_pairs={{0,3},{1,0},{2,1},{3,2},{4,7},{5,4},{6,5},{7,6},{8,11},{9,8},{10,9... | collective-permute-start | bytes 3145736 | tf_op jit(solution)/shard_map/ppermute | solution.py:82
  405.8 52.3 %collective-permute-start.16 = (bf16[256,2048]{1,0:T(8,128)(2,1)S(1)}, bf16[256,2048]{1,0:T(8,128)(2,1)S(1)}, u32[]{:S(2)}, u32[]{:S(2)}) collective-permute-start(bf16[256,2048]{1,0:T(8,128)(2,1)S(1)} %collective-permute-done.14), channel_id=1, source_target_pairs={{0,1},{1,2},{2,3},{3,0},{4,5},{5,6},{6,7},{7,4},{8,9},{9,10},{10,1... | collective-permute-start | bytes 3145736 | tf_op jit(solution)/shard_map/ppermute | solution.py:81
  440.4 40.0 %collective-permute-start.17 = (bf16[256,2048]{1,0:T(8,128)(2,1)S(1)}, bf16[256,2048]{1,0:T(8,128)(2,1)S(1)}, u32[]{:S(2)}, u32[]{:S(2)}) collective-permute-start(bf16[256,2048]{1,0:T(8,128)(2,1)S(1)} %collective-permute-done.15), channel_id=1, source_target_pairs={{0,3},{1,0},{2,1},{3,2},{4,7},{5,4},{6,5},{7,6},{8,11},{9,8},{10,9... | collective-permute-start | bytes 3145736 | tf_op jit(solution)/shard_map/ppermute | solution.py:82
  498.7 45.1 %collective-permute-start.7 = (bf16[256,2048]{1,0:T(8,128)(2,1)S(1)}, bf16[256,2048]{1,0:T(8,128)(2,1)S(1)}, u32[]{:S(2)}, u32[]{:S(2)}) collective-permute-start(bf16[256,2048]{1,0:T(8,128)(2,1)S(1)} %get-tuple-element.170), channel_id=1, source_target_pairs={{0,3},{1,0},{2,1},{3,2},{4,7},{5,4},{6,5},{7,6},{8,11},{9,8},{10,9... | collective-permute-start | bytes 3145736 | tf_op jit(solution)/shard_map/ppermute | solution.py:82
  498.7 48.7 %collective-permute-start.6 = (bf16[256,2048]{1,0:T(8,128)(2,1)S(1)}, bf16[256,2048]{1,0:T(8,128)(2,1)S(1)}, u32[]{:S(2)}, u32[]{:S(2)}) collective-permute-start(bf16[256,2048]{1,0:T(8,128)(2,1)S(1)} %get-tuple-element.171), channel_id=1, source_target_pairs={{0,1},{1,2},{2,3},{3,0},{4,5},{5,6},{6,7},{7,4},{8,9},{9,10},{10,1... | collective-permute-start | bytes 3145736 | tf_op jit(solution)/shard_map/ppermute | solution.py:81
  543.8 47.7 %collective-permute-start.9 = (bf16[256,2048]{1,0:T(8,128)(2,1)S(1)}, bf16[256,2048]{1,0:T(8,128)(2,1)S(1)}, u32[]{:S(2)}, u32[]{:S(2)}) collective-permute-start(bf16[256,2048]{1,0:T(8,128)(2,1)S(1)} %collective-permute-done.7), channel_id=1, source_target_pairs={{0,3},{1,0},{2,1},{3,2},{4,7},{5,4},{6,5},{7,6},{8,11},{9,8},{10,9... | collective-permute-start | bytes 3145736 | tf_op jit(solution)/shard_map/ppermute | solution.py:82
  547.4 47.0 %collective-permute-start.8 = (bf16[256,2048]{1,0:T(8,128)(2,1)S(1)}, bf16[256,2048]{1,0:T(8,128)(2,1)S(1)}, u32[]{:S(2)}, u32[]{:S(2)}) collective-permute-start(bf16[256,2048]{1,0:T(8,128)(2,1)S(1)} %collective-permute-done.6), channel_id=1, source_target_pairs={{0,1},{1,2},{2,3},{3,0},{4,5},{5,6},{6,7},{7,4},{8,9},{9,10},{10,1... | collective-permute-start | bytes 3145736 | tf_op jit(solution)/shard_map/ppermute | solution.py:81
  591.5 50.9 %collective-permute-start.11 = (bf16[256,2048]{1,0:T(8,128)(2,1)S(1)}, bf16[256,2048]{1,0:T(8,128)(2,1)S(1)}, u32[]{:S(2)}, u32[]{:S(2)}) collective-permute-start(bf16[256,2048]{1,0:T(8,128)(2,1)S(1)} %collective-permute-done.9), channel_id=1, source_target_pairs={{0,3},{1,0},{2,1},{3,2},{4,7},{5,4},{6,5},{7,6},{8,11},{9,8},{10,9... | collective-permute-start | bytes 3145736 | tf_op jit(solution)/shard_map/ppermute | solution.py:82
  594.4 41.1 %collective-permute-start.10 = (bf16[256,2048]{1,0:T(8,128)(2,1)S(1)}, bf16[256,2048]{1,0:T(8,128)(2,1)S(1)}, u32[]{:S(2)}, u32[]{:S(2)}) collective-permute-start(bf16[256,2048]{1,0:T(8,128)(2,1)S(1)} %collective-permute-done.8), channel_id=1, source_target_pairs={{0,1},{1,2},{2,3},{3,0},{4,5},{5,6},{6,7},{7,4},{8,9},{9,10},{10,1... | collective-permute-start | bytes 3145736 | tf_op jit(solution)/shard_map/ppermute | solution.py:81
  734.7 27.9 %collective-permute-start.18 = (bf16[256,2048]{1,0:T(8,128)(2,1)S(1)}, bf16[256,2048]{1,0:T(8,128)(2,1)S(1)}, u32[]{:S(2)}, u32[]{:S(2)}) collective-permute-start(bf16[256,2048]{1,0:T(8,128)(2,1)S(1)} %get-tuple-element.165), channel_id=1, source_target_pairs={{0,1},{1,2},{2,3},{3,0},{4,5},{5,6},{6,7},{7,4},{8,9},{9,10},{10,1... | collective-permute-start | bytes 3145736 | tf_op jit(solution)/shard_map/ppermute | solution.py:105
  735.1 47.0 %collective-permute-start.21 = (bf16[256,2048]{1,0:T(8,128)(2,1)S(1)}, bf16[256,2048]{1,0:T(8,128)(2,1)S(1)}, u32[]{:S(2)}, u32[]{:S(2)}) collective-permute-start(bf16[256,2048]{1,0:T(8,128)(2,1)S(1)} %get-tuple-element.166), channel_id=1, source_target_pairs={{0,3},{1,0},{2,1},{3,2},{4,7},{5,4},{6,5},{7,6},{8,11},{9,8},{10,9... | collective-permute-start | bytes 3145736 | tf_op jit(solution)/shard_map/ppermute | solution.py:106
  785.0 27.9 %collective-permute-start.19 = (bf16[256,2048]{1,0:T(8,128)(2,1)S(1)}, bf16[256,2048]{1,0:T(8,128)(2,1)S(1)}, u32[]{:S(2)}, u32[]{:S(2)}) collective-permute-start(bf16[256,2048]{1,0:T(8,128)(2,1)S(1)} %get-tuple-element.163), channel_id=1, source_target_pairs={{0,1},{1,2},{2,3},{3,0},{4,5},{5,6},{6,7},{7,4},{8,9},{9,10},{10,1... | collective-permute-start | bytes 3145736 | tf_op jit(solution)/shard_map/ppermute | solution.py:105
  786.2 47.3 %collective-permute-start.22 = (bf16[256,2048]{1,0:T(8,128)(2,1)S(1)}, bf16[256,2048]{1,0:T(8,128)(2,1)S(1)}, u32[]{:S(2)}, u32[]{:S(2)}) collective-permute-start(bf16[256,2048]{1,0:T(8,128)(2,1)S(1)} %get-tuple-element.164), channel_id=1, source_target_pairs={{0,3},{1,0},{2,1},{3,2},{4,7},{5,4},{6,5},{7,6},{8,11},{9,8},{10,9... | collective-permute-start | bytes 3145736 | tf_op jit(solution)/shard_map/ppermute | solution.py:106
  837.4 28.2 %collective-permute-start.20 = (bf16[256,2048]{1,0:T(8,128)(2,1)}, bf16[256,2048]{1,0:T(8,128)(2,1)}, u32[]{:S(2)}, u32[]{:S(2)}) collective-permute-start(bf16[256,2048]{1,0:T(8,128)(2,1)} %get-tuple-element.161), channel_id=1, source_target_pairs={{0,1},{1,2},{2,3},{3,0},{4,5},{5,6},{6,7},{7,4},{8,9},{9,10},{10,1... | collective-permute-start | bytes 3145736 | tf_op jit(solution)/shard_map/ppermute | solution.py:105
  837.7 46.9 %collective-permute-start.23 = (bf16[256,2048]{1,0:T(8,128)(2,1)S(1)}, bf16[256,2048]{1,0:T(8,128)(2,1)}, u32[]{:S(2)}, u32[]{:S(2)}) collective-permute-start(bf16[256,2048]{1,0:T(8,128)(2,1)S(1)} %get-tuple-element.162), channel_id=1, source_target_pairs={{0,3},{1,0},{2,1},{3,2},{4,7},{5,4},{6,5},{7,6},{8,11},{9,8},{10,9... | collective-permute-start | bytes 3145736 | tf_op jit(solution)/shard_map/ppermute | solution.py:106
  841.3 46.8 %copy-start.52 = (f32[2048]{0:T(1024)S(1)}, f32[2048]{0:T(1024)}, u32[]{:S(2)}) copy-start(f32[2048]{0:T(1024)} %param.20) | copy-start | bytes 24580
  841.3 46.8 %copy-start.58 = (f32[512]{0:T(512)S(1)}, f32[512]{0:T(512)}, u32[]{:S(2)}) copy-start(f32[512]{0:T(512)} %copy-done.57) | copy-start | bytes 6148
  904.0 51.9 %all-to-all-start.1 = ((bf16[512,4,512]{2,0,1:T(8,128)(2,1)}), bf16[512,4,512]{2,0,1:T(8,128)(2,1)}, u32[]{:S(2)}, u32[]{:S(2)}) async-start(bf16[512,4,512]{2,0,1:T(8,128)(2,1)} %bitcast.192), calls=%async_computation.1 | async-start | bytes 4194304 | tf_op jit(solution)/shard_map/all_to_all | solution.py:382
  908.5 205.6 %all-gather.11.cloned.1.call-start = ((), (), s32[]{:S(2)}) async-start(), calls=%async_computation.12 | async-start | bytes 1198080 | tf_op jit(solution)/shard_map/all_gather | solution.py:26
  990.0 495.0 %reduce-scatter.15.cloned.1.call-start = ((), (), s32[]{:S(2)}) async-start(), calls=%async_computation.16 | async-start | bytes 9437184 | tf_op jit(solution)/shard_map/reduce_scatter | solution.py:452
  1000.7 489.7 %reduce-scatter.9.cloned.1.call-start = ((), (), s32[]{:S(2)}) async-start(), calls=%async_computation.13 | async-start | bytes 2359296 | tf_op jit(solution)/shard_map/reduce_scatter | solution.py:452
  1013.7 76.3 %copy-start.44 = (f32[512,128]{1,0:T(8,128)S(1)}, f32[512,128]{1,0:T(8,128)}, u32[]{:S(2)}) copy-start(f32[512,128]{1,0:T(8,128)} %copy-done.43) | copy-start | bytes 786436
  1013.7 76.3 %copy-start.68 = (f32[4,128]{1,0:T(4,128)S(1)}, f32[4,128]{1,0:T(4,128)}, u32[]{:S(2)}) copy-start(f32[4,128]{1,0:T(4,128)} %copy-done.67) | copy-start | bytes 6148
  1114.0 378.3 %reduce-scatter.11.cloned.1.call-start = ((), (), s32[]{:S(2)}) async-start(), calls=%async_computation.14 | async-start | bytes 2359296 | tf_op jit(solution)/shard_map/reduce_scatter | solution.py:452
  1136.7 357.3 %reduce-scatter.13.cloned.1.call-start = ((), (), s32[]{:S(2)}) async-start(), calls=%async_computation.15 | async-start | bytes 2359296 | tf_op jit(solution)/shard_map/reduce_scatter | solution.py:452
  1158.9 433.5 %reduce-scatter.23.cloned.1.call-start = ((), (), s32[]{:S(2)}) async-start(), calls=%async_computation.20 | async-start | bytes 9437184 | tf_op jit(solution)/shard_map/reduce_scatter | solution.py:452
  1185.8 409.3 %reduce-scatter.21.cloned.1.call-start = ((), (), s32[]{:S(2)}) async-start(), calls=%async_computation.19 | async-start | bytes 9437184 | tf_op jit(solution)/shard_map/reduce_scatter | solution.py:452
  1217.6 380.3 %reduce-scatter.19.cloned.1.call-start = ((), (), s32[]{:S(2)}) async-start(), calls=%async_computation.18 | async-start | bytes 9437184 | tf_op jit(solution)/shard_map/reduce_scatter | solution.py:452
  1241.5 359.2 %reduce-scatter.17.cloned.1.call-start = ((), (), s32[]{:S(2)}) async-start(), calls=%async_computation.17 | async-start | bytes 1310720 | tf_op jit(solution)/shard_map/reduce_scatter | solution.py:456
  1245.6 52.5 %collective-permute-start.24 = (bf16[256,2048]{1,0:T(8,128)(2,1)}, bf16[256,2048]{1,0:T(8,128)(2,1)S(1)}, u32[]{:S(2)}, u32[]{:S(2)}) collective-permute-start(bf16[256,2048]{1,0:T(8,128)(2,1)} %get-tuple-element.157), channel_id=1, source_target_pairs={{0,1},{1,2},{2,3},{3,0},{4,5},{5,6},{6,7},{7,4},{8,9},{9,10},{10,1... | collective-permute-start | bytes 3145736 | tf_op jit(solution)/shard_map/ppermute | solution.py:105
  1245.6 52.5 %collective-permute-start.27 = (bf16[256,2048]{1,0:T(8,128)(2,1)}, bf16[256,2048]{1,0:T(8,128)(2,1)}, u32[]{:S(2)}, u32[]{:S(2)}) collective-permute-start(bf16[256,2048]{1,0:T(8,128)(2,1)} %get-tuple-element.158), channel_id=1, source_target_pairs={{0,3},{1,0},{2,1},{3,2},{4,7},{5,4},{6,5},{7,6},{8,11},{9,8},{10,9... | collective-permute-start | bytes 3145736 | tf_op jit(solution)/shard_map/ppermute | solution.py:106
  1294.2 27.9 %collective-permute-start.30 = (bf16[256,2048]{1,0:T(8,128)(2,1)S(1)}, bf16[256,2048]{1,0:T(8,128)(2,1)S(1)}, u32[]{:S(2)}, u32[]{:S(2)}) collective-permute-start(bf16[256,2048]{1,0:T(8,128)(2,1)S(1)} %get-tuple-element.149), channel_id=1, source_target_pairs={{0,1},{1,2},{2,3},{3,0},{4,5},{5,6},{6,7},{7,4},{8,9},{9,10},{10,1... | collective-permute-start | bytes 3145736 | tf_op jit(solution)/shard_map/ppermute | solution.py:105
  1294.3 50.2 %collective-permute-start.33 = (bf16[256,2048]{1,0:T(8,128)(2,1)S(1)}, bf16[256,2048]{1,0:T(8,128)(2,1)S(1)}, u32[]{:S(2)}, u32[]{:S(2)}) collective-permute-start(bf16[256,2048]{1,0:T(8,128)(2,1)S(1)} %get-tuple-element.150), channel_id=1, source_target_pairs={{0,3},{1,0},{2,1},{3,2},{4,7},{5,4},{6,5},{7,6},{8,11},{9,8},{10,9... | collective-permute-start | bytes 3145736 | tf_op jit(solution)/shard_map/ppermute | solution.py:106
  1301.3 65.8 %collective-permute-start.25 = (bf16[256,2048]{1,0:T(8,128)(2,1)S(1)}, bf16[256,2048]{1,0:T(8,128)(2,1)S(1)}, u32[]{:S(2)}, u32[]{:S(2)}) collective-permute-start(bf16[256,2048]{1,0:T(8,128)(2,1)S(1)} %get-tuple-element.155), channel_id=1, source_target_pairs={{0,1},{1,2},{2,3},{3,0},{4,5},{5,6},{6,7},{7,4},{8,9},{9,10},{10,1... | collective-permute-start | bytes 3145736 | tf_op jit(solution)/shard_map/ppermute | solution.py:105
  1301.4 88.0 %collective-permute-start.28 = (bf16[256,2048]{1,0:T(8,128)(2,1)S(1)}, bf16[256,2048]{1,0:T(8,128)(2,1)S(1)}, u32[]{:S(2)}, u32[]{:S(2)}) collective-permute-start(bf16[256,2048]{1,0:T(8,128)(2,1)S(1)} %get-tuple-element.156), channel_id=1, source_target_pairs={{0,3},{1,0},{2,1},{3,2},{4,7},{5,4},{6,5},{7,6},{8,11},{9,8},{10,9... | collective-permute-start | bytes 3145736 | tf_op jit(solution)/shard_map/ppermute | solution.py:106
  1348.7 63.4 %collective-permute-start.31 = (bf16[256,2048]{1,0:T(8,128)(2,1)}, bf16[256,2048]{1,0:T(8,128)(2,1)S(1)}, u32[]{:S(2)}, u32[]{:S(2)}) collective-permute-start(bf16[256,2048]{1,0:T(8,128)(2,1)} %get-tuple-element.147), channel_id=1, source_target_pairs={{0,1},{1,2},{2,3},{3,0},{4,5},{5,6},{6,7},{7,4},{8,9},{9,10},{10,1... | collective-permute-start | bytes 3145736 | tf_op jit(solution)/shard_map/ppermute | solution.py:105
  1348.7 48.8 %copy-start.63 = (f32[4]{0:T(128)S(1)}, f32[4]{0:T(128)}, u32[]{:S(2)}) copy-start(f32[4]{0:T(128)} %copy-done.61) | copy-start | bytes 52
  1348.7 48.8 %copy-start.66 = (f32[4]{0:T(128)S(1)}, f32[4]{0:T(128)}, u32[]{:S(2)}) copy-start(f32[4]{0:T(128)} %get-tuple-element.115) | copy-start | bytes 52
  1348.8 85.6 %collective-permute-start.34 = (bf16[256,2048]{1,0:T(8,128)(2,1)}, bf16[256,2048]{1,0:T(8,128)(2,1)}, u32[]{:S(2)}, u32[]{:S(2)}) collective-permute-start(bf16[256,2048]{1,0:T(8,128)(2,1)} %get-tuple-element.148), channel_id=1, source_target_pairs={{0,3},{1,0},{2,1},{3,2},{4,7},{5,4},{6,5},{7,6},{8,11},{9,8},{10,9... | collective-permute-start | bytes 3145736 | tf_op jit(solution)/shard_map/ppermute | solution.py:106
  1393.7 63.5 %collective-permute-start.26 = (bf16[256,2048]{1,0:T(8,128)(2,1)}, bf16[256,2048]{1,0:T(8,128)(2,1)}, u32[]{:S(2)}, u32[]{:S(2)}) collective-permute-start(bf16[256,2048]{1,0:T(8,128)(2,1)} %get-tuple-element.153), channel_id=1, source_target_pairs={{0,1},{1,2},{2,3},{3,0},{4,5},{5,6},{6,7},{7,4},{8,9},{9,10},{10,1... | collective-permute-start | bytes 3145736 | tf_op jit(solution)/shard_map/ppermute | solution.py:105
  1393.7 85.5 %collective-permute-start.29 = (bf16[256,2048]{1,0:T(8,128)(2,1)}, bf16[256,2048]{1,0:T(8,128)(2,1)}, u32[]{:S(2)}, u32[]{:S(2)}) collective-permute-start(bf16[256,2048]{1,0:T(8,128)(2,1)} %get-tuple-element.154), channel_id=1, source_target_pairs={{0,3},{1,0},{2,1},{3,2},{4,7},{5,4},{6,5},{7,6},{8,11},{9,8},{10,9... | collective-permute-start | bytes 3145736 | tf_op jit(solution)/shard_map/ppermute | solution.py:106
  1438.9 70.5 %collective-permute-start.32 = (bf16[256,2048]{1,0:T(8,128)(2,1)}, bf16[256,2048]{1,0:T(8,128)(2,1)}, u32[]{:S(2)}, u32[]{:S(2)}) collective-permute-start(bf16[256,2048]{1,0:T(8,128)(2,1)} %get-tuple-element.145), channel_id=1, source_target_pairs={{0,1},{1,2},{2,3},{3,0},{4,5},{5,6},{6,7},{7,4},{8,9},{9,10},{10,1... | collective-permute-start | bytes 3145736 | tf_op jit(solution)/shard_map/ppermute | solution.py:105
  1438.9 99.0 %collective-permute-start.35 = (bf16[256,2048]{1,0:T(8,128)(2,1)S(1)}, bf16[256,2048]{1,0:T(8,128)(2,1)}, u32[]{:S(2)}, u32[]{:S(2)}) collective-permute-start(bf16[256,2048]{1,0:T(8,128)(2,1)S(1)} %get-tuple-element.146), channel_id=1, source_target_pairs={{0,3},{1,0},{2,1},{3,2},{4,7},{5,4},{6,5},{7,6},{8,11},{9,8},{10,9... | collective-permute-start | bytes 3145736 | tf_op jit(solution)/shard_map/ppermute | solution.py:106
  (64 other events, 621.5 us)
Sparse Core Ops, SparseCore 0:
  9.6 41.3 all-gather.6
  213.0 26.1 all-gather.12
  241.1 55.8 all-gather.8
  990.1 23.0 all-gather.10
  1016.5 71.2 reduce-scatter.14
  1114.1 40.5 reduce-scatter.8
  1158.0 41.1 reduce-scatter.10
  1202.4 41.1 reduce-scatter.12
  1247.1 71.2 reduce-scatter.22
  1321.7 71.4 reduce-scatter.20
  1396.7 71.4 reduce-scatter.18
  1485.1 43.0 reduce-scatter.16

commit v5 on v4

--- a/solution.py
+++ b/solution.py
@@ -69,7 +69,7 @@
     n, place = lax.axis_size(axis), lax.axis_index(axis)
     count = rows.shape[0]
     half = count // 2
-    own = compute(rows)
+    own = compute(rows, place * count)
     outs = [
         lax.dynamic_update_slice_in_dim(
             jnp.zeros((n * count,) + part.shape[1:], part.dtype), part, place * count, 0
@@ -81,8 +81,8 @@
         ahead = lax.ppermute(ahead, axis, ring_pairs(n, 1))
         behind = lax.ppermute(behind, axis, ring_pairs(n, -1))
         for got, start in (
-            (compute(ahead), ((place - step) % n) * count),
-            (compute(behind), ((place + step) % n) * count + half),
+            (compute(ahead, ((place - step) % n) * count), ((place - step) % n) * count),
+            (compute(behind, ((place + step) % n) * count + half), ((place + step) % n) * count + half),
         ):
             outs = [
                 lax.dynamic_update_slice_in_dim(out, part, start, 0)
@@ -300,7 +300,7 @@
     inverse1 = inverse_rms(x_rows)
     normed1 = (x_rows * inverse1 * norm1_gain).astype(jnp.bfloat16)
 
-    def project_qkv(rows):
+    def project_qkv(rows, first):
         return (rows,) + tuple(
             jnp.dot(rows, weight, preferred_element_type=jnp.float32).astype(jnp.bfloat16)
             for weight in (w_query, w_key, w_value)
@@ -348,31 +348,33 @@
     resid = x_rows + attn_sum
     inverse2 = inverse_rms(resid)
     normed2 = (resid * inverse2 * norm2_gain).astype(jnp.bfloat16)
-
-    def project_ffn(rows):
-        return (rows,) + tuple(
-            jnp.dot(rows, weight, preferred_element_type=jnp.float32).astype(jnp.bfloat16)
-            for weight in (w_gate, w_up)
+    (grad_rows_all,) = ring_gather(grad_rows, "mp", lambda rows, first: (rows,))
+
+    def ffn_rows(rows, first):
+        grad_rows = lax.dynamic_slice_in_dim(grad_rows_all, first, rows.shape[0], 0)
+        gate_f = jnp.dot(rows, w_gate, preferred_element_type=jnp.float32)
+        up_f = jnp.dot(rows, w_up, preferred_element_type=jnp.float32)
+        gate_f = gate_f.astype(jnp.bfloat16).astype(jnp.float32)
+        up_f = up_f.astype(jnp.bfloat16).astype(jnp.float32)
+        sig_gate = jax.nn.sigmoid(gate_f)
+        act = (gate_f * sig_gate * up_f).astype(jnp.bfloat16)
+        d_act = jnp.dot(grad_rows, w_down.T, preferred_element_type=jnp.float32)
+        d_gate = (d_act * up_f * sig_gate * (1.0 + gate_f * (1.0 - sig_gate))).astype(jnp.bfloat16)
+        d_up = (d_act * gate_f * sig_gate).astype(jnp.bfloat16)
+        mlp_rows = jnp.dot(act, w_down, preferred_element_type=jnp.float32)
+        norm_rows = jnp.dot(d_gate, w_gate.T, preferred_element_type=jnp.float32) + jnp.dot(
+            d_up, w_up.T, preferred_element_type=jnp.float32
         )
-
-    normed2_all, gate_pre, up_pre = ring_gather(normed2, "mp", project_ffn)
-    gate_f = gate_pre.astype(jnp.float32)
-    up_f = up_pre.astype(jnp.float32)
-    sig_gate = jax.nn.sigmoid(gate_f)
-    act = (gate_f * sig_gate * up_f).astype(jnp.bfloat16)
-    mlp_part = jnp.dot(act, w_down, preferred_element_type=jnp.float32)
-    (grad_rows_all,) = ring_gather(grad_rows, "mp", lambda rows: (rows,))
-    d_act = jnp.dot(grad_rows_all, w_down.T, preferred_element_type=jnp.float32)
-    grad_down = jnp.dot(act.T, grad_rows_all, preferred_element_type=jnp.float32)
-    d_gate = (d_act * up_f * sig_gate * (1.0 + gate_f * (1.0 - sig_gate))).astype(jnp.bfloat16)
-    d_up = (d_act * gate_f * sig_gate).astype(jnp.bfloat16)
+        return (rows, act, d_gate, d_up, mlp_rows, norm_rows)
+
+    normed2_all, act, d_gate, d_up, mlp_part, norm2_part = ring_gather(normed2, "mp", ffn_rows)
+    norm2_part, normed2_all, act, d_gate, d_up = lax.optimization_barrier(
+        (norm2_part, normed2_all, act, d_gate, d_up)
+    )
     grad_gate = jnp.dot(normed2_all.T, d_gate, preferred_element_type=jnp.float32)
     grad_up = jnp.dot(normed2_all.T, d_up, preferred_element_type=jnp.float32)
-    d_norm2 = ring_scatter(
-        jnp.dot(d_gate, w_gate.T, preferred_element_type=jnp.float32)
-        + jnp.dot(d_up, w_up.T, preferred_element_type=jnp.float32),
-        "mp",
-    )
+    grad_down = jnp.dot(act.T, grad_rows_all, preferred_element_type=jnp.float32)
+    d_norm2 = ring_scatter(norm2_part, "mp")
     gain2_part = jnp.sum(d_norm2 * resid * inverse2, axis=0)
     d_resid = out_grad.astype(jnp.float32) + norm_backward(resid, inverse2, norm2_gain, d_norm2)
     d_resid_low = d_resid.astype(jnp.bfloat16)

time: 1620 us -> 1670 us (1.031)
  matrix products: 458 us -> 578 us
  waiting for transfers between devices: 581 us -> 498 us
    dot_general x18 -> x42, matrix products: 168 us -> 286 us  [the longest x7 59.4 us: ffn_rows(): gate_f = jnp.dot(rows, w_gate, preferred_element_type=jnp.float32)]
    ppermute x9, waiting for transfers between devices: 135 us -> 99.7 us  [ring_gather(): ahead = lax.ppermute(ahead, axis, ring_pairs(n, 1))]
    ppermute x9, waiting for transfers between devices: 103 us -> 68 us  [ring_gather(): behind = lax.ppermute(behind, axis, ring_pairs(n, -1))]
    ppermute x9, waiting for transfers between devices: 146 us -> 123 us  [ring_scatter(): ahead = lax.ppermute(ahead.astype(kind), axis, ring_pairs(n, 1))]
    all_to_all x1, waiting for transfers between devices: 0.01 us -> 20.7 us  [local(): mixed = lax.all_to_all(mixed_cols, 'mp', 0, 1, tiled=True)]
    another operation x9 -> x12, local copies, waits for them, and re-layouts: 20.1 us -> 37.2 us
  transfers between devices with their start and end apart: 50 -> 50, of which waited for: 30 -> 29; matrix products, arithmetic and copies ran while one was open for 34% -> 41% of each run, Pallas kernels for 8% -> 8%
where the time goes in v5:
time: 1670 us; the launch traced here: 1650 us
  matrix products  578 us (35%)
  waiting for transfers between devices  498 us (30%)
  local copies, waits for them, and re-layouts  186 us (11%)
  Pallas kernels  127 us (8%)
  starting transfers between devices  108 us (6%)
  other arithmetic  98.2 us (6%)
  blocking collectives  40.7 us (2%)
  between operations  18.1 us (1%)
    ppermute x9, waiting for transfers between devices, ring_scatter(): behind = lax.ppermute(behind.astype(kind), axis, ring_pairs(n, -1))  163 us
    ppermute x9, waiting for transfers between devices, ring_scatter(): ahead = lax.ppermute(ahead.astype(kind), axis, ring_pairs(n, 1))  123 us
    ppermute x9, waiting for transfers between devices, ring_gather(): ahead = lax.ppermute(ahead, axis, ring_pairs(n, 1))  99.7 us
    pallas_call x1, Pallas kernels, attention_bwd(): pl.pallas_call(functools.partial(_bwd_kernel, scale, seg), grid=(H, nq),...  76.4 us
    ppermute x9, waiting for transfers between devices, ring_gather(): behind = lax.ppermute(behind, axis, ring_pairs(n, -1))  68 us
    dot_general x7, matrix products, ffn_rows(): gate_f = jnp.dot(rows, w_gate, preferred_element_type=jnp.float32)  59.4 us
    dot_general x21, matrix products, project_qkv(): jnp.dot(rows, weight, preferred_element_type=jnp.float32)  57 us
    dot_general x7, matrix products, ffn_rows(): jnp.dot(d_up, w_up.T, preferred_element_type=jnp.float32)  54.1 us
  transfers between devices with their start and end apart: 50, of which 29 were waited for; matrix products, arithmetic and copies ran while one was open for 41% of the time, Pallas kernels for 8%

profile of v5, /device:TPU:0, one launch (start us, length us, event | category | flops | bytes accessed | tf_op | source)
XLA Modules:
  0.0 1654.5 jit_solution(6891195474378933295)
XLA Ops:
  40.6 15.7 collective-permute-done
  56.4 26.0 %collective-permute-start.2 = (bf16[256,2048]{1,0:T(8,128)(2,1)S(1)}, bf16[256,2048]{1,0:T(8,128)(2,1)}, u32[]{:S(2)}, u32[]{:S(2)}) collective-permute-start(bf16[256,2048]{1,0:T(8,128)(2,1)S(1)} %collective-permute-done), channel_id=1, source_target_pairs={{0,1},{1,2},{2,3},{3,0},{4,5},{5,6},{6,7},{7,4},{8,9},{9,10},{10,1... | collective-permute-start | bytes 3145736 | tf_op jit(solution)/shard_map/ppermute | solution.py:81
  113.9 15.2 collective-permute-done.3
  156.5 8.3 collective-permute-done.4
  169.2 14.8 collective-permute-done.5
  251.4 24.0 %collective-permute-done.12 = bf16[256,2048]{1,0:T(8,128)(2,1)S(1)} collective-permute-done((bf16[256,2048]{1,0:T(8,128)(2,1)S(1)}, bf16[256,2048]{1,0:T(8,128)(2,1)S(1)}, u32[]{:S(2)}, u32[]{:S(2)}) %collective-permute-start.12) | collective-permute-done | bytes 1048608 | tf_op jit(solution)/shard_map/ppermute | solution.py:81
  277.5 18.5 %collective-permute-done.13 = bf16[256,2048]{1,0:T(8,128)(2,1)} collective-permute-done((bf16[256,2048]{1,0:T(8,128)(2,1)}, bf16[256,2048]{1,0:T(8,128)(2,1)}, u32[]{:S(2)}, u32[]{:S(2)}) %collective-permute-start.13) | collective-permute-done | bytes 1048608 | tf_op jit(solution)/shard_map/ppermute | solution.py:82
  298.8 50.7 %shard_map.220 = (f32[4,2048,128]{2,1,0:T(8,128)}, f32[4,2048,1]{2,1,0:T(8,128)}) custom-call(bf16[4,2048,128]{2,1,0:T(8,128)(2,1)} %bitcast.228, bf16[4,2048,128]{2,1,0:T(8,128)(2,1)} %bitcast.226, bf16[4,2048,128]{2,1,0:T(8,128)(2,1)} %bitcast.224, s32[2048,1]{1,0:T(8,128)} %copy.243.docq_ref, s32[1,2048]{1,0:T(1,128)} %bitcast.250), custom_call_target="tpu_custom_call" | custom-call | flops 8589934592 | bytes 10485760 | tf_op jit(solution)/shard_map/pallas_call | solution.py:210
  359.4 18.3 %collective-permute-done.16 = bf16[256,2048]{1,0:T(8,128)(2,1)S(1)} collective-permute-done((bf16[256,2048]{1,0:T(8,128)(2,1)}, bf16[256,2048]{1,0:T(8,128)(2,1)S(1)}, u32[]{:S(2)}, u32[]{:S(2)}) %collective-permute-start.16) | collective-permute-done | bytes 1048608 | tf_op jit(solution)/shard_map/ppermute | solution.py:81
  377.8 19.5 %collective-permute-done.17 = bf16[256,2048]{1,0:T(8,128)(2,1)S(1)} collective-permute-done((bf16[256,2048]{1,0:T(8,128)(2,1)}, bf16[256,2048]{1,0:T(8,128)(2,1)S(1)}, u32[]{:S(2)}, u32[]{:S(2)}) %collective-permute-start.17) | collective-permute-done | bytes 1048608 | tf_op jit(solution)/shard_map/ppermute | solution.py:82
  397.5 10.2 fusion.166
  432.4 10.7 copy.244
  459.5 7.6 fusion.158
  472.0 8.0 fusion.122
  480.0 20.7 %all-to-all-done = bf16[4,512,512]{2,1,0:T(8,128)(2,1)} async-done(((bf16[4,512,512]{2,1,0:T(8,128)(2,1)}), bf16[4,512,512]{2,1,0:T(8,128)(2,1)}, u32[]{:S(2)}, u32[]{:S(2)}) %all-to-all-start) | async-done | bytes 2097184 | tf_op jit(solution)/shard_map/all_to_all | solution.py:346
  504.7 9.8 multiply_reduce_fusion.4
  522.4 8.6 convolution_convert_fusion.8
  536.3 10.4 constant_dynamic-update-slice_fusion.20
  546.8 7.7 fusion.226
  554.5 7.9 broadcast.233.clone.1
  562.3 10.1 add_dynamic-update-slice_fusion
  606.0 9.1 constant_dynamic-update-slice_fusion.18
  644.6 12.9 collective-permute-done.8
  663.2 9.5 constant_dynamic-update-slice_fusion.17
  722.3 14.3 collective-permute-done.10
  742.4 9.2 constant_dynamic-update-slice_fusion.15
  779.4 7.7 fusion.54
  806.1 24.1 %collective-permute-done.18 = bf16[256,2048]{1,0:T(8,128)(2,1)S(1)} collective-permute-done((bf16[256,2048]{1,0:T(8,128)(2,1)}, bf16[256,2048]{1,0:T(8,128)(2,1)S(1)}, u32[]{:S(2)}, u32[]{:S(2)}) %collective-permute-start.18) | collective-permute-done | bytes 1048608 | tf_op jit(solution)/shard_map/ppermute | solution.py:105
  830.3 11.1 collective-permute-done.21
  848.8 7.9 broadcast.233.clone
  863.4 9.2 collective-permute-done.19
  872.6 18.2 %collective-permute-done.22 = bf16[256,2048]{1,0:T(8,128)(2,1)S(1)} collective-permute-done((bf16[256,2048]{1,0:T(8,128)(2,1)S(1)}, bf16[256,2048]{1,0:T(8,128)(2,1)S(1)}, u32[]{:S(2)}, u32[]{:S(2)}) %collective-permute-start.22) | collective-permute-done | bytes 1048608 | tf_op jit(solution)/shard_map/ppermute | solution.py:106
  905.5 16.1 collective-permute-done.20
  921.7 18.3 %collective-permute-done.23 = bf16[256,2048]{1,0:T(8,128)(2,1)S(1)} collective-permute-done((bf16[256,2048]{1,0:T(8,128)(2,1)S(1)}, bf16[256,2048]{1,0:T(8,128)(2,1)S(1)}, u32[]{:S(2)}, u32[]{:S(2)}) %collective-permute-start.23) | collective-permute-done | bytes 1048608 | tf_op jit(solution)/shard_map/ppermute | solution.py:106
  947.3 9.8 convolution_convert_fusion.7
  963.3 7.8 convolution_dynamic-update-slice_fusion.4
  986.6 23.5 %all-to-all-done.1 = bf16[512,4,512]{2,0,1:T(8,128)(2,1)} async-done(((bf16[512,4,512]{2,0,1:T(8,128)(2,1)}), bf16[512,4,512]{2,0,1:T(8,128)(2,1)}, u32[]{:S(2)}, u32[]{:S(2)}) %all-to-all-start.1) | async-done | bytes 2097184 | tf_op jit(solution)/shard_map/all_to_all | solution.py:384
  1022.7 9.2 fusion.151
  1041.1 10.6 convolution_convert_fusion.3
  1065.8 76.4 %shard_map.221 = (f32[4,2048,128]{2,1,0:T(8,128)}, f32[4,2048,128]{2,1,0:T(8,128)}, f32[4,2048,128]{2,1,0:T(8,128)}) custom-call(bf16[4,2048,128]{2,1,0:T(8,128)(2,1)} %bitcast.230, bf16[4,2048,128]{2,1,0:T(8,128)(2,1)} %bitcast.227, bf16[4,2048,128]{2,1,0:T(8,128)(2,1)} %bitcast.225, bf16[4,2048,128]{2,1,0:T(8,128)(2,1)} %get-tuple-element.189.do_ref, ...), custom_call_target="tpu_custom_call" | custom-call | flops 21474836480 | bytes 25165824 | tf_op jit(solution)/shard_map/pallas_call | solution.py:235
  1142.2 10.1 fusion.52
  1156.2 9.9 convolution_convert_fusion.6
  1169.4 7.9 fusion.48
  1181.3 9.9 convolution_convert_fusion.4
  1192.1 8.1 fusion.51
  1204.4 10.0 convolution_convert_fusion.5
  1214.5 24.2 %convolution_convert_fusion = bf16[2048,2048]{1,0:T(8,128)(2,1)} fusion(bf16[2048,2048]{1,0:T(8,128)(2,1)} %get-tuple-element.132, bf16[2048,2048]{1,0:T(8,128)(2,1)} %copy-done.20), kind=kOutput, calls=%fused_computation.6 | convolution fusion | flops 17184063488 | bytes 25165824 | tf_op jit(solution)/shard_map/dot_general | solution.py:376
  1238.8 24.0 %convolution_convert_fusion.1 = bf16[2048,2048]{1,0:T(8,128)(2,1)} fusion(bf16[2048,2048]{1,0:T(8,128)(2,1)} %constant_dynamic-update-slice_fusion.28, bf16[2048,2048]{1,0:T(8,128)(2,1)} %get-tuple-element.131), kind=kOutput, calls=%fused_computation.7 | convolution fusion | flops 17184063488 | bytes 25165824 | tf_op jit(solution)/shard_map/dot_general | solution.py:375
  1262.9 24.3 %convolution_convert_fusion.2 = bf16[2048,2048]{1,0:T(8,128)(2,1)} fusion(bf16[2048,2048]{1,0:T(8,128)(2,1)} %constant_dynamic-update-slice_fusion.28, bf16[2048,2048]{1,0:T(8,128)(2,1)} %get-tuple-element.130), kind=kOutput, calls=%fused_computation.8 | convolution fusion | flops 17184063488 | bytes 25165824 | tf_op jit(solution)/shard_map/dot_general | solution.py:374
  1295.0 8.6 fusion.233
  1303.6 10.9 fusion.234
  1314.5 23.7 %add_add_fusion = f32[2048,2048]{1,0:T(8,128)} fusion(f32[2048,2048]{1,0:T(8,128)} %fusion.233, f32[2048,2048]{1,0:T(8,128)} %fusion.234, bf16[2048,512]{0,1:T(8,128)(2,1)} %bitcast.219, bf16[2048,512]{1,0:T(8,128)(2,1)} %param.17), kind=kOutput, calls=%fused_computation | convolution fusion | flops 4303355904 | bytes 54525952 | tf_op jit(solution)/shard_map/dot_general | solution.py:439
  1352.0 16.8 %collective-permute-done.30 = bf16[256,2048]{1,0:T(8,128)(2,1)S(1)} collective-permute-done((bf16[256,2048]{1,0:T(8,128)(2,1)S(1)}, bf16[256,2048]{1,0:T(8,128)(2,1)S(1)}, u32[]{:S(2)}, u32[]{:S(2)}) %collective-permute-start.30) | collective-permute-done | bytes 1048608 | tf_op jit(solution)/shard_map/ppermute | solution.py:105
  1368.8 22.5 %collective-permute-done.33 = bf16[256,2048]{1,0:T(8,128)(2,1)S(1)} collective-permute-done((bf16[256,2048]{1,0:T(8,128)(2,1)S(1)}, bf16[256,2048]{1,0:T(8,128)(2,1)S(1)}, u32[]{:S(2)}, u32[]{:S(2)}) %collective-permute-start.33) | collective-permute-done | bytes 1048608 | tf_op jit(solution)/shard_map/ppermute | solution.py:106
  1399.7 14.1 collective-permute-done.25
  1413.8 22.5 %collective-permute-done.28 = bf16[256,2048]{1,0:T(8,128)(2,1)S(1)} collective-permute-done((bf16[256,2048]{1,0:T(8,128)(2,1)S(1)}, bf16[256,2048]{1,0:T(8,128)(2,1)S(1)}, u32[]{:S(2)}, u32[]{:S(2)}) %collective-permute-start.28) | collective-permute-done | bytes 1048608 | tf_op jit(solution)/shard_map/ppermute | solution.py:106
  1444.6 14.2 collective-permute-done.31
  1459.8 21.5 %collective-permute-done.34 = bf16[256,2048]{1,0:T(8,128)(2,1)} collective-permute-done((bf16[256,2048]{1,0:T(8,128)(2,1)}, bf16[256,2048]{1,0:T(8,128)(2,1)}, u32[]{:S(2)}, u32[]{:S(2)}) %collective-permute-start.34) | collective-permute-done | bytes 1048608 | tf_op jit(solution)/shard_map/ppermute | solution.py:106
  1489.7 14.2 collective-permute-done.26
  1503.9 22.3 %collective-permute-done.29 = bf16[256,2048]{1,0:T(8,128)(2,1)} collective-permute-done((bf16[256,2048]{1,0:T(8,128)(2,1)}, bf16[256,2048]{1,0:T(8,128)(2,1)}, u32[]{:S(2)}, u32[]{:S(2)}) %collective-permute-start.29) | collective-permute-done | bytes 1048608 | tf_op jit(solution)/shard_map/ppermute | solution.py:106
  1542.8 14.6 collective-permute-done.32
  1557.3 26.5 %collective-permute-done.35 = bf16[256,2048]{1,0:T(8,128)(2,1)} collective-permute-done((bf16[256,2048]{1,0:T(8,128)(2,1)S(1)}, bf16[256,2048]{1,0:T(8,128)(2,1)}, u32[]{:S(2)}, u32[]{:S(2)}) %collective-permute-start.35) | collective-permute-done | bytes 1048608 | tf_op jit(solution)/shard_map/ppermute | solution.py:106
  1589.2 17.7 %all-reduce.1 = (f32[2048]{0:T(1024)S(1)}, f32[16]{0:T(128)S(1)}, f32[2048]{0:T(1024)S(1)}) all-reduce(f32[2048]{0:T(1024)S(1)} %get-tuple-element.137, f32[16]{0:T(128)S(1)} %multiply_dynamic-update-slice_fusion, f32[2048]{0:T(1024)S(1)} %copy-done.52), channel_id=1, replica_groups=mesh['dp'=8,'mp'=4] {'mp'}, use_global_device_ids=true, to_apply=%region_14.15 | all-reduce | flops 4112 | bytes 32896 | tf_op jit(solution)/shard_map/psum | solution.py:450
  1607.0 22.9 %all-reduce = (f32[2048]{0:T(1024)}, f32[16]{0:T(128)}, f32[2048]{0:T(1024)}) all-reduce(f32[2048]{0:T(1024)S(1)} %get-tuple-element.142, f32[16]{0:T(128)S(1)} %get-tuple-element.143, f32[2048]{0:T(1024)S(1)} %get-tuple-element.144), channel_id=1, replica_groups=mesh['dp'=8,'mp'=4] {'dp'}, use_global_device_ids=true, to_apply=%region_15.16 | all-reduce | flops 4112 | bytes 32896 | tf_op jit(solution)/shard_map/psum | solution.py:449
  (530 shorter events, 607.0 us)
Async XLA Ops:
  7.2 214.5 %copy-start = (bf16[2048,512]{1,0:T(8,128)(2,1)S(1)}, bf16[2048,512]{1,0:T(8,128)(2,1)}, u32[]{:S(2)}) copy-start(bf16[2048,512]{1,0:T(8,128)(2,1)} %param.15) | copy-start | bytes 6291460
  7.2 222.5 %all-gather.7.cloned.1.call-start = ((), (), s32[]{:S(2)}) async-start(), calls=%async_computation.10 | async-start | bytes 1310720 | tf_op jit(solution)/shard_map/all_gather | solution.py:297
  16.3 40.0 %collective-permute-start = (bf16[256,2048]{1,0:T(8,128)(2,1)}, bf16[256,2048]{1,0:T(8,128)(2,1)S(1)}, u32[]{:S(2)}, u32[]{:S(2)}) collective-permute-start(bf16[256,2048]{1,0:T(8,128)(2,1)} %get-tuple-element.207), channel_id=1, source_target_pairs={{0,1},{1,2},{2,3},{3,0},{4,5},{5,6},{6,7},{7,4},{8,9},{9,10},{10,1... | collective-permute-start | bytes 3145736 | tf_op jit(solution)/shard_map/ppermute | solution.py:81
  19.4 65.2 %collective-permute-start.1 = (bf16[256,2048]{1,0:T(8,128)(2,1)}, bf16[256,2048]{1,0:T(8,128)(2,1)}, u32[]{:S(2)}, u32[]{:S(2)}) collective-permute-start(bf16[256,2048]{1,0:T(8,128)(2,1)} %get-tuple-element.206), channel_id=1, source_target_pairs={{0,3},{1,0},{2,1},{3,2},{4,7},{5,4},{6,5},{7,6},{8,11},{9,8},{10,9... | collective-permute-start | bytes 3145736 | tf_op jit(solution)/shard_map/ppermute | solution.py:82
  23.1 392.0 %all-gather.13.cloned.1.call-start = ((), (), s32[]{:S(2)}) async-start(), calls=%async_computation.21 | async-start | bytes 2396160 | tf_op jit(solution)/shard_map/all_gather | solution.py:26
  24.8 251.3 %copy-start.51 = (s32[2048]{0:T(1024)}, s32[2048]{0:T(1024)S(1)}, u32[]{:S(2)}) copy-start(s32[2048]{0:T(1024)S(1)} %slice.70) | copy-start | bytes 24580
  32.6 181.8 %copy-start.57 = (f32[2048]{0:T(1024)}, f32[2048]{0:T(1024)S(1)}, u32[]{:S(2)}) copy-start(f32[2048]{0:T(1024)S(1)} %get-tuple-element.209) | copy-start | bytes 24580
  32.6 397.9 %copy-start.47 = (f32[2048]{0:T(1024)}, f32[2048]{0:T(1024)S(1)}, u32[]{:S(2)}) copy-start(f32[2048]{0:T(1024)S(1)} %get-tuple-element.208) | copy-start | bytes 24580
  36.2 46.2 %copy-start.68 = (bf16[2048,512]{1,0:T(8,128)(2,1)S(1)}, bf16[2048,512]{1,0:T(8,128)(2,1)}, u32[]{:S(2)}) copy-start(bf16[2048,512]{1,0:T(8,128)(2,1)} %param.16) | copy-start | bytes 6291460
  36.2 47.7 %copy-start.24 = (bf16[2048,512]{1,0:T(8,128)(2,1)S(1)}, bf16[2048,512]{1,0:T(8,128)(2,1)}, u32[]{:S(2)}) copy-start(bf16[2048,512]{1,0:T(8,128)(2,1)} %param.17) | copy-start | bytes 6291460
  56.4 169.0 %copy-start.36 = (bf16[256,2048]{1,0:T(8,128)(2,1)}, bf16[256,2048]{1,0:T(8,128)(2,1)S(1)}, u32[]{:S(2)}) copy-start(bf16[256,2048]{1,0:T(8,128)(2,1)S(1)} %collective-permute-done) | copy-start | bytes 3145732
  56.4 53.2 %collective-permute-start.2 = (bf16[256,2048]{1,0:T(8,128)(2,1)S(1)}, bf16[256,2048]{1,0:T(8,128)(2,1)}, u32[]{:S(2)}, u32[]{:S(2)}) collective-permute-start(bf16[256,2048]{1,0:T(8,128)(2,1)S(1)} %collective-permute-done), channel_id=1, source_target_pairs={{0,1},{1,2},{2,3},{3,0},{4,5},{5,6},{6,7},{7,4},{8,9},{9,10},{10,1... | collective-permute-start | bytes 3145736 | tf_op jit(solution)/shard_map/ppermute | solution.py:81
  84.6 44.6 %collective-permute-start.3 = (bf16[256,2048]{1,0:T(8,128)(2,1)}, bf16[256,2048]{1,0:T(8,128)(2,1)}, u32[]{:S(2)}, u32[]{:S(2)}) collective-permute-start(bf16[256,2048]{1,0:T(8,128)(2,1)} %collective-permute-done.1), channel_id=1, source_target_pairs={{0,3},{1,0},{2,1},{3,2},{4,7},{5,4},{6,5},{7,6},{8,11},{9,8},{10,9... | collective-permute-start | bytes 3145736 | tf_op jit(solution)/shard_map/ppermute | solution.py:82
  134.3 30.5 %collective-permute-start.4 = (bf16[256,2048]{1,0:T(8,128)(2,1)}, bf16[256,2048]{1,0:T(8,128)(2,1)}, u32[]{:S(2)}, u32[]{:S(2)}) collective-permute-start(bf16[256,2048]{1,0:T(8,128)(2,1)} %collective-permute-done.2), channel_id=1, source_target_pairs={{0,1},{1,2},{2,3},{3,0},{4,5},{5,6},{6,7},{7,4},{8,9},{9,10},{10,1... | collective-permute-start | bytes 3145736 | tf_op jit(solution)/shard_map/ppermute | solution.py:81
  140.0 44.0 %collective-permute-start.5 = (bf16[256,2048]{1,0:T(8,128)(2,1)}, bf16[256,2048]{1,0:T(8,128)(2,1)}, u32[]{:S(2)}, u32[]{:S(2)}) collective-permute-start(bf16[256,2048]{1,0:T(8,128)(2,1)} %collective-permute-done.3), channel_id=1, source_target_pairs={{0,3},{1,0},{2,1},{3,2},{4,7},{5,4},{6,5},{7,6},{8,11},{9,8},{10,9... | collective-permute-start | bytes 3145736 | tf_op jit(solution)/shard_map/ppermute | solution.py:82
  219.8 285.0 %all-gather.9.cloned.1.call-start = ((), (), s32[]{:S(2)}) async-start(), calls=%async_computation.11 | async-start | bytes 9437184 | tf_op jit(solution)/shard_map/all_gather | solution.py:296
  247.6 27.8 %collective-permute-start.12 = (bf16[256,2048]{1,0:T(8,128)(2,1)S(1)}, bf16[256,2048]{1,0:T(8,128)(2,1)S(1)}, u32[]{:S(2)}, u32[]{:S(2)}) collective-permute-start(bf16[256,2048]{1,0:T(8,128)(2,1)S(1)} %get-tuple-element.203), channel_id=1, source_target_pairs={{0,1},{1,2},{2,3},{3,0},{4,5},{5,6},{6,7},{7,4},{8,9},{9,10},{10,1... | collective-permute-start | bytes 3145736 | tf_op jit(solution)/shard_map/ppermute | solution.py:81
  248.4 47.7 %collective-permute-start.13 = (bf16[256,2048]{1,0:T(8,128)(2,1)}, bf16[256,2048]{1,0:T(8,128)(2,1)}, u32[]{:S(2)}, u32[]{:S(2)}) collective-permute-start(bf16[256,2048]{1,0:T(8,128)(2,1)} %get-tuple-element.202), channel_id=1, source_target_pairs={{0,3},{1,0},{2,1},{3,2},{4,7},{5,4},{6,5},{7,6},{8,11},{9,8},{10,9... | collective-permute-start | bytes 3145736 | tf_op jit(solution)/shard_map/ppermute | solution.py:82
  275.5 74.1 %collective-permute-start.14 = (bf16[256,2048]{1,0:T(8,128)(2,1)S(1)}, bf16[256,2048]{1,0:T(8,128)(2,1)}, u32[]{:S(2)}, u32[]{:S(2)}) collective-permute-start(bf16[256,2048]{1,0:T(8,128)(2,1)S(1)} %collective-permute-done.12), channel_id=1, source_target_pairs={{0,1},{1,2},{2,3},{3,0},{4,5},{5,6},{6,7},{7,4},{8,9},{9,10},{10,1... | collective-permute-start | bytes 3145736 | tf_op jit(solution)/shard_map/ppermute | solution.py:81
  277.5 153.0 %copy-start.59 = (f32[4]{0:T(128)}, f32[4]{0:T(128)S(1)}, u32[]{:S(2)}) copy-start(f32[4]{0:T(128)S(1)} %get-tuple-element.164) | copy-start | bytes 52
  277.5 153.0 %copy-start.62 = (f32[4]{0:T(128)}, f32[4]{0:T(128)S(1)}, u32[]{:S(2)}) copy-start(f32[4]{0:T(128)S(1)} %get-tuple-element.163) | copy-start | bytes 52
  296.0 55.4 %collective-permute-start.15 = (bf16[256,2048]{1,0:T(8,128)(2,1)}, bf16[256,2048]{1,0:T(8,128)(2,1)}, u32[]{:S(2)}, u32[]{:S(2)}) collective-permute-start(bf16[256,2048]{1,0:T(8,128)(2,1)} %collective-permute-done.13), channel_id=1, source_target_pairs={{0,3},{1,0},{2,1},{3,2},{4,7},{5,4},{6,5},{7,6},{8,11},{9,8},{10,9... | collective-permute-start | bytes 3145736 | tf_op jit(solution)/shard_map/ppermute | solution.py:82
  349.6 28.1 %collective-permute-start.16 = (bf16[256,2048]{1,0:T(8,128)(2,1)}, bf16[256,2048]{1,0:T(8,128)(2,1)S(1)}, u32[]{:S(2)}, u32[]{:S(2)}) collective-permute-start(bf16[256,2048]{1,0:T(8,128)(2,1)} %collective-permute-done.14), channel_id=1, source_target_pairs={{0,1},{1,2},{2,3},{3,0},{4,5},{5,6},{6,7},{7,4},{8,9},{9,10},{10,1... | collective-permute-start | bytes 3145736 | tf_op jit(solution)/shard_map/ppermute | solution.py:81
  351.5 45.9 %collective-permute-start.17 = (bf16[256,2048]{1,0:T(8,128)(2,1)}, bf16[256,2048]{1,0:T(8,128)(2,1)S(1)}, u32[]{:S(2)}, u32[]{:S(2)}) collective-permute-start(bf16[256,2048]{1,0:T(8,128)(2,1)} %collective-permute-done.15), channel_id=1, source_target_pairs={{0,3},{1,0},{2,1},{3,2},{4,7},{5,4},{6,5},{7,6},{8,11},{9,8},{10,9... | collective-permute-start | bytes 3145736 | tf_op jit(solution)/shard_map/ppermute | solution.py:82
  447.2 53.4 %all-to-all-start = ((bf16[4,512,512]{2,1,0:T(8,128)(2,1)}), bf16[4,512,512]{2,1,0:T(8,128)(2,1)}, u32[]{:S(2)}, u32[]{:S(2)}) async-start(bf16[4,512,512]{2,1,0:T(8,128)(2,1)} %convert_element_type.484), calls=%async_computation | async-start | bytes 4194304 | tf_op jit(solution)/shard_map/all_to_all | solution.py:346
  518.6 67.8 %collective-permute-start.6 = (bf16[256,2048]{1,0:T(8,128)(2,1)}, bf16[256,2048]{1,0:T(8,128)(2,1)}, u32[]{:S(2)}, u32[]{:S(2)}) collective-permute-start(bf16[256,2048]{1,0:T(8,128)(2,1)} %get-tuple-element.205), channel_id=1, source_target_pairs={{0,1},{1,2},{2,3},{3,0},{4,5},{5,6},{6,7},{7,4},{8,9},{9,10},{10,1... | collective-permute-start | bytes 3145736 | tf_op jit(solution)/shard_map/ppermute | solution.py:81
  518.6 84.8 %collective-permute-start.7 = (bf16[256,2048]{1,0:T(8,128)(2,1)}, bf16[256,2048]{1,0:T(8,128)(2,1)S(1)}, u32[]{:S(2)}, u32[]{:S(2)}) collective-permute-start(bf16[256,2048]{1,0:T(8,128)(2,1)} %get-tuple-element.204), channel_id=1, source_target_pairs={{0,3},{1,0},{2,1},{3,2},{4,7},{5,4},{6,5},{7,6},{8,11},{9,8},{10,9... | collective-permute-start | bytes 3145736 | tf_op jit(solution)/shard_map/ppermute | solution.py:82
  629.4 28.1 %collective-permute-start.8 = (bf16[256,2048]{1,0:T(8,128)(2,1)}, bf16[256,2048]{1,0:T(8,128)(2,1)S(1)}, u32[]{:S(2)}, u32[]{:S(2)}) collective-permute-start(bf16[256,2048]{1,0:T(8,128)(2,1)} %collective-permute-done.6), channel_id=1, source_target_pairs={{0,1},{1,2},{2,3},{3,0},{4,5},{5,6},{6,7},{7,4},{8,9},{9,10},{10,1... | collective-permute-start | bytes 3145736 | tf_op jit(solution)/shard_map/ppermute | solution.py:81
  629.4 50.9 %collective-permute-start.9 = (bf16[256,2048]{1,0:T(8,128)(2,1)S(1)}, bf16[256,2048]{1,0:T(8,128)(2,1)S(1)}, u32[]{:S(2)}, u32[]{:S(2)}) collective-permute-start(bf16[256,2048]{1,0:T(8,128)(2,1)S(1)} %collective-permute-done.7), channel_id=1, source_target_pairs={{0,3},{1,0},{2,1},{3,2},{4,7},{5,4},{6,5},{7,6},{8,11},{9,8},{10,9... | collective-permute-start | bytes 3145736 | tf_op jit(solution)/shard_map/ppermute | solution.py:82
  708.8 27.9 %collective-permute-start.10 = (bf16[256,2048]{1,0:T(8,128)(2,1)S(1)}, bf16[256,2048]{1,0:T(8,128)(2,1)S(1)}, u32[]{:S(2)}, u32[]{:S(2)}) collective-permute-start(bf16[256,2048]{1,0:T(8,128)(2,1)S(1)} %collective-permute-done.8), channel_id=1, source_target_pairs={{0,1},{1,2},{2,3},{3,0},{4,5},{5,6},{6,7},{7,4},{8,9},{9,10},{10,1... | collective-permute-start | bytes 3145736 | tf_op jit(solution)/shard_map/ppermute | solution.py:81
  708.8 50.0 %collective-permute-start.11 = (bf16[256,2048]{1,0:T(8,128)(2,1)S(1)}, bf16[256,2048]{1,0:T(8,128)(2,1)}, u32[]{:S(2)}, u32[]{:S(2)}) collective-permute-start(bf16[256,2048]{1,0:T(8,128)(2,1)S(1)} %collective-permute-done.9), channel_id=1, source_target_pairs={{0,3},{1,0},{2,1},{3,2},{4,7},{5,4},{6,5},{7,6},{8,11},{9,8},{10,9... | collective-permute-start | bytes 3145736 | tf_op jit(solution)/shard_map/ppermute | solution.py:82
  802.2 28.0 %collective-permute-start.18 = (bf16[256,2048]{1,0:T(8,128)(2,1)}, bf16[256,2048]{1,0:T(8,128)(2,1)S(1)}, u32[]{:S(2)}, u32[]{:S(2)}) collective-permute-start(bf16[256,2048]{1,0:T(8,128)(2,1)} %get-tuple-element.187), channel_id=1, source_target_pairs={{0,1},{1,2},{2,3},{3,0},{4,5},{5,6},{6,7},{7,4},{8,9},{9,10},{10,1... | collective-permute-start | bytes 3145736 | tf_op jit(solution)/shard_map/ppermute | solution.py:105
  802.2 39.2 %collective-permute-start.21 = (bf16[256,2048]{1,0:T(8,128)(2,1)}, bf16[256,2048]{1,0:T(8,128)(2,1)}, u32[]{:S(2)}, u32[]{:S(2)}) collective-permute-start(bf16[256,2048]{1,0:T(8,128)(2,1)} %get-tuple-element.188), channel_id=1, source_target_pairs={{0,3},{1,0},{2,1},{3,2},{4,7},{5,4},{6,5},{7,6},{8,11},{9,8},{10,9... | collective-permute-start | bytes 3145736 | tf_op jit(solution)/shard_map/ppermute | solution.py:106
  844.7 27.9 %collective-permute-start.19 = (bf16[256,2048]{1,0:T(8,128)(2,1)S(1)}, bf16[256,2048]{1,0:T(8,128)(2,1)S(1)}, u32[]{:S(2)}, u32[]{:S(2)}) collective-permute-start(bf16[256,2048]{1,0:T(8,128)(2,1)S(1)} %get-tuple-element.185), channel_id=1, source_target_pairs={{0,1},{1,2},{2,3},{3,0},{4,5},{5,6},{6,7},{7,4},{8,9},{9,10},{10,1... | collective-permute-start | bytes 3145736 | tf_op jit(solution)/shard_map/ppermute | solution.py:105
  844.8 46.0 %collective-permute-start.22 = (bf16[256,2048]{1,0:T(8,128)(2,1)S(1)}, bf16[256,2048]{1,0:T(8,128)(2,1)S(1)}, u32[]{:S(2)}, u32[]{:S(2)}) collective-permute-start(bf16[256,2048]{1,0:T(8,128)(2,1)S(1)} %get-tuple-element.186), channel_id=1, source_target_pairs={{0,3},{1,0},{2,1},{3,2},{4,7},{5,4},{6,5},{7,6},{8,11},{9,8},{10,9... | collective-permute-start | bytes 3145736 | tf_op jit(solution)/shard_map/ppermute | solution.py:106
  893.8 27.9 %collective-permute-start.20 = (bf16[256,2048]{1,0:T(8,128)(2,1)S(1)}, bf16[256,2048]{1,0:T(8,128)(2,1)S(1)}, u32[]{:S(2)}, u32[]{:S(2)}) collective-permute-start(bf16[256,2048]{1,0:T(8,128)(2,1)S(1)} %get-tuple-element.183), channel_id=1, source_target_pairs={{0,1},{1,2},{2,3},{3,0},{4,5},{5,6},{6,7},{7,4},{8,9},{9,10},{10,1... | collective-permute-start | bytes 3145736 | tf_op jit(solution)/shard_map/ppermute | solution.py:105
  893.9 46.1 %collective-permute-start.23 = (bf16[256,2048]{1,0:T(8,128)(2,1)S(1)}, bf16[256,2048]{1,0:T(8,128)(2,1)S(1)}, u32[]{:S(2)}, u32[]{:S(2)}) collective-permute-start(bf16[256,2048]{1,0:T(8,128)(2,1)S(1)} %get-tuple-element.184), channel_id=1, source_target_pairs={{0,3},{1,0},{2,1},{3,2},{4,7},{5,4},{6,5},{7,6},{8,11},{9,8},{10,9... | collective-permute-start | bytes 3145736 | tf_op jit(solution)/shard_map/ppermute | solution.py:106
  958.6 51.4 %all-to-all-start.1 = ((bf16[512,4,512]{2,0,1:T(8,128)(2,1)}), bf16[512,4,512]{2,0,1:T(8,128)(2,1)}, u32[]{:S(2)}, u32[]{:S(2)}) async-start(bf16[512,4,512]{2,0,1:T(8,128)(2,1)} %bitcast.223), calls=%async_computation.1 | async-start | bytes 4194304 | tf_op jit(solution)/shard_map/all_to_all | solution.py:384
  963.0 203.2 %all-gather.11.cloned.1.call-start = ((), (), s32[]{:S(2)}) async-start(), calls=%async_computation.12 | async-start | bytes 1198080 | tf_op jit(solution)/shard_map/all_gather | solution.py:26
  1041.0 490.9 %reduce-scatter.15.cloned.1.call-start = ((), (), s32[]{:S(2)}) async-start(), calls=%async_computation.16 | async-start | bytes 9437184 | tf_op jit(solution)/shard_map/reduce_scatter | solution.py:454
  1051.7 485.6 %reduce-scatter.9.cloned.1.call-start = ((), (), s32[]{:S(2)}) async-start(), calls=%async_computation.13 | async-start | bytes 2359296 | tf_op jit(solution)/shard_map/reduce_scatter | solution.py:454
  1065.8 76.4 %copy-start.42 = (f32[512,128]{1,0:T(8,128)S(1)}, f32[512,128]{1,0:T(8,128)}, u32[]{:S(2)}) copy-start(f32[512,128]{1,0:T(8,128)} %copy-done.41) | copy-start | bytes 786436
  1065.8 76.5 %copy-start.66 = (f32[4,128]{1,0:T(4,128)S(1)}, f32[4,128]{1,0:T(4,128)}, u32[]{:S(2)}) copy-start(f32[4,128]{1,0:T(4,128)} %copy-done.65) | copy-start | bytes 6148
  1166.2 373.0 %reduce-scatter.13.cloned.1.call-start = ((), (), s32[]{:S(2)}) async-start(), calls=%async_computation.15 | async-start | bytes 2359296 | tf_op jit(solution)/shard_map/reduce_scatter | solution.py:454
  1191.3 349.7 %reduce-scatter.11.cloned.1.call-start = ((), (), s32[]{:S(2)}) async-start(), calls=%async_computation.14 | async-start | bytes 2359296 | tf_op jit(solution)/shard_map/reduce_scatter | solution.py:454
  1214.4 423.0 %reduce-scatter.23.cloned.1.call-start = ((), (), s32[]{:S(2)}) async-start(), calls=%async_computation.20 | async-start | bytes 9437184 | tf_op jit(solution)/shard_map/reduce_scatter | solution.py:454
  1238.7 401.4 %reduce-scatter.21.cloned.1.call-start = ((), (), s32[]{:S(2)}) async-start(), calls=%async_computation.19 | async-start | bytes 9437184 | tf_op jit(solution)/shard_map/reduce_scatter | solution.py:454
  1262.8 380.1 %reduce-scatter.19.cloned.1.call-start = ((), (), s32[]{:S(2)}) async-start(), calls=%async_computation.18 | async-start | bytes 9437184 | tf_op jit(solution)/shard_map/reduce_scatter | solution.py:454
  1287.1 358.6 %reduce-scatter.17.cloned.1.call-start = ((), (), s32[]{:S(2)}) async-start(), calls=%async_computation.17 | async-start | bytes 1310720 | tf_op jit(solution)/shard_map/reduce_scatter | solution.py:458
  1291.2 53.6 %collective-permute-start.24 = (bf16[256,2048]{1,0:T(8,128)(2,1)}, bf16[256,2048]{1,0:T(8,128)(2,1)S(1)}, u32[]{:S(2)}, u32[]{:S(2)}) collective-permute-start(bf16[256,2048]{1,0:T(8,128)(2,1)} %get-tuple-element.179), channel_id=1, source_target_pairs={{0,1},{1,2},{2,3},{3,0},{4,5},{5,6},{6,7},{7,4},{8,9},{9,10},{10,1... | collective-permute-start | bytes 3145736 | tf_op jit(solution)/shard_map/ppermute | solution.py:105
  1291.2 53.6 %collective-permute-start.27 = (bf16[256,2048]{1,0:T(8,128)(2,1)}, bf16[256,2048]{1,0:T(8,128)(2,1)}, u32[]{:S(2)}, u32[]{:S(2)}) collective-permute-start(bf16[256,2048]{1,0:T(8,128)(2,1)} %get-tuple-element.180), channel_id=1, source_target_pairs={{0,3},{1,0},{2,1},{3,2},{4,7},{5,4},{6,5},{7,6},{8,11},{9,8},{10,9... | collective-permute-start | bytes 3145736 | tf_op jit(solution)/shard_map/ppermute | solution.py:106
  1340.9 27.9 %collective-permute-start.30 = (bf16[256,2048]{1,0:T(8,128)(2,1)S(1)}, bf16[256,2048]{1,0:T(8,128)(2,1)S(1)}, u32[]{:S(2)}, u32[]{:S(2)}) collective-permute-start(bf16[256,2048]{1,0:T(8,128)(2,1)S(1)} %get-tuple-element.171), channel_id=1, source_target_pairs={{0,1},{1,2},{2,3},{3,0},{4,5},{5,6},{6,7},{7,4},{8,9},{9,10},{10,1... | collective-permute-start | bytes 3145736 | tf_op jit(solution)/shard_map/ppermute | solution.py:105
  1341.0 50.4 %collective-permute-start.33 = (bf16[256,2048]{1,0:T(8,128)(2,1)S(1)}, bf16[256,2048]{1,0:T(8,128)(2,1)S(1)}, u32[]{:S(2)}, u32[]{:S(2)}) collective-permute-start(bf16[256,2048]{1,0:T(8,128)(2,1)S(1)} %get-tuple-element.172), channel_id=1, source_target_pairs={{0,3},{1,0},{2,1},{3,2},{4,7},{5,4},{6,5},{7,6},{8,11},{9,8},{10,9... | collective-permute-start | bytes 3145736 | tf_op jit(solution)/shard_map/ppermute | solution.py:106
  1348.1 65.7 %collective-permute-start.25 = (bf16[256,2048]{1,0:T(8,128)(2,1)S(1)}, bf16[256,2048]{1,0:T(8,128)(2,1)S(1)}, u32[]{:S(2)}, u32[]{:S(2)}) collective-permute-start(bf16[256,2048]{1,0:T(8,128)(2,1)S(1)} %get-tuple-element.177), channel_id=1, source_target_pairs={{0,1},{1,2},{2,3},{3,0},{4,5},{5,6},{6,7},{7,4},{8,9},{9,10},{10,1... | collective-permute-start | bytes 3145736 | tf_op jit(solution)/shard_map/ppermute | solution.py:105
  1348.2 88.1 %collective-permute-start.28 = (bf16[256,2048]{1,0:T(8,128)(2,1)S(1)}, bf16[256,2048]{1,0:T(8,128)(2,1)S(1)}, u32[]{:S(2)}, u32[]{:S(2)}) collective-permute-start(bf16[256,2048]{1,0:T(8,128)(2,1)S(1)} %get-tuple-element.178), channel_id=1, source_target_pairs={{0,3},{1,0},{2,1},{3,2},{4,7},{5,4},{6,5},{7,6},{8,11},{9,8},{10,9... | collective-permute-start | bytes 3145736 | tf_op jit(solution)/shard_map/ppermute | solution.py:106
  1395.7 63.1 %collective-permute-start.31 = (bf16[256,2048]{1,0:T(8,128)(2,1)}, bf16[256,2048]{1,0:T(8,128)(2,1)S(1)}, u32[]{:S(2)}, u32[]{:S(2)}) collective-permute-start(bf16[256,2048]{1,0:T(8,128)(2,1)} %get-tuple-element.169), channel_id=1, source_target_pairs={{0,1},{1,2},{2,3},{3,0},{4,5},{5,6},{6,7},{7,4},{8,9},{9,10},{10,1... | collective-permute-start | bytes 3145736 | tf_op jit(solution)/shard_map/ppermute | solution.py:105
  1395.7 48.8 %copy-start.61 = (f32[4]{0:T(128)S(1)}, f32[4]{0:T(128)}, u32[]{:S(2)}) copy-start(f32[4]{0:T(128)} %copy-done.59) | copy-start | bytes 52
  1395.7 48.8 %copy-start.64 = (f32[4]{0:T(128)S(1)}, f32[4]{0:T(128)}, u32[]{:S(2)}) copy-start(f32[4]{0:T(128)} %get-tuple-element.133) | copy-start | bytes 52
  1395.7 85.6 %collective-permute-start.34 = (bf16[256,2048]{1,0:T(8,128)(2,1)}, bf16[256,2048]{1,0:T(8,128)(2,1)}, u32[]{:S(2)}, u32[]{:S(2)}) collective-permute-start(bf16[256,2048]{1,0:T(8,128)(2,1)} %get-tuple-element.170), channel_id=1, source_target_pairs={{0,3},{1,0},{2,1},{3,2},{4,7},{5,4},{6,5},{7,6},{8,11},{9,8},{10,9... | collective-permute-start | bytes 3145736 | tf_op jit(solution)/shard_map/ppermute | solution.py:106
  1440.6 63.2 %collective-permute-start.26 = (bf16[256,2048]{1,0:T(8,128)(2,1)}, bf16[256,2048]{1,0:T(8,128)(2,1)}, u32[]{:S(2)}, u32[]{:S(2)}) collective-permute-start(bf16[256,2048]{1,0:T(8,128)(2,1)} %get-tuple-element.175), channel_id=1, source_target_pairs={{0,1},{1,2},{2,3},{3,0},{4,5},{5,6},{6,7},{7,4},{8,9},{9,10},{10,1... | collective-permute-start | bytes 3145736 | tf_op jit(solution)/shard_map/ppermute | solution.py:105
  1440.6 85.5 %collective-permute-start.29 = (bf16[256,2048]{1,0:T(8,128)(2,1)}, bf16[256,2048]{1,0:T(8,128)(2,1)}, u32[]{:S(2)}, u32[]{:S(2)}) collective-permute-start(bf16[256,2048]{1,0:T(8,128)(2,1)} %get-tuple-element.176), channel_id=1, source_target_pairs={{0,3},{1,0},{2,1},{3,2},{4,7},{5,4},{6,5},{7,6},{8,11},{9,8},{10,9... | collective-permute-start | bytes 3145736 | tf_op jit(solution)/shard_map/ppermute | solution.py:106
  1485.8 71.5 %collective-permute-start.32 = (bf16[256,2048]{1,0:T(8,128)(2,1)}, bf16[256,2048]{1,0:T(8,128)(2,1)}, u32[]{:S(2)}, u32[]{:S(2)}) collective-permute-start(bf16[256,2048]{1,0:T(8,128)(2,1)} %get-tuple-element.167), channel_id=1, source_target_pairs={{0,1},{1,2},{2,3},{3,0},{4,5},{5,6},{6,7},{7,4},{8,9},{9,10},{10,1... | collective-permute-start | bytes 3145736 | tf_op jit(solution)/shard_map/ppermute | solution.py:105
  1485.8 98.0 %collective-permute-start.35 = (bf16[256,2048]{1,0:T(8,128)(2,1)S(1)}, bf16[256,2048]{1,0:T(8,128)(2,1)}, u32[]{:S(2)}, u32[]{:S(2)}) collective-permute-start(bf16[256,2048]{1,0:T(8,128)(2,1)S(1)} %get-tuple-element.168), channel_id=1, source_target_pairs={{0,3},{1,0},{2,1},{3,2},{4,7},{5,4},{6,5},{7,6},{8,11},{9,8},{10,9... | collective-permute-start | bytes 3145736 | tf_op jit(solution)/shard_map/ppermute | solution.py:106
  1542.8 44.5 %copy-start.54 = (f32[512]{0:T(512)S(1)}, f32[512]{0:T(512)}, u32[]{:S(2)}) copy-start(f32[512]{0:T(512)} %copy-done.53) | copy-start | bytes 6148
  (101 other events, 1047.3 us)
Sparse Core Ops, SparseCore 0:
  23.2 47.2 all-gather.6
  219.9 26.1 all-gather.12
  248.0 55.8 all-gather.8
  1041.1 22.8 all-gather.10
  1067.3 71.2 reduce-scatter.14
  1166.3 40.6 reduce-scatter.8
  1210.2 41.0 reduce-scatter.12
  1255.2 41.0 reduce-scatter.10
  1299.8 71.2 reduce-scatter.22
  1374.4 71.5 reduce-scatter.20
  1449.5 71.5 reduce-scatter.18
  1532.0 41.6 reduce-scatter.16

commit v6 on v4

--- a/solution.py
+++ b/solution.py
@@ -284,6 +284,11 @@
     write_mask = jnp.where(seg_docs == seg_last[:, None], 1.0, 0.0).astype(jnp.float32)
     width = w_out.shape[1]
 
+    def over_dp(grad, dim):
+        return lax.psum_scatter(
+            grad.astype(jnp.bfloat16), "dp", scatter_dimension=dim, tiled=True
+        ).astype(jnp.float32)
+
     def to_heads(rows):
         return rows.reshape(group_rows, heads_here, head_size).transpose(1, 0, 2)
 
@@ -363,25 +368,35 @@
     mlp_part = jnp.dot(act, w_down, preferred_element_type=jnp.float32)
     (grad_rows_all,) = ring_gather(grad_rows, "mp", lambda rows: (rows,))
     d_act = jnp.dot(grad_rows_all, w_down.T, preferred_element_type=jnp.float32)
-    grad_down = jnp.dot(act.T, grad_rows_all, preferred_element_type=jnp.float32)
     d_gate = (d_act * up_f * sig_gate * (1.0 + gate_f * (1.0 - sig_gate))).astype(jnp.bfloat16)
     d_up = (d_act * gate_f * sig_gate).astype(jnp.bfloat16)
+    norm2_part = jnp.dot(d_gate, w_gate.T, preferred_element_type=jnp.float32) + jnp.dot(
+        d_up, w_up.T, preferred_element_type=jnp.float32
+    )
+    norm2_part, normed2_all, act, d_gate, d_up = lax.optimization_barrier(
+        (norm2_part, normed2_all, act, d_gate, d_up)
+    )
     grad_gate = jnp.dot(normed2_all.T, d_gate, preferred_element_type=jnp.float32)
     grad_up = jnp.dot(normed2_all.T, d_up, preferred_element_type=jnp.float32)
-    d_norm2 = ring_scatter(
-        jnp.dot(d_gate, w_gate.T, preferred_element_type=jnp.float32)
-        + jnp.dot(d_up, w_up.T, preferred_element_type=jnp.float32),
-        "mp",
-    )
+    grad_down = jnp.dot(act.T, grad_rows_all, preferred_element_type=jnp.float32)
+    d_norm2 = ring_scatter(norm2_part, "mp")
+    gate_w_sum = over_dp(grad_gate, 0)
+    up_sum = over_dp(grad_up, 0)
+    down_sum = over_dp(grad_down, 1)
     gain2_part = jnp.sum(d_norm2 * resid * inverse2, axis=0)
     d_resid = out_grad.astype(jnp.float32) + norm_backward(resid, inverse2, norm2_gain, d_norm2)
     d_resid_low = d_resid.astype(jnp.bfloat16)
     grad_out = jnp.dot(mixed.T, d_resid_low, preferred_element_type=jnp.float32)
+    out_sum = lax.psum_scatter(
+        over_dp(grad_out, 1).astype(jnp.bfloat16), "mp", scatter_dimension=0, tiled=True
+    ).astype(jnp.float32)
     d_mixed_rows = jnp.dot(d_resid_low, w_out_full.T, preferred_element_type=jnp.float32)
     d_mixed = to_heads(
         lax.all_to_all(d_mixed_rows.astype(jnp.bfloat16), "mp", 1, 0, tiled=True)
     ).astype(jnp.float32)
-    mlp_part, d_mixed = lax.optimization_barrier((mlp_part, d_mixed))
+    mlp_part, d_mixed, gate_w_sum, up_sum = lax.optimization_barrier(
+        (mlp_part, d_mixed, gate_w_sum, up_sum)
+    )
     output = (resid + ring_scatter(mlp_part, "mp")).astype(jnp.bfloat16)
     gate_part = jnp.sum(d_mixed * (mem_out - dot_out), axis=(1, 2)) * gate_vec * (1.0 - gate_vec)
     d_dot = ((1.0 - gate) * d_mixed).astype(jnp.bfloat16)
@@ -389,6 +404,7 @@
     dq_dot, dk_dot, dv_dot = attention_bwd(
         query_h, key_h, value_h, d_dot, log_sums, doc_index, score_scale
     )
+    dq_dot, down_sum, out_sum = lax.optimization_barrier((dq_dot, down_sum, out_sum))
     d_numer = read_mask[None, :, :, None] * d_mem / denom[..., None]
     d_denom = -jnp.sum(d_numer * numer, axis=-1) / denom * jnp.where(denom_raw > 1.0, 1.0, 0.0)
     d_sig_q = (
@@ -448,22 +464,8 @@
         lax.psum((gain1_part, gain2_part, gate_full), "mp"), "dp"
     )
 
-    def over_dp(grad, dim):
-        return lax.psum_scatter(
-            grad.astype(jnp.bfloat16), "dp", scatter_dimension=dim, tiled=True
-        ).astype(jnp.float32)
-
-    out_sum = lax.psum_scatter(
-        over_dp(grad_out, 1).astype(jnp.bfloat16), "mp", scatter_dimension=0, tiled=True
-    ).astype(jnp.float32)
-    query_sum, key_sum, value_sum, gate_w_sum, up_sum, down_sum = (
-        over_dp(grad_query, 0),
-        over_dp(grad_key, 0),
-        over_dp(grad_value, 0),
-        over_dp(grad_gate, 0),
-        over_dp(grad_up, 0),
-        over_dp(grad_down, 1),
-    )
+    qkv_sum = over_dp(jnp.concatenate([grad_query, grad_key, grad_value], axis=1), 0)
+    query_sum, key_sum, value_sum = jnp.split(qkv_sum, 3, axis=1)
     return (
         output,
         input_grad,

time: 1620 us -> 1610 us (level)
  waiting for transfers between devices: 581 us -> 561 us
    ppermute x9, waiting for transfers between devices: 146 us -> 127 us  [ring_scatter(): ahead = lax.ppermute(ahead.astype(kind), axis, ring_pairs(n, 1))]
  transfers between devices with their start and end apart: 50 -> 48, of which waited for: 30 -> 31; matrix products, arithmetic and copies ran while one was open for 34% -> 37% of each run, Pallas kernels for 8% -> 8%
where the time goes in v6:
time: 1610 us; the launch traced here: 1600 us
  waiting for transfers between devices  561 us (35%)
  matrix products  461 us (29%)
  local copies, waits for them, and re-layouts  173 us (11%)
  Pallas kernels  127 us (8%)
  starting transfers between devices  119 us (7%)
  other arithmetic  97.7 us (6%)
  blocking collectives  40.8 us (3%)
  between operations  17.8 us (1%)
    ppermute x9, waiting for transfers between devices, ring_scatter(): behind = lax.ppermute(behind.astype(kind), axis, ring_pairs(n, -1))  165 us
    ppermute x9, waiting for transfers between devices, ring_gather(): ahead = lax.ppermute(ahead, axis, ring_pairs(n, 1))  140 us
    ppermute x9, waiting for transfers between devices, ring_scatter(): ahead = lax.ppermute(ahead.astype(kind), axis, ring_pairs(n, 1))  127 us
    ppermute x9, waiting for transfers between devices, ring_gather(): behind = lax.ppermute(behind, axis, ring_pairs(n, -1))  97 us
    pallas_call x1, Pallas kernels, attention_bwd(): pl.pallas_call(functools.partial(_bwd_kernel, scale, seg), grid=(H, nq),...  76.2 us
    dot_general x14, matrix products, project_ffn(): jnp.dot(rows, weight, preferred_element_type=jnp.float32)  59.5 us
    dot_general x21, matrix products, project_qkv(): jnp.dot(rows, weight, preferred_element_type=jnp.float32)  58.6 us
    pallas_call x1, Pallas kernels, attention_fwd(): pl.pallas_call(functools.partial(_fwd_kernel, scale, seg), grid=(H, nq),...  50.7 us
  transfers between devices with their start and end apart: 48, of which 31 were waited for; matrix products, arithmetic and copies ran while one was open for 37% of the time, Pallas kernels for 8%

profile of v6, /device:TPU:0, one launch (start us, length us, event | category | flops | bytes accessed | tf_op | source)
XLA Modules:
  0.0 1596.5 jit_solution(13446549827446366082)
XLA Ops:
  40.0 21.7 %collective-permute-done.1 = bf16[256,2048]{1,0:T(8,128)(2,1)S(1)} collective-permute-done((bf16[256,2048]{1,0:T(8,128)(2,1)}, bf16[256,2048]{1,0:T(8,128)(2,1)S(1)}, u32[]{:S(2)}, u32[]{:S(2)}) %collective-permute-start.1) | collective-permute-done | bytes 1048608 | tf_op jit(solution)/shard_map/ppermute | solution.py:82
  66.4 20.1 %collective-permute-done = bf16[256,2048]{1,0:T(8,128)(2,1)} collective-permute-done((bf16[256,2048]{1,0:T(8,128)(2,1)}, bf16[256,2048]{1,0:T(8,128)(2,1)}, u32[]{:S(2)}, u32[]{:S(2)}) %collective-permute-start) | collective-permute-done | bytes 1048608 | tf_op jit(solution)/shard_map/ppermute | solution.py:81
  115.3 18.0 %collective-permute-start.5 = (bf16[256,2048]{1,0:T(8,128)(2,1)}, bf16[256,2048]{1,0:T(8,128)(2,1)}, u32[]{:S(2)}, u32[]{:S(2)}) collective-permute-start(bf16[256,2048]{1,0:T(8,128)(2,1)} %collective-permute-done.3), channel_id=1, source_target_pairs={{0,3},{1,0},{2,1},{3,2},{4,7},{5,4},{6,5},{7,6},{8,11},{9,8},{10,9... | collective-permute-start | bytes 3145736 | tf_op jit(solution)/shard_map/ppermute | solution.py:82
  149.3 10.2 collective-permute-done.5
  164.0 12.1 collective-permute-done.4
  212.0 11.5 all-gather.9.cloned.1.call-start
  260.6 50.7 %shard_map.220 = (f32[4,2048,128]{2,1,0:T(8,128)}, f32[4,2048,1]{2,1,0:T(8,128)}) custom-call(bf16[4,2048,128]{2,1,0:T(8,128)(2,1)} %bitcast.199, bf16[4,2048,128]{2,1,0:T(8,128)(2,1)} %bitcast.197, bf16[4,2048,128]{2,1,0:T(8,128)(2,1)} %bitcast.195, s32[2048,1]{1,0:T(8,128)} %copy.258.docq_ref, s32[1,2048]{1,0:T(1,128)} %bitcast.221), custom_call_target="tpu_custom_call" | custom-call | flops 8589934592 | bytes 10485760 | tf_op jit(solution)/shard_map/pallas_call | solution.py:210
  315.1 6.2 fusion.46
  328.6 10.9 copy.259
  352.0 57.7 %collective-permute-done.14 = bf16[256,2048]{1,0:T(8,128)(2,1)S(1)} collective-permute-done((bf16[256,2048]{1,0:T(8,128)(2,1)}, bf16[256,2048]{1,0:T(8,128)(2,1)S(1)}, u32[]{:S(2)}, u32[]{:S(2)}) %collective-permute-start.14) | collective-permute-done | bytes 1048608 | tf_op jit(solution)/shard_map/ppermute | solution.py:81
  409.7 28.8 %collective-permute-start.16 = (bf16[256,2048]{1,0:T(8,128)(2,1)S(1)}, bf16[256,2048]{1,0:T(8,128)(2,1)S(1)}, u32[]{:S(2)}, u32[]{:S(2)}) collective-permute-start(bf16[256,2048]{1,0:T(8,128)(2,1)S(1)} %collective-permute-done.14), channel_id=1, source_target_pairs={{0,1},{1,2},{2,3},{3,0},{4,5},{5,6},{6,7},{7,4},{8,9},{9,10},{10,1... | collective-permute-start | bytes 3145736 | tf_op jit(solution)/shard_map/ppermute | solution.py:81
  450.0 12.1 collective-permute-done.16
  463.1 20.3 %collective-permute-done.17 = bf16[256,2048]{1,0:T(8,128)(2,1)S(1)} collective-permute-done((bf16[256,2048]{1,0:T(8,128)(2,1)S(1)}, bf16[256,2048]{1,0:T(8,128)(2,1)S(1)}, u32[]{:S(2)}, u32[]{:S(2)}) %collective-permute-start.17) | collective-permute-done | bytes 1048608 | tf_op jit(solution)/shard_map/ppermute | solution.py:82
  489.0 9.8 multiply_reduce_fusion.4
  508.0 9.0 fusion.40
  518.1 8.1 fusion.41
  526.2 20.5 %collective-permute-done.7 = bf16[256,2048]{1,0:T(8,128)(2,1)S(1)} collective-permute-done((bf16[256,2048]{1,0:T(8,128)(2,1)S(1)}, bf16[256,2048]{1,0:T(8,128)(2,1)S(1)}, u32[]{:S(2)}, u32[]{:S(2)}) %collective-permute-start.7) | collective-permute-done | bytes 1048608 | tf_op jit(solution)/shard_map/ppermute | solution.py:82
  550.5 7.0 fusion.60
  557.5 6.9 fusion.59
  571.4 19.4 %collective-permute-done.9 = bf16[256,2048]{1,0:T(8,128)(2,1)S(1)} collective-permute-done((bf16[256,2048]{1,0:T(8,128)(2,1)S(1)}, bf16[256,2048]{1,0:T(8,128)(2,1)S(1)}, u32[]{:S(2)}, u32[]{:S(2)}) %collective-permute-start.9) | collective-permute-done | bytes 1048608 | tf_op jit(solution)/shard_map/ppermute | solution.py:82
  590.9 5.8 collective-permute-done.8
  610.6 27.6 %collective-permute-done.10 = bf16[256,2048]{1,0:T(8,128)(2,1)S(1)} collective-permute-done((bf16[256,2048]{1,0:T(8,128)(2,1)S(1)}, bf16[256,2048]{1,0:T(8,128)(2,1)S(1)}, u32[]{:S(2)}, u32[]{:S(2)}) %collective-permute-start.10) | collective-permute-done | bytes 1048608 | tf_op jit(solution)/shard_map/ppermute | solution.py:81
  650.3 34.6 %fusion.9 = (bf16[2048,2048]{1,0:T(8,128)(2,1)}, bf16[2048,2048]{1,0:T(8,128)(2,1)}, bf16[2048,2048]{1,0:T(8,128)(2,1)}) fusion(bf16[2048,2048]{1,0:T(8,128)(2,1)S(1)} %fusion.61, bf16[2048,2048]{1,0:T(8,128)(2,1)} %fusion.55, bf16[2048,2048]{1,0:T(8,128)(2,1)} %constant_dynamic-update-slice_fusion.14, bf16[2048,2048]{1,0:T(8,128)(2,1)} %param.23), kind=kOutput, calls=%fused_computation.15 | convolution fusion | flops 17255366656 | bytes 58720256 | tf_op jit(solution)/shard_map/dot_general | solution.py:370
  684.9 24.4 %fusion.134 = f32[2048,2048]{1,0:T(8,128)} fusion(bf16[2048,2048]{1,0:T(8,128)(2,1)} %get-tuple-element.129, bf16[2048,2048]{1,0:T(8,128)(2,1)} %param.21), kind=kOutput, calls=%fused_computation.296 | convolution fusion | flops 17179869184 | bytes 33554432 | tf_op jit(solution)/shard_map/dot_general | solution.py:373
  709.3 26.5 %convolution_add_fusion = f32[2048,2048]{1,0:T(8,128)} fusion(f32[2048,2048]{1,0:T(8,128)} %fusion.134, bf16[2048,2048]{1,0:T(8,128)(2,1)} %get-tuple-element.130, bf16[2048,2048]{1,0:T(8,128)(2,1)} %param.22), kind=kOutput, calls=%fused_computation.17 | convolution fusion | flops 17184063488 | bytes 50331648 | tf_op jit(solution)/shard_map/dot_general | solution.py:373
  739.2 23.8 %convolution_convert_fusion.3 = bf16[2048,2048]{1,0:T(8,128)(2,1)} fusion(bf16[2048,2048]{1,0:T(8,128)(2,1)} %constant_dynamic-update-slice_fusion.7, bf16[2048,2048]{1,0:T(8,128)(2,1)} %get-tuple-element.129), kind=kOutput, calls=%fused_computation.26 | convolution fusion | flops 17184063488 | bytes 25165824 | tf_op jit(solution)/shard_map/dot_general | solution.py:379
  763.1 24.0 %convolution_convert_fusion.2 = bf16[2048,2048]{1,0:T(8,128)(2,1)} fusion(bf16[2048,2048]{1,0:T(8,128)(2,1)} %constant_dynamic-update-slice_fusion.7, bf16[2048,2048]{1,0:T(8,128)(2,1)} %get-tuple-element.130), kind=kOutput, calls=%fused_computation.25 | convolution fusion | flops 17184063488 | bytes 25165824 | tf_op jit(solution)/shard_map/dot_general | solution.py:380
  793.6 24.0 %collective-permute-done.18 = bf16[256,2048]{1,0:T(8,128)(2,1)S(1)} collective-permute-done((bf16[256,2048]{1,0:T(8,128)(2,1)S(1)}, bf16[256,2048]{1,0:T(8,128)(2,1)S(1)}, u32[]{:S(2)}, u32[]{:S(2)}) %collective-permute-start.18) | collective-permute-done | bytes 1048608 | tf_op jit(solution)/shard_map/ppermute | solution.py:105
  817.6 19.5 %collective-permute-done.21 = bf16[256,2048]{1,0:T(8,128)(2,1)S(1)} collective-permute-done((bf16[256,2048]{1,0:T(8,128)(2,1)S(1)}, bf16[256,2048]{1,0:T(8,128)(2,1)S(1)}, u32[]{:S(2)}, u32[]{:S(2)}) %collective-permute-start.21) | collective-permute-done | bytes 1048608 | tf_op jit(solution)/shard_map/ppermute | solution.py:106
  845.2 25.1 %convolution_convert_fusion.1 = bf16[2048,2048]{1,0:T(8,128)(2,1)} fusion(bf16[2048,2048]{1,0:T(8,128)(2,1)} %get-tuple-element.135, bf16[2048,2048]{1,0:T(8,128)(2,1)} %constant_dynamic-update-slice_fusion.14), kind=kOutput, calls=%fused_computation.24 | convolution fusion | flops 17184063488 | bytes 25165824 | tf_op jit(solution)/shard_map/dot_general | solution.py:381
  871.2 18.7 %collective-permute-done.22 = bf16[256,2048]{1,0:T(8,128)(2,1)} collective-permute-done((bf16[256,2048]{1,0:T(8,128)(2,1)}, bf16[256,2048]{1,0:T(8,128)(2,1)}, u32[]{:S(2)}, u32[]{:S(2)}) %collective-permute-start.22) | collective-permute-done | bytes 1048608 | tf_op jit(solution)/shard_map/ppermute | solution.py:106
  898.8 23.9 %collective-permute-done.20 = bf16[256,2048]{1,0:T(8,128)(2,1)} collective-permute-done((bf16[256,2048]{1,0:T(8,128)(2,1)}, bf16[256,2048]{1,0:T(8,128)(2,1)}, u32[]{:S(2)}, u32[]{:S(2)}) %collective-permute-start.20) | collective-permute-done | bytes 1048608 | tf_op jit(solution)/shard_map/ppermute | solution.py:105
  922.7 19.3 %collective-permute-done.23 = bf16[256,2048]{1,0:T(8,128)(2,1)} collective-permute-done((bf16[256,2048]{1,0:T(8,128)(2,1)S(1)}, bf16[256,2048]{1,0:T(8,128)(2,1)}, u32[]{:S(2)}, u32[]{:S(2)}) %collective-permute-start.23) | collective-permute-done | bytes 1048608 | tf_op jit(solution)/shard_map/ppermute | solution.py:106
  950.1 10.0 convolution_convert_fusion.7
  966.1 24.2 %fusion.133 = f32[2048,2048]{1,0:T(8,128)} fusion(bf16[2048,2048]{1,0:T(8,128)(2,1)} %get-tuple-element.135, bf16[2048,2048]{1,0:T(8,128)(2,1)} %param.23), kind=kOutput, calls=%fused_computation.295 | convolution fusion | flops 17179869184 | bytes 33554432 | tf_op jit(solution)/shard_map/dot_general | solution.py:368
  990.3 22.6 %all-to-all-done.1 = bf16[512,4,512]{2,0,1:T(8,128)(2,1)} async-done(((bf16[512,4,512]{2,0,1:T(8,128)(2,1)}), bf16[512,4,512]{2,0,1:T(8,128)(2,1)}, u32[]{:S(2)}, u32[]{:S(2)}) %all-to-all-start.1) | async-done | bytes 2097184 | tf_op jit(solution)/shard_map/all_to_all | solution.py:395
  1032.7 8.5 multiply_reduce_fusion.1
  1044.3 9.4 fusion.97
  1054.6 10.7 convolution_convert_fusion
  1088.5 76.2 %shard_map.221 = (f32[4,2048,128]{2,1,0:T(8,128)}, f32[4,2048,128]{2,1,0:T(8,128)}, f32[4,2048,128]{2,1,0:T(8,128)}) custom-call(bf16[4,2048,128]{2,1,0:T(8,128)(2,1)} %bitcast.201, bf16[4,2048,128]{2,1,0:T(8,128)(2,1)} %bitcast.198, bf16[4,2048,128]{2,1,0:T(8,128)(2,1)} %bitcast.196, bf16[4,2048,128]{2,1,0:T(8,128)(2,1)} %get-tuple-element.260.do_ref, ...), custom_call_target="tpu_custom_call" | custom-call | flops 21474836480 | bytes 25165824 | tf_op jit(solution)/shard_map/pallas_call | solution.py:235
  1167.9 7.5 fusion.50
  1180.2 8.0 fusion.53
  1192.5 9.8 convolution_convert_fusion.5
  1202.4 10.0 convolution_convert_fusion.4
  1212.4 8.3 fusion.136
  1220.8 9.7 reduce-scatter.15.cloned.1.call-done
  1232.2 10.0 fusion.54
  1246.2 8.7 convolution_convert_fusion.6
  1254.9 8.1 fusion.135
  1263.1 11.4 pad_maximum_fusion
  1274.5 26.3 %add_add_fusion = f32[2048,2048]{1,0:T(8,128)} fusion(f32[2048,2048]{1,0:T(8,128)} %fusion.135, f32[2048,2048]{1,0:T(8,128)} %fusion.136, bf16[2048,512]{0,1:T(8,128)(2,1)} %bitcast.190, bf16[2048,512]{1,0:T(8,128)(2,1)} %param.17), kind=kOutput, calls=%fused_computation.16 | convolution fusion | flops 4303355904 | bytes 54525952 | tf_op jit(solution)/shard_map/dot_general | solution.py:453
  1314.3 16.9 %collective-permute-done.30 = bf16[256,2048]{1,0:T(8,128)(2,1)S(1)} collective-permute-done((bf16[256,2048]{1,0:T(8,128)(2,1)S(1)}, bf16[256,2048]{1,0:T(8,128)(2,1)S(1)}, u32[]{:S(2)}, u32[]{:S(2)}) %collective-permute-start.30) | collective-permute-done | bytes 1048608 | tf_op jit(solution)/shard_map/ppermute | solution.py:105
  1331.2 22.2 %collective-permute-done.33 = bf16[256,2048]{1,0:T(8,128)(2,1)S(1)} collective-permute-done((bf16[256,2048]{1,0:T(8,128)(2,1)S(1)}, bf16[256,2048]{1,0:T(8,128)(2,1)S(1)}, u32[]{:S(2)}, u32[]{:S(2)}) %collective-permute-start.33) | collective-permute-done | bytes 1048608 | tf_op jit(solution)/shard_map/ppermute | solution.py:106
  1361.4 14.8 collective-permute-done.25
  1376.2 22.1 %collective-permute-done.28 = bf16[256,2048]{1,0:T(8,128)(2,1)S(1)} collective-permute-done((bf16[256,2048]{1,0:T(8,128)(2,1)S(1)}, bf16[256,2048]{1,0:T(8,128)(2,1)S(1)}, u32[]{:S(2)}, u32[]{:S(2)}) %collective-permute-start.28) | collective-permute-done | bytes 1048608 | tf_op jit(solution)/shard_map/ppermute | solution.py:106
  1406.7 14.5 collective-permute-done.31
  1421.2 22.1 %collective-permute-done.34 = bf16[256,2048]{1,0:T(8,128)(2,1)} collective-permute-done((bf16[256,2048]{1,0:T(8,128)(2,1)}, bf16[256,2048]{1,0:T(8,128)(2,1)}, u32[]{:S(2)}, u32[]{:S(2)}) %collective-permute-start.34) | collective-permute-done | bytes 1048608 | tf_op jit(solution)/shard_map/ppermute | solution.py:106
  1450.3 15.9 collective-permute-done.26
  1466.3 21.9 %collective-permute-done.29 = bf16[256,2048]{1,0:T(8,128)(2,1)} collective-permute-done((bf16[256,2048]{1,0:T(8,128)(2,1)}, bf16[256,2048]{1,0:T(8,128)(2,1)}, u32[]{:S(2)}, u32[]{:S(2)}) %collective-permute-start.29) | collective-permute-done | bytes 1048608 | tf_op jit(solution)/shard_map/ppermute | solution.py:106
  1493.8 17.3 %collective-permute-done.32 = bf16[256,2048]{1,0:T(8,128)(2,1)S(1)} collective-permute-done((bf16[256,2048]{1,0:T(8,128)(2,1)S(1)}, bf16[256,2048]{1,0:T(8,128)(2,1)S(1)}, u32[]{:S(2)}, u32[]{:S(2)}) %collective-permute-start.32) | collective-permute-done | bytes 1048608 | tf_op jit(solution)/shard_map/ppermute | solution.py:105
  1511.1 18.9 %collective-permute-done.35 = bf16[256,2048]{1,0:T(8,128)(2,1)S(1)} collective-permute-done((bf16[256,2048]{1,0:T(8,128)(2,1)S(1)}, bf16[256,2048]{1,0:T(8,128)(2,1)S(1)}, u32[]{:S(2)}, u32[]{:S(2)}) %collective-permute-start.35) | collective-permute-done | bytes 1048608 | tf_op jit(solution)/shard_map/ppermute | solution.py:106
  1534.9 17.8 %all-reduce.1 = (f32[2048]{0:T(1024)S(1)}, f32[16]{0:T(128)S(1)}, f32[2048]{0:T(1024)S(1)}) all-reduce(f32[2048]{0:T(1024)S(1)} %get-tuple-element.219, f32[16]{0:T(128)S(1)} %multiply_dynamic-update-slice_fusion, f32[2048]{0:T(1024)S(1)} %copy-done.47), channel_id=1, replica_groups=mesh['dp'=8,'mp'=4] {'mp'}, use_global_device_ids=true, to_apply=%region_19.20 | all-reduce | flops 4112 | bytes 32896 | tf_op jit(solution)/shard_map/psum | solution.py:464
  1552.7 22.9 %all-reduce = (f32[2048]{0:T(1024)}, f32[16]{0:T(128)}, f32[2048]{0:T(1024)}) all-reduce(f32[2048]{0:T(1024)S(1)} %get-tuple-element.224, f32[16]{0:T(128)S(1)} %get-tuple-element.225, f32[2048]{0:T(1024)S(1)} %get-tuple-element.226), channel_id=1, replica_groups=mesh['dp'=8,'mp'=4] {'dp'}, use_global_device_ids=true, to_apply=%region_20.21 | all-reduce | flops 4112 | bytes 32896 | tf_op jit(solution)/shard_map/psum | solution.py:463
  1575.7 7.5 fusion.16
  (398 shorter events, 406.1 us)
Async XLA Ops:
  7.2 216.3 %all-gather.7.cloned.1.call-start = ((), (), s32[]{:S(2)}) async-start(), calls=%async_computation.8 | async-start | bytes 1310720 | tf_op jit(solution)/shard_map/all_gather | solution.py:302
  9.1 302.2 %all-gather.13.cloned.1.call-start = ((), (), s32[]{:S(2)}) async-start(), calls=%async_computation.17 | async-start | bytes 2396160 | tf_op jit(solution)/shard_map/all_gather | solution.py:26
  18.0 43.7 %collective-permute-start.1 = (bf16[256,2048]{1,0:T(8,128)(2,1)}, bf16[256,2048]{1,0:T(8,128)(2,1)S(1)}, u32[]{:S(2)}, u32[]{:S(2)}) collective-permute-start(bf16[256,2048]{1,0:T(8,128)(2,1)} %get-tuple-element.265), channel_id=1, source_target_pairs={{0,3},{1,0},{2,1},{3,2},{4,7},{5,4},{6,5},{7,6},{8,11},{9,8},{10,9... | collective-permute-start | bytes 3145736 | tf_op jit(solution)/shard_map/ppermute | solution.py:82
  23.1 63.5 %collective-permute-start = (bf16[256,2048]{1,0:T(8,128)(2,1)}, bf16[256,2048]{1,0:T(8,128)(2,1)}, u32[]{:S(2)}, u32[]{:S(2)}) collective-permute-start(bf16[256,2048]{1,0:T(8,128)(2,1)} %get-tuple-element.266), channel_id=1, source_target_pairs={{0,1},{1,2},{2,3},{3,0},{4,5},{5,6},{6,7},{7,4},{8,9},{9,10},{10,1... | collective-permute-start | bytes 3145736 | tf_op jit(solution)/shard_map/ppermute | solution.py:81
  24.7 199.5 %copy-start.46 = (s32[2048]{0:T(1024)}, s32[2048]{0:T(1024)S(1)}, u32[]{:S(2)}) copy-start(s32[2048]{0:T(1024)S(1)} %slice.70) | copy-start | bytes 24580
  31.9 174.7 %copy-start.52 = (f32[2048]{0:T(1024)}, f32[2048]{0:T(1024)S(1)}, u32[]{:S(2)}) copy-start(f32[2048]{0:T(1024)S(1)} %get-tuple-element.271) | copy-start | bytes 24580
  31.9 294.5 %copy-start.42 = (f32[2048]{0:T(1024)}, f32[2048]{0:T(1024)S(1)}, u32[]{:S(2)}) copy-start(f32[2048]{0:T(1024)S(1)} %get-tuple-element.270) | copy-start | bytes 24580
  61.7 170.3 %copy-start.29 = (bf16[256,2048]{1,0:T(8,128)(2,1)}, bf16[256,2048]{1,0:T(8,128)(2,1)S(1)}, u32[]{:S(2)}) copy-start(bf16[256,2048]{1,0:T(8,128)(2,1)S(1)} %collective-permute-done.1) | copy-start | bytes 3145732
  61.7 44.8 %collective-permute-start.3 = (bf16[256,2048]{1,0:T(8,128)(2,1)S(1)}, bf16[256,2048]{1,0:T(8,128)(2,1)}, u32[]{:S(2)}, u32[]{:S(2)}) collective-permute-start(bf16[256,2048]{1,0:T(8,128)(2,1)S(1)} %collective-permute-done.1), channel_id=1, source_target_pairs={{0,3},{1,0},{2,1},{3,2},{4,7},{5,4},{6,5},{7,6},{8,11},{9,8},{10,9... | collective-permute-start | bytes 3145736 | tf_op jit(solution)/shard_map/ppermute | solution.py:82
  86.6 47.2 %collective-permute-start.2 = (bf16[256,2048]{1,0:T(8,128)(2,1)}, bf16[256,2048]{1,0:T(8,128)(2,1)}, u32[]{:S(2)}, u32[]{:S(2)}) collective-permute-start(bf16[256,2048]{1,0:T(8,128)(2,1)} %collective-permute-done), channel_id=1, source_target_pairs={{0,1},{1,2},{2,3},{3,0},{4,5},{5,6},{6,7},{7,4},{8,9},{9,10},{10,1... | collective-permute-start | bytes 3145736 | tf_op jit(solution)/shard_map/ppermute | solution.py:81
  115.3 44.2 %collective-permute-start.5 = (bf16[256,2048]{1,0:T(8,128)(2,1)}, bf16[256,2048]{1,0:T(8,128)(2,1)}, u32[]{:S(2)}, u32[]{:S(2)}) collective-permute-start(bf16[256,2048]{1,0:T(8,128)(2,1)} %collective-permute-done.3), channel_id=1, source_target_pairs={{0,3},{1,0},{2,1},{3,2},{4,7},{5,4},{6,5},{7,6},{8,11},{9,8},{10,9... | collective-permute-start | bytes 3145736 | tf_op jit(solution)/shard_map/ppermute | solution.py:82
  138.9 37.1 %collective-permute-start.4 = (bf16[256,2048]{1,0:T(8,128)(2,1)}, bf16[256,2048]{1,0:T(8,128)(2,1)}, u32[]{:S(2)}, u32[]{:S(2)}) collective-permute-start(bf16[256,2048]{1,0:T(8,128)(2,1)} %collective-permute-done.2), channel_id=1, source_target_pairs={{0,1},{1,2},{2,3},{3,0},{4,5},{5,6},{6,7},{7,4},{8,9},{9,10},{10,1... | collective-permute-start | bytes 3145736 | tf_op jit(solution)/shard_map/ppermute | solution.py:81
  212.0 277.0 %all-gather.9.cloned.1.call-start = ((), (), s32[]{:S(2)}) async-start(), calls=%async_computation.9 | async-start | bytes 9437184 | tf_op jit(solution)/shard_map/all_gather | solution.py:301
  225.6 100.9 %copy-start.54 = (f32[4]{0:T(128)}, f32[4]{0:T(128)S(1)}, u32[]{:S(2)}) copy-start(f32[4]{0:T(128)S(1)} %get-tuple-element.232) | copy-start | bytes 52
  225.6 100.9 %copy-start.56 = (f32[4]{0:T(128)}, f32[4]{0:T(128)S(1)}, u32[]{:S(2)}) copy-start(f32[4]{0:T(128)S(1)} %get-tuple-element.231) | copy-start | bytes 52
  258.5 91.6 %collective-permute-start.13 = (bf16[256,2048]{1,0:T(8,128)(2,1)}, bf16[256,2048]{1,0:T(8,128)(2,1)S(1)}, u32[]{:S(2)}, u32[]{:S(2)}) collective-permute-start(bf16[256,2048]{1,0:T(8,128)(2,1)} %get-tuple-element.261), channel_id=1, source_target_pairs={{0,3},{1,0},{2,1},{3,2},{4,7},{5,4},{6,5},{7,6},{8,11},{9,8},{10,9... | collective-permute-start | bytes 3145736 | tf_op jit(solution)/shard_map/ppermute | solution.py:82
  258.5 89.6 %collective-permute-start.12 = (bf16[256,2048]{1,0:T(8,128)(2,1)}, bf16[256,2048]{1,0:T(8,128)(2,1)}, u32[]{:S(2)}, u32[]{:S(2)}) collective-permute-start(bf16[256,2048]{1,0:T(8,128)(2,1)} %get-tuple-element.262), channel_id=1, source_target_pairs={{0,1},{1,2},{2,3},{3,0},{4,5},{5,6},{6,7},{7,4},{8,9},{9,10},{10,1... | collective-permute-start | bytes 3145736 | tf_op jit(solution)/shard_map/ppermute | solution.py:81
  343.6 141.0 %all-to-all-start = ((bf16[4,512,512]{2,1,0:T(8,128)(2,1)}), bf16[4,512,512]{2,1,0:T(8,128)(2,1)}, u32[]{:S(2)}, u32[]{:S(2)}) async-start(bf16[4,512,512]{2,1,0:T(8,128)(2,1)} %convert_element_type.380), calls=%async_computation | async-start | bytes 4194304 | tf_op jit(solution)/shard_map/all_to_all | solution.py:351
  348.0 679.0 %reduce-scatter.7.cloned.1.call-start = ((), (), s32[]{:S(2)}) async-start(), calls=%async_computation.10 | async-start | bytes 9437184 | tf_op jit(solution)/shard_map/reduce_scatter | solution.py:288
  348.1 94.8 %copy-start.6 = (bf16[512,2048]{1,0:T(8,128)(2,1)S(1)}, bf16[512,2048]{1,0:T(8,128)(2,1)}, u32[]{:S(2)}) copy-start(bf16[512,2048]{1,0:T(8,128)(2,1)} %param.25) | copy-start | bytes 6291460
  348.1 61.6 %collective-permute-start.14 = (bf16[256,2048]{1,0:T(8,128)(2,1)}, bf16[256,2048]{1,0:T(8,128)(2,1)S(1)}, u32[]{:S(2)}, u32[]{:S(2)}) collective-permute-start(bf16[256,2048]{1,0:T(8,128)(2,1)} %collective-permute-done.12), channel_id=1, source_target_pairs={{0,1},{1,2},{2,3},{3,0},{4,5},{5,6},{6,7},{7,4},{8,9},{9,10},{10,1... | collective-permute-start | bytes 3145736 | tf_op jit(solution)/shard_map/ppermute | solution.py:81
  350.1 94.3 %collective-permute-start.15 = (bf16[256,2048]{1,0:T(8,128)(2,1)S(1)}, bf16[256,2048]{1,0:T(8,128)(2,1)S(1)}, u32[]{:S(2)}, u32[]{:S(2)}) collective-permute-start(bf16[256,2048]{1,0:T(8,128)(2,1)S(1)} %collective-permute-done.13), channel_id=1, source_target_pairs={{0,3},{1,0},{2,1},{3,2},{4,7},{5,4},{6,5},{7,6},{8,11},{9,8},{10,9... | collective-permute-start | bytes 3145736 | tf_op jit(solution)/shard_map/ppermute | solution.py:82
  409.7 52.3 %collective-permute-start.16 = (bf16[256,2048]{1,0:T(8,128)(2,1)S(1)}, bf16[256,2048]{1,0:T(8,128)(2,1)S(1)}, u32[]{:S(2)}, u32[]{:S(2)}) collective-permute-start(bf16[256,2048]{1,0:T(8,128)(2,1)S(1)} %collective-permute-done.14), channel_id=1, source_target_pairs={{0,1},{1,2},{2,3},{3,0},{4,5},{5,6},{6,7},{7,4},{8,9},{9,10},{10,1... | collective-permute-start | bytes 3145736 | tf_op jit(solution)/shard_map/ppermute | solution.py:81
  444.4 39.0 %collective-permute-start.17 = (bf16[256,2048]{1,0:T(8,128)(2,1)S(1)}, bf16[256,2048]{1,0:T(8,128)(2,1)S(1)}, u32[]{:S(2)}, u32[]{:S(2)}) collective-permute-start(bf16[256,2048]{1,0:T(8,128)(2,1)S(1)} %collective-permute-done.15), channel_id=1, source_target_pairs={{0,3},{1,0},{2,1},{3,2},{4,7},{5,4},{6,5},{7,6},{8,11},{9,8},{10,9... | collective-permute-start | bytes 3145736 | tf_op jit(solution)/shard_map/ppermute | solution.py:82
  501.5 45.1 %collective-permute-start.7 = (bf16[256,2048]{1,0:T(8,128)(2,1)S(1)}, bf16[256,2048]{1,0:T(8,128)(2,1)S(1)}, u32[]{:S(2)}, u32[]{:S(2)}) collective-permute-start(bf16[256,2048]{1,0:T(8,128)(2,1)S(1)} %get-tuple-element.263), channel_id=1, source_target_pairs={{0,3},{1,0},{2,1},{3,2},{4,7},{5,4},{6,5},{7,6},{8,11},{9,8},{10,9... | collective-permute-start | bytes 3145736 | tf_op jit(solution)/shard_map/ppermute | solution.py:82
  501.6 48.7 %collective-permute-start.6 = (bf16[256,2048]{1,0:T(8,128)(2,1)S(1)}, bf16[256,2048]{1,0:T(8,128)(2,1)S(1)}, u32[]{:S(2)}, u32[]{:S(2)}) collective-permute-start(bf16[256,2048]{1,0:T(8,128)(2,1)S(1)} %get-tuple-element.264), channel_id=1, source_target_pairs={{0,1},{1,2},{2,3},{3,0},{4,5},{5,6},{6,7},{7,4},{8,9},{9,10},{10,1... | collective-permute-start | bytes 3145736 | tf_op jit(solution)/shard_map/ppermute | solution.py:81
  546.6 44.2 %collective-permute-start.9 = (bf16[256,2048]{1,0:T(8,128)(2,1)S(1)}, bf16[256,2048]{1,0:T(8,128)(2,1)S(1)}, u32[]{:S(2)}, u32[]{:S(2)}) collective-permute-start(bf16[256,2048]{1,0:T(8,128)(2,1)S(1)} %collective-permute-done.7), channel_id=1, source_target_pairs={{0,3},{1,0},{2,1},{3,2},{4,7},{5,4},{6,5},{7,6},{8,11},{9,8},{10,9... | collective-permute-start | bytes 3145736 | tf_op jit(solution)/shard_map/ppermute | solution.py:82
  550.3 46.3 %collective-permute-start.8 = (bf16[256,2048]{1,0:T(8,128)(2,1)S(1)}, bf16[256,2048]{1,0:T(8,128)(2,1)S(1)}, u32[]{:S(2)}, u32[]{:S(2)}) collective-permute-start(bf16[256,2048]{1,0:T(8,128)(2,1)S(1)} %collective-permute-done.6), channel_id=1, source_target_pairs={{0,1},{1,2},{2,3},{3,0},{4,5},{5,6},{6,7},{7,4},{8,9},{9,10},{10,1... | collective-permute-start | bytes 3145736 | tf_op jit(solution)/shard_map/ppermute | solution.py:81
  564.4 32.5 %slice-start.2 = ((s8[8388608]{0:T(1024)(128)(4,1)}), s8[4194304]{0:T(1024)(128)(4,1)S(1)}, s32[]{:S(2)}) async-start(s8[8388608]{0:T(1024)(128)(4,1)} %bitcast.231), calls=%async_computation.20 | async-start | bytes 8388608
  590.9 53.2 %collective-permute-start.11 = (bf16[256,2048]{1,0:T(8,128)(2,1)S(1)}, bf16[256,2048]{1,0:T(8,128)(2,1)S(1)}, u32[]{:S(2)}, u32[]{:S(2)}) collective-permute-start(bf16[256,2048]{1,0:T(8,128)(2,1)S(1)} %collective-permute-done.9), channel_id=1, source_target_pairs={{0,3},{1,0},{2,1},{3,2},{4,7},{5,4},{6,5},{7,6},{8,11},{9,8},{10,9... | collective-permute-start | bytes 3145736 | tf_op jit(solution)/shard_map/ppermute | solution.py:82
  596.6 41.6 %collective-permute-start.10 = (bf16[256,2048]{1,0:T(8,128)(2,1)S(1)}, bf16[256,2048]{1,0:T(8,128)(2,1)S(1)}, u32[]{:S(2)}, u32[]{:S(2)}) collective-permute-start(bf16[256,2048]{1,0:T(8,128)(2,1)S(1)} %collective-permute-done.8), channel_id=1, source_target_pairs={{0,1},{1,2},{2,3},{3,0},{4,5},{5,6},{6,7},{7,4},{8,9},{9,10},{10,1... | collective-permute-start | bytes 3145736 | tf_op jit(solution)/shard_map/ppermute | solution.py:81
  763.0 266.8 %reduce-scatter.9.cloned.1.call-start = ((), (), s32[]{:S(2)}) async-start(), calls=%async_computation.11 | async-start | bytes 9437184 | tf_op jit(solution)/shard_map/reduce_scatter | solution.py:288
  787.1 298.7 %reduce-scatter.11.cloned.1.call-start = ((), (), s32[]{:S(2)}) async-start(), calls=%async_computation.12 | async-start | bytes 9437184 | tf_op jit(solution)/shard_map/reduce_scatter | solution.py:288
  789.7 27.9 %collective-permute-start.18 = (bf16[256,2048]{1,0:T(8,128)(2,1)S(1)}, bf16[256,2048]{1,0:T(8,128)(2,1)S(1)}, u32[]{:S(2)}, u32[]{:S(2)}) collective-permute-start(bf16[256,2048]{1,0:T(8,128)(2,1)S(1)} %get-tuple-element.258), channel_id=1, source_target_pairs={{0,1},{1,2},{2,3},{3,0},{4,5},{5,6},{6,7},{7,4},{8,9},{9,10},{10,1... | collective-permute-start | bytes 3145736 | tf_op jit(solution)/shard_map/ppermute | solution.py:105
  789.9 47.2 %collective-permute-start.21 = (bf16[256,2048]{1,0:T(8,128)(2,1)S(1)}, bf16[256,2048]{1,0:T(8,128)(2,1)S(1)}, u32[]{:S(2)}, u32[]{:S(2)}) collective-permute-start(bf16[256,2048]{1,0:T(8,128)(2,1)S(1)} %get-tuple-element.259), channel_id=1, source_target_pairs={{0,3},{1,0},{2,1},{3,2},{4,7},{5,4},{6,5},{7,6},{8,11},{9,8},{10,9... | collective-permute-start | bytes 3145736 | tf_op jit(solution)/shard_map/ppermute | solution.py:106
  841.4 28.9 %collective-permute-start.19 = (bf16[256,2048]{1,0:T(8,128)(2,1)}, bf16[256,2048]{1,0:T(8,128)(2,1)S(1)}, u32[]{:S(2)}, u32[]{:S(2)}) collective-permute-start(bf16[256,2048]{1,0:T(8,128)(2,1)} %get-tuple-element.256), channel_id=1, source_target_pairs={{0,1},{1,2},{2,3},{3,0},{4,5},{5,6},{6,7},{7,4},{8,9},{9,10},{10,1... | collective-permute-start | bytes 3145736 | tf_op jit(solution)/shard_map/ppermute | solution.py:105
  842.4 47.6 %collective-permute-start.22 = (bf16[256,2048]{1,0:T(8,128)(2,1)}, bf16[256,2048]{1,0:T(8,128)(2,1)}, u32[]{:S(2)}, u32[]{:S(2)}) collective-permute-start(bf16[256,2048]{1,0:T(8,128)(2,1)} %get-tuple-element.257), channel_id=1, source_target_pairs={{0,3},{1,0},{2,1},{3,2},{4,7},{5,4},{6,5},{7,6},{8,11},{9,8},{10,9... | collective-permute-start | bytes 3145736 | tf_op jit(solution)/shard_map/ppermute | solution.py:106
  894.5 28.1 %collective-permute-start.20 = (bf16[256,2048]{1,0:T(8,128)(2,1)}, bf16[256,2048]{1,0:T(8,128)(2,1)}, u32[]{:S(2)}, u32[]{:S(2)}) collective-permute-start(bf16[256,2048]{1,0:T(8,128)(2,1)} %get-tuple-element.254), channel_id=1, source_target_pairs={{0,1},{1,2},{2,3},{3,0},{4,5},{5,6},{6,7},{7,4},{8,9},{9,10},{10,1... | collective-permute-start | bytes 3145736 | tf_op jit(solution)/shard_map/ppermute | solution.py:105
  894.8 47.1 %collective-permute-start.23 = (bf16[256,2048]{1,0:T(8,128)(2,1)S(1)}, bf16[256,2048]{1,0:T(8,128)(2,1)}, u32[]{:S(2)}, u32[]{:S(2)}) collective-permute-start(bf16[256,2048]{1,0:T(8,128)(2,1)S(1)} %get-tuple-element.255), channel_id=1, source_target_pairs={{0,3},{1,0},{2,1},{3,2},{4,7},{5,4},{6,5},{7,6},{8,11},{9,8},{10,9... | collective-permute-start | bytes 3145736 | tf_op jit(solution)/shard_map/ppermute | solution.py:106
  898.8 46.5 %copy-start.2 = (f32[512,2048]{1,0:T(8,128)S(1)}, f32[512,2048]{1,0:T(8,128)}, u32[]{:S(2)}) copy-start(f32[512,2048]{1,0:T(8,128)} %copy-done.1) | copy-start | bytes 12582916
  898.8 46.5 %copy-start.45 = (f32[2048]{0:T(1024)S(1)}, f32[2048]{0:T(1024)}, u32[]{:S(2)}) copy-start(f32[2048]{0:T(1024)} %param.20) | copy-start | bytes 24580
  898.8 46.6 %copy-start.51 = (f32[512]{0:T(512)S(1)}, f32[512]{0:T(512)}, u32[]{:S(2)}) copy-start(f32[512]{0:T(512)} %copy-done.50) | copy-start | bytes 6148
  961.6 51.4 %all-to-all-start.1 = ((bf16[512,4,512]{2,0,1:T(8,128)(2,1)}), bf16[512,4,512]{2,0,1:T(8,128)(2,1)}, u32[]{:S(2)}, u32[]{:S(2)}) async-start(bf16[512,4,512]{2,0,1:T(8,128)(2,1)} %bitcast.194), calls=%async_computation.1 | async-start | bytes 4194304 | tf_op jit(solution)/shard_map/all_to_all | solution.py:395
  966.0 198.7 %all-gather.11.cloned.1.call-start = ((), (), s32[]{:S(2)}) async-start(), calls=%async_computation.15 | async-start | bytes 1198080 | tf_op jit(solution)/shard_map/all_gather | solution.py:26
  1054.5 147.8 %reduce-scatter.13.cloned.1.call-start = ((), (), s32[]{:S(2)}) async-start(), calls=%async_computation.13 | async-start | bytes 9437184 | tf_op jit(solution)/shard_map/reduce_scatter | solution.py:288
  1065.3 165.2 %reduce-scatter.15.cloned.1.call-start = ((), (), s32[]{:S(2)}) async-start(), calls=%async_computation.14 | async-start | bytes 1310720 | tf_op jit(solution)/shard_map/reduce_scatter | solution.py:390
  1082.0 225.2 %collective-permute-start.24 = (bf16[256,2048]{1,0:T(8,128)(2,1)}, bf16[256,2048]{1,0:T(8,128)(2,1)S(1)}, u32[]{:S(2)}, u32[]{:S(2)}) collective-permute-start(bf16[256,2048]{1,0:T(8,128)(2,1)} %get-tuple-element.250), channel_id=1, source_target_pairs={{0,1},{1,2},{2,3},{3,0},{4,5},{5,6},{6,7},{7,4},{8,9},{9,10},{10,1... | collective-permute-start | bytes 3145736 | tf_op jit(solution)/shard_map/ppermute | solution.py:105
  1082.0 225.2 %collective-permute-start.27 = (bf16[256,2048]{1,0:T(8,128)(2,1)}, bf16[256,2048]{1,0:T(8,128)(2,1)}, u32[]{:S(2)}, u32[]{:S(2)}) collective-permute-start(bf16[256,2048]{1,0:T(8,128)(2,1)} %get-tuple-element.251), channel_id=1, source_target_pairs={{0,3},{1,0},{2,1},{3,2},{4,7},{5,4},{6,5},{7,6},{8,11},{9,8},{10,9... | collective-permute-start | bytes 3145736 | tf_op jit(solution)/shard_map/ppermute | solution.py:106
  1202.3 380.8 %reduce-scatter.17.cloned.1.call-start = ((), (), s32[]{:S(2)}) async-start(), calls=%async_computation.16 | async-start | bytes 7077888 | tf_op jit(solution)/shard_map/reduce_scatter | solution.py:288
  1303.3 27.9 %collective-permute-start.30 = (bf16[256,2048]{1,0:T(8,128)(2,1)S(1)}, bf16[256,2048]{1,0:T(8,128)(2,1)S(1)}, u32[]{:S(2)}, u32[]{:S(2)}) collective-permute-start(bf16[256,2048]{1,0:T(8,128)(2,1)S(1)} %get-tuple-element.242), channel_id=1, source_target_pairs={{0,1},{1,2},{2,3},{3,0},{4,5},{5,6},{6,7},{7,4},{8,9},{9,10},{10,1... | collective-permute-start | bytes 3145736 | tf_op jit(solution)/shard_map/ppermute | solution.py:105
  1303.4 50.0 %collective-permute-start.33 = (bf16[256,2048]{1,0:T(8,128)(2,1)S(1)}, bf16[256,2048]{1,0:T(8,128)(2,1)S(1)}, u32[]{:S(2)}, u32[]{:S(2)}) collective-permute-start(bf16[256,2048]{1,0:T(8,128)(2,1)S(1)} %get-tuple-element.243), channel_id=1, source_target_pairs={{0,3},{1,0},{2,1},{3,2},{4,7},{5,4},{6,5},{7,6},{8,11},{9,8},{10,9... | collective-permute-start | bytes 3145736 | tf_op jit(solution)/shard_map/ppermute | solution.py:106
  1310.4 65.7 %collective-permute-start.25 = (bf16[256,2048]{1,0:T(8,128)(2,1)S(1)}, bf16[256,2048]{1,0:T(8,128)(2,1)S(1)}, u32[]{:S(2)}, u32[]{:S(2)}) collective-permute-start(bf16[256,2048]{1,0:T(8,128)(2,1)S(1)} %get-tuple-element.248), channel_id=1, source_target_pairs={{0,1},{1,2},{2,3},{3,0},{4,5},{5,6},{6,7},{7,4},{8,9},{9,10},{10,1... | collective-permute-start | bytes 3145736 | tf_op jit(solution)/shard_map/ppermute | solution.py:105
  1310.5 87.7 %collective-permute-start.28 = (bf16[256,2048]{1,0:T(8,128)(2,1)S(1)}, bf16[256,2048]{1,0:T(8,128)(2,1)S(1)}, u32[]{:S(2)}, u32[]{:S(2)}) collective-permute-start(bf16[256,2048]{1,0:T(8,128)(2,1)S(1)} %get-tuple-element.249), channel_id=1, source_target_pairs={{0,3},{1,0},{2,1},{3,2},{4,7},{5,4},{6,5},{7,6},{8,11},{9,8},{10,9... | collective-permute-start | bytes 3145736 | tf_op jit(solution)/shard_map/ppermute | solution.py:106
  1357.6 63.6 %collective-permute-start.31 = (bf16[256,2048]{1,0:T(8,128)(2,1)}, bf16[256,2048]{1,0:T(8,128)(2,1)S(1)}, u32[]{:S(2)}, u32[]{:S(2)}) collective-permute-start(bf16[256,2048]{1,0:T(8,128)(2,1)} %get-tuple-element.240), channel_id=1, source_target_pairs={{0,1},{1,2},{2,3},{3,0},{4,5},{5,6},{6,7},{7,4},{8,9},{9,10},{10,1... | collective-permute-start | bytes 3145736 | tf_op jit(solution)/shard_map/ppermute | solution.py:105
  1358.5 47.8 %copy-start.58 = (f32[4]{0:T(128)S(1)}, f32[4]{0:T(128)}, u32[]{:S(2)}) copy-start(f32[4]{0:T(128)} %get-tuple-element.215) | copy-start | bytes 52
  1358.5 84.8 %collective-permute-start.34 = (bf16[256,2048]{1,0:T(8,128)(2,1)}, bf16[256,2048]{1,0:T(8,128)(2,1)}, u32[]{:S(2)}, u32[]{:S(2)}) collective-permute-start(bf16[256,2048]{1,0:T(8,128)(2,1)} %get-tuple-element.241), channel_id=1, source_target_pairs={{0,3},{1,0},{2,1},{3,2},{4,7},{5,4},{6,5},{7,6},{8,11},{9,8},{10,9... | collective-permute-start | bytes 3145736 | tf_op jit(solution)/shard_map/ppermute | solution.py:106
  1402.5 63.7 %collective-permute-start.26 = (bf16[256,2048]{1,0:T(8,128)(2,1)}, bf16[256,2048]{1,0:T(8,128)(2,1)}, u32[]{:S(2)}, u32[]{:S(2)}) collective-permute-start(bf16[256,2048]{1,0:T(8,128)(2,1)} %get-tuple-element.246), channel_id=1, source_target_pairs={{0,1},{1,2},{2,3},{3,0},{4,5},{5,6},{6,7},{7,4},{8,9},{9,10},{10,1... | collective-permute-start | bytes 3145736 | tf_op jit(solution)/shard_map/ppermute | solution.py:105
  1403.5 84.7 %collective-permute-start.29 = (bf16[256,2048]{1,0:T(8,128)(2,1)}, bf16[256,2048]{1,0:T(8,128)(2,1)}, u32[]{:S(2)}, u32[]{:S(2)}) collective-permute-start(bf16[256,2048]{1,0:T(8,128)(2,1)} %get-tuple-element.247), channel_id=1, source_target_pairs={{0,3},{1,0},{2,1},{3,2},{4,7},{5,4},{6,5},{7,6},{8,11},{9,8},{10,9... | collective-permute-start | bytes 3145736 | tf_op jit(solution)/shard_map/ppermute | solution.py:106
  1446.4 64.7 %collective-permute-start.32 = (bf16[256,2048]{1,0:T(8,128)(2,1)S(1)}, bf16[256,2048]{1,0:T(8,128)(2,1)S(1)}, u32[]{:S(2)}, u32[]{:S(2)}) collective-permute-start(bf16[256,2048]{1,0:T(8,128)(2,1)S(1)} %get-tuple-element.238), channel_id=1, source_target_pairs={{0,1},{1,2},{2,3},{3,0},{4,5},{5,6},{6,7},{7,4},{8,9},{9,10},{10,1... | collective-permute-start | bytes 3145736 | tf_op jit(solution)/shard_map/ppermute | solution.py:105
  1447.5 44.4 %copy-start.3 = (f32[512,2048]{1,0:T(8,128)S(1)}, f32[512,2048]{1,0:T(8,128)}, u32[]{:S(2)}) copy-start(f32[512,2048]{1,0:T(8,128)} %copy-done.1) | copy-start | bytes 12582916
  1447.5 82.6 %collective-permute-start.35 = (bf16[256,2048]{1,0:T(8,128)(2,1)S(1)}, bf16[256,2048]{1,0:T(8,128)(2,1)S(1)}, u32[]{:S(2)}, u32[]{:S(2)}) collective-permute-start(bf16[256,2048]{1,0:T(8,128)(2,1)S(1)} %get-tuple-element.239), channel_id=1, source_target_pairs={{0,3},{1,0},{2,1},{3,2},{4,7},{5,4},{6,5},{7,6},{8,11},{9,8},{10,9... | collective-permute-start | bytes 3145736 | tf_op jit(solution)/shard_map/ppermute | solution.py:106
  1493.8 39.1 %copy-start.5 = (bf16[512,2048]{1,0:T(8,128)(2,1)S(1)}, bf16[512,2048]{1,0:T(8,128)(2,1)}, u32[]{:S(2)}) copy-start(bf16[512,2048]{1,0:T(8,128)(2,1)} %param.13) | copy-start | bytes 6291460
  1493.8 39.1 %copy-start.41 = (f32[2048]{0:T(1024)S(1)}, f32[2048]{0:T(1024)}, u32[]{:S(2)}) copy-start(f32[2048]{0:T(1024)} %param.14) | copy-start | bytes 24580
  1493.8 39.1 %copy-start.49 = (f32[512]{0:T(512)S(1)}, f32[512]{0:T(512)}, u32[]{:S(2)}) copy-start(f32[512]{0:T(512)} %copy-done.48) | copy-start | bytes 6148
  (53 other events, 398.7 us)
Sparse Core Ops, SparseCore 0:
  9.6 41.3 all-gather.6
  212.1 26.1 all-gather.12
  240.2 55.8 all-gather.8
  763.1 72.9 reduce-scatter.6
  839.4 71.5 reduce-scatter.8
  914.3 71.2 reduce-scatter.10
  1054.6 24.3 all-gather.10
  1082.5 71.2 reduce-scatter.12
  1202.5 27.9 reduce-scatter.14
  1274.6 60.0 reduce-scatter.16

commit v7 on v6

--- a/solution.py
+++ b/solution.py
@@ -59,6 +59,15 @@
     factors = jnp.where((j > place) & (j < k), flags[None, :], 1.0)
     weights = jnp.where(jnp.arange(size) > place, jnp.prod(factors, axis=1), 0.0)
     return combine_selected(weights, states)
+
+
+def tree_sum(value, axis):
+    n = lax.axis_size(axis)
+    step = 1
+    while step < n:
+        value = value + lax.ppermute(value, axis, [(j, j ^ step) for j in range(n)])
+        step *= 2
+    return value
 
 
 def ring_pairs(n, step):
@@ -367,7 +376,9 @@
     act = (gate_f * sig_gate * up_f).astype(jnp.bfloat16)
     mlp_part = jnp.dot(act, w_down, preferred_element_type=jnp.float32)
     (grad_rows_all,) = ring_gather(grad_rows, "mp", lambda rows: (rows,))
-    d_act = jnp.dot(grad_rows_all, w_down.T, preferred_element_type=jnp.float32)
+    d_act = lax.optimization_barrier(
+        jnp.dot(grad_rows_all, w_down.T, preferred_element_type=jnp.float32)
+    )
     d_gate = (d_act * up_f * sig_gate * (1.0 + gate_f * (1.0 - sig_gate))).astype(jnp.bfloat16)
     d_up = (d_act * gate_f * sig_gate).astype(jnp.bfloat16)
     norm2_part = jnp.dot(d_gate, w_gate.T, preferred_element_type=jnp.float32) + jnp.dot(
@@ -460,10 +471,10 @@
         lax.axis_index("mp") * heads_here,
         0,
     )
-    gain1_sum, gain2_sum, gate_sum = lax.psum(
-        lax.psum((gain1_part, gain2_part, gate_full), "mp"), "dp"
-    )
-
+    gains = tree_sum(tree_sum(jnp.concatenate([gain1_part, gain2_part, gate_full]), "mp"), "dp")
+    gain1_sum, gain2_sum, gate_sum = jnp.split(
+        gains, [gain1_part.shape[0], gain1_part.shape[0] + gain2_part.shape[0]]
+    )
     qkv_sum = over_dp(jnp.concatenate([grad_query, grad_key, grad_value], axis=1), 0)
     query_sum, key_sum, value_sum = jnp.split(qkv_sum, 3, axis=1)
     return (

time: 1610 us -> 1590 us (0.988)
  blocking collectives: 40.8 us -> 0 us
  waiting for transfers between devices: 561 us -> 592 us
  other arithmetic: 97.7 us -> 114 us
    psum x2 -> x0, blocking collectives: 40.8 us -> none  [the longest x1 22.9 us: local(): lax.psum(lax.psum((gain1_part, gain2_part, gate_full), 'mp'), 'dp')]
    ppermute x9, waiting for transfers between devices: 140 us -> 100 us  [ring_gather(): ahead = lax.ppermute(ahead, axis, ring_pairs(n, 1))]
    ppermute x0 -> x5, waiting for transfers between devices: none -> 39 us  [tree_sum(): value = value + lax.ppermute(value, axis, [(j, j ^ step) for j in range(n)])]
    all_to_all x1, waiting for transfers between devices: 0.01 us -> 23.9 us  [local(): mixed = lax.all_to_all(mixed_cols, 'mp', 0, 1, tiled=True)]
    convert_element_type x0 -> x1, other arithmetic: none -> 19.1 us  [local(): d_up = (d_act * gate_f * sig_gate).astype(jnp.bfloat16)]
  transfers between devices with their start and end apart: 48 -> 53, of which waited for: 31 -> 35; matrix products, arithmetic and copies ran while one was open for 37% -> 35% of each run, Pallas kernels for 8% -> 8%
where the time goes in v7:
time: 1590 us; the launch traced here: 1580 us
  waiting for transfers between devices  592 us (37%)
  matrix products  446 us (28%)
  local copies, waits for them, and re-layouts  174 us (11%)
  Pallas kernels  127 us (8%)
  other arithmetic  114 us (7%)
  starting transfers between devices  109 us (7%)
  between operations  17.9 us (1%)
    ppermute x9, waiting for transfers between devices, ring_scatter(): behind = lax.ppermute(behind.astype(kind), axis, ring_pairs(n, -1))  169 us
    ppermute x9, waiting for transfers between devices, ring_scatter(): ahead = lax.ppermute(ahead.astype(kind), axis, ring_pairs(n, 1))  127 us
    ppermute x9, waiting for transfers between devices, ring_gather(): behind = lax.ppermute(behind, axis, ring_pairs(n, -1))  104 us
    ppermute x9, waiting for transfers between devices, ring_gather(): ahead = lax.ppermute(ahead, axis, ring_pairs(n, 1))  100 us
    pallas_call x1, Pallas kernels, attention_bwd(): pl.pallas_call(functools.partial(_bwd_kernel, scale, seg), grid=(H, nq),...  76.2 us
    dot_general x21, matrix products, project_qkv(): jnp.dot(rows, weight, preferred_element_type=jnp.float32)  57.8 us
    dot_general x14, matrix products, project_ffn(): jnp.dot(rows, weight, preferred_element_type=jnp.float32)  54.6 us
    dynamic_update_slice x35, local copies, waits for them, and re-layouts, ring_gather(): lax.dynamic_update_slice_in_dim(out, part, start, 0)  51.1 us
  transfers between devices with their start and end apart: 53, of which 35 were waited for; matrix products, arithmetic and copies ran while one was open for 35% of the time, Pallas kernels for 8%

profile of v7, /device:TPU:0, one launch (start us, length us, event | category | flops | bytes accessed | tf_op | source)
XLA Modules:
  0.0 1579.6 jit_solution(9652047218978248196)
XLA Ops:
  40.0 21.7 %collective-permute-done.1 = bf16[256,2048]{1,0:T(8,128)(2,1)S(1)} collective-permute-done((bf16[256,2048]{1,0:T(8,128)(2,1)}, bf16[256,2048]{1,0:T(8,128)(2,1)S(1)}, u32[]{:S(2)}, u32[]{:S(2)}) %collective-permute-start.1) | collective-permute-done | bytes 1048608 | tf_op jit(solution)/shard_map/ppermute | solution.py:91
  66.4 20.1 %collective-permute-done = bf16[256,2048]{1,0:T(8,128)(2,1)} collective-permute-done((bf16[256,2048]{1,0:T(8,128)(2,1)}, bf16[256,2048]{1,0:T(8,128)(2,1)}, u32[]{:S(2)}, u32[]{:S(2)}) %collective-permute-start) | collective-permute-done | bytes 1048608 | tf_op jit(solution)/shard_map/ppermute | solution.py:90
  115.4 18.0 %collective-permute-start.5 = (bf16[256,2048]{1,0:T(8,128)(2,1)}, bf16[256,2048]{1,0:T(8,128)(2,1)}, u32[]{:S(2)}, u32[]{:S(2)}) collective-permute-start(bf16[256,2048]{1,0:T(8,128)(2,1)} %collective-permute-done.3), channel_id=1, source_target_pairs={{0,3},{1,0},{2,1},{3,2},{4,7},{5,4},{6,5},{7,6},{8,11},{9,8},{10,9... | collective-permute-start | bytes 3145736 | tf_op jit(solution)/shard_map/ppermute | solution.py:91
  149.3 10.3 collective-permute-done.5
  164.0 12.1 collective-permute-done.4
  248.4 24.0 %collective-permute-done.12 = bf16[256,2048]{1,0:T(8,128)(2,1)S(1)} collective-permute-done((bf16[256,2048]{1,0:T(8,128)(2,1)S(1)}, bf16[256,2048]{1,0:T(8,128)(2,1)S(1)}, u32[]{:S(2)}, u32[]{:S(2)}) %collective-permute-start.12) | collective-permute-done | bytes 1048608 | tf_op jit(solution)/shard_map/ppermute | solution.py:90
  272.4 17.9 %collective-permute-start.14 = (bf16[256,2048]{1,0:T(8,128)(2,1)S(1)}, bf16[256,2048]{1,0:T(8,128)(2,1)}, u32[]{:S(2)}, u32[]{:S(2)}) collective-permute-start(bf16[256,2048]{1,0:T(8,128)(2,1)S(1)} %collective-permute-done.12), channel_id=1, source_target_pairs={{0,1},{1,2},{2,3},{3,0},{4,5},{5,6},{6,7},{7,4},{8,9},{9,10},{10,1... | collective-permute-start | bytes 3145736 | tf_op jit(solution)/shard_map/ppermute | solution.py:90
  294.8 50.8 %shard_map.220 = (f32[4,2048,128]{2,1,0:T(8,128)}, f32[4,2048,1]{2,1,0:T(8,128)}) custom-call(bf16[4,2048,128]{2,1,0:T(8,128)(2,1)} %bitcast.199, bf16[4,2048,128]{2,1,0:T(8,128)(2,1)} %bitcast.197, bf16[4,2048,128]{2,1,0:T(8,128)(2,1)} %bitcast.195, s32[2048,1]{1,0:T(8,128)} %copy.258.docq_ref, s32[1,2048]{1,0:T(1,128)} %bitcast.221), custom_call_target="tpu_custom_call" | custom-call | flops 8589934592 | bytes 10485760 | tf_op jit(solution)/shard_map/pallas_call | solution.py:219
  363.7 10.1 collective-permute-done.16
  374.8 20.3 %collective-permute-done.17 = bf16[256,2048]{1,0:T(8,128)(2,1)S(1)} collective-permute-done((bf16[256,2048]{1,0:T(8,128)(2,1)}, bf16[256,2048]{1,0:T(8,128)(2,1)S(1)}, u32[]{:S(2)}, u32[]{:S(2)}) %collective-permute-start.17) | collective-permute-done | bytes 1048608 | tf_op jit(solution)/shard_map/ppermute | solution.py:91
  400.0 6.2 fusion.46
  413.5 10.7 copy.259
  432.8 24.8 %fusion.136 = f32[2048,2048]{1,0:T(8,128)} fusion(bf16[2048,2048]{1,0:T(8,128)(2,1)} %constant_dynamic-update-slice_fusion.14, bf16[2048,2048]{1,0:T(8,128)(2,1)} %param.23), kind=kOutput, calls=%fused_computation.299 | convolution fusion | flops 17179869184 | bytes 33554432 | tf_op jit(solution)/shard_map/dot_general | solution.py:380
  457.6 23.9 %all-to-all-done = bf16[4,512,512]{2,1,0:T(8,128)(2,1)} async-done(((bf16[4,512,512]{2,1,0:T(8,128)(2,1)}), bf16[4,512,512]{2,1,0:T(8,128)(2,1)}, u32[]{:S(2)}, u32[]{:S(2)}) %all-to-all-start) | async-done | bytes 2097184 | tf_op jit(solution)/shard_map/all_to_all | solution.py:360
  485.6 9.8 multiply_reduce_fusion.4
  503.0 8.4 fusion.40
  512.4 8.2 fusion.41
  520.6 25.4 %collective-permute-done.7 = bf16[256,2048]{1,0:T(8,128)(2,1)S(1)} collective-permute-done((bf16[256,2048]{1,0:T(8,128)(2,1)}, bf16[256,2048]{1,0:T(8,128)(2,1)S(1)}, u32[]{:S(2)}, u32[]{:S(2)}) %collective-permute-start.7) | collective-permute-done | bytes 1048608 | tf_op jit(solution)/shard_map/ppermute | solution.py:91
  549.8 6.2 fusion.60
  556.0 5.9 fusion.59
  571.8 18.5 %collective-permute-done.9 = bf16[256,2048]{1,0:T(8,128)(2,1)S(1)} collective-permute-done((bf16[256,2048]{1,0:T(8,128)(2,1)S(1)}, bf16[256,2048]{1,0:T(8,128)(2,1)S(1)}, u32[]{:S(2)}, u32[]{:S(2)}) %collective-permute-start.9) | collective-permute-done | bytes 1048608 | tf_op jit(solution)/shard_map/ppermute | solution.py:91
  606.8 29.5 %collective-permute-done.10 = bf16[256,2048]{1,0:T(8,128)(2,1)S(1)} collective-permute-done((bf16[256,2048]{1,0:T(8,128)(2,1)S(1)}, bf16[256,2048]{1,0:T(8,128)(2,1)S(1)}, u32[]{:S(2)}, u32[]{:S(2)}) %collective-permute-start.10) | collective-permute-done | bytes 1048608 | tf_op jit(solution)/shard_map/ppermute | solution.py:90
  646.4 19.1 %fusion.9 = (bf16[2048,2048]{1,0:T(8,128)(2,1)}, bf16[2048,2048]{1,0:T(8,128)(2,1)}, bf16[2048,2048]{1,0:T(8,128)(2,1)}) fusion(f32[2048,2048]{1,0:T(8,128)} %fusion.136, bf16[2048,2048]{1,0:T(8,128)(2,1)S(1)} %fusion.61, bf16[2048,2048]{1,0:T(8,128)(2,1)S(1)} %fusion.55), kind=kLoop, calls=%fused_computation.15 | loop fusion | flops 75497472 | bytes 58720256 | tf_op jit(solution)/shard_map/convert_element_type | solution.py:383
  665.6 24.4 %fusion.137 = f32[2048,2048]{1,0:T(8,128)} fusion(bf16[2048,2048]{1,0:T(8,128)(2,1)} %get-tuple-element.129, bf16[2048,2048]{1,0:T(8,128)(2,1)} %param.21), kind=kOutput, calls=%fused_computation.300 | convolution fusion | flops 17179869184 | bytes 33554432 | tf_op jit(solution)/shard_map/dot_general | solution.py:384
  689.9 26.4 %convolution_add_fusion = f32[2048,2048]{1,0:T(8,128)} fusion(f32[2048,2048]{1,0:T(8,128)} %fusion.137, bf16[2048,2048]{1,0:T(8,128)(2,1)} %get-tuple-element.130, bf16[2048,2048]{1,0:T(8,128)(2,1)} %param.22), kind=kOutput, calls=%fused_computation.17 | convolution fusion | flops 17184063488 | bytes 50331648 | tf_op jit(solution)/shard_map/dot_general | solution.py:384
  719.7 23.7 %convolution_convert_fusion.3 = bf16[2048,2048]{1,0:T(8,128)(2,1)} fusion(bf16[2048,2048]{1,0:T(8,128)(2,1)} %constant_dynamic-update-slice_fusion.7, bf16[2048,2048]{1,0:T(8,128)(2,1)} %get-tuple-element.129), kind=kOutput, calls=%fused_computation.26 | convolution fusion | flops 17184063488 | bytes 25165824 | tf_op jit(solution)/shard_map/dot_general | solution.py:390
  743.5 24.0 %convolution_convert_fusion.2 = bf16[2048,2048]{1,0:T(8,128)(2,1)} fusion(bf16[2048,2048]{1,0:T(8,128)(2,1)} %constant_dynamic-update-slice_fusion.7, bf16[2048,2048]{1,0:T(8,128)(2,1)} %get-tuple-element.130), kind=kOutput, calls=%fused_computation.25 | convolution fusion | flops 17184063488 | bytes 25165824 | tf_op jit(solution)/shard_map/dot_general | solution.py:391
  774.6 24.1 %collective-permute-done.18 = bf16[256,2048]{1,0:T(8,128)(2,1)S(1)} collective-permute-done((bf16[256,2048]{1,0:T(8,128)(2,1)S(1)}, bf16[256,2048]{1,0:T(8,128)(2,1)S(1)}, u32[]{:S(2)}, u32[]{:S(2)}) %collective-permute-start.18) | collective-permute-done | bytes 1048608 | tf_op jit(solution)/shard_map/ppermute | solution.py:114
  798.6 20.9 %collective-permute-done.21 = bf16[256,2048]{1,0:T(8,128)(2,1)S(1)} collective-permute-done((bf16[256,2048]{1,0:T(8,128)(2,1)S(1)}, bf16[256,2048]{1,0:T(8,128)(2,1)S(1)}, u32[]{:S(2)}, u32[]{:S(2)}) %collective-permute-start.21) | collective-permute-done | bytes 1048608 | tf_op jit(solution)/shard_map/ppermute | solution.py:115
  827.6 25.6 %convolution_convert_fusion.1 = bf16[2048,2048]{1,0:T(8,128)(2,1)} fusion(bf16[2048,2048]{1,0:T(8,128)(2,1)} %get-tuple-element.135, bf16[2048,2048]{1,0:T(8,128)(2,1)} %constant_dynamic-update-slice_fusion.14), kind=kOutput, calls=%fused_computation.24 | convolution fusion | flops 17184063488 | bytes 25165824 | tf_op jit(solution)/shard_map/dot_general | solution.py:392
  854.3 18.3 %collective-permute-done.22 = bf16[256,2048]{1,0:T(8,128)(2,1)} collective-permute-done((bf16[256,2048]{1,0:T(8,128)(2,1)}, bf16[256,2048]{1,0:T(8,128)(2,1)}, u32[]{:S(2)}, u32[]{:S(2)}) %collective-permute-start.22) | collective-permute-done | bytes 1048608 | tf_op jit(solution)/shard_map/ppermute | solution.py:115
  872.6 5.2 add_convert_fusion.12
  882.0 23.9 %collective-permute-done.20 = bf16[256,2048]{1,0:T(8,128)(2,1)} collective-permute-done((bf16[256,2048]{1,0:T(8,128)(2,1)}, bf16[256,2048]{1,0:T(8,128)(2,1)}, u32[]{:S(2)}, u32[]{:S(2)}) %collective-permute-start.20) | collective-permute-done | bytes 1048608 | tf_op jit(solution)/shard_map/ppermute | solution.py:114
  905.9 19.4 %collective-permute-done.23 = bf16[256,2048]{1,0:T(8,128)(2,1)} collective-permute-done((bf16[256,2048]{1,0:T(8,128)(2,1)S(1)}, bf16[256,2048]{1,0:T(8,128)(2,1)}, u32[]{:S(2)}, u32[]{:S(2)}) %collective-permute-start.23) | collective-permute-done | bytes 1048608 | tf_op jit(solution)/shard_map/ppermute | solution.py:115
  933.7 9.8 convolution_convert_fusion.7
  949.5 24.2 %fusion.135 = f32[2048,2048]{1,0:T(8,128)} fusion(bf16[2048,2048]{1,0:T(8,128)(2,1)} %get-tuple-element.135, bf16[2048,2048]{1,0:T(8,128)(2,1)} %param.23), kind=kOutput, calls=%fused_computation.298 | convolution fusion | flops 17179869184 | bytes 33554432 | tf_op jit(solution)/shard_map/dot_general | solution.py:377
  973.8 22.8 %all-to-all-done.1 = bf16[512,4,512]{2,0,1:T(8,128)(2,1)} async-done(((bf16[512,4,512]{2,0,1:T(8,128)(2,1)}), bf16[512,4,512]{2,0,1:T(8,128)(2,1)}, u32[]{:S(2)}, u32[]{:S(2)}) %all-to-all-start.1) | async-done | bytes 2097184 | tf_op jit(solution)/shard_map/all_to_all | solution.py:406
  1000.7 5.3 reshape.367
  1016.2 8.6 multiply_reduce_fusion
  1027.8 9.4 fusion.97
  1038.1 10.7 convolution_convert_fusion
  1064.4 76.2 %shard_map.221 = (f32[4,2048,128]{2,1,0:T(8,128)}, f32[4,2048,128]{2,1,0:T(8,128)}, f32[4,2048,128]{2,1,0:T(8,128)}) custom-call(bf16[4,2048,128]{2,1,0:T(8,128)(2,1)} %bitcast.201, bf16[4,2048,128]{2,1,0:T(8,128)(2,1)} %bitcast.198, bf16[4,2048,128]{2,1,0:T(8,128)(2,1)} %bitcast.196, bf16[4,2048,128]{2,1,0:T(8,128)(2,1)} %get-tuple-element.254.do_ref, ...), custom_call_target="tpu_custom_call" | custom-call | flops 21474836480 | bytes 25165824 | tf_op jit(solution)/shard_map/pallas_call | solution.py:244
  1143.7 7.5 fusion.50
  1156.1 8.0 fusion.53
  1168.4 9.8 convolution_convert_fusion.5
  1178.3 10.2 convolution_convert_fusion.4
  1188.5 8.5 fusion.139
  1197.0 5.8 reduce-scatter.15.cloned.1.call-done
  1204.6 10.0 fusion.54
  1218.6 8.7 convolution_convert_fusion.6
  1227.3 8.3 fusion.138
  1235.6 11.4 pad_maximum_fusion
  1247.0 26.3 %add_add_fusion = f32[2048,2048]{1,0:T(8,128)} fusion(f32[2048,2048]{1,0:T(8,128)} %fusion.138, f32[2048,2048]{1,0:T(8,128)} %fusion.139, bf16[2048,512]{0,1:T(8,128)(2,1)} %bitcast.190, bf16[2048,512]{1,0:T(8,128)(2,1)} %param.17), kind=kOutput, calls=%fused_computation.16 | convolution fusion | flops 4303355904 | bytes 54525952 | tf_op jit(solution)/shard_map/dot_general | solution.py:464
  1286.1 17.6 %collective-permute-done.30 = bf16[256,2048]{1,0:T(8,128)(2,1)S(1)} collective-permute-done((bf16[256,2048]{1,0:T(8,128)(2,1)S(1)}, bf16[256,2048]{1,0:T(8,128)(2,1)S(1)}, u32[]{:S(2)}, u32[]{:S(2)}) %collective-permute-start.30) | collective-permute-done | bytes 1048608 | tf_op jit(solution)/shard_map/ppermute | solution.py:114
  1303.7 22.2 %collective-permute-done.33 = bf16[256,2048]{1,0:T(8,128)(2,1)S(1)} collective-permute-done((bf16[256,2048]{1,0:T(8,128)(2,1)S(1)}, bf16[256,2048]{1,0:T(8,128)(2,1)S(1)}, u32[]{:S(2)}, u32[]{:S(2)}) %collective-permute-start.33) | collective-permute-done | bytes 1048608 | tf_op jit(solution)/shard_map/ppermute | solution.py:115
  1332.7 16.0 %collective-permute-done.24 = bf16[256,2048]{1,0:T(8,128)(2,1)S(1)} collective-permute-done((bf16[256,2048]{1,0:T(8,128)(2,1)S(1)}, bf16[256,2048]{1,0:T(8,128)(2,1)S(1)}, u32[]{:S(2)}, u32[]{:S(2)}) %collective-permute-start.24) | collective-permute-done | bytes 1048608 | tf_op jit(solution)/shard_map/ppermute | solution.py:114
  1348.7 22.1 %collective-permute-done.27 = bf16[256,2048]{1,0:T(8,128)(2,1)S(1)} collective-permute-done((bf16[256,2048]{1,0:T(8,128)(2,1)S(1)}, bf16[256,2048]{1,0:T(8,128)(2,1)S(1)}, u32[]{:S(2)}, u32[]{:S(2)}) %collective-permute-start.27) | collective-permute-done | bytes 1048608 | tf_op jit(solution)/shard_map/ppermute | solution.py:115
  1378.9 14.8 collective-permute-done.31
  1393.7 22.0 %collective-permute-done.34 = bf16[256,2048]{1,0:T(8,128)(2,1)S(1)} collective-permute-done((bf16[256,2048]{1,0:T(8,128)(2,1)S(1)}, bf16[256,2048]{1,0:T(8,128)(2,1)S(1)}, u32[]{:S(2)}, u32[]{:S(2)}) %collective-permute-start.34) | collective-permute-done | bytes 1048608 | tf_op jit(solution)/shard_map/ppermute | solution.py:115
  1424.1 14.6 collective-permute-done.25
  1438.7 22.0 %collective-permute-done.28 = bf16[256,2048]{1,0:T(8,128)(2,1)} collective-permute-done((bf16[256,2048]{1,0:T(8,128)(2,1)}, bf16[256,2048]{1,0:T(8,128)(2,1)}, u32[]{:S(2)}, u32[]{:S(2)}) %collective-permute-start.28) | collective-permute-done | bytes 1048608 | tf_op jit(solution)/shard_map/ppermute | solution.py:115
  1467.7 16.0 %collective-permute-done.32 = bf16[256,2048]{1,0:T(8,128)(2,1)} collective-permute-done((bf16[256,2048]{1,0:T(8,128)(2,1)}, bf16[256,2048]{1,0:T(8,128)(2,1)}, u32[]{:S(2)}, u32[]{:S(2)}) %collective-permute-start.32) | collective-permute-done | bytes 1048608 | tf_op jit(solution)/shard_map/ppermute | solution.py:114
  1483.8 21.8 %collective-permute-done.35 = bf16[256,2048]{1,0:T(8,128)(2,1)} collective-permute-done((bf16[256,2048]{1,0:T(8,128)(2,1)}, bf16[256,2048]{1,0:T(8,128)(2,1)}, u32[]{:S(2)}, u32[]{:S(2)}) %collective-permute-start.35) | collective-permute-done | bytes 1048608 | tf_op jit(solution)/shard_map/ppermute | solution.py:115
  1511.3 36.6 %collective-permute-done.36 = f32[4112]{0:T(1024)S(1)} collective-permute-done((f32[4112]{0:T(1024)S(1)}, f32[4112]{0:T(1024)S(1)}, u32[]{:S(2)}, u32[]{:S(2)}) %collective-permute-start.36) | collective-permute-done | bytes 16480 | tf_op jit(solution)/shard_map/ppermute | solution.py:68
  (409 shorter events, 417.0 us)
Async XLA Ops:
  7.2 205.3 %all-gather.7.cloned.1.call-start = ((), (), s32[]{:S(2)}) async-start(), calls=%async_computation.8 | async-start | bytes 1310720 | tf_op jit(solution)/shard_map/all_gather | solution.py:311
  9.1 387.2 %all-gather.13.cloned.1.call-start = ((), (), s32[]{:S(2)}) async-start(), calls=%async_computation.17 | async-start | bytes 2396160 | tf_op jit(solution)/shard_map/all_gather | solution.py:26
  18.0 43.7 %collective-permute-start.1 = (bf16[256,2048]{1,0:T(8,128)(2,1)}, bf16[256,2048]{1,0:T(8,128)(2,1)S(1)}, u32[]{:S(2)}, u32[]{:S(2)}) collective-permute-start(bf16[256,2048]{1,0:T(8,128)(2,1)} %get-tuple-element.259), channel_id=1, source_target_pairs={{0,3},{1,0},{2,1},{3,2},{4,7},{5,4},{6,5},{7,6},{8,11},{9,8},{10,9... | collective-permute-start | bytes 3145736 | tf_op jit(solution)/shard_map/ppermute | solution.py:91
  23.1 63.5 %collective-permute-start = (bf16[256,2048]{1,0:T(8,128)(2,1)}, bf16[256,2048]{1,0:T(8,128)(2,1)}, u32[]{:S(2)}, u32[]{:S(2)}) collective-permute-start(bf16[256,2048]{1,0:T(8,128)(2,1)} %get-tuple-element.260), channel_id=1, source_target_pairs={{0,1},{1,2},{2,3},{3,0},{4,5},{5,6},{6,7},{7,4},{8,9},{9,10},{10,1... | collective-permute-start | bytes 3145736 | tf_op jit(solution)/shard_map/ppermute | solution.py:90
  24.7 266.1 %copy-start.44 = (s32[2048]{0:T(1024)}, s32[2048]{0:T(1024)S(1)}, u32[]{:S(2)}) copy-start(s32[2048]{0:T(1024)S(1)} %slice.70) | copy-start | bytes 24580
  31.9 174.7 %copy-start.49 = (f32[2048]{0:T(1024)}, f32[2048]{0:T(1024)S(1)}, u32[]{:S(2)}) copy-start(f32[2048]{0:T(1024)S(1)} %get-tuple-element.267) | copy-start | bytes 24580
  32.0 379.5 %copy-start.39 = (f32[2048]{0:T(1024)}, f32[2048]{0:T(1024)S(1)}, u32[]{:S(2)}) copy-start(f32[2048]{0:T(1024)S(1)} %get-tuple-element.266) | copy-start | bytes 24580
  61.7 157.1 %copy-start.28 = (bf16[256,2048]{1,0:T(8,128)(2,1)}, bf16[256,2048]{1,0:T(8,128)(2,1)S(1)}, u32[]{:S(2)}) copy-start(bf16[256,2048]{1,0:T(8,128)(2,1)S(1)} %collective-permute-done.1) | copy-start | bytes 3145732
  61.7 44.8 %collective-permute-start.3 = (bf16[256,2048]{1,0:T(8,128)(2,1)S(1)}, bf16[256,2048]{1,0:T(8,128)(2,1)}, u32[]{:S(2)}, u32[]{:S(2)}) collective-permute-start(bf16[256,2048]{1,0:T(8,128)(2,1)S(1)} %collective-permute-done.1), channel_id=1, source_target_pairs={{0,3},{1,0},{2,1},{3,2},{4,7},{5,4},{6,5},{7,6},{8,11},{9,8},{10,9... | collective-permute-start | bytes 3145736 | tf_op jit(solution)/shard_map/ppermute | solution.py:91
  86.6 47.2 %collective-permute-start.2 = (bf16[256,2048]{1,0:T(8,128)(2,1)}, bf16[256,2048]{1,0:T(8,128)(2,1)}, u32[]{:S(2)}, u32[]{:S(2)}) collective-permute-start(bf16[256,2048]{1,0:T(8,128)(2,1)} %collective-permute-done), channel_id=1, source_target_pairs={{0,1},{1,2},{2,3},{3,0},{4,5},{5,6},{6,7},{7,4},{8,9},{9,10},{10,1... | collective-permute-start | bytes 3145736 | tf_op jit(solution)/shard_map/ppermute | solution.py:90
  115.4 44.2 %collective-permute-start.5 = (bf16[256,2048]{1,0:T(8,128)(2,1)}, bf16[256,2048]{1,0:T(8,128)(2,1)}, u32[]{:S(2)}, u32[]{:S(2)}) collective-permute-start(bf16[256,2048]{1,0:T(8,128)(2,1)} %collective-permute-done.3), channel_id=1, source_target_pairs={{0,3},{1,0},{2,1},{3,2},{4,7},{5,4},{6,5},{7,6},{8,11},{9,8},{10,9... | collective-permute-start | bytes 3145736 | tf_op jit(solution)/shard_map/ppermute | solution.py:91
  138.9 37.2 %collective-permute-start.4 = (bf16[256,2048]{1,0:T(8,128)(2,1)}, bf16[256,2048]{1,0:T(8,128)(2,1)}, u32[]{:S(2)}, u32[]{:S(2)}) collective-permute-start(bf16[256,2048]{1,0:T(8,128)(2,1)} %collective-permute-done.2), channel_id=1, source_target_pairs={{0,1},{1,2},{2,3},{3,0},{4,5},{5,6},{6,7},{7,4},{8,9},{9,10},{10,1... | collective-permute-start | bytes 3145736 | tf_op jit(solution)/shard_map/ppermute | solution.py:90
  212.0 273.6 %all-gather.9.cloned.1.call-start = ((), (), s32[]{:S(2)}) async-start(), calls=%async_computation.9 | async-start | bytes 9437184 | tf_op jit(solution)/shard_map/all_gather | solution.py:310
  237.9 54.4 %copy-start.61 = (f32[4]{0:T(128)S(1)}, f32[4]{0:T(128)}, u32[]{:S(2)}) copy-start(f32[4]{0:T(128)} %param.19) | copy-start | bytes 52
  244.5 27.8 %collective-permute-start.12 = (bf16[256,2048]{1,0:T(8,128)(2,1)S(1)}, bf16[256,2048]{1,0:T(8,128)(2,1)S(1)}, u32[]{:S(2)}, u32[]{:S(2)}) collective-permute-start(bf16[256,2048]{1,0:T(8,128)(2,1)S(1)} %get-tuple-element.256), channel_id=1, source_target_pairs={{0,1},{1,2},{2,3},{3,0},{4,5},{5,6},{6,7},{7,4},{8,9},{9,10},{10,1... | collective-permute-start | bytes 3145736 | tf_op jit(solution)/shard_map/ppermute | solution.py:90
  244.5 50.3 %collective-permute-start.13 = (bf16[256,2048]{1,0:T(8,128)(2,1)}, bf16[256,2048]{1,0:T(8,128)(2,1)}, u32[]{:S(2)}, u32[]{:S(2)}) collective-permute-start(bf16[256,2048]{1,0:T(8,128)(2,1)} %get-tuple-element.255), channel_id=1, source_target_pairs={{0,3},{1,0},{2,1},{3,2},{4,7},{5,4},{6,5},{7,6},{8,11},{9,8},{10,9... | collective-permute-start | bytes 3145736 | tf_op jit(solution)/shard_map/ppermute | solution.py:91
  272.4 73.3 %collective-permute-start.14 = (bf16[256,2048]{1,0:T(8,128)(2,1)S(1)}, bf16[256,2048]{1,0:T(8,128)(2,1)}, u32[]{:S(2)}, u32[]{:S(2)}) collective-permute-start(bf16[256,2048]{1,0:T(8,128)(2,1)S(1)} %collective-permute-done.12), channel_id=1, source_target_pairs={{0,1},{1,2},{2,3},{3,0},{4,5},{5,6},{6,7},{7,4},{8,9},{9,10},{10,1... | collective-permute-start | bytes 3145736 | tf_op jit(solution)/shard_map/ppermute | solution.py:90
  292.2 119.2 %copy-start.51 = (f32[4]{0:T(128)}, f32[4]{0:T(128)S(1)}, u32[]{:S(2)}) copy-start(f32[4]{0:T(128)S(1)} %get-tuple-element.226) | copy-start | bytes 52
  292.3 119.2 %copy-start.53 = (f32[4]{0:T(128)}, f32[4]{0:T(128)S(1)}, u32[]{:S(2)}) copy-start(f32[4]{0:T(128)S(1)} %get-tuple-element.225) | copy-start | bytes 52
  294.8 58.7 %collective-permute-start.15 = (bf16[256,2048]{1,0:T(8,128)(2,1)}, bf16[256,2048]{1,0:T(8,128)(2,1)}, u32[]{:S(2)}, u32[]{:S(2)}) collective-permute-start(bf16[256,2048]{1,0:T(8,128)(2,1)} %collective-permute-done.13), channel_id=1, source_target_pairs={{0,3},{1,0},{2,1},{3,2},{4,7},{5,4},{6,5},{7,6},{8,11},{9,8},{10,9... | collective-permute-start | bytes 3145736 | tf_op jit(solution)/shard_map/ppermute | solution.py:91
  345.6 28.1 %collective-permute-start.16 = (bf16[256,2048]{1,0:T(8,128)(2,1)}, bf16[256,2048]{1,0:T(8,128)(2,1)S(1)}, u32[]{:S(2)}, u32[]{:S(2)}) collective-permute-start(bf16[256,2048]{1,0:T(8,128)(2,1)} %collective-permute-done.14), channel_id=1, source_target_pairs={{0,1},{1,2},{2,3},{3,0},{4,5},{5,6},{6,7},{7,4},{8,9},{9,10},{10,1... | collective-permute-start | bytes 3145736 | tf_op jit(solution)/shard_map/ppermute | solution.py:90
  353.6 41.6 %collective-permute-start.17 = (bf16[256,2048]{1,0:T(8,128)(2,1)}, bf16[256,2048]{1,0:T(8,128)(2,1)S(1)}, u32[]{:S(2)}, u32[]{:S(2)}) collective-permute-start(bf16[256,2048]{1,0:T(8,128)(2,1)} %collective-permute-done.15), channel_id=1, source_target_pairs={{0,3},{1,0},{2,1},{3,2},{4,7},{5,4},{6,5},{7,6},{8,11},{9,8},{10,9... | collective-permute-start | bytes 3145736 | tf_op jit(solution)/shard_map/ppermute | solution.py:91
  428.3 53.2 %all-to-all-start = ((bf16[4,512,512]{2,1,0:T(8,128)(2,1)}), bf16[4,512,512]{2,1,0:T(8,128)(2,1)}, u32[]{:S(2)}, u32[]{:S(2)}) async-start(bf16[4,512,512]{2,1,0:T(8,128)(2,1)} %convert_element_type.380), calls=%async_computation | async-start | bytes 4194304 | tf_op jit(solution)/shard_map/all_to_all | solution.py:360
  432.8 577.8 %reduce-scatter.7.cloned.1.call-start = ((), (), s32[]{:S(2)}) async-start(), calls=%async_computation.10 | async-start | bytes 9437184 | tf_op jit(solution)/shard_map/reduce_scatter | solution.py:297
  499.5 46.5 %collective-permute-start.7 = (bf16[256,2048]{1,0:T(8,128)(2,1)}, bf16[256,2048]{1,0:T(8,128)(2,1)S(1)}, u32[]{:S(2)}, u32[]{:S(2)}) collective-permute-start(bf16[256,2048]{1,0:T(8,128)(2,1)} %get-tuple-element.257), channel_id=1, source_target_pairs={{0,3},{1,0},{2,1},{3,2},{4,7},{5,4},{6,5},{7,6},{8,11},{9,8},{10,9... | collective-permute-start | bytes 3145736 | tf_op jit(solution)/shard_map/ppermute | solution.py:91
  501.9 45.9 %collective-permute-start.6 = (bf16[256,2048]{1,0:T(8,128)(2,1)}, bf16[256,2048]{1,0:T(8,128)(2,1)}, u32[]{:S(2)}, u32[]{:S(2)}) collective-permute-start(bf16[256,2048]{1,0:T(8,128)(2,1)} %get-tuple-element.258), channel_id=1, source_target_pairs={{0,1},{1,2},{2,3},{3,0},{4,5},{5,6},{6,7},{7,4},{8,9},{9,10},{10,1... | collective-permute-start | bytes 3145736 | tf_op jit(solution)/shard_map/ppermute | solution.py:90
  546.0 44.3 %collective-permute-start.9 = (bf16[256,2048]{1,0:T(8,128)(2,1)S(1)}, bf16[256,2048]{1,0:T(8,128)(2,1)S(1)}, u32[]{:S(2)}, u32[]{:S(2)}) collective-permute-start(bf16[256,2048]{1,0:T(8,128)(2,1)S(1)} %collective-permute-done.7), channel_id=1, source_target_pairs={{0,3},{1,0},{2,1},{3,2},{4,7},{5,4},{6,5},{7,6},{8,11},{9,8},{10,9... | collective-permute-start | bytes 3145736 | tf_op jit(solution)/shard_map/ppermute | solution.py:91
  547.8 44.9 %collective-permute-start.8 = (bf16[256,2048]{1,0:T(8,128)(2,1)}, bf16[256,2048]{1,0:T(8,128)(2,1)S(1)}, u32[]{:S(2)}, u32[]{:S(2)}) collective-permute-start(bf16[256,2048]{1,0:T(8,128)(2,1)} %collective-permute-done.6), channel_id=1, source_target_pairs={{0,1},{1,2},{2,3},{3,0},{4,5},{5,6},{6,7},{7,4},{8,9},{9,10},{10,1... | collective-permute-start | bytes 3145736 | tf_op jit(solution)/shard_map/ppermute | solution.py:90
  590.3 50.8 %collective-permute-start.11 = (bf16[256,2048]{1,0:T(8,128)(2,1)S(1)}, bf16[256,2048]{1,0:T(8,128)(2,1)S(1)}, u32[]{:S(2)}, u32[]{:S(2)}) collective-permute-start(bf16[256,2048]{1,0:T(8,128)(2,1)S(1)} %collective-permute-done.9), channel_id=1, source_target_pairs={{0,3},{1,0},{2,1},{3,2},{4,7},{5,4},{6,5},{7,6},{8,11},{9,8},{10,9... | collective-permute-start | bytes 3145736 | tf_op jit(solution)/shard_map/ppermute | solution.py:91
  592.7 43.5 %collective-permute-start.10 = (bf16[256,2048]{1,0:T(8,128)(2,1)S(1)}, bf16[256,2048]{1,0:T(8,128)(2,1)S(1)}, u32[]{:S(2)}, u32[]{:S(2)}) collective-permute-start(bf16[256,2048]{1,0:T(8,128)(2,1)S(1)} %collective-permute-done.8), channel_id=1, source_target_pairs={{0,1},{1,2},{2,3},{3,0},{4,5},{5,6},{6,7},{7,4},{8,9},{9,10},{10,1... | collective-permute-start | bytes 3145736 | tf_op jit(solution)/shard_map/ppermute | solution.py:90
  743.5 269.9 %reduce-scatter.9.cloned.1.call-start = ((), (), s32[]{:S(2)}) async-start(), calls=%async_computation.11 | async-start | bytes 9437184 | tf_op jit(solution)/shard_map/reduce_scatter | solution.py:297
  767.5 294.2 %reduce-scatter.11.cloned.1.call-start = ((), (), s32[]{:S(2)}) async-start(), calls=%async_computation.12 | async-start | bytes 9437184 | tf_op jit(solution)/shard_map/reduce_scatter | solution.py:297
  770.7 27.9 %collective-permute-start.18 = (bf16[256,2048]{1,0:T(8,128)(2,1)S(1)}, bf16[256,2048]{1,0:T(8,128)(2,1)S(1)}, u32[]{:S(2)}, u32[]{:S(2)}) collective-permute-start(bf16[256,2048]{1,0:T(8,128)(2,1)S(1)} %get-tuple-element.252), channel_id=1, source_target_pairs={{0,1},{1,2},{2,3},{3,0},{4,5},{5,6},{6,7},{7,4},{8,9},{9,10},{10,1... | collective-permute-start | bytes 3145736 | tf_op jit(solution)/shard_map/ppermute | solution.py:114
  772.5 47.1 %collective-permute-start.21 = (bf16[256,2048]{1,0:T(8,128)(2,1)S(1)}, bf16[256,2048]{1,0:T(8,128)(2,1)S(1)}, u32[]{:S(2)}, u32[]{:S(2)}) collective-permute-start(bf16[256,2048]{1,0:T(8,128)(2,1)S(1)} %get-tuple-element.253), channel_id=1, source_target_pairs={{0,3},{1,0},{2,1},{3,2},{4,7},{5,4},{6,5},{7,6},{8,11},{9,8},{10,9... | collective-permute-start | bytes 3145736 | tf_op jit(solution)/shard_map/ppermute | solution.py:115
  823.8 29.5 %collective-permute-start.19 = (bf16[256,2048]{1,0:T(8,128)(2,1)}, bf16[256,2048]{1,0:T(8,128)(2,1)S(1)}, u32[]{:S(2)}, u32[]{:S(2)}) collective-permute-start(bf16[256,2048]{1,0:T(8,128)(2,1)} %get-tuple-element.250), channel_id=1, source_target_pairs={{0,1},{1,2},{2,3},{3,0},{4,5},{5,6},{6,7},{7,4},{8,9},{9,10},{10,1... | collective-permute-start | bytes 3145736 | tf_op jit(solution)/shard_map/ppermute | solution.py:114
  825.0 47.6 %collective-permute-start.22 = (bf16[256,2048]{1,0:T(8,128)(2,1)}, bf16[256,2048]{1,0:T(8,128)(2,1)}, u32[]{:S(2)}, u32[]{:S(2)}) collective-permute-start(bf16[256,2048]{1,0:T(8,128)(2,1)} %get-tuple-element.251), channel_id=1, source_target_pairs={{0,3},{1,0},{2,1},{3,2},{4,7},{5,4},{6,5},{7,6},{8,11},{9,8},{10,9... | collective-permute-start | bytes 3145736 | tf_op jit(solution)/shard_map/ppermute | solution.py:115
  877.8 28.2 %collective-permute-start.20 = (bf16[256,2048]{1,0:T(8,128)(2,1)}, bf16[256,2048]{1,0:T(8,128)(2,1)}, u32[]{:S(2)}, u32[]{:S(2)}) collective-permute-start(bf16[256,2048]{1,0:T(8,128)(2,1)} %get-tuple-element.248), channel_id=1, source_target_pairs={{0,1},{1,2},{2,3},{3,0},{4,5},{5,6},{6,7},{7,4},{8,9},{9,10},{10,1... | collective-permute-start | bytes 3145736 | tf_op jit(solution)/shard_map/ppermute | solution.py:114
  877.8 47.6 %collective-permute-start.23 = (bf16[256,2048]{1,0:T(8,128)(2,1)S(1)}, bf16[256,2048]{1,0:T(8,128)(2,1)}, u32[]{:S(2)}, u32[]{:S(2)}) collective-permute-start(bf16[256,2048]{1,0:T(8,128)(2,1)S(1)} %get-tuple-element.249), channel_id=1, source_target_pairs={{0,3},{1,0},{2,1},{3,2},{4,7},{5,4},{6,5},{7,6},{8,11},{9,8},{10,9... | collective-permute-start | bytes 3145736 | tf_op jit(solution)/shard_map/ppermute | solution.py:115
  882.0 47.0 %copy-start.2 = (f32[512,2048]{1,0:T(8,128)S(1)}, f32[512,2048]{1,0:T(8,128)}, u32[]{:S(2)}) copy-start(f32[512,2048]{1,0:T(8,128)} %copy-done.1) | copy-start | bytes 12582916
  882.0 47.0 %copy-start.43 = (f32[2048]{0:T(1024)S(1)}, f32[2048]{0:T(1024)}, u32[]{:S(2)}) copy-start(f32[2048]{0:T(1024)} %param.20) | copy-start | bytes 24580
  882.0 47.0 %copy-start.48 = (f32[512]{0:T(512)S(1)}, f32[512]{0:T(512)}, u32[]{:S(2)}) copy-start(f32[512]{0:T(512)} %copy-done.47) | copy-start | bytes 6148
  945.0 51.5 %all-to-all-start.1 = ((bf16[512,4,512]{2,0,1:T(8,128)(2,1)}), bf16[512,4,512]{2,0,1:T(8,128)(2,1)}, u32[]{:S(2)}, u32[]{:S(2)}) async-start(bf16[512,4,512]{2,0,1:T(8,128)(2,1)} %bitcast.194), calls=%async_computation.1 | async-start | bytes 4194304 | tf_op jit(solution)/shard_map/all_to_all | solution.py:406
  949.5 191.2 %all-gather.11.cloned.1.call-start = ((), (), s32[]{:S(2)}) async-start(), calls=%async_computation.15 | async-start | bytes 1198080 | tf_op jit(solution)/shard_map/all_gather | solution.py:26
  1038.1 140.1 %reduce-scatter.13.cloned.1.call-start = ((), (), s32[]{:S(2)}) async-start(), calls=%async_computation.13 | async-start | bytes 9437184 | tf_op jit(solution)/shard_map/reduce_scatter | solution.py:297
  1048.9 154.0 %reduce-scatter.15.cloned.1.call-start = ((), (), s32[]{:S(2)}) async-start(), calls=%async_computation.14 | async-start | bytes 1310720 | tf_op jit(solution)/shard_map/reduce_scatter | solution.py:401
  1178.2 388.0 %reduce-scatter.17.cloned.1.call-start = ((), (), s32[]{:S(2)}) async-start(), calls=%async_computation.16 | async-start | bytes 7077888 | tf_op jit(solution)/shard_map/reduce_scatter | solution.py:297
  1275.8 27.9 %collective-permute-start.30 = (bf16[256,2048]{1,0:T(8,128)(2,1)S(1)}, bf16[256,2048]{1,0:T(8,128)(2,1)S(1)}, u32[]{:S(2)}, u32[]{:S(2)}) collective-permute-start(bf16[256,2048]{1,0:T(8,128)(2,1)S(1)} %get-tuple-element.236), channel_id=1, source_target_pairs={{0,1},{1,2},{2,3},{3,0},{4,5},{5,6},{6,7},{7,4},{8,9},{9,10},{10,1... | collective-permute-start | bytes 3145736 | tf_op jit(solution)/shard_map/ppermute | solution.py:114
  1275.9 50.0 %collective-permute-start.33 = (bf16[256,2048]{1,0:T(8,128)(2,1)S(1)}, bf16[256,2048]{1,0:T(8,128)(2,1)S(1)}, u32[]{:S(2)}, u32[]{:S(2)}) collective-permute-start(bf16[256,2048]{1,0:T(8,128)(2,1)S(1)} %get-tuple-element.237), channel_id=1, source_target_pairs={{0,3},{1,0},{2,1},{3,2},{4,7},{5,4},{6,5},{7,6},{8,11},{9,8},{10,9... | collective-permute-start | bytes 3145736 | tf_op jit(solution)/shard_map/ppermute | solution.py:115
  1282.2 66.4 %collective-permute-start.24 = (bf16[256,2048]{1,0:T(8,128)(2,1)S(1)}, bf16[256,2048]{1,0:T(8,128)(2,1)S(1)}, u32[]{:S(2)}, u32[]{:S(2)}) collective-permute-start(bf16[256,2048]{1,0:T(8,128)(2,1)S(1)} %get-tuple-element.244), channel_id=1, source_target_pairs={{0,1},{1,2},{2,3},{3,0},{4,5},{5,6},{6,7},{7,4},{8,9},{9,10},{10,1... | collective-permute-start | bytes 3145736 | tf_op jit(solution)/shard_map/ppermute | solution.py:114
  1282.3 88.5 %collective-permute-start.27 = (bf16[256,2048]{1,0:T(8,128)(2,1)S(1)}, bf16[256,2048]{1,0:T(8,128)(2,1)S(1)}, u32[]{:S(2)}, u32[]{:S(2)}) collective-permute-start(bf16[256,2048]{1,0:T(8,128)(2,1)S(1)} %get-tuple-element.245), channel_id=1, source_target_pairs={{0,3},{1,0},{2,1},{3,2},{4,7},{5,4},{6,5},{7,6},{8,11},{9,8},{10,9... | collective-permute-start | bytes 3145736 | tf_op jit(solution)/shard_map/ppermute | solution.py:115
  1328.8 64.9 %collective-permute-start.31 = (bf16[256,2048]{1,0:T(8,128)(2,1)S(1)}, bf16[256,2048]{1,0:T(8,128)(2,1)S(1)}, u32[]{:S(2)}, u32[]{:S(2)}) collective-permute-start(bf16[256,2048]{1,0:T(8,128)(2,1)S(1)} %get-tuple-element.234), channel_id=1, source_target_pairs={{0,1},{1,2},{2,3},{3,0},{4,5},{5,6},{6,7},{7,4},{8,9},{9,10},{10,1... | collective-permute-start | bytes 3145736 | tf_op jit(solution)/shard_map/ppermute | solution.py:114
  1329.8 85.9 %collective-permute-start.34 = (bf16[256,2048]{1,0:T(8,128)(2,1)S(1)}, bf16[256,2048]{1,0:T(8,128)(2,1)S(1)}, u32[]{:S(2)}, u32[]{:S(2)}) collective-permute-start(bf16[256,2048]{1,0:T(8,128)(2,1)S(1)} %get-tuple-element.235), channel_id=1, source_target_pairs={{0,3},{1,0},{2,1},{3,2},{4,7},{5,4},{6,5},{7,6},{8,11},{9,8},{10,9... | collective-permute-start | bytes 3145736 | tf_op jit(solution)/shard_map/ppermute | solution.py:115
  1375.0 63.6 %collective-permute-start.25 = (bf16[256,2048]{1,0:T(8,128)(2,1)}, bf16[256,2048]{1,0:T(8,128)(2,1)S(1)}, u32[]{:S(2)}, u32[]{:S(2)}) collective-permute-start(bf16[256,2048]{1,0:T(8,128)(2,1)} %get-tuple-element.242), channel_id=1, source_target_pairs={{0,1},{1,2},{2,3},{3,0},{4,5},{5,6},{6,7},{7,4},{8,9},{9,10},{10,1... | collective-permute-start | bytes 3145736 | tf_op jit(solution)/shard_map/ppermute | solution.py:114
  1376.0 47.8 %copy-start.55 = (f32[4]{0:T(128)S(1)}, f32[4]{0:T(128)}, u32[]{:S(2)}) copy-start(f32[4]{0:T(128)} %get-tuple-element.215) | copy-start | bytes 52
  1376.0 84.7 %collective-permute-start.28 = (bf16[256,2048]{1,0:T(8,128)(2,1)}, bf16[256,2048]{1,0:T(8,128)(2,1)}, u32[]{:S(2)}, u32[]{:S(2)}) collective-permute-start(bf16[256,2048]{1,0:T(8,128)(2,1)} %get-tuple-element.243), channel_id=1, source_target_pairs={{0,3},{1,0},{2,1},{3,2},{4,7},{5,4},{6,5},{7,6},{8,11},{9,8},{10,9... | collective-permute-start | bytes 3145736 | tf_op jit(solution)/shard_map/ppermute | solution.py:115
  1420.0 63.8 %collective-permute-start.32 = (bf16[256,2048]{1,0:T(8,128)(2,1)}, bf16[256,2048]{1,0:T(8,128)(2,1)}, u32[]{:S(2)}, u32[]{:S(2)}) collective-permute-start(bf16[256,2048]{1,0:T(8,128)(2,1)} %get-tuple-element.232), channel_id=1, source_target_pairs={{0,1},{1,2},{2,3},{3,0},{4,5},{5,6},{6,7},{7,4},{8,9},{9,10},{10,1... | collective-permute-start | bytes 3145736 | tf_op jit(solution)/shard_map/ppermute | solution.py:114
  1420.9 84.7 %collective-permute-start.35 = (bf16[256,2048]{1,0:T(8,128)(2,1)}, bf16[256,2048]{1,0:T(8,128)(2,1)}, u32[]{:S(2)}, u32[]{:S(2)}) collective-permute-start(bf16[256,2048]{1,0:T(8,128)(2,1)} %get-tuple-element.233), channel_id=1, source_target_pairs={{0,3},{1,0},{2,1},{3,2},{4,7},{5,4},{6,5},{7,6},{8,11},{9,8},{10,9... | collective-permute-start | bytes 3145736 | tf_op jit(solution)/shard_map/ppermute | solution.py:115
  1463.9 86.7 %collective-permute-start.26 = (bf16[256,2048]{1,0:T(8,128)(2,1)S(1)}, bf16[256,2048]{1,0:T(8,128)(2,1)S(1)}, u32[]{:S(2)}, u32[]{:S(2)}) collective-permute-start(bf16[256,2048]{1,0:T(8,128)(2,1)S(1)} %get-tuple-element.240), channel_id=1, source_target_pairs={{0,1},{1,2},{2,3},{3,0},{4,5},{5,6},{6,7},{7,4},{8,9},{9,10},{10,1... | collective-permute-start | bytes 3145736 | tf_op jit(solution)/shard_map/ppermute | solution.py:114
  1464.9 85.7 %collective-permute-start.29 = (bf16[256,2048]{1,0:T(8,128)(2,1)S(1)}, bf16[256,2048]{1,0:T(8,128)(2,1)S(1)}, u32[]{:S(2)}, u32[]{:S(2)}) collective-permute-start(bf16[256,2048]{1,0:T(8,128)(2,1)S(1)} %get-tuple-element.241), channel_id=1, source_target_pairs={{0,3},{1,0},{2,1},{3,2},{4,7},{5,4},{6,5},{7,6},{8,11},{9,8},{10,9... | collective-permute-start | bytes 3145736 | tf_op jit(solution)/shard_map/ppermute | solution.py:115
  1510.3 37.6 %collective-permute-start.36 = (f32[4112]{0:T(1024)S(1)}, f32[4112]{0:T(1024)S(1)}, u32[]{:S(2)}, u32[]{:S(2)}) collective-permute-start(f32[4112]{0:T(1024)S(1)} %pad_maximum_fusion.3), channel_id=1, source_target_pairs={{0,1},{1,0},{2,3},{3,2},{4,5},{5,4},{6,7},{7,6},{8,9},{9,8},{10,11... | collective-permute-start | bytes 49352 | tf_op jit(solution)/shard_map/ppermute | solution.py:68
  1548.0 5.5 collective-permute-start.37
  1553.5 2.1 collective-permute-start.38
  1555.6 3.8 collective-permute-start.39
  1559.4 5.7 collective-permute-start.40
  (55 other events, 514.1 us)
Sparse Core Ops, SparseCore 0:
  9.6 41.3 all-gather.6
  212.2 26.1 all-gather.12
  240.2 55.8 all-gather.8
  743.6 70.7 reduce-scatter.6
  817.7 71.5 reduce-scatter.8
  892.6 71.2 reduce-scatter.10
  1038.2 20.6 all-gather.10
  1062.4 71.2 reduce-scatter.12
  1178.4 24.4 reduce-scatter.14
  1247.1 60.0 reduce-scatter.16

commit v8 on v7

--- a/solution.py
+++ b/solution.py
@@ -102,11 +102,11 @@
 
 def ring_scatter(partial, axis, kind=jnp.bfloat16):
     n, place = lax.axis_size(axis), lax.axis_index(axis)
-    count = partial.shape[0] // n
+    count = partial.count // n
     half = count // 2
 
     def chunk(owner, start):
-        return lax.dynamic_slice_in_dim(partial, owner * count + start, half, 0).astype(jnp.float32)
+        return partial(owner * count + start, half).astype(jnp.float32)
 
     ahead = chunk((place - 1) % n, 0)
     behind = chunk((place + 1) % n, half)
@@ -116,6 +116,30 @@
         ahead = ahead.astype(jnp.float32) + chunk((place - 1 - step) % n, 0)
         behind = behind.astype(jnp.float32) + chunk((place + 1 + step) % n, half)
     return jnp.concatenate([ahead, behind], axis=0)
+
+
+class Rows:
+    def __init__(self, terms):
+        self.terms = terms
+        self.count = terms[0][0].shape[0]
+
+    def __call__(self, first, count):
+        total = None
+        for lhs, rhs in self.terms:
+            part = jnp.dot(
+                lax.dynamic_slice_in_dim(lhs, first, count, 0), rhs, preferred_element_type=jnp.float32
+            )
+            total = part if total is None else total + part
+        return total
+
+
+class Given:
+    def __init__(self, value):
+        self.value = value
+        self.count = value.shape[0]
+
+    def __call__(self, first, count):
+        return lax.dynamic_slice_in_dim(self.value, first, count, 0)
 
 
 def inverse_rms(values):
@@ -381,16 +405,11 @@
     )
     d_gate = (d_act * up_f * sig_gate * (1.0 + gate_f * (1.0 - sig_gate))).astype(jnp.bfloat16)
     d_up = (d_act * gate_f * sig_gate).astype(jnp.bfloat16)
-    norm2_part = jnp.dot(d_gate, w_gate.T, preferred_element_type=jnp.float32) + jnp.dot(
-        d_up, w_up.T, preferred_element_type=jnp.float32
-    )
-    norm2_part, normed2_all, act, d_gate, d_up = lax.optimization_barrier(
-        (norm2_part, normed2_all, act, d_gate, d_up)
-    )
+    normed2_all, act, d_gate, d_up = lax.optimization_barrier((normed2_all, act, d_gate, d_up))
     grad_gate = jnp.dot(normed2_all.T, d_gate, preferred_element_type=jnp.float32)
     grad_up = jnp.dot(normed2_all.T, d_up, preferred_element_type=jnp.float32)
     grad_down = jnp.dot(act.T, grad_rows_all, preferred_element_type=jnp.float32)
-    d_norm2 = ring_scatter(norm2_part, "mp")
+    d_norm2 = ring_scatter(Rows(((d_gate, w_gate.T), (d_up, w_up.T))), "mp")
     gate_w_sum = over_dp(grad_gate, 0)
     up_sum = over_dp(grad_up, 0)
     down_sum = over_dp(grad_down, 1)
@@ -408,7 +427,7 @@
     mlp_part, d_mixed, gate_w_sum, up_sum = lax.optimization_barrier(
         (mlp_part, d_mixed, gate_w_sum, up_sum)
     )
-    output = (resid + ring_scatter(mlp_part, "mp")).astype(jnp.bfloat16)
+    output = (resid + ring_scatter(Given(mlp_part), "mp")).astype(jnp.bfloat16)
     gate_part = jnp.sum(d_mixed * (mem_out - dot_out), axis=(1, 2)) * gate_vec * (1.0 - gate_vec)
     d_dot = ((1.0 - gate) * d_mixed).astype(jnp.bfloat16)
     d_mem = (gate * d_mixed).reshape(seg_shape)
@@ -458,10 +477,10 @@
     grad_query = jnp.dot(normed1_all.T, d_query, preferred_element_type=jnp.float32)
     grad_key = jnp.dot(normed1_all.T, d_key, preferred_element_type=jnp.float32)
     grad_value = jnp.dot(normed1_all.T, d_value, preferred_element_type=jnp.float32)
-    total_term = jnp.dot(d_query, w_query.T, preferred_element_type=jnp.float32)
-    total_term = total_term + jnp.dot(d_key, w_key.T, preferred_element_type=jnp.float32)
+    qkv_grads = jnp.concatenate([grad_query, grad_key, grad_value], axis=1).astype(jnp.bfloat16)
+    qkv_sum = over_dp(qkv_grads, 0)
     d_norm1 = ring_scatter(
-        total_term + jnp.dot(d_value, w_value.T, preferred_element_type=jnp.float32), "mp"
+        Rows(((d_query, w_query.T), (d_key, w_key.T), (d_value, w_value.T))), "mp"
     )
     gain1_part = jnp.sum(d_norm1 * x_rows * inverse1, axis=0)
     input_grad = d_resid + norm_backward(x_rows, inverse1, norm1_gain, d_norm1)
@@ -475,7 +494,6 @@
     gain1_sum, gain2_sum, gate_sum = jnp.split(
         gains, [gain1_part.shape[0], gain1_part.shape[0] + gain2_part.shape[0]]
     )
-    qkv_sum = over_dp(jnp.concatenate([grad_query, grad_key, grad_value], axis=1), 0)
     query_sum, key_sum, value_sum = jnp.split(qkv_sum, 3, axis=1)
     return (
         output,

time: 1590 us -> 1420 us (0.89)
  waiting for transfers between devices: 592 us -> 437 us
  matrix products: 446 us -> 470 us
  other arithmetic: 114 us -> 92.9 us
  starting transfers between devices: 109 us -> 92.4 us
    ppermute x9, waiting for transfers between devices: 169 us -> 74.5 us  [ring_scatter(): behind = lax.ppermute(behind.astype(kind), axis, ring_pairs(n, -1))]
    dot_general x5 -> x40, matrix products: 93.9 us -> 129 us  [__call__(): jnp.dot(lax.dynamic_slice_in_dim(lhs, first, count, 0), rhs, preferred_el...]
    ppermute x5, waiting for transfers between devices: 39 us -> 8.6 us  [tree_sum(): value = value + lax.ppermute(value, axis, [(j, j ^ step) for j in range(n)])]
    ppermute x9, waiting for transfers between devices: 127 us -> 101 us  [ring_scatter(): ahead = lax.ppermute(ahead.astype(kind), axis, ring_pairs(n, 1))]
  transfers between devices with their start and end apart: 53 -> 53, of which waited for: 35 -> 30; matrix products, arithmetic and copies ran while one was open for 35% -> 46% of each run, Pallas kernels for 8% -> 9%
where the time goes in v8:
time: 1420 us; the launch traced here: 1410 us
  matrix products  470 us (33%)
  waiting for transfers between devices  437 us (31%)
  local copies, waits for them, and re-layouts  173 us (12%)
  Pallas kernels  127 us (9%)
  other arithmetic  92.9 us (7%)
  starting transfers between devices  92.4 us (7%)
  between operations  18.2 us (1%)
    dot_general x40, matrix products, __call__(): jnp.dot(lax.dynamic_slice_in_dim(lhs, first, count, 0), rhs, preferred_el...  129 us
    ppermute x9, waiting for transfers between devices, ring_gather(): behind = lax.ppermute(behind, axis, ring_pairs(n, -1))  106 us
    ppermute x9, waiting for transfers between devices, ring_scatter(): ahead = lax.ppermute(ahead.astype(kind), axis, ring_pairs(n, 1))  101 us
    ppermute x9, waiting for transfers between devices, ring_gather(): ahead = lax.ppermute(ahead, axis, ring_pairs(n, 1))  99.3 us
    pallas_call x1, Pallas kernels, attention_bwd(): pl.pallas_call(functools.partial(_bwd_kernel, scale, seg), grid=(H, nq),...  76.5 us
    ppermute x9, waiting for transfers between devices, ring_scatter(): behind = lax.ppermute(behind.astype(kind), axis, ring_pairs(n, -1))  74.5 us
    dot_general x21, matrix products, project_qkv(): jnp.dot(rows, weight, preferred_element_type=jnp.float32)  54.9 us
    dot_general x14, matrix products, project_ffn(): jnp.dot(rows, weight, preferred_element_type=jnp.float32)  54.3 us
  transfers between devices with their start and end apart: 53, of which 30 were waited for; matrix products, arithmetic and copies ran while one was open for 46% of the time, Pallas kernels for 9%

profile of v8, /device:TPU:0, one launch (start us, length us, event | category | flops | bytes accessed | tf_op | source)
XLA Modules:
  0.0 1411.9 jit_solution(13327008048423517956)
XLA Ops:
  18.0 5.1 collective-permute-start.1
  39.4 22.3 %collective-permute-done.1 = bf16[256,2048]{1,0:T(8,128)(2,1)S(1)} collective-permute-done((bf16[256,2048]{1,0:T(8,128)(2,1)}, bf16[256,2048]{1,0:T(8,128)(2,1)S(1)}, u32[]{:S(2)}, u32[]{:S(2)}) %collective-permute-start.1) | collective-permute-done | bytes 1048608 | tf_op jit(solution)/shard_map/ppermute | solution.py:91
  66.5 20.1 %collective-permute-done = bf16[256,2048]{1,0:T(8,128)(2,1)} collective-permute-done((bf16[256,2048]{1,0:T(8,128)(2,1)}, bf16[256,2048]{1,0:T(8,128)(2,1)}, u32[]{:S(2)}, u32[]{:S(2)}) %collective-permute-start) | collective-permute-done | bytes 1048608 | tf_op jit(solution)/shard_map/ppermute | solution.py:90
  116.1 17.9 %collective-permute-start.5 = (bf16[256,2048]{1,0:T(8,128)(2,1)}, bf16[256,2048]{1,0:T(8,128)(2,1)}, u32[]{:S(2)}, u32[]{:S(2)}) collective-permute-start(bf16[256,2048]{1,0:T(8,128)(2,1)} %collective-permute-done.3), channel_id=1, source_target_pairs={{0,3},{1,0},{2,1},{3,2},{4,7},{5,4},{6,5},{7,6},{8,11},{9,8},{10,9... | collective-permute-start | bytes 3145736 | tf_op jit(solution)/shard_map/ppermute | solution.py:91
  150.1 10.1 collective-permute-done.5
  164.7 11.4 collective-permute-done.4
  245.1 24.0 %collective-permute-done.12 = bf16[256,2048]{1,0:T(8,128)(2,1)S(1)} collective-permute-done((bf16[256,2048]{1,0:T(8,128)(2,1)S(1)}, bf16[256,2048]{1,0:T(8,128)(2,1)S(1)}, u32[]{:S(2)}, u32[]{:S(2)}) %collective-permute-start.12) | collective-permute-done | bytes 1048608 | tf_op jit(solution)/shard_map/ppermute | solution.py:90
  269.1 16.0 %collective-permute-start.14 = (bf16[256,2048]{1,0:T(8,128)(2,1)S(1)}, bf16[256,2048]{1,0:T(8,128)(2,1)}, u32[]{:S(2)}, u32[]{:S(2)}) collective-permute-start(bf16[256,2048]{1,0:T(8,128)(2,1)S(1)} %collective-permute-done.12), channel_id=1, source_target_pairs={{0,1},{1,2},{2,3},{3,0},{4,5},{5,6},{6,7},{7,4},{8,9},{9,10},{10,1... | collective-permute-start | bytes 3145736 | tf_op jit(solution)/shard_map/ppermute | solution.py:90
  291.7 50.7 %shard_map.220 = (f32[4,2048,128]{2,1,0:T(8,128)}, f32[4,2048,1]{2,1,0:T(8,128)}) custom-call(bf16[4,2048,128]{2,1,0:T(8,128)(2,1)} %bitcast.257, bf16[4,2048,128]{2,1,0:T(8,128)(2,1)} %bitcast.253, bf16[4,2048,128]{2,1,0:T(8,128)(2,1)} %bitcast.255, s32[2048,1]{1,0:T(8,128)} %copy.258.docq_ref, s32[1,2048]{1,0:T(1,128)} %bitcast.275), custom_call_target="tpu_custom_call" | custom-call | flops 8589934592 | bytes 10485760 | tf_op jit(solution)/shard_map/pallas_call | solution.py:243
  360.5 10.2 collective-permute-done.16
  371.7 20.2 %collective-permute-done.17 = bf16[256,2048]{1,0:T(8,128)(2,1)S(1)} collective-permute-done((bf16[256,2048]{1,0:T(8,128)(2,1)}, bf16[256,2048]{1,0:T(8,128)(2,1)S(1)}, u32[]{:S(2)}, u32[]{:S(2)}) %collective-permute-start.17) | collective-permute-done | bytes 1048608 | tf_op jit(solution)/shard_map/ppermute | solution.py:91
  408.8 10.7 copy.259
  428.2 24.5 %fusion.252 = f32[2048,2048]{1,0:T(8,128)} fusion(bf16[2048,2048]{1,0:T(8,128)(2,1)} %constant_dynamic-update-slice_fusion.7, bf16[2048,2048]{1,0:T(8,128)(2,1)} %param.23), kind=kOutput, calls=%fused_computation.417 | convolution fusion | flops 17179869184 | bytes 33554432 | tf_op jit(solution)/shard_map/dot_general | solution.py:404
  452.7 24.2 %all-to-all-done = bf16[4,512,512]{2,1,0:T(8,128)(2,1)} async-done(((bf16[4,512,512]{2,1,0:T(8,128)(2,1)}), bf16[4,512,512]{2,1,0:T(8,128)(2,1)}, u32[]{:S(2)}, u32[]{:S(2)}) %all-to-all-start) | async-done | bytes 2097184 | tf_op jit(solution)/shard_map/all_to_all | solution.py:384
  481.0 9.8 multiply_reduce_fusion.4
  498.2 8.4 fusion.40
  507.7 8.2 fusion.41
  515.8 25.3 %collective-permute-done.7 = bf16[256,2048]{1,0:T(8,128)(2,1)} collective-permute-done((bf16[256,2048]{1,0:T(8,128)(2,1)}, bf16[256,2048]{1,0:T(8,128)(2,1)}, u32[]{:S(2)}, u32[]{:S(2)}) %collective-permute-start.7) | collective-permute-done | bytes 1048608 | tf_op jit(solution)/shard_map/ppermute | solution.py:91
  545.1 5.9 fusion.64
  551.0 6.2 fusion.63
  567.2 18.4 %collective-permute-done.9 = bf16[256,2048]{1,0:T(8,128)(2,1)S(1)} collective-permute-done((bf16[256,2048]{1,0:T(8,128)(2,1)}, bf16[256,2048]{1,0:T(8,128)(2,1)S(1)}, u32[]{:S(2)}, u32[]{:S(2)}) %collective-permute-start.9) | collective-permute-done | bytes 1048608 | tf_op jit(solution)/shard_map/ppermute | solution.py:91
  602.3 29.2 %collective-permute-done.10 = bf16[256,2048]{1,0:T(8,128)(2,1)S(1)} collective-permute-done((bf16[256,2048]{1,0:T(8,128)(2,1)S(1)}, bf16[256,2048]{1,0:T(8,128)(2,1)S(1)}, u32[]{:S(2)}, u32[]{:S(2)}) %collective-permute-start.10) | collective-permute-done | bytes 1048608 | tf_op jit(solution)/shard_map/ppermute | solution.py:90
  641.5 19.1 %fusion.9 = (bf16[2048,2048]{1,0:T(8,128)(2,1)}, bf16[2048,2048]{1,0:T(8,128)(2,1)}, bf16[2048,2048]{1,0:T(8,128)(2,1)}) fusion(f32[2048,2048]{1,0:T(8,128)} %fusion.252, bf16[2048,2048]{1,0:T(8,128)(2,1)S(1)} %fusion.65, bf16[2048,2048]{1,0:T(8,128)(2,1)S(1)} %fusion.59), kind=kLoop, calls=%fused_computation.15 | loop fusion | flops 75497472 | bytes 58720256 | tf_op jit(solution)/shard_map/convert_element_type | solution.py:407
  662.6 23.8 %convolution_convert_fusion.3 = bf16[2048,2048]{1,0:T(8,128)(2,1)} fusion(bf16[2048,2048]{1,0:T(8,128)(2,1)} %constant_dynamic-update-slice_fusion.14, bf16[2048,2048]{1,0:T(8,128)(2,1)} %get-tuple-element.126), kind=kOutput, calls=%fused_computation.24 | convolution fusion | flops 17184063488 | bytes 25165824 | tf_op jit(solution)/shard_map/dot_general | solution.py:409
  686.7 23.8 %convolution_convert_fusion.2 = bf16[2048,2048]{1,0:T(8,128)(2,1)} fusion(bf16[2048,2048]{1,0:T(8,128)(2,1)} %constant_dynamic-update-slice_fusion.14, bf16[2048,2048]{1,0:T(8,128)(2,1)} %get-tuple-element.127), kind=kOutput, calls=%fused_computation.23 | convolution fusion | flops 17184063488 | bytes 25165824 | tf_op jit(solution)/shard_map/dot_general | solution.py:410
  711.2 6.3 fusion.122
  717.5 6.6 fusion.56
  733.2 5.1 fusion.119
  738.4 5.1 fusion.140
  743.5 5.5 fusion.55
  749.1 22.4 %convolution_convert_fusion.1 = bf16[2048,2048]{1,0:T(8,128)(2,1)} fusion(bf16[2048,2048]{1,0:T(8,128)(2,1)S(1)} %bitcast.223, bf16[2048,2048]{1,0:T(8,128)(2,1)} %constant_dynamic-update-slice_fusion.7), kind=kOutput, calls=%fused_computation.22 | convolution fusion | flops 17184063488 | bytes 25165824 | tf_op jit(solution)/shard_map/dot_general | solution.py:411
  771.5 9.1 fusion.132
  780.7 7.5 fusion.137
  796.4 12.3 collective-permute-done.18
  808.7 5.6 add_convert_fusion.13
  819.3 11.9 collective-permute-done.22
  831.3 7.2 add_convert_fusion.10
  838.6 15.2 %collective-permute-done.19 = bf16[256,2048]{1,0:T(8,128)(2,1)} collective-permute-done((bf16[256,2048]{1,0:T(8,128)(2,1)}, bf16[256,2048]{1,0:T(8,128)(2,1)}, u32[]{:S(2)}, u32[]{:S(2)}) %collective-permute-start.19) | collective-permute-done | bytes 1048608 | tf_op jit(solution)/shard_map/ppermute | solution.py:114
  853.8 6.3 add_convert_fusion.12
  865.0 11.1 collective-permute-done.23
  876.1 6.2 convert_add_fusion.5
  882.3 15.4 %collective-permute-done.20 = bf16[256,2048]{1,0:T(8,128)(2,1)S(1)} collective-permute-done((bf16[256,2048]{1,0:T(8,128)(2,1)S(1)}, bf16[256,2048]{1,0:T(8,128)(2,1)S(1)}, u32[]{:S(2)}, u32[]{:S(2)}) %collective-permute-start.20) | collective-permute-done | bytes 1048608 | tf_op jit(solution)/shard_map/ppermute | solution.py:114
  897.7 6.3 convert_add_fusion.6
  908.5 9.8 convolution_convert_fusion.7
  924.5 24.3 %fusion.251 = f32[2048,2048]{1,0:T(8,128)} fusion(bf16[2048,2048]{1,0:T(8,128)(2,1)} %get-tuple-element.133, bf16[2048,2048]{1,0:T(8,128)(2,1)} %param.23), kind=kOutput, calls=%fused_computation.416 | convolution fusion | flops 17179869184 | bytes 33554432 | tf_op jit(solution)/shard_map/dot_general | solution.py:401
  948.8 23.4 %all-to-all-done.1 = bf16[512,4,512]{2,0,1:T(8,128)(2,1)} async-done(((bf16[512,4,512]{2,0,1:T(8,128)(2,1)}), bf16[512,4,512]{2,0,1:T(8,128)(2,1)}, u32[]{:S(2)}, u32[]{:S(2)}) %all-to-all-start.1) | async-done | bytes 2097184 | tf_op jit(solution)/shard_map/all_to_all | solution.py:425
  976.4 5.3 reshape.367
  991.8 7.9 multiply_reduce_fusion
  1002.8 9.6 fusion.101
  1013.3 10.7 convolution_convert_fusion
  1044.6 76.5 %shard_map.221 = (f32[4,2048,128]{2,1,0:T(8,128)}, f32[4,2048,128]{2,1,0:T(8,128)}, f32[4,2048,128]{2,1,0:T(8,128)}) custom-call(bf16[4,2048,128]{2,1,0:T(8,128)(2,1)} %bitcast.258, bf16[4,2048,128]{2,1,0:T(8,128)(2,1)} %bitcast.254, bf16[4,2048,128]{2,1,0:T(8,128)(2,1)} %bitcast.256, bf16[4,2048,128]{2,1,0:T(8,128)(2,1)} %get-tuple-element.236.do_ref, ...), custom_call_target="tpu_custom_call" | custom-call | flops 21474836480 | bytes 25165824 | tf_op jit(solution)/shard_map/pallas_call | solution.py:268
  1134.8 6.1 fusion.53
  1144.9 9.9 convolution_convert_fusion.5
  1154.9 7.8 fusion.50
  1166.7 9.9 convolution_convert_fusion.4
  1177.6 13.2 collective-permute-done.28
  1200.9 10.0 fusion.54
  1215.3 8.7 convolution_convert_fusion.6
  1244.8 11.5 pad_maximum_fusion
  1272.4 18.4 %collective-permute-done.30 = bf16[256,2048]{1,0:T(8,128)(2,1)S(1)} collective-permute-done((bf16[256,2048]{1,0:T(8,128)(2,1)}, bf16[256,2048]{1,0:T(8,128)(2,1)S(1)}, u32[]{:S(2)}, u32[]{:S(2)}) %collective-permute-start.30) | collective-permute-done | bytes 1048608 | tf_op jit(solution)/shard_map/ppermute | solution.py:114
  1294.2 19.0 %collective-permute-done.34 = bf16[256,2048]{1,0:T(8,128)(2,1)S(1)} collective-permute-done((bf16[256,2048]{1,0:T(8,128)(2,1)S(1)}, bf16[256,2048]{1,0:T(8,128)(2,1)S(1)}, u32[]{:S(2)}, u32[]{:S(2)}) %collective-permute-start.34) | collective-permute-done | bytes 1048608 | tf_op jit(solution)/shard_map/ppermute | solution.py:115
  1314.9 20.9 %collective-permute-done.31 = bf16[256,2048]{1,0:T(8,128)(2,1)S(1)} collective-permute-done((bf16[256,2048]{1,0:T(8,128)(2,1)S(1)}, bf16[256,2048]{1,0:T(8,128)(2,1)S(1)}, u32[]{:S(2)}, u32[]{:S(2)}) %collective-permute-start.31) | collective-permute-done | bytes 1048608 | tf_op jit(solution)/shard_map/ppermute | solution.py:114
  1338.9 19.3 %collective-permute-done.35 = bf16[256,2048]{1,0:T(8,128)(2,1)S(1)} collective-permute-done((bf16[256,2048]{1,0:T(8,128)(2,1)S(1)}, bf16[256,2048]{1,0:T(8,128)(2,1)S(1)}, u32[]{:S(2)}, u32[]{:S(2)}) %collective-permute-start.35) | collective-permute-done | bytes 1048608 | tf_op jit(solution)/shard_map/ppermute | solution.py:115
  1358.5 18.8 %collective-permute-done.32 = bf16[256,2048]{1,0:T(8,128)(2,1)S(1)} collective-permute-done((bf16[256,2048]{1,0:T(8,128)(2,1)S(1)}, bf16[256,2048]{1,0:T(8,128)(2,1)S(1)}, u32[]{:S(2)}, u32[]{:S(2)}) %collective-permute-start.32) | collective-permute-done | bytes 1048608 | tf_op jit(solution)/shard_map/ppermute | solution.py:114
  (496 shorter events, 442.0 us)
Async XLA Ops:
  7.2 208.0 %copy-start = (bf16[2048,512]{1,0:T(8,128)(2,1)S(1)}, bf16[2048,512]{1,0:T(8,128)(2,1)}, u32[]{:S(2)}) copy-start(bf16[2048,512]{1,0:T(8,128)(2,1)} %param.15) | copy-start | bytes 6291460
  7.2 206.0 %all-gather.7.cloned.1.call-start = ((), (), s32[]{:S(2)}) async-start(), calls=%async_computation.8 | async-start | bytes 1310720 | tf_op jit(solution)/shard_map/all_gather | solution.py:335
  9.1 383.8 %all-gather.13.cloned.1.call-start = ((), (), s32[]{:S(2)}) async-start(), calls=%async_computation.17 | async-start | bytes 2396160 | tf_op jit(solution)/shard_map/all_gather | solution.py:26
  18.0 43.6 %collective-permute-start.1 = (bf16[256,2048]{1,0:T(8,128)(2,1)}, bf16[256,2048]{1,0:T(8,128)(2,1)S(1)}, u32[]{:S(2)}, u32[]{:S(2)}) collective-permute-start(bf16[256,2048]{1,0:T(8,128)(2,1)} %get-tuple-element.241), channel_id=1, source_target_pairs={{0,3},{1,0},{2,1},{3,2},{4,7},{5,4},{6,5},{7,6},{8,11},{9,8},{10,9... | collective-permute-start | bytes 3145736 | tf_op jit(solution)/shard_map/ppermute | solution.py:91
  23.1 63.5 %collective-permute-start = (bf16[256,2048]{1,0:T(8,128)(2,1)}, bf16[256,2048]{1,0:T(8,128)(2,1)}, u32[]{:S(2)}, u32[]{:S(2)}) collective-permute-start(bf16[256,2048]{1,0:T(8,128)(2,1)} %get-tuple-element.242), channel_id=1, source_target_pairs={{0,1},{1,2},{2,3},{3,0},{4,5},{5,6},{6,7},{7,4},{8,9},{9,10},{10,1... | collective-permute-start | bytes 3145736 | tf_op jit(solution)/shard_map/ppermute | solution.py:90
  24.9 260.8 %copy-start.56 = (s32[2048]{0:T(1024)}, s32[2048]{0:T(1024)S(1)}, u32[]{:S(2)}) copy-start(s32[2048]{0:T(1024)S(1)} %slice.70) | copy-start | bytes 24580
  31.3 176.2 %copy-start.62 = (f32[2048]{0:T(1024)}, f32[2048]{0:T(1024)S(1)}, u32[]{:S(2)}) copy-start(f32[2048]{0:T(1024)S(1)} %get-tuple-element.249) | copy-start | bytes 24580
  31.3 375.1 %copy-start.51 = (f32[2048]{0:T(1024)}, f32[2048]{0:T(1024)S(1)}, u32[]{:S(2)}) copy-start(f32[2048]{0:T(1024)S(1)} %get-tuple-element.248) | copy-start | bytes 24580
  61.7 157.2 %copy-start.41 = (bf16[256,2048]{1,0:T(8,128)(2,1)}, bf16[256,2048]{1,0:T(8,128)(2,1)S(1)}, u32[]{:S(2)}) copy-start(bf16[256,2048]{1,0:T(8,128)(2,1)S(1)} %collective-permute-done.1) | copy-start | bytes 3145732
  61.7 44.9 %collective-permute-start.3 = (bf16[256,2048]{1,0:T(8,128)(2,1)S(1)}, bf16[256,2048]{1,0:T(8,128)(2,1)}, u32[]{:S(2)}, u32[]{:S(2)}) collective-permute-start(bf16[256,2048]{1,0:T(8,128)(2,1)S(1)} %collective-permute-done.1), channel_id=1, source_target_pairs={{0,3},{1,0},{2,1},{3,2},{4,7},{5,4},{6,5},{7,6},{8,11},{9,8},{10,9... | collective-permute-start | bytes 3145736 | tf_op jit(solution)/shard_map/ppermute | solution.py:91
  86.6 47.4 %collective-permute-start.2 = (bf16[256,2048]{1,0:T(8,128)(2,1)}, bf16[256,2048]{1,0:T(8,128)(2,1)}, u32[]{:S(2)}, u32[]{:S(2)}) collective-permute-start(bf16[256,2048]{1,0:T(8,128)(2,1)} %collective-permute-done), channel_id=1, source_target_pairs={{0,1},{1,2},{2,3},{3,0},{4,5},{5,6},{6,7},{7,4},{8,9},{9,10},{10,1... | collective-permute-start | bytes 3145736 | tf_op jit(solution)/shard_map/ppermute | solution.py:90
  116.1 44.2 %collective-permute-start.5 = (bf16[256,2048]{1,0:T(8,128)(2,1)}, bf16[256,2048]{1,0:T(8,128)(2,1)}, u32[]{:S(2)}, u32[]{:S(2)}) collective-permute-start(bf16[256,2048]{1,0:T(8,128)(2,1)} %collective-permute-done.3), channel_id=1, source_target_pairs={{0,3},{1,0},{2,1},{3,2},{4,7},{5,4},{6,5},{7,6},{8,11},{9,8},{10,9... | collective-permute-start | bytes 3145736 | tf_op jit(solution)/shard_map/ppermute | solution.py:91
  139.1 36.9 %collective-permute-start.4 = (bf16[256,2048]{1,0:T(8,128)(2,1)}, bf16[256,2048]{1,0:T(8,128)(2,1)}, u32[]{:S(2)}, u32[]{:S(2)}) collective-permute-start(bf16[256,2048]{1,0:T(8,128)(2,1)} %collective-permute-done.2), channel_id=1, source_target_pairs={{0,1},{1,2},{2,3},{3,0},{4,5},{5,6},{6,7},{7,4},{8,9},{9,10},{10,1... | collective-permute-start | bytes 3145736 | tf_op jit(solution)/shard_map/ppermute | solution.py:90
  212.9 268.1 %all-gather.9.cloned.1.call-start = ((), (), s32[]{:S(2)}) async-start(), calls=%async_computation.9 | async-start | bytes 9437184 | tf_op jit(solution)/shard_map/all_gather | solution.py:334
  238.5 48.5 %copy-start.71 = (f32[4]{0:T(128)S(1)}, f32[4]{0:T(128)}, u32[]{:S(2)}) copy-start(f32[4]{0:T(128)} %param.19) | copy-start | bytes 52
  241.2 27.8 %collective-permute-start.12 = (bf16[256,2048]{1,0:T(8,128)(2,1)S(1)}, bf16[256,2048]{1,0:T(8,128)(2,1)S(1)}, u32[]{:S(2)}, u32[]{:S(2)}) collective-permute-start(bf16[256,2048]{1,0:T(8,128)(2,1)S(1)} %get-tuple-element.238), channel_id=1, source_target_pairs={{0,1},{1,2},{2,3},{3,0},{4,5},{5,6},{6,7},{7,4},{8,9},{9,10},{10,1... | collective-permute-start | bytes 3145736 | tf_op jit(solution)/shard_map/ppermute | solution.py:90
  241.3 50.3 %collective-permute-start.13 = (bf16[256,2048]{1,0:T(8,128)(2,1)}, bf16[256,2048]{1,0:T(8,128)(2,1)}, u32[]{:S(2)}, u32[]{:S(2)}) collective-permute-start(bf16[256,2048]{1,0:T(8,128)(2,1)} %get-tuple-element.237), channel_id=1, source_target_pairs={{0,3},{1,0},{2,1},{3,2},{4,7},{5,4},{6,5},{7,6},{8,11},{9,8},{10,9... | collective-permute-start | bytes 3145736 | tf_op jit(solution)/shard_map/ppermute | solution.py:91
  269.1 73.4 %collective-permute-start.14 = (bf16[256,2048]{1,0:T(8,128)(2,1)S(1)}, bf16[256,2048]{1,0:T(8,128)(2,1)}, u32[]{:S(2)}, u32[]{:S(2)}) collective-permute-start(bf16[256,2048]{1,0:T(8,128)(2,1)S(1)} %collective-permute-done.12), channel_id=1, source_target_pairs={{0,1},{1,2},{2,3},{3,0},{4,5},{5,6},{6,7},{7,4},{8,9},{9,10},{10,1... | collective-permute-start | bytes 3145736 | tf_op jit(solution)/shard_map/ppermute | solution.py:90
  287.1 119.4 %copy-start.64 = (f32[4]{0:T(128)}, f32[4]{0:T(128)S(1)}, u32[]{:S(2)}) copy-start(f32[4]{0:T(128)S(1)} %get-tuple-element.224) | copy-start | bytes 52
  287.1 119.4 %copy-start.66 = (f32[4]{0:T(128)}, f32[4]{0:T(128)S(1)}, u32[]{:S(2)}) copy-start(f32[4]{0:T(128)S(1)} %get-tuple-element.223) | copy-start | bytes 52
  291.6 58.7 %collective-permute-start.15 = (bf16[256,2048]{1,0:T(8,128)(2,1)}, bf16[256,2048]{1,0:T(8,128)(2,1)}, u32[]{:S(2)}, u32[]{:S(2)}) collective-permute-start(bf16[256,2048]{1,0:T(8,128)(2,1)} %collective-permute-done.13), channel_id=1, source_target_pairs={{0,3},{1,0},{2,1},{3,2},{4,7},{5,4},{6,5},{7,6},{8,11},{9,8},{10,9... | collective-permute-start | bytes 3145736 | tf_op jit(solution)/shard_map/ppermute | solution.py:91
  342.5 28.1 %collective-permute-start.16 = (bf16[256,2048]{1,0:T(8,128)(2,1)}, bf16[256,2048]{1,0:T(8,128)(2,1)S(1)}, u32[]{:S(2)}, u32[]{:S(2)}) collective-permute-start(bf16[256,2048]{1,0:T(8,128)(2,1)} %collective-permute-done.14), channel_id=1, source_target_pairs={{0,1},{1,2},{2,3},{3,0},{4,5},{5,6},{6,7},{7,4},{8,9},{9,10},{10,1... | collective-permute-start | bytes 3145736 | tf_op jit(solution)/shard_map/ppermute | solution.py:90
  350.2 41.6 %collective-permute-start.17 = (bf16[256,2048]{1,0:T(8,128)(2,1)}, bf16[256,2048]{1,0:T(8,128)(2,1)S(1)}, u32[]{:S(2)}, u32[]{:S(2)}) collective-permute-start(bf16[256,2048]{1,0:T(8,128)(2,1)} %collective-permute-done.15), channel_id=1, source_target_pairs={{0,3},{1,0},{2,1},{3,2},{4,7},{5,4},{6,5},{7,6},{8,11},{9,8},{10,9... | collective-permute-start | bytes 3145736 | tf_op jit(solution)/shard_map/ppermute | solution.py:91
  423.6 53.2 %all-to-all-start = ((bf16[4,512,512]{2,1,0:T(8,128)(2,1)}), bf16[4,512,512]{2,1,0:T(8,128)(2,1)}, u32[]{:S(2)}, u32[]{:S(2)}) async-start(bf16[4,512,512]{2,1,0:T(8,128)(2,1)} %convert_element_type.380), calls=%async_computation | async-start | bytes 4194304 | tf_op jit(solution)/shard_map/all_to_all | solution.py:384
  428.1 558.0 %reduce-scatter.7.cloned.1.call-start = ((), (), s32[]{:S(2)}) async-start(), calls=%async_computation.10 | async-start | bytes 9437184 | tf_op jit(solution)/shard_map/reduce_scatter | solution.py:321
  494.8 46.3 %collective-permute-start.7 = (bf16[256,2048]{1,0:T(8,128)(2,1)}, bf16[256,2048]{1,0:T(8,128)(2,1)}, u32[]{:S(2)}, u32[]{:S(2)}) collective-permute-start(bf16[256,2048]{1,0:T(8,128)(2,1)} %get-tuple-element.239), channel_id=1, source_target_pairs={{0,3},{1,0},{2,1},{3,2},{4,7},{5,4},{6,5},{7,6},{8,11},{9,8},{10,9... | collective-permute-start | bytes 3145736 | tf_op jit(solution)/shard_map/ppermute | solution.py:91
  497.1 45.9 %collective-permute-start.6 = (bf16[256,2048]{1,0:T(8,128)(2,1)}, bf16[256,2048]{1,0:T(8,128)(2,1)S(1)}, u32[]{:S(2)}, u32[]{:S(2)}) collective-permute-start(bf16[256,2048]{1,0:T(8,128)(2,1)} %get-tuple-element.240), channel_id=1, source_target_pairs={{0,1},{1,2},{2,3},{3,0},{4,5},{5,6},{6,7},{7,4},{8,9},{9,10},{10,1... | collective-permute-start | bytes 3145736 | tf_op jit(solution)/shard_map/ppermute | solution.py:90
  541.1 44.5 %collective-permute-start.9 = (bf16[256,2048]{1,0:T(8,128)(2,1)}, bf16[256,2048]{1,0:T(8,128)(2,1)S(1)}, u32[]{:S(2)}, u32[]{:S(2)}) collective-permute-start(bf16[256,2048]{1,0:T(8,128)(2,1)} %collective-permute-done.7), channel_id=1, source_target_pairs={{0,3},{1,0},{2,1},{3,2},{4,7},{5,4},{6,5},{7,6},{8,11},{9,8},{10,9... | collective-permute-start | bytes 3145736 | tf_op jit(solution)/shard_map/ppermute | solution.py:91
  543.0 45.0 %collective-permute-start.8 = (bf16[256,2048]{1,0:T(8,128)(2,1)S(1)}, bf16[256,2048]{1,0:T(8,128)(2,1)S(1)}, u32[]{:S(2)}, u32[]{:S(2)}) collective-permute-start(bf16[256,2048]{1,0:T(8,128)(2,1)S(1)} %collective-permute-done.6), channel_id=1, source_target_pairs={{0,1},{1,2},{2,3},{3,0},{4,5},{5,6},{6,7},{7,4},{8,9},{9,10},{10,1... | collective-permute-start | bytes 3145736 | tf_op jit(solution)/shard_map/ppermute | solution.py:90
  557.2 33.3 %slice-start.10 = ((s8[8388608]{0:T(1024)(128)(4,1)}), s8[4194304]{0:T(1024)(128)(4,1)S(1)}, s32[]{:S(2)}) async-start(s8[8388608]{0:T(1024)(128)(4,1)} %bitcast.291), calls=%async_computation.28 | async-start | bytes 8388608
  559.6 30.8 %slice-start.11 = ((s8[8388608]{0:T(1024)(128)(4,1)}), s8[4194304]{0:T(1024)(128)(4,1)S(1)}, s32[]{:S(2)}) async-start(s8[8388608]{0:T(1024)(128)(4,1)} %bitcast.291), calls=%async_computation.29 | async-start | bytes 8388608
  585.7 50.8 %collective-permute-start.11 = (bf16[256,2048]{1,0:T(8,128)(2,1)S(1)}, bf16[256,2048]{1,0:T(8,128)(2,1)S(1)}, u32[]{:S(2)}, u32[]{:S(2)}) collective-permute-start(bf16[256,2048]{1,0:T(8,128)(2,1)S(1)} %collective-permute-done.9), channel_id=1, source_target_pairs={{0,3},{1,0},{2,1},{3,2},{4,7},{5,4},{6,5},{7,6},{8,11},{9,8},{10,9... | collective-permute-start | bytes 3145736 | tf_op jit(solution)/shard_map/ppermute | solution.py:91
  588.1 43.5 %collective-permute-start.10 = (bf16[256,2048]{1,0:T(8,128)(2,1)S(1)}, bf16[256,2048]{1,0:T(8,128)(2,1)S(1)}, u32[]{:S(2)}, u32[]{:S(2)}) collective-permute-start(bf16[256,2048]{1,0:T(8,128)(2,1)S(1)} %collective-permute-done.8), channel_id=1, source_target_pairs={{0,1},{1,2},{2,3},{3,0},{4,5},{5,6},{6,7},{7,4},{8,9},{9,10},{10,1... | collective-permute-start | bytes 3145736 | tf_op jit(solution)/shard_map/ppermute | solution.py:90
  686.4 302.5 %reduce-scatter.9.cloned.1.call-start = ((), (), s32[]{:S(2)}) async-start(), calls=%async_computation.11 | async-start | bytes 9437184 | tf_op jit(solution)/shard_map/reduce_scatter | solution.py:321
  710.5 410.6 %reduce-scatter.11.cloned.1.call-start = ((), (), s32[]{:S(2)}) async-start(), calls=%async_computation.12 | async-start | bytes 9437184 | tf_op jit(solution)/shard_map/reduce_scatter | solution.py:321
  724.2 64.0 %collective-permute-start.21 = (bf16[256,2048]{1,0:T(8,128)(2,1)S(1)}, bf16[256,2048]{1,0:T(8,128)(2,1)}, u32[]{:S(2)}, u32[]{:S(2)}) collective-permute-start(bf16[256,2048]{1,0:T(8,128)(2,1)S(1)} %fusion.56), channel_id=1, source_target_pairs={{0,3},{1,0},{2,1},{3,2},{4,7},{5,4},{6,5},{7,6},{8,11},{9,8},{10,9... | collective-permute-start | bytes 3145736 | tf_op jit(solution)/shard_map/ppermute | solution.py:115
  780.6 28.1 %collective-permute-start.18 = (bf16[256,2048]{1,0:T(8,128)(2,1)}, bf16[256,2048]{1,0:T(8,128)(2,1)S(1)}, u32[]{:S(2)}, u32[]{:S(2)}) collective-permute-start(bf16[256,2048]{1,0:T(8,128)(2,1)} %fusion.55), channel_id=1, source_target_pairs={{0,1},{1,2},{2,3},{3,0},{4,5},{5,6},{6,7},{7,4},{8,9},{9,10},{10,1... | collective-permute-start | bytes 3145736 | tf_op jit(solution)/shard_map/ppermute | solution.py:114
  792.4 38.8 %collective-permute-start.22 = (bf16[256,2048]{1,0:T(8,128)(2,1)S(1)}, bf16[256,2048]{1,0:T(8,128)(2,1)}, u32[]{:S(2)}, u32[]{:S(2)}) collective-permute-start(bf16[256,2048]{1,0:T(8,128)(2,1)S(1)} %add_convert_fusion.11), channel_id=1, source_target_pairs={{0,3},{1,0},{2,1},{3,2},{4,7},{5,4},{6,5},{7,6},{8,11},{9,8},{10,9... | collective-permute-start | bytes 3145736 | tf_op jit(solution)/shard_map/ppermute | solution.py:115
  814.3 39.5 %collective-permute-start.19 = (bf16[256,2048]{1,0:T(8,128)(2,1)}, bf16[256,2048]{1,0:T(8,128)(2,1)}, u32[]{:S(2)}, u32[]{:S(2)}) collective-permute-start(bf16[256,2048]{1,0:T(8,128)(2,1)} %add_convert_fusion.13), channel_id=1, source_target_pairs={{0,1},{1,2},{2,3},{3,0},{4,5},{5,6},{6,7},{7,4},{8,9},{9,10},{10,1... | collective-permute-start | bytes 3145736 | tf_op jit(solution)/shard_map/ppermute | solution.py:114
  819.3 34.5 %copy-start.73 = (f32[256,2048]{1,0:T(8,128)S(1)}, f32[256,2048]{1,0:T(8,128)}, u32[]{:S(2)}) copy-start(f32[256,2048]{1,0:T(8,128)} %fusion.132) | copy-start | bytes 6291460
  838.5 37.6 %collective-permute-start.23 = (bf16[256,2048]{1,0:T(8,128)(2,1)S(1)}, bf16[256,2048]{1,0:T(8,128)(2,1)S(1)}, u32[]{:S(2)}, u32[]{:S(2)}) collective-permute-start(bf16[256,2048]{1,0:T(8,128)(2,1)S(1)} %add_convert_fusion.10), channel_id=1, source_target_pairs={{0,3},{1,0},{2,1},{3,2},{4,7},{5,4},{6,5},{7,6},{8,11},{9,8},{10,9... | collective-permute-start | bytes 3145736 | tf_op jit(solution)/shard_map/ppermute | solution.py:115
  860.2 37.5 %collective-permute-start.20 = (bf16[256,2048]{1,0:T(8,128)(2,1)S(1)}, bf16[256,2048]{1,0:T(8,128)(2,1)S(1)}, u32[]{:S(2)}, u32[]{:S(2)}) collective-permute-start(bf16[256,2048]{1,0:T(8,128)(2,1)S(1)} %add_convert_fusion.12), channel_id=1, source_target_pairs={{0,1},{1,2},{2,3},{3,0},{4,5},{5,6},{6,7},{7,4},{8,9},{9,10},{10,1... | collective-permute-start | bytes 3145736 | tf_op jit(solution)/shard_map/ppermute | solution.py:114
  919.8 52.4 %all-to-all-start.1 = ((bf16[512,4,512]{2,0,1:T(8,128)(2,1)}), bf16[512,4,512]{2,0,1:T(8,128)(2,1)}, u32[]{:S(2)}, u32[]{:S(2)}) async-start(bf16[512,4,512]{2,0,1:T(8,128)(2,1)} %bitcast.233), calls=%async_computation.1 | async-start | bytes 4194304 | tf_op jit(solution)/shard_map/all_to_all | solution.py:425
  924.3 207.9 %all-gather.11.cloned.1.call-start = ((), (), s32[]{:S(2)}) async-start(), calls=%async_computation.15 | async-start | bytes 1198080 | tf_op jit(solution)/shard_map/all_gather | solution.py:26
  1013.3 141.5 %reduce-scatter.13.cloned.1.call-start = ((), (), s32[]{:S(2)}) async-start(), calls=%async_computation.13 | async-start | bytes 9437184 | tf_op jit(solution)/shard_map/reduce_scatter | solution.py:321
  1024.0 175.1 %reduce-scatter.15.cloned.1.call-start = ((), (), s32[]{:S(2)}) async-start(), calls=%async_computation.14 | async-start | bytes 1310720 | tf_op jit(solution)/shard_map/reduce_scatter | solution.py:420
  1040.8 83.2 %collective-permute-start.24 = (bf16[256,2048]{1,0:T(8,128)(2,1)}, bf16[256,2048]{1,0:T(8,128)(2,1)S(1)}, u32[]{:S(2)}, u32[]{:S(2)}) collective-permute-start(bf16[256,2048]{1,0:T(8,128)(2,1)} %get-tuple-element.234), channel_id=1, source_target_pairs={{0,1},{1,2},{2,3},{3,0},{4,5},{5,6},{6,7},{7,4},{8,9},{9,10},{10,1... | collective-permute-start | bytes 3145736 | tf_op jit(solution)/shard_map/ppermute | solution.py:114
  1040.8 83.2 %collective-permute-start.27 = (bf16[256,2048]{1,0:T(8,128)(2,1)}, bf16[256,2048]{1,0:T(8,128)(2,1)}, u32[]{:S(2)}, u32[]{:S(2)}) collective-permute-start(bf16[256,2048]{1,0:T(8,128)(2,1)} %get-tuple-element.235), channel_id=1, source_target_pairs={{0,3},{1,0},{2,1},{3,2},{4,7},{5,4},{6,5},{7,6},{8,11},{9,8},{10,9... | collective-permute-start | bytes 3145736 | tf_op jit(solution)/shard_map/ppermute | solution.py:115
  1128.4 48.2 %collective-permute-start.25 = (bf16[256,2048]{1,0:T(8,128)(2,1)}, bf16[256,2048]{1,0:T(8,128)(2,1)S(1)}, u32[]{:S(2)}, u32[]{:S(2)}) collective-permute-start(bf16[256,2048]{1,0:T(8,128)(2,1)} %get-tuple-element.232), channel_id=1, source_target_pairs={{0,1},{1,2},{2,3},{3,0},{4,5},{5,6},{6,7},{7,4},{8,9},{9,10},{10,1... | collective-permute-start | bytes 3145736 | tf_op jit(solution)/shard_map/ppermute | solution.py:114
  1128.4 62.4 %collective-permute-start.28 = (bf16[256,2048]{1,0:T(8,128)(2,1)}, bf16[256,2048]{1,0:T(8,128)(2,1)}, u32[]{:S(2)}, u32[]{:S(2)}) collective-permute-start(bf16[256,2048]{1,0:T(8,128)(2,1)} %get-tuple-element.233), channel_id=1, source_target_pairs={{0,3},{1,0},{2,1},{3,2},{4,7},{5,4},{6,5},{7,6},{8,11},{9,8},{10,9... | collective-permute-start | bytes 3145736 | tf_op jit(solution)/shard_map/ppermute | solution.py:115
  1154.8 244.0 %reduce-scatter.17.cloned.1.call-start = ((), (), s32[]{:S(2)}) async-start(), calls=%async_computation.16 | async-start | bytes 7077888 | tf_op jit(solution)/shard_map/reduce_scatter | solution.py:321
  1195.3 187.5 %collective-permute-start.26 = (bf16[256,2048]{1,0:T(8,128)(2,1)}, bf16[256,2048]{1,0:T(8,128)(2,1)}, u32[]{:S(2)}, u32[]{:S(2)}) collective-permute-start(bf16[256,2048]{1,0:T(8,128)(2,1)} %get-tuple-element.230), channel_id=1, source_target_pairs={{0,1},{1,2},{2,3},{3,0},{4,5},{5,6},{6,7},{7,4},{8,9},{9,10},{10,1... | collective-permute-start | bytes 3145736 | tf_op jit(solution)/shard_map/ppermute | solution.py:114
  1195.3 187.5 %collective-permute-start.29 = (bf16[256,2048]{1,0:T(8,128)(2,1)S(1)}, bf16[256,2048]{1,0:T(8,128)(2,1)}, u32[]{:S(2)}, u32[]{:S(2)}) collective-permute-start(bf16[256,2048]{1,0:T(8,128)(2,1)S(1)} %get-tuple-element.231), channel_id=1, source_target_pairs={{0,3},{1,0},{2,1},{3,2},{4,7},{5,4},{6,5},{7,6},{8,11},{9,8},{10,9... | collective-permute-start | bytes 3145736 | tf_op jit(solution)/shard_map/ppermute | solution.py:115
  1240.4 26.2 %collective-permute-start.33 = (bf16[256,2048]{1,0:T(8,128)(2,1)}, bf16[256,2048]{1,0:T(8,128)(2,1)}, u32[]{:S(2)}, u32[]{:S(2)}) collective-permute-start(bf16[256,2048]{1,0:T(8,128)(2,1)} %fusion.58), channel_id=1, source_target_pairs={{0,3},{1,0},{2,1},{3,2},{4,7},{5,4},{6,5},{7,6},{8,11},{9,8},{10,9... | collective-permute-start | bytes 3145736 | tf_op jit(solution)/shard_map/ppermute | solution.py:115
  1256.3 34.5 %collective-permute-start.30 = (bf16[256,2048]{1,0:T(8,128)(2,1)}, bf16[256,2048]{1,0:T(8,128)(2,1)S(1)}, u32[]{:S(2)}, u32[]{:S(2)}) collective-permute-start(bf16[256,2048]{1,0:T(8,128)(2,1)} %fusion.57), channel_id=1, source_target_pairs={{0,1},{1,2},{2,3},{3,0},{4,5},{5,6},{6,7},{7,4},{8,9},{9,10},{10,1... | collective-permute-start | bytes 3145736 | tf_op jit(solution)/shard_map/ppermute | solution.py:114
  1269.8 43.5 %collective-permute-start.34 = (bf16[256,2048]{1,0:T(8,128)(2,1)S(1)}, bf16[256,2048]{1,0:T(8,128)(2,1)S(1)}, u32[]{:S(2)}, u32[]{:S(2)}) collective-permute-start(bf16[256,2048]{1,0:T(8,128)(2,1)S(1)} %add_convert_fusion.3), channel_id=1, source_target_pairs={{0,3},{1,0},{2,1},{3,2},{4,7},{5,4},{6,5},{7,6},{8,11},{9,8},{10,9... | collective-permute-start | bytes 3145736 | tf_op jit(solution)/shard_map/ppermute | solution.py:115
  1291.6 44.2 %collective-permute-start.31 = (bf16[256,2048]{1,0:T(8,128)(2,1)S(1)}, bf16[256,2048]{1,0:T(8,128)(2,1)S(1)}, u32[]{:S(2)}, u32[]{:S(2)}) collective-permute-start(bf16[256,2048]{1,0:T(8,128)(2,1)S(1)} %add_convert_fusion.5), channel_id=1, source_target_pairs={{0,1},{1,2},{2,3},{3,0},{4,5},{5,6},{6,7},{7,4},{8,9},{9,10},{10,1... | collective-permute-start | bytes 3145736 | tf_op jit(solution)/shard_map/ppermute | solution.py:114
  1313.6 44.6 %collective-permute-start.35 = (bf16[256,2048]{1,0:T(8,128)(2,1)S(1)}, bf16[256,2048]{1,0:T(8,128)(2,1)S(1)}, u32[]{:S(2)}, u32[]{:S(2)}) collective-permute-start(bf16[256,2048]{1,0:T(8,128)(2,1)S(1)} %add_convert_fusion.2), channel_id=1, source_target_pairs={{0,3},{1,0},{2,1},{3,2},{4,7},{5,4},{6,5},{7,6},{8,11},{9,8},{10,9... | collective-permute-start | bytes 3145736 | tf_op jit(solution)/shard_map/ppermute | solution.py:115
  1336.1 41.2 %collective-permute-start.32 = (bf16[256,2048]{1,0:T(8,128)(2,1)S(1)}, bf16[256,2048]{1,0:T(8,128)(2,1)S(1)}, u32[]{:S(2)}, u32[]{:S(2)}) collective-permute-start(bf16[256,2048]{1,0:T(8,128)(2,1)S(1)} %add_convert_fusion.4), channel_id=1, source_target_pairs={{0,1},{1,2},{2,3},{3,0},{4,5},{5,6},{6,7},{7,4},{8,9},{9,10},{10,1... | collective-permute-start | bytes 3145736 | tf_op jit(solution)/shard_map/ppermute | solution.py:114
  1379.0 3.8 collective-permute-start.36
  1382.8 4.7 collective-permute-start.37
  1387.5 2.0 collective-permute-start.38
  1389.5 3.8 collective-permute-start.39
  1393.4 4.3 collective-permute-start.40
  (80 other events, 666.8 us)
Sparse Core Ops, SparseCore 0:
  9.6 41.3 all-gather.6
  213.0 26.1 all-gather.12
  241.1 55.8 all-gather.8
  686.5 70.8 reduce-scatter.6
  760.8 71.4 reduce-scatter.8
  835.6 71.2 reduce-scatter.10
  1013.4 20.8 all-gather.10
  1037.7 71.2 reduce-scatter.12
  1154.9 37.8 reduce-scatter.14
  1256.4 59.1 reduce-scatter.16

commit v9 on v8

--- a/solution.py
+++ b/solution.py
@@ -183,26 +183,45 @@
 BQ = 256
 
 
-def _mask(qi, docq, dock, seg):
-    row = (qi * BQ) % seg + lax.broadcasted_iota(jnp.int32, (BQ, seg), 0)
-    col = lax.broadcasted_iota(jnp.int32, (BQ, seg), 1)
+def _mask(qi, docq, dock, seg, width):
+    row = (qi * BQ) % seg + lax.broadcasted_iota(jnp.int32, (BQ, width), 0)
+    col = lax.broadcasted_iota(jnp.int32, (BQ, width), 1)
     return (col <= row) & (docq == dock)
+
+
+LEVEL = 256
+
+
+def _levels(qi, seg, body):
+    local = (qi * BQ) % seg
+    need = local + BQ
+    for lvl in range(seg // LEVEL):
+        width = (lvl + 1) * LEVEL
+        low = lvl * LEVEL
+
+        @pl.when((need > low) & (need <= width))
+        def _():
+            body(width)
 
 
 def _fwd_kernel(scale, seg, q_ref, k_ref, v_ref, docq_ref, dock_ref, o_ref, lse_ref):
     qi = pl.program_id(1)
-    q = q_ref[0]
-    k = k_ref[0]
-    v = v_ref[0]
-    s = lax.dot_general(q, k, (((1,), (1,)), ((), ())), preferred_element_type=jnp.float32)
-    allowed = _mask(qi, docq_ref[...], dock_ref[...], seg)
-    s = jnp.where(allowed, s * scale, NEG)
-    m = jnp.max(s, axis=1, keepdims=True)
-    e = jnp.exp(s - m)
-    l = jnp.sum(e, axis=1, keepdims=True)
-    p = (e / l).astype(jnp.bfloat16)
-    o_ref[0] = jnp.dot(p, v, preferred_element_type=jnp.float32)
-    lse_ref[0] = m + jnp.log(l)
+
+    def body(width):
+        q = q_ref[0]
+        k = k_ref[0, :width]
+        v = v_ref[0, :width]
+        s = lax.dot_general(q, k, (((1,), (1,)), ((), ())), preferred_element_type=jnp.float32)
+        allowed = _mask(qi, docq_ref[...], dock_ref[:, :width], seg, width)
+        s = jnp.where(allowed, s * scale, NEG)
+        m = jnp.max(s, axis=1, keepdims=True)
+        e = jnp.exp(s - m)
+        l = jnp.sum(e, axis=1, keepdims=True)
+        p = (e / l).astype(jnp.bfloat16)
+        o_ref[0] = jnp.dot(p, v, preferred_element_type=jnp.float32)
+        lse_ref[0] = m + jnp.log(l)
+
+    _levels(qi, seg, body)
 
 
 def _bwd_kernel(scale, seg, q_ref, k_ref, v_ref, do_ref, lse_ref, docq_ref, dock_ref,
@@ -214,21 +233,25 @@
         dk_ref[...] = jnp.zeros_like(dk_ref)
         dv_ref[...] = jnp.zeros_like(dv_ref)
 
-    q = q_ref[0]
-    k = k_ref[0]
-    v = v_ref[0]
-    do = do_ref[0]
-    s = lax.dot_general(q, k, (((1,), (1,)), ((), ())), preferred_element_type=jnp.float32)
-    allowed = _mask(qi, docq_ref[...], dock_ref[...], seg)
-    s = jnp.where(allowed, s * scale, NEG)
-    p = jnp.exp(s - lse_ref[0])
-    dp = lax.dot_general(do, v, (((1,), (1,)), ((), ())), preferred_element_type=jnp.float32)
-    delta = jnp.sum(p * dp, axis=1, keepdims=True)
-    ds = (p * (dp - delta) * scale).astype(jnp.bfloat16)
-    dq_ref[0] = jnp.dot(ds, k, preferred_element_type=jnp.float32)
-    dk_ref[0] += lax.dot_general(ds, q, (((0,), (0,)), ((), ())), preferred_element_type=jnp.float32)
-    dv_ref[0] += lax.dot_general(p.astype(jnp.bfloat16), do, (((0,), (0,)), ((), ())),
-                                 preferred_element_type=jnp.float32)
+    def body(width):
+        q = q_ref[0]
+        k = k_ref[0, :width]
+        v = v_ref[0, :width]
+        do = do_ref[0]
+        s = lax.dot_general(q, k, (((1,), (1,)), ((), ())), preferred_element_type=jnp.float32)
+        allowed = _mask(qi, docq_ref[...], dock_ref[:, :width], seg, width)
+        s = jnp.where(allowed, s * scale, NEG)
+        p = jnp.exp(s - lse_ref[0])
+        dp = lax.dot_general(do, v, (((1,), (1,)), ((), ())), preferred_element_type=jnp.float32)
+        delta = jnp.sum(p * dp, axis=1, keepdims=True)
+        ds = (p * (dp - delta) * scale).astype(jnp.bfloat16)
+        dq_ref[0] = jnp.dot(ds, k, preferred_element_type=jnp.float32)
+        dk_ref[0, :width] += lax.dot_general(ds, q, (((0,), (0,)), ((), ())),
+                                             preferred_element_type=jnp.float32)
+        dv_ref[0, :width] += lax.dot_general(p.astype(jnp.bfloat16), do, (((0,), (0,)), ((), ())),
+                                             preferred_element_type=jnp.float32)
+
+    _levels(qi, seg, body)
 
 
 def attention_fwd(q, k, v, doc, scale):
@@ -331,9 +354,6 @@
     seg_shape = (heads_here, seg_count, SEG, head_size)
     piece = width // dp_size
     w_out_piece = lax.dynamic_slice_in_dim(w_out, lax.axis_index("dp") * piece, piece, axis=1)
-    w_out_full = lax.all_gather(
-        lax.all_gather(w_out_piece, "mp", axis=0, tiled=True), "dp", axis=1, tiled=True
-    )
     x_rows = tokens.astype(jnp.float32)
     inverse1 = inverse_rms(x_rows)
     normed1 = (x_rows * inverse1 * norm1_gain).astype(jnp.bfloat16)
@@ -345,8 +365,11 @@
         )
 
     normed1_all, query_rows, key_rows, value_rows = ring_gather(normed1, "mp", project_qkv)
+    grad_rows, query_rows, w_out_piece = lax.optimization_barrier((out_grad, query_rows, w_out_piece))
+    w_out_full = lax.all_gather(
+        lax.all_gather(w_out_piece, "mp", axis=0, tiled=True), "dp", axis=1, tiled=True
+    )
     query_h, key_h, value_h = (to_heads(a) for a in (query_rows, key_rows, value_rows))
-    grad_rows, query_h = lax.optimization_barrier((out_grad, query_h))
     dot_out, log_sums = attention_fwd(query_h, key_h, value_h, doc_index, score_scale)
     query_f = query_h.astype(jnp.float32).reshape(seg_shape)
     key_f = key_h.astype(jnp.float32).reshape(seg_shape)

time: 1420 us -> 1350 us (0.951)
  Pallas kernels: 127 us -> 93 us
  starting transfers between devices: 92.4 us -> 69.1 us
    ppermute x9, waiting for transfers between devices: 106 us -> 83 us  [ring_gather(): behind = lax.ppermute(behind, axis, ring_pairs(n, -1))]
    pallas_call x1, Pallas kernels: 76.5 us -> 54.6 us  [attention_bwd(): pl.pallas_call(functools.partial(_bwd_kernel, scale, seg), grid=(H, nq),...]
    ppermute x9, starting transfers between devices: 22.4 us -> 7.84 us  [ring_gather(): ahead = lax.ppermute(ahead, axis, ring_pairs(n, 1))]
  transfers between devices with their start and end apart: 53 -> 53, of which waited for: 30 -> 31; matrix products, arithmetic and copies ran while one was open for 46% -> 47% of each run, Pallas kernels for 9% -> 7%
where the time goes in v9:
time: 1350 us; the launch traced here: 1340 us
  matrix products  460 us (34%)
  waiting for transfers between devices  427 us (32%)
  local copies, waits for them, and re-layouts  175 us (13%)
  Pallas kernels  93 us (7%)
  other arithmetic  92.7 us (7%)
  starting transfers between devices  69.1 us (5%)
  between operations  18.4 us (1%)
    dot_general x40, matrix products, __call__(): jnp.dot(lax.dynamic_slice_in_dim(lhs, first, count, 0), rhs, preferred_el...  126 us
    ppermute x9, waiting for transfers between devices, ring_scatter(): ahead = lax.ppermute(ahead.astype(kind), axis, ring_pairs(n, 1))  105 us
    ppermute x9, waiting for transfers between devices, ring_gather(): ahead = lax.ppermute(ahead, axis, ring_pairs(n, 1))  105 us
    ppermute x9, waiting for transfers between devices, ring_gather(): behind = lax.ppermute(behind, axis, ring_pairs(n, -1))  83 us
    ppermute x9, waiting for transfers between devices, ring_scatter(): behind = lax.ppermute(behind.astype(kind), axis, ring_pairs(n, -1))  75.4 us
    pallas_call x1, Pallas kernels, attention_bwd(): pl.pallas_call(functools.partial(_bwd_kernel, scale, seg), grid=(H, nq),...  54.6 us
    dot_general x14, matrix products, project_ffn(): jnp.dot(rows, weight, preferred_element_type=jnp.float32)  54.5 us
    dynamic_update_slice x35, local copies, waits for them, and re-layouts, ring_gather(): lax.dynamic_update_slice_in_dim(out, part, start, 0)  50.9 us
  transfers between devices with their start and end apart: 53, of which 31 were waited for; matrix products, arithmetic and copies ran while one was open for 47% of the time, Pallas kernels for 7%

profile of v9, /device:TPU:0, one launch (start us, length us, event | category | flops | bytes accessed | tf_op | source)
XLA Modules:
  0.0 1335.2 jit_solution(8661097936785064093)
XLA Ops:
  16.3 5.1 collective-permute-start.1
  39.8 5.4 collective-permute-done.1
  57.7 10.9 collective-permute-done
  101.6 12.8 collective-permute-done.2
  144.3 13.2 collective-permute-done.4
  200.2 24.0 %collective-permute-done.12 = bf16[256,2048]{1,0:T(8,128)(2,1)S(1)} collective-permute-done((bf16[256,2048]{1,0:T(8,128)(2,1)S(1)}, bf16[256,2048]{1,0:T(8,128)(2,1)S(1)}, u32[]{:S(2)}, u32[]{:S(2)}) %collective-permute-start.12) | collective-permute-done | bytes 1048608 | tf_op jit(solution)/shard_map/ppermute | solution.py:90
  230.2 15.0 %collective-permute-done.13 = bf16[256,2048]{1,0:T(8,128)(2,1)} collective-permute-done((bf16[256,2048]{1,0:T(8,128)(2,1)}, bf16[256,2048]{1,0:T(8,128)(2,1)}, u32[]{:S(2)}, u32[]{:S(2)}) %collective-permute-start.13) | collective-permute-done | bytes 1048608 | tf_op jit(solution)/shard_map/ppermute | solution.py:91
  248.4 38.3 %shard_map.220 = (f32[4,2048,128]{2,1,0:T(8,128)}, f32[4,2048,1]{2,1,0:T(8,128)}) custom-call(bf16[4,2048,128]{2,1,0:T(8,128)(2,1)} %bitcast.275, bf16[4,2048,128]{2,1,0:T(8,128)(2,1)} %bitcast.271, bf16[4,2048,128]{2,1,0:T(8,128)(2,1)} %bitcast.273, s32[2048,1]{1,0:T(8,128)} %copy.247.docq_ref, s32[1,2048]{1,0:T(1,128)} %bitcast.288), custom_call_target="tpu_custom_call" | custom-call | flops 8589934592 | bytes 10485760 | tf_op jit(solution)/shard_map/pallas_call | solution.py:266
  304.9 10.0 collective-permute-done.16
  316.0 19.1 %collective-permute-done.17 = bf16[256,2048]{1,0:T(8,128)(2,1)S(1)} collective-permute-done((bf16[256,2048]{1,0:T(8,128)(2,1)}, bf16[256,2048]{1,0:T(8,128)(2,1)S(1)}, u32[]{:S(2)}, u32[]{:S(2)}) %collective-permute-start.17) | collective-permute-done | bytes 1048608 | tf_op jit(solution)/shard_map/ppermute | solution.py:91
  344.5 5.1 fusion.48
  351.7 10.7 copy.248
  371.0 24.6 %fusion.255 = f32[2048,2048]{1,0:T(8,128)} fusion(bf16[2048,2048]{1,0:T(8,128)(2,1)} %constant_dynamic-update-slice_fusion.7, bf16[2048,2048]{1,0:T(8,128)(2,1)} %param.23), kind=kOutput, calls=%fused_computation.421 | convolution fusion | flops 17179869184 | bytes 33554432 | tf_op jit(solution)/shard_map/dot_general | solution.py:427
  395.6 24.0 %all-to-all-done = bf16[4,512,512]{2,1,0:T(8,128)(2,1)} async-done(((bf16[4,512,512]{2,1,0:T(8,128)(2,1)}), bf16[4,512,512]{2,1,0:T(8,128)(2,1)}, u32[]{:S(2)}, u32[]{:S(2)}) %all-to-all-start) | async-done | bytes 2097184 | tf_op jit(solution)/shard_map/all_to_all | solution.py:407
  423.8 9.8 multiply_reduce_fusion.4
  441.1 8.6 fusion.40
  450.7 8.2 fusion.41
  458.9 25.1 %collective-permute-done.7 = bf16[256,2048]{1,0:T(8,128)(2,1)} collective-permute-done((bf16[256,2048]{1,0:T(8,128)(2,1)}, bf16[256,2048]{1,0:T(8,128)(2,1)}, u32[]{:S(2)}, u32[]{:S(2)}) %collective-permute-start.7) | collective-permute-done | bytes 1048608 | tf_op jit(solution)/shard_map/ppermute | solution.py:91
  487.9 5.9 fusion.64
  493.8 6.2 fusion.63
  510.1 18.4 %collective-permute-done.9 = bf16[256,2048]{1,0:T(8,128)(2,1)S(1)} collective-permute-done((bf16[256,2048]{1,0:T(8,128)(2,1)}, bf16[256,2048]{1,0:T(8,128)(2,1)S(1)}, u32[]{:S(2)}, u32[]{:S(2)}) %collective-permute-start.9) | collective-permute-done | bytes 1048608 | tf_op jit(solution)/shard_map/ppermute | solution.py:91
  545.0 29.5 %collective-permute-done.10 = bf16[256,2048]{1,0:T(8,128)(2,1)S(1)} collective-permute-done((bf16[256,2048]{1,0:T(8,128)(2,1)S(1)}, bf16[256,2048]{1,0:T(8,128)(2,1)S(1)}, u32[]{:S(2)}, u32[]{:S(2)}) %collective-permute-start.10) | collective-permute-done | bytes 1048608 | tf_op jit(solution)/shard_map/ppermute | solution.py:90
  584.4 19.1 %fusion.9 = (bf16[2048,2048]{1,0:T(8,128)(2,1)}, bf16[2048,2048]{1,0:T(8,128)(2,1)}, bf16[2048,2048]{1,0:T(8,128)(2,1)}) fusion(f32[2048,2048]{1,0:T(8,128)} %fusion.255, bf16[2048,2048]{1,0:T(8,128)(2,1)S(1)} %fusion.65, bf16[2048,2048]{1,0:T(8,128)(2,1)S(1)} %fusion.59), kind=kLoop, calls=%fused_computation.15 | loop fusion | flops 75497472 | bytes 58720256 | tf_op jit(solution)/shard_map/convert_element_type | solution.py:430
  605.5 23.7 %convolution_convert_fusion.3 = bf16[2048,2048]{1,0:T(8,128)(2,1)} fusion(bf16[2048,2048]{1,0:T(8,128)(2,1)} %constant_dynamic-update-slice_fusion.14, bf16[2048,2048]{1,0:T(8,128)(2,1)} %get-tuple-element.128), kind=kOutput, calls=%fused_computation.24 | convolution fusion | flops 17184063488 | bytes 25165824 | tf_op jit(solution)/shard_map/dot_general | solution.py:432
  629.7 23.8 %convolution_convert_fusion.2 = bf16[2048,2048]{1,0:T(8,128)(2,1)} fusion(bf16[2048,2048]{1,0:T(8,128)(2,1)} %constant_dynamic-update-slice_fusion.14, bf16[2048,2048]{1,0:T(8,128)(2,1)} %get-tuple-element.129), kind=kOutput, calls=%fused_computation.23 | convolution fusion | flops 17184063488 | bytes 25165824 | tf_op jit(solution)/shard_map/dot_general | solution.py:433
  654.3 6.9 fusion.121
  661.2 6.5 fusion.56
  676.6 5.1 fusion.118
  681.7 5.1 fusion.139
  686.9 5.9 fusion.55
  692.7 22.6 %convolution_convert_fusion.1 = bf16[2048,2048]{1,0:T(8,128)(2,1)} fusion(bf16[2048,2048]{1,0:T(8,128)(2,1)S(1)} %bitcast.240, bf16[2048,2048]{1,0:T(8,128)(2,1)} %constant_dynamic-update-slice_fusion.7), kind=kOutput, calls=%fused_computation.22 | convolution fusion | flops 17184063488 | bytes 25165824 | tf_op jit(solution)/shard_map/dot_general | solution.py:434
  715.3 9.2 fusion.131
  724.5 7.5 fusion.136
  740.4 12.2 collective-permute-done.18
  752.6 5.5 add_convert_fusion.13
  763.1 12.1 collective-permute-done.22
  775.2 7.2 add_convert_fusion.10
  782.5 15.2 %collective-permute-done.19 = bf16[256,2048]{1,0:T(8,128)(2,1)} collective-permute-done((bf16[256,2048]{1,0:T(8,128)(2,1)}, bf16[256,2048]{1,0:T(8,128)(2,1)}, u32[]{:S(2)}, u32[]{:S(2)}) %collective-permute-start.19) | collective-permute-done | bytes 1048608 | tf_op jit(solution)/shard_map/ppermute | solution.py:114
  797.7 6.3 add_convert_fusion.12
  808.4 11.6 collective-permute-done.23
  820.0 6.4 convert_add_fusion.5
  826.4 15.3 %collective-permute-done.20 = bf16[256,2048]{1,0:T(8,128)(2,1)S(1)} collective-permute-done((bf16[256,2048]{1,0:T(8,128)(2,1)S(1)}, bf16[256,2048]{1,0:T(8,128)(2,1)S(1)}, u32[]{:S(2)}, u32[]{:S(2)}) %collective-permute-start.20) | collective-permute-done | bytes 1048608 | tf_op jit(solution)/shard_map/ppermute | solution.py:114
  841.6 6.3 convert_add_fusion.6
  852.5 9.8 convolution_convert_fusion.7
  868.8 24.2 %fusion.254 = f32[2048,2048]{1,0:T(8,128)} fusion(bf16[2048,2048]{1,0:T(8,128)(2,1)} %get-tuple-element.135, bf16[2048,2048]{1,0:T(8,128)(2,1)} %param.23), kind=kOutput, calls=%fused_computation.420 | convolution fusion | flops 17179869184 | bytes 33554432 | tf_op jit(solution)/shard_map/dot_general | solution.py:424
  893.0 23.2 %all-to-all-done.1 = bf16[512,4,512]{2,0,1:T(8,128)(2,1)} async-done(((bf16[512,4,512]{2,0,1:T(8,128)(2,1)}), bf16[512,4,512]{2,0,1:T(8,128)(2,1)}, u32[]{:S(2)}, u32[]{:S(2)}) %all-to-all-start.1) | async-done | bytes 2097184 | tf_op jit(solution)/shard_map/all_to_all | solution.py:448
  920.4 5.2 reshape.367
  935.8 7.9 multiply_reduce_fusion
  946.9 9.4 fusion.100
  957.1 10.7 convolution_convert_fusion
  987.3 54.6 %shard_map.221 = (f32[4,2048,128]{2,1,0:T(8,128)}, f32[4,2048,128]{2,1,0:T(8,128)}, f32[4,2048,128]{2,1,0:T(8,128)}) custom-call(bf16[4,2048,128]{2,1,0:T(8,128)(2,1)} %bitcast.276, bf16[4,2048,128]{2,1,0:T(8,128)(2,1)} %bitcast.272, bf16[4,2048,128]{2,1,0:T(8,128)(2,1)} %bitcast.274, bf16[4,2048,128]{2,1,0:T(8,128)(2,1)} %get-tuple-element.238.do_ref, ...), custom_call_target="tpu_custom_call" | custom-call | flops 21474836480 | bytes 25165824 | tf_op jit(solution)/shard_map/pallas_call | solution.py:291
  1056.2 6.0 fusion.53
  1066.2 9.9 convolution_convert_fusion.5
  1076.1 7.8 fusion.50
  1087.9 9.9 convolution_convert_fusion.4
  1098.9 13.3 collective-permute-done.28
  1122.3 10.0 fusion.54
  1136.4 8.7 convolution_convert_fusion.6
  1164.3 11.5 pad_maximum_fusion
  1191.6 20.6 %collective-permute-done.30 = bf16[256,2048]{1,0:T(8,128)(2,1)S(1)} collective-permute-done((bf16[256,2048]{1,0:T(8,128)(2,1)}, bf16[256,2048]{1,0:T(8,128)(2,1)S(1)}, u32[]{:S(2)}, u32[]{:S(2)}) %collective-permute-start.30) | collective-permute-done | bytes 1048608 | tf_op jit(solution)/shard_map/ppermute | solution.py:114
  1215.6 17.9 %collective-permute-done.34 = bf16[256,2048]{1,0:T(8,128)(2,1)S(1)} collective-permute-done((bf16[256,2048]{1,0:T(8,128)(2,1)S(1)}, bf16[256,2048]{1,0:T(8,128)(2,1)S(1)}, u32[]{:S(2)}, u32[]{:S(2)}) %collective-permute-start.34) | collective-permute-done | bytes 1048608 | tf_op jit(solution)/shard_map/ppermute | solution.py:115
  1234.6 22.6 %collective-permute-done.31 = bf16[256,2048]{1,0:T(8,128)(2,1)S(1)} collective-permute-done((bf16[256,2048]{1,0:T(8,128)(2,1)S(1)}, bf16[256,2048]{1,0:T(8,128)(2,1)S(1)}, u32[]{:S(2)}, u32[]{:S(2)}) %collective-permute-start.31) | collective-permute-done | bytes 1048608 | tf_op jit(solution)/shard_map/ppermute | solution.py:114
  1259.4 20.1 %collective-permute-done.35 = bf16[256,2048]{1,0:T(8,128)(2,1)S(1)} collective-permute-done((bf16[256,2048]{1,0:T(8,128)(2,1)S(1)}, bf16[256,2048]{1,0:T(8,128)(2,1)S(1)}, u32[]{:S(2)}, u32[]{:S(2)}) %collective-permute-start.35) | collective-permute-done | bytes 1048608 | tf_op jit(solution)/shard_map/ppermute | solution.py:115
  1279.8 19.2 %collective-permute-done.32 = bf16[256,2048]{1,0:T(8,128)(2,1)S(1)} collective-permute-done((bf16[256,2048]{1,0:T(8,128)(2,1)S(1)}, bf16[256,2048]{1,0:T(8,128)(2,1)S(1)}, u32[]{:S(2)}, u32[]{:S(2)}) %collective-permute-start.32) | collective-permute-done | bytes 1048608 | tf_op jit(solution)/shard_map/ppermute | solution.py:114
  (512 shorter events, 430.8 us)
Async XLA Ops:
  7.2 186.4 %all-gather.7.cloned.1.call-start = ((), (), s32[]{:S(2)}) async-start(), calls=%async_computation.8 | async-start | bytes 1310720 | tf_op jit(solution)/shard_map/all_gather | solution.py:370
  16.3 28.9 %collective-permute-start.1 = (bf16[256,2048]{1,0:T(8,128)(2,1)}, bf16[256,2048]{1,0:T(8,128)(2,1)}, u32[]{:S(2)}, u32[]{:S(2)}) collective-permute-start(bf16[256,2048]{1,0:T(8,128)(2,1)} %get-tuple-element.243), channel_id=1, source_target_pairs={{0,3},{1,0},{2,1},{3,2},{4,7},{5,4},{6,5},{7,6},{8,11},{9,8},{10,9... | collective-permute-start | bytes 3145736 | tf_op jit(solution)/shard_map/ppermute | solution.py:91
  21.4 47.3 %collective-permute-start = (bf16[256,2048]{1,0:T(8,128)(2,1)}, bf16[256,2048]{1,0:T(8,128)(2,1)}, u32[]{:S(2)}, u32[]{:S(2)}) collective-permute-start(bf16[256,2048]{1,0:T(8,128)(2,1)} %get-tuple-element.244), channel_id=1, source_target_pairs={{0,1},{1,2},{2,3},{3,0},{4,5},{5,6},{6,7},{7,4},{8,9},{9,10},{10,1... | collective-permute-start | bytes 3145736 | tf_op jit(solution)/shard_map/ppermute | solution.py:90
  23.5 201.3 %copy-start.63 = (s32[2048]{0:T(1024)}, s32[2048]{0:T(1024)S(1)}, u32[]{:S(2)}) copy-start(s32[2048]{0:T(1024)S(1)} %slice.70) | copy-start | bytes 24580
  30.6 153.6 %copy-start.69 = (f32[2048]{0:T(1024)}, f32[2048]{0:T(1024)S(1)}, u32[]{:S(2)}) copy-start(f32[2048]{0:T(1024)S(1)} %get-tuple-element.251) | copy-start | bytes 24580
  30.6 319.1 %copy-start.58 = (f32[2048]{0:T(1024)}, f32[2048]{0:T(1024)S(1)}, u32[]{:S(2)}) copy-start(f32[2048]{0:T(1024)S(1)} %get-tuple-element.250) | copy-start | bytes 24580
  45.2 50.2 %collective-permute-start.3 = (bf16[256,2048]{1,0:T(8,128)(2,1)}, bf16[256,2048]{1,0:T(8,128)(2,1)S(1)}, u32[]{:S(2)}, u32[]{:S(2)}) collective-permute-start(bf16[256,2048]{1,0:T(8,128)(2,1)} %collective-permute-done.1), channel_id=1, source_target_pairs={{0,3},{1,0},{2,1},{3,2},{4,7},{5,4},{6,5},{7,6},{8,11},{9,8},{10,9... | collective-permute-start | bytes 3145736 | tf_op jit(solution)/shard_map/ppermute | solution.py:91
  86.4 28.1 %collective-permute-start.2 = (bf16[256,2048]{1,0:T(8,128)(2,1)}, bf16[256,2048]{1,0:T(8,128)(2,1)S(1)}, u32[]{:S(2)}, u32[]{:S(2)}) collective-permute-start(bf16[256,2048]{1,0:T(8,128)(2,1)} %collective-permute-done), channel_id=1, source_target_pairs={{0,1},{1,2},{2,3},{3,0},{4,5},{5,6},{6,7},{7,4},{8,9},{9,10},{10,1... | collective-permute-start | bytes 3145736 | tf_op jit(solution)/shard_map/ppermute | solution.py:90
  95.5 43.9 %collective-permute-start.5 = (bf16[256,2048]{1,0:T(8,128)(2,1)S(1)}, bf16[256,2048]{1,0:T(8,128)(2,1)}, u32[]{:S(2)}, u32[]{:S(2)}) collective-permute-start(bf16[256,2048]{1,0:T(8,128)(2,1)S(1)} %collective-permute-done.3), channel_id=1, source_target_pairs={{0,3},{1,0},{2,1},{3,2},{4,7},{5,4},{6,5},{7,6},{8,11},{9,8},{10,9... | collective-permute-start | bytes 3145736 | tf_op jit(solution)/shard_map/ppermute | solution.py:91
  129.7 27.8 %collective-permute-start.4 = (bf16[256,2048]{1,0:T(8,128)(2,1)}, bf16[256,2048]{1,0:T(8,128)(2,1)}, u32[]{:S(2)}, u32[]{:S(2)}) collective-permute-start(bf16[256,2048]{1,0:T(8,128)(2,1)} %copy-done.48), channel_id=1, source_target_pairs={{0,1},{1,2},{2,3},{3,0},{4,5},{5,6},{6,7},{7,4},{8,9},{9,10},{10,1... | collective-permute-start | bytes 3145736 | tf_op jit(solution)/shard_map/ppermute | solution.py:90
  164.5 171.6 %all-gather.13.cloned.1.call-start = ((), (), s32[]{:S(2)}) async-start(), calls=%async_computation.17 | async-start | bytes 2396160 | tf_op jit(solution)/shard_map/all_gather | solution.py:26
  189.5 234.3 %all-gather.9.cloned.1.call-start = ((), (), s32[]{:S(2)}) async-start(), calls=%async_computation.9 | async-start | bytes 9437184 | tf_op jit(solution)/shard_map/all_gather | solution.py:369
  193.6 32.6 %copy-start.78 = (f32[4]{0:T(128)S(1)}, f32[4]{0:T(128)}, u32[]{:S(2)}) copy-start(f32[4]{0:T(128)} %param.19) | copy-start | bytes 52
  196.4 27.8 %collective-permute-start.12 = (bf16[256,2048]{1,0:T(8,128)(2,1)S(1)}, bf16[256,2048]{1,0:T(8,128)(2,1)S(1)}, u32[]{:S(2)}, u32[]{:S(2)}) collective-permute-start(bf16[256,2048]{1,0:T(8,128)(2,1)S(1)} %get-tuple-element.240), channel_id=1, source_target_pairs={{0,1},{1,2},{2,3},{3,0},{4,5},{5,6},{6,7},{7,4},{8,9},{9,10},{10,1... | collective-permute-start | bytes 3145736 | tf_op jit(solution)/shard_map/ppermute | solution.py:90
  197.8 47.4 %collective-permute-start.13 = (bf16[256,2048]{1,0:T(8,128)(2,1)}, bf16[256,2048]{1,0:T(8,128)(2,1)}, u32[]{:S(2)}, u32[]{:S(2)}) collective-permute-start(bf16[256,2048]{1,0:T(8,128)(2,1)} %get-tuple-element.239), channel_id=1, source_target_pairs={{0,3},{1,0},{2,1},{3,2},{4,7},{5,4},{6,5},{7,6},{8,11},{9,8},{10,9... | collective-permute-start | bytes 3145736 | tf_op jit(solution)/shard_map/ppermute | solution.py:91
  224.2 62.6 %collective-permute-start.14 = (bf16[256,2048]{1,0:T(8,128)(2,1)S(1)}, bf16[256,2048]{1,0:T(8,128)(2,1)}, u32[]{:S(2)}, u32[]{:S(2)}) collective-permute-start(bf16[256,2048]{1,0:T(8,128)(2,1)S(1)} %collective-permute-done.12), channel_id=1, source_target_pairs={{0,1},{1,2},{2,3},{3,0},{4,5},{5,6},{6,7},{7,4},{8,9},{9,10},{10,1... | collective-permute-start | bytes 3145736 | tf_op jit(solution)/shard_map/ppermute | solution.py:90
  226.2 123.4 %copy-start.71 = (f32[4]{0:T(128)}, f32[4]{0:T(128)S(1)}, u32[]{:S(2)}) copy-start(f32[4]{0:T(128)S(1)} %get-tuple-element.226) | copy-start | bytes 52
  226.3 123.4 %copy-start.73 = (f32[4]{0:T(128)}, f32[4]{0:T(128)S(1)}, u32[]{:S(2)}) copy-start(f32[4]{0:T(128)S(1)} %get-tuple-element.225) | copy-start | bytes 52
  245.2 47.5 %collective-permute-start.15 = (bf16[256,2048]{1,0:T(8,128)(2,1)}, bf16[256,2048]{1,0:T(8,128)(2,1)}, u32[]{:S(2)}, u32[]{:S(2)}) collective-permute-start(bf16[256,2048]{1,0:T(8,128)(2,1)} %collective-permute-done.13), channel_id=1, source_target_pairs={{0,3},{1,0},{2,1},{3,2},{4,7},{5,4},{6,5},{7,6},{8,11},{9,8},{10,9... | collective-permute-start | bytes 3145736 | tf_op jit(solution)/shard_map/ppermute | solution.py:91
  286.8 28.1 %collective-permute-start.16 = (bf16[256,2048]{1,0:T(8,128)(2,1)}, bf16[256,2048]{1,0:T(8,128)(2,1)S(1)}, u32[]{:S(2)}, u32[]{:S(2)}) collective-permute-start(bf16[256,2048]{1,0:T(8,128)(2,1)} %collective-permute-done.14), channel_id=1, source_target_pairs={{0,1},{1,2},{2,3},{3,0},{4,5},{5,6},{6,7},{7,4},{8,9},{9,10},{10,1... | collective-permute-start | bytes 3145736 | tf_op jit(solution)/shard_map/ppermute | solution.py:90
  292.7 42.3 %collective-permute-start.17 = (bf16[256,2048]{1,0:T(8,128)(2,1)}, bf16[256,2048]{1,0:T(8,128)(2,1)S(1)}, u32[]{:S(2)}, u32[]{:S(2)}) collective-permute-start(bf16[256,2048]{1,0:T(8,128)(2,1)} %collective-permute-done.15), channel_id=1, source_target_pairs={{0,3},{1,0},{2,1},{3,2},{4,7},{5,4},{6,5},{7,6},{8,11},{9,8},{10,9... | collective-permute-start | bytes 3145736 | tf_op jit(solution)/shard_map/ppermute | solution.py:91
  366.5 53.2 %all-to-all-start = ((bf16[4,512,512]{2,1,0:T(8,128)(2,1)}), bf16[4,512,512]{2,1,0:T(8,128)(2,1)}, u32[]{:S(2)}, u32[]{:S(2)}) async-start(bf16[4,512,512]{2,1,0:T(8,128)(2,1)} %convert_element_type.380), calls=%async_computation | async-start | bytes 4194304 | tf_op jit(solution)/shard_map/all_to_all | solution.py:407
  371.0 559.2 %reduce-scatter.7.cloned.1.call-start = ((), (), s32[]{:S(2)}) async-start(), calls=%async_computation.10 | async-start | bytes 9437184 | tf_op jit(solution)/shard_map/reduce_scatter | solution.py:344
  437.7 46.3 %collective-permute-start.7 = (bf16[256,2048]{1,0:T(8,128)(2,1)}, bf16[256,2048]{1,0:T(8,128)(2,1)}, u32[]{:S(2)}, u32[]{:S(2)}) collective-permute-start(bf16[256,2048]{1,0:T(8,128)(2,1)} %get-tuple-element.241), channel_id=1, source_target_pairs={{0,3},{1,0},{2,1},{3,2},{4,7},{5,4},{6,5},{7,6},{8,11},{9,8},{10,9... | collective-permute-start | bytes 3145736 | tf_op jit(solution)/shard_map/ppermute | solution.py:91
  440.0 45.9 %collective-permute-start.6 = (bf16[256,2048]{1,0:T(8,128)(2,1)}, bf16[256,2048]{1,0:T(8,128)(2,1)S(1)}, u32[]{:S(2)}, u32[]{:S(2)}) collective-permute-start(bf16[256,2048]{1,0:T(8,128)(2,1)} %get-tuple-element.242), channel_id=1, source_target_pairs={{0,1},{1,2},{2,3},{3,0},{4,5},{5,6},{6,7},{7,4},{8,9},{9,10},{10,1... | collective-permute-start | bytes 3145736 | tf_op jit(solution)/shard_map/ppermute | solution.py:90
  484.0 44.5 %collective-permute-start.9 = (bf16[256,2048]{1,0:T(8,128)(2,1)}, bf16[256,2048]{1,0:T(8,128)(2,1)S(1)}, u32[]{:S(2)}, u32[]{:S(2)}) collective-permute-start(bf16[256,2048]{1,0:T(8,128)(2,1)} %collective-permute-done.7), channel_id=1, source_target_pairs={{0,3},{1,0},{2,1},{3,2},{4,7},{5,4},{6,5},{7,6},{8,11},{9,8},{10,9... | collective-permute-start | bytes 3145736 | tf_op jit(solution)/shard_map/ppermute | solution.py:91
  485.9 45.0 %collective-permute-start.8 = (bf16[256,2048]{1,0:T(8,128)(2,1)S(1)}, bf16[256,2048]{1,0:T(8,128)(2,1)S(1)}, u32[]{:S(2)}, u32[]{:S(2)}) collective-permute-start(bf16[256,2048]{1,0:T(8,128)(2,1)S(1)} %collective-permute-done.6), channel_id=1, source_target_pairs={{0,1},{1,2},{2,3},{3,0},{4,5},{5,6},{6,7},{7,4},{8,9},{9,10},{10,1... | collective-permute-start | bytes 3145736 | tf_op jit(solution)/shard_map/ppermute | solution.py:90
  500.1 33.0 %slice-start.10 = ((s8[8388608]{0:T(1024)(128)(4,1)}), s8[4194304]{0:T(1024)(128)(4,1)S(1)}, s32[]{:S(2)}) async-start(s8[8388608]{0:T(1024)(128)(4,1)} %bitcast.304), calls=%async_computation.28 | async-start | bytes 8388608
  502.5 30.6 %slice-start.11 = ((s8[8388608]{0:T(1024)(128)(4,1)}), s8[4194304]{0:T(1024)(128)(4,1)S(1)}, s32[]{:S(2)}) async-start(s8[8388608]{0:T(1024)(128)(4,1)} %bitcast.304), calls=%async_computation.29 | async-start | bytes 8388608
  528.5 50.8 %collective-permute-start.11 = (bf16[256,2048]{1,0:T(8,128)(2,1)S(1)}, bf16[256,2048]{1,0:T(8,128)(2,1)S(1)}, u32[]{:S(2)}, u32[]{:S(2)}) collective-permute-start(bf16[256,2048]{1,0:T(8,128)(2,1)S(1)} %collective-permute-done.9), channel_id=1, source_target_pairs={{0,3},{1,0},{2,1},{3,2},{4,7},{5,4},{6,5},{7,6},{8,11},{9,8},{10,9... | collective-permute-start | bytes 3145736 | tf_op jit(solution)/shard_map/ppermute | solution.py:91
  530.9 43.5 %collective-permute-start.10 = (bf16[256,2048]{1,0:T(8,128)(2,1)S(1)}, bf16[256,2048]{1,0:T(8,128)(2,1)S(1)}, u32[]{:S(2)}, u32[]{:S(2)}) collective-permute-start(bf16[256,2048]{1,0:T(8,128)(2,1)S(1)} %collective-permute-done.8), channel_id=1, source_target_pairs={{0,1},{1,2},{2,3},{3,0},{4,5},{5,6},{6,7},{7,4},{8,9},{9,10},{10,1... | collective-permute-start | bytes 3145736 | tf_op jit(solution)/shard_map/ppermute | solution.py:90
  629.3 303.7 %reduce-scatter.9.cloned.1.call-start = ((), (), s32[]{:S(2)}) async-start(), calls=%async_computation.11 | async-start | bytes 9437184 | tf_op jit(solution)/shard_map/reduce_scatter | solution.py:344
  653.5 388.4 %reduce-scatter.11.cloned.1.call-start = ((), (), s32[]{:S(2)}) async-start(), calls=%async_computation.12 | async-start | bytes 9437184 | tf_op jit(solution)/shard_map/reduce_scatter | solution.py:344
  667.7 64.3 %collective-permute-start.21 = (bf16[256,2048]{1,0:T(8,128)(2,1)S(1)}, bf16[256,2048]{1,0:T(8,128)(2,1)}, u32[]{:S(2)}, u32[]{:S(2)}) collective-permute-start(bf16[256,2048]{1,0:T(8,128)(2,1)S(1)} %fusion.56), channel_id=1, source_target_pairs={{0,3},{1,0},{2,1},{3,2},{4,7},{5,4},{6,5},{7,6},{8,11},{9,8},{10,9... | collective-permute-start | bytes 3145736 | tf_op jit(solution)/shard_map/ppermute | solution.py:115
  724.5 28.1 %collective-permute-start.18 = (bf16[256,2048]{1,0:T(8,128)(2,1)}, bf16[256,2048]{1,0:T(8,128)(2,1)S(1)}, u32[]{:S(2)}, u32[]{:S(2)}) collective-permute-start(bf16[256,2048]{1,0:T(8,128)(2,1)} %fusion.55), channel_id=1, source_target_pairs={{0,1},{1,2},{2,3},{3,0},{4,5},{5,6},{6,7},{7,4},{8,9},{9,10},{10,1... | collective-permute-start | bytes 3145736 | tf_op jit(solution)/shard_map/ppermute | solution.py:114
  732.0 26.0 %slice-start.6 = ((s8[8388608]{0:T(1024)(128)(4,1)}), s8[4194304]{0:T(1024)(128)(4,1)S(1)}, s32[]{:S(2)}) async-start(s8[8388608]{0:T(1024)(128)(4,1)} %bitcast.300), calls=%async_computation.24 | async-start | bytes 8388608
  736.3 38.9 %collective-permute-start.22 = (bf16[256,2048]{1,0:T(8,128)(2,1)S(1)}, bf16[256,2048]{1,0:T(8,128)(2,1)}, u32[]{:S(2)}, u32[]{:S(2)}) collective-permute-start(bf16[256,2048]{1,0:T(8,128)(2,1)S(1)} %add_convert_fusion.11), channel_id=1, source_target_pairs={{0,3},{1,0},{2,1},{3,2},{4,7},{5,4},{6,5},{7,6},{8,11},{9,8},{10,9... | collective-permute-start | bytes 3145736 | tf_op jit(solution)/shard_map/ppermute | solution.py:115
  758.1 39.6 %collective-permute-start.19 = (bf16[256,2048]{1,0:T(8,128)(2,1)}, bf16[256,2048]{1,0:T(8,128)(2,1)}, u32[]{:S(2)}, u32[]{:S(2)}) collective-permute-start(bf16[256,2048]{1,0:T(8,128)(2,1)} %add_convert_fusion.13), channel_id=1, source_target_pairs={{0,1},{1,2},{2,3},{3,0},{4,5},{5,6},{6,7},{7,4},{8,9},{9,10},{10,1... | collective-permute-start | bytes 3145736 | tf_op jit(solution)/shard_map/ppermute | solution.py:114
  763.1 34.6 %copy-start.80 = (f32[256,2048]{1,0:T(8,128)S(1)}, f32[256,2048]{1,0:T(8,128)}, u32[]{:S(2)}) copy-start(f32[256,2048]{1,0:T(8,128)} %fusion.131) | copy-start | bytes 6291460
  775.2 29.1 %slice-start.8 = ((s8[8388608]{0:T(1024)(128)(4,1)}), s8[4194304]{0:T(1024)(128)(4,1)S(1)}, s32[]{:S(2)}) async-start(s8[8388608]{0:T(1024)(128)(4,1)} %bitcast.302), calls=%async_computation.26 | async-start | bytes 8388608
  782.4 37.6 %collective-permute-start.23 = (bf16[256,2048]{1,0:T(8,128)(2,1)S(1)}, bf16[256,2048]{1,0:T(8,128)(2,1)S(1)}, u32[]{:S(2)}, u32[]{:S(2)}) collective-permute-start(bf16[256,2048]{1,0:T(8,128)(2,1)S(1)} %add_convert_fusion.10), channel_id=1, source_target_pairs={{0,3},{1,0},{2,1},{3,2},{4,7},{5,4},{6,5},{7,6},{8,11},{9,8},{10,9... | collective-permute-start | bytes 3145736 | tf_op jit(solution)/shard_map/ppermute | solution.py:115
  804.1 37.6 %collective-permute-start.20 = (bf16[256,2048]{1,0:T(8,128)(2,1)S(1)}, bf16[256,2048]{1,0:T(8,128)(2,1)S(1)}, u32[]{:S(2)}, u32[]{:S(2)}) collective-permute-start(bf16[256,2048]{1,0:T(8,128)(2,1)S(1)} %add_convert_fusion.12), channel_id=1, source_target_pairs={{0,1},{1,2},{2,3},{3,0},{4,5},{5,6},{6,7},{7,4},{8,9},{9,10},{10,1... | collective-permute-start | bytes 3145736 | tf_op jit(solution)/shard_map/ppermute | solution.py:114
  863.8 52.4 %all-to-all-start.1 = ((bf16[512,4,512]{2,0,1:T(8,128)(2,1)}), bf16[512,4,512]{2,0,1:T(8,128)(2,1)}, u32[]{:S(2)}, u32[]{:S(2)}) async-start(bf16[512,4,512]{2,0,1:T(8,128)(2,1)} %bitcast.250), calls=%async_computation.1 | async-start | bytes 4194304 | tf_op jit(solution)/shard_map/all_to_all | solution.py:448
  868.3 185.3 %all-gather.11.cloned.1.call-start = ((), (), s32[]{:S(2)}) async-start(), calls=%async_computation.15 | async-start | bytes 1198080 | tf_op jit(solution)/shard_map/all_gather | solution.py:26
  957.1 119.0 %reduce-scatter.13.cloned.1.call-start = ((), (), s32[]{:S(2)}) async-start(), calls=%async_computation.13 | async-start | bytes 9437184 | tf_op jit(solution)/shard_map/reduce_scatter | solution.py:344
  967.8 152.7 %reduce-scatter.15.cloned.1.call-start = ((), (), s32[]{:S(2)}) async-start(), calls=%async_computation.14 | async-start | bytes 1310720 | tf_op jit(solution)/shard_map/reduce_scatter | solution.py:443
  983.5 61.3 %collective-permute-start.24 = (bf16[256,2048]{1,0:T(8,128)(2,1)}, bf16[256,2048]{1,0:T(8,128)(2,1)S(1)}, u32[]{:S(2)}, u32[]{:S(2)}) collective-permute-start(bf16[256,2048]{1,0:T(8,128)(2,1)} %get-tuple-element.236), channel_id=1, source_target_pairs={{0,1},{1,2},{2,3},{3,0},{4,5},{5,6},{6,7},{7,4},{8,9},{9,10},{10,1... | collective-permute-start | bytes 3145736 | tf_op jit(solution)/shard_map/ppermute | solution.py:114
  983.5 61.3 %collective-permute-start.27 = (bf16[256,2048]{1,0:T(8,128)(2,1)}, bf16[256,2048]{1,0:T(8,128)(2,1)}, u32[]{:S(2)}, u32[]{:S(2)}) collective-permute-start(bf16[256,2048]{1,0:T(8,128)(2,1)} %get-tuple-element.237), channel_id=1, source_target_pairs={{0,3},{1,0},{2,1},{3,2},{4,7},{5,4},{6,5},{7,6},{8,11},{9,8},{10,9... | collective-permute-start | bytes 3145736 | tf_op jit(solution)/shard_map/ppermute | solution.py:115
  1049.4 48.4 %collective-permute-start.25 = (bf16[256,2048]{1,0:T(8,128)(2,1)}, bf16[256,2048]{1,0:T(8,128)(2,1)S(1)}, u32[]{:S(2)}, u32[]{:S(2)}) collective-permute-start(bf16[256,2048]{1,0:T(8,128)(2,1)} %get-tuple-element.234), channel_id=1, source_target_pairs={{0,1},{1,2},{2,3},{3,0},{4,5},{5,6},{6,7},{7,4},{8,9},{9,10},{10,1... | collective-permute-start | bytes 3145736 | tf_op jit(solution)/shard_map/ppermute | solution.py:114
  1049.4 62.8 %collective-permute-start.28 = (bf16[256,2048]{1,0:T(8,128)(2,1)}, bf16[256,2048]{1,0:T(8,128)(2,1)}, u32[]{:S(2)}, u32[]{:S(2)}) collective-permute-start(bf16[256,2048]{1,0:T(8,128)(2,1)} %get-tuple-element.235), channel_id=1, source_target_pairs={{0,3},{1,0},{2,1},{3,2},{4,7},{5,4},{6,5},{7,6},{8,11},{9,8},{10,9... | collective-permute-start | bytes 3145736 | tf_op jit(solution)/shard_map/ppermute | solution.py:115
  1076.1 245.7 %reduce-scatter.17.cloned.1.call-start = ((), (), s32[]{:S(2)}) async-start(), calls=%async_computation.16 | async-start | bytes 7077888 | tf_op jit(solution)/shard_map/reduce_scatter | solution.py:344
  1116.7 187.9 %collective-permute-start.26 = (bf16[256,2048]{1,0:T(8,128)(2,1)}, bf16[256,2048]{1,0:T(8,128)(2,1)}, u32[]{:S(2)}, u32[]{:S(2)}) collective-permute-start(bf16[256,2048]{1,0:T(8,128)(2,1)} %get-tuple-element.232), channel_id=1, source_target_pairs={{0,1},{1,2},{2,3},{3,0},{4,5},{5,6},{6,7},{7,4},{8,9},{9,10},{10,1... | collective-permute-start | bytes 3145736 | tf_op jit(solution)/shard_map/ppermute | solution.py:114
  1116.7 187.9 %collective-permute-start.29 = (bf16[256,2048]{1,0:T(8,128)(2,1)S(1)}, bf16[256,2048]{1,0:T(8,128)(2,1)}, u32[]{:S(2)}, u32[]{:S(2)}) collective-permute-start(bf16[256,2048]{1,0:T(8,128)(2,1)S(1)} %get-tuple-element.233), channel_id=1, source_target_pairs={{0,3},{1,0},{2,1},{3,2},{4,7},{5,4},{6,5},{7,6},{8,11},{9,8},{10,9... | collective-permute-start | bytes 3145736 | tf_op jit(solution)/shard_map/ppermute | solution.py:115
  1160.9 24.7 %collective-permute-start.33 = (bf16[256,2048]{1,0:T(8,128)(2,1)}, bf16[256,2048]{1,0:T(8,128)(2,1)}, u32[]{:S(2)}, u32[]{:S(2)}) collective-permute-start(bf16[256,2048]{1,0:T(8,128)(2,1)} %fusion.58), channel_id=1, source_target_pairs={{0,3},{1,0},{2,1},{3,2},{4,7},{5,4},{6,5},{7,6},{8,11},{9,8},{10,9... | collective-permute-start | bytes 3145736 | tf_op jit(solution)/shard_map/ppermute | solution.py:115
  1175.9 36.3 %collective-permute-start.30 = (bf16[256,2048]{1,0:T(8,128)(2,1)}, bf16[256,2048]{1,0:T(8,128)(2,1)S(1)}, u32[]{:S(2)}, u32[]{:S(2)}) collective-permute-start(bf16[256,2048]{1,0:T(8,128)(2,1)} %fusion.57), channel_id=1, source_target_pairs={{0,1},{1,2},{2,3},{3,0},{4,5},{5,6},{6,7},{7,4},{8,9},{9,10},{10,1... | collective-permute-start | bytes 3145736 | tf_op jit(solution)/shard_map/ppermute | solution.py:114
  1189.6 43.9 %collective-permute-start.34 = (bf16[256,2048]{1,0:T(8,128)(2,1)S(1)}, bf16[256,2048]{1,0:T(8,128)(2,1)S(1)}, u32[]{:S(2)}, u32[]{:S(2)}) collective-permute-start(bf16[256,2048]{1,0:T(8,128)(2,1)S(1)} %add_convert_fusion.3), channel_id=1, source_target_pairs={{0,3},{1,0},{2,1},{3,2},{4,7},{5,4},{6,5},{7,6},{8,11},{9,8},{10,9... | collective-permute-start | bytes 3145736 | tf_op jit(solution)/shard_map/ppermute | solution.py:115
  1213.0 44.2 %collective-permute-start.31 = (bf16[256,2048]{1,0:T(8,128)(2,1)S(1)}, bf16[256,2048]{1,0:T(8,128)(2,1)S(1)}, u32[]{:S(2)}, u32[]{:S(2)}) collective-permute-start(bf16[256,2048]{1,0:T(8,128)(2,1)S(1)} %add_convert_fusion.5), channel_id=1, source_target_pairs={{0,1},{1,2},{2,3},{3,0},{4,5},{5,6},{6,7},{7,4},{8,9},{9,10},{10,1... | collective-permute-start | bytes 3145736 | tf_op jit(solution)/shard_map/ppermute | solution.py:114
  1233.8 45.7 %collective-permute-start.35 = (bf16[256,2048]{1,0:T(8,128)(2,1)S(1)}, bf16[256,2048]{1,0:T(8,128)(2,1)S(1)}, u32[]{:S(2)}, u32[]{:S(2)}) collective-permute-start(bf16[256,2048]{1,0:T(8,128)(2,1)S(1)} %add_convert_fusion.2), channel_id=1, source_target_pairs={{0,3},{1,0},{2,1},{3,2},{4,7},{5,4},{6,5},{7,6},{8,11},{9,8},{10,9... | collective-permute-start | bytes 3145736 | tf_op jit(solution)/shard_map/ppermute | solution.py:115
  1257.5 41.6 %collective-permute-start.32 = (bf16[256,2048]{1,0:T(8,128)(2,1)S(1)}, bf16[256,2048]{1,0:T(8,128)(2,1)S(1)}, u32[]{:S(2)}, u32[]{:S(2)}) collective-permute-start(bf16[256,2048]{1,0:T(8,128)(2,1)S(1)} %add_convert_fusion.4), channel_id=1, source_target_pairs={{0,1},{1,2},{2,3},{3,0},{4,5},{5,6},{6,7},{7,4},{8,9},{9,10},{10,1... | collective-permute-start | bytes 3145736 | tf_op jit(solution)/shard_map/ppermute | solution.py:114
  1300.7 3.8 collective-permute-start.36
  1304.5 4.7 collective-permute-start.37
  1309.2 2.0 collective-permute-start.38
  1311.2 3.8 collective-permute-start.39
  1315.1 5.6 collective-permute-start.40
  (87 other events, 645.5 us)
Sparse Core Ops, SparseCore 0:
  164.6 28.9 all-gather.6
  196.1 27.2 all-gather.12
  225.3 55.9 all-gather.8
  629.4 72.6 reduce-scatter.6
  705.4 71.4 reduce-scatter.8
  780.3 71.2 reduce-scatter.10
  957.2 22.3 all-gather.10
  983.1 71.2 reduce-scatter.12
  1076.2 38.3 reduce-scatter.14
  1176.0 61.1 reduce-scatter.16
